TPU v7x, 32 devices: a whole 2x2x4 slice. The times are simulated.
32 devices in a mesh: dp: 8 (over z, y), tensor: 4 (over x, core).
Axes of the slice: x: 2, y: 2, z: 4, core: 2. Of those that a mesh axis runs over, the one named last changes fastest.
Arguments:
- hidden: bfloat16 [2048, 1024], P('dp'), may hold values from -6 to 6
- lengths: int32 [8, 16], P('dp'), may hold values from 1 to 64, 256 in all within a row
- w_qkv: bfloat16 [3, 1024, 1024], P(None, None, 'tensor')
- b_qkv: float32 [3, 1024], P(None, 'tensor'), may hold values from -3 to 3
- w_output: bfloat16 [1024, 1024], P('tensor'), may hold values from -0.1875 to 0.1875
- b_output: float32 [1024], replicated, may hold values from -3 to 3
- first_gain: float32 [1024], replicated, may hold values from 0.25 to 1.75
- first_shift: float32 [1024], replicated, may hold values from -3 to 3
- w_up: bfloat16 [1024, 4096], P(None, 'tensor'), may hold values from -0.1875 to 0.1875
- b_up: float32 [4096], P('tensor'), may hold values from -3 to 3
- w_down: bfloat16 [4096, 1024], P('tensor'), may hold values from -0.09375 to 0.09375
- b_down: float32 [1024], replicated, may hold values from -3 to 3
- second_gain: float32 [1024], replicated, may hold values from 0.25 to 1.75
- second_shift: float32 [1024], replicated, may hold values from -3 to 3
- index: bfloat16 [16384, 1024], P('dp', 'tensor'), may hold values from -6 to 6
- candidates: int32 [128, 64], replicated, may hold values from 0 to 16383, as said below
Outputs:
- states: bfloat16 [2048, 1024], P('dp')
- scores: float32 [128, 64], P('dp')
Inputs may be any that keep to these rules, and one draw needn't show every extreme that they name: `candidates`: each index of dp holds exactly 1024 of the 8192 named rows, counted with repetition.
All inputs are finite; a program needn't handle non-finite values.
Results may differ from a plain program's by a relative error of at most 0.014.
Values may be sent and summed in bfloat16 or wider, within the bound.
No kernel may reach another device: no remote copies, remote signals or barrier semaphores. Data moves between devices by JAX's collectives and lax.ppermute only.
A program may use at most 64 MiB of HBM per device.

v0:
```python
import math

import jax
import jax.numpy as jnp
from jax import lax
from jax.sharding import PartitionSpec as P

HEAD = 64


def layer_norm(values, gain, shift):
    centre = jnp.mean(values, axis=-1, keepdims=True)
    centred = values - centre
    spread = jnp.mean(centred * centred, axis=-1, keepdims=True)
    return centred * lax.rsqrt(spread + 1e-05) * gain + shift


def segment_of(pack_lengths, count):
    ends = jnp.cumsum(pack_lengths)
    position = jnp.arange(count, dtype=jnp.int32)
    return jnp.sum((position[:, None] >= ends[None, :]).astype(jnp.int32), axis=1)


def settle_attention(partial_value, residual, bias, gain, shift):
    total = lax.psum(partial_value.astype(jnp.bfloat16), "tensor").astype(jnp.float32)
    return layer_norm(total + bias + residual.astype(jnp.float32), gain, shift).astype(jnp.bfloat16)


def settle_forward(partial_value, residual, bias, gain, shift):
    total = lax.psum(partial_value.astype(jnp.bfloat16), "tensor").astype(jnp.float32)
    return layer_norm(total + bias + residual.astype(jnp.float32), gain, shift).astype(jnp.bfloat16)


def body(
    hidden,
    lengths,
    w_qkv,
    b_qkv,
    w_output,
    b_output,
    first_gain,
    first_shift,
    w_up,
    b_up,
    w_down,
    b_down,
    second_gain,
    second_shift,
    index,
    candidates,
):
    tokens_here = hidden.shape[0]
    local_width = w_qkv.shape[2]
    local_heads = local_width // HEAD
    projected = [
        jnp.dot(hidden, w_qkv[j], preferred_element_type=jnp.float32) + b_qkv[j] for j in range(3)
    ]
    queries = (projected[0] * 0.125).astype(jnp.bfloat16).reshape(tokens_here, local_heads, HEAD)
    keys = projected[1].astype(jnp.bfloat16).reshape(tokens_here, local_heads, HEAD)
    values = projected[2].astype(jnp.bfloat16).reshape(tokens_here, local_heads, HEAD)
    segment = segment_of(lengths[0], tokens_here)
    same = segment[:, None] == segment[None, :]
    logits = jnp.einsum("thd,shd->hts", queries, keys, preferred_element_type=jnp.float32)
    logits = jnp.where(same[None], logits, -1e30)
    top = jnp.max(logits, axis=-1, keepdims=True)
    expo = jnp.exp(logits - top)
    weights = (expo / jnp.sum(expo, axis=-1, keepdims=True)).astype(jnp.bfloat16)
    context = jnp.einsum("hts,shd->thd", weights, values, preferred_element_type=jnp.float32)
    context = context.astype(jnp.bfloat16).reshape(tokens_here, local_width)
    partial_value = jnp.dot(context, w_output, preferred_element_type=jnp.float32)
    attended = settle_attention(partial_value, hidden, b_output, first_gain, first_shift)
    activated = jax.nn.gelu(
        jnp.dot(attended, w_up, preferred_element_type=jnp.float32) + b_up, approximate=False
    ).astype(jnp.bfloat16)
    partial_value = jnp.dot(activated, w_down, preferred_element_type=jnp.float32)
    states = settle_forward(partial_value, attended, b_down, second_gain, second_shift)
    texts_here = lengths.shape[1]
    member = (segment[None, :] == jnp.arange(texts_here, dtype=jnp.int32)[:, None]).astype(
        jnp.bfloat16
    )
    pooled = (
        jnp.dot(member, states, preferred_element_type=jnp.float32)
        / lengths[0].astype(jnp.float32)[:, None]
    )
    unit = pooled * lax.rsqrt(jnp.sum(pooled * pooled, axis=-1, keepdims=True) + 1e-06)
    quarter = index.shape[1]
    unit_quarter = lax.dynamic_slice_in_dim(
        unit, lax.axis_index("tensor") * quarter, quarter, 1
    ).astype(jnp.bfloat16)
    row_base = lax.axis_index("dp") * index.shape[0]
    gathered = lax.all_gather(unit_quarter, "dp", axis=0, tiled=True)
    all_texts = candidates.shape[0]
    cand_count = candidates.shape[1]
    shard_rows = index.shape[0]
    block_rows = math.gcd(all_texts, 128)
    block_count = all_texts // block_rows
    local_rows = candidates - row_base
    row_ids = jnp.arange(shard_rows, dtype=jnp.int32)

    def score_block(packed):
        query_block, wanted = packed
        tile = lax.dot_general(
            query_block, index, (((1,), (1,)), ((), ())), preferred_element_type=jnp.float32
        )
        chosen = wanted[:, :, None] == row_ids[None, None, :]
        return jnp.sum(jnp.where(chosen, tile[:, None, :], 0.0), axis=2)

    partial_scores = lax.map(
        score_block,
        (
            gathered.reshape(block_count, block_rows, quarter),
            local_rows.reshape(block_count, block_rows, cand_count),
        ),
    )
    partial_scores = partial_scores.reshape(all_texts, cand_count)
    slice_scores = lax.psum_scatter(
        partial_scores, ("dp", "tensor"), scatter_dimension=0, tiled=True
    )
    scores = lax.all_gather(slice_scores, "tensor", axis=0, tiled=True)
    return (states, scores)


def solution(mesh):
    placed = (
        P("dp", None),
        P("dp", None),
        P(None, None, "tensor"),
        P(None, "tensor"),
        P("tensor", None),
        P(),
        P(),
        P(),
        P(None, "tensor"),
        P("tensor"),
        P("tensor", None),
        P(),
        P(),
        P(),
        P("dp", "tensor"),
        P(),
    )
    return jax.shard_map(
        body, mesh=mesh, in_specs=placed, out_specs=(P("dp", None), P("dp", None)), check_vma=False
    )
```

profile of v0, /device:TPU:0, one launch (start us, length us, event | category | flops | bytes accessed | tf_op | source)
XLA Modules:
  0.0 194.0 jit_solution(16302811454098410085)
XLA Ops:
  7.2 0.9 fusion.90
  8.1 1.6 fusion.6
  9.7 1.6 fusion.5
  11.8 1.3 convolution_select_fusion
  13.1 0.5 fusion.91
  13.6 1.4 fusion.4
  15.0 2.0 %convolution_convert_fusion.2 = bf16[4,64,256]{2,1,0:T(8,128)(2,1)S(1)} fusion(bf16[256,4,64]{0,2,1:T(8,128)(2,1)S(1)} %bitcast.51, f32[4,256]{1,0:T(4,128)S(1)} %fusion.91, f32[4,256,256]{1,2,0:T(8,128)} %convolution_select_fusion), kind=kOutput, calls=%fused_computation.14 | convolution fusion | flops 34407680 | bytes 1314816 | tf_op jit(solution)/shard_map/hts,shd->thd/dot_general | solution.py:68
  17.1 1.1 convolution_convert_fusion
  18.3 36.0 %all-reduce.4.cloned.1.call-done = bf16[256,1024]{1,0:T(8,128)(2,1)} async-done(((bf16[256,1024]{1,0:T(8,128)(2,1)}), bf16[256,1024]{1,0:T(8,128)(2,1)}) %all-reduce.4.cloned.1.call-update) | async-done | bytes 524304 | tf_op jit(solution)/shard_map/psum | solution.py:25
  54.3 1.4 fusion.17
  55.6 1.4 multiply_reduce_fusion.1
  57.0 0.3 add_convert_fusion.1
  57.4 5.9 %convolution_convert_fusion.1 = bf16[256,1024]{1,0:T(8,128)(2,1)} fusion(bf16[1024,1024]{1,0:T(8,128)(2,1)S(1)} %copy-done, bf16[256,1024]{1,0:T(8,128)(2,1)S(1)} %add_convert_fusion.1, bf16[1024,1024]{1,0:T(8,128)(2,1)} %param.24, f32[1024]{0:T(1024)S(1)} %copy-done.15), kind=kOutput, calls=%fused_computation.9 | convolution fusion | flops 1091305472 | bytes 5246976 | tf_op jit(solution)/shard_map/dot_general | solution.py:75
  63.5 33.2 %all-reduce.6.cloned.1.call-done = bf16[256,1024]{1,0:T(8,128)(2,1)} async-done(((bf16[256,1024]{1,0:T(8,128)(2,1)}), bf16[256,1024]{1,0:T(8,128)(2,1)}) %all-reduce.6.cloned.1.call-update) | async-done | bytes 524304 | tf_op jit(solution)/shard_map/psum | solution.py:30
  96.7 1.4 fusion.18
  98.1 1.4 multiply_reduce_fusion
  99.5 0.3 add_convert_fusion
  99.9 0.3 multiply_reduce_fusion.2
  100.2 30.6 %all_gather.6 = bf16[128,256]{1,0:T(8,128)(2,1)S(1)} all-gather(bf16[16,256]{1,0:T(8,128)(2,1)S(1)} %fusion.56), channel_id=1, replica_groups=mesh['dp'=8,'tensor'=4] {'dp'}, dimensions={0}, use_global_device_ids=true | all-gather | bytes 73728 | tf_op jit(solution)/shard_map/all_gather | solution.py:91
  130.8 0.5 fusion.92
  131.3 10.9 %select_reduce_fusion = f32[128,64]{1,0:T(8,128)S(1)} fusion(f32[128,2048]{1,0:T(8,128)S(1)} %fusion.92, s32[128,64]{1,0:T(8,128)S(1)} %copy.29), kind=kLoop, calls=%fused_computation.1 | loop fusion | flops 50323456 | bytes 1114112 | tf_op jit(solution)/shard_map/while/body/eval_jaxpr/reduce_sum | solution.py:106
  142.2 38.8 %all-reduce = f32[128,64]{1,0:T(8,128)S(1)} all-reduce(f32[128,64]{1,0:T(8,128)S(1)} %select_reduce_fusion), channel_id=2, replica_groups=mesh['dp'=8,'tensor'=4] {'dp','tensor'}, use_global_device_ids=true, to_apply=%region_12.13.clone | all-reduce | flops 8192 | bytes 65536
  181.1 5.4 %all-gather = f32[4,4,64]{2,1,0:T(4,128)S(1)} all-gather(f32[1,4,64]{2,1,0:T(4,128)S(1)} %dynamic-slice_bitcast_fusion), channel_id=1, replica_groups=mesh['dp'=8,'tensor'=4] {'tensor'}, dimensions={0}, use_global_device_ids=true | all-gather | bytes 5120 | tf_op jit(solution)/shard_map/all_gather | solution.py:119
  186.5 0.6 copy.34
  (51 shorter events, 0.9 us)
Async XLA Ops:
  7.2 50.2 %copy-start = (bf16[1024,1024]{1,0:T(8,128)(2,1)S(1)}, bf16[1024,1024]{1,0:T(8,128)(2,1)}, u32[]{:S(2)}) copy-start(bf16[1024,1024]{1,0:T(8,128)(2,1)} %param.26) | copy-start | bytes 6291460
  7.2 4.1 %copy-start.14 = (s32[1,16]{1,0:T(1,128)S(1)}, s32[1,16]{1,0:T(1,128)}, u32[]{:S(2)}) copy-start(s32[1,16]{1,0:T(1,128)} %param.17) | copy-start | bytes 196
  7.2 47.1 %all-reduce.4.cloned.1.call-start = ((), (), s32[]{:S(2)}) async-start(), calls=%async_computation | async-start | bytes 1048576 | tf_op jit(solution)/shard_map/psum | solution.py:25
  9.7 3.9 %copy-start.1 = (bf16[256,1024]{1,0:T(8,128)(2,1)S(1)}, bf16[256,1024]{1,0:T(8,128)(2,1)}, u32[]{:S(2)}) copy-start(bf16[256,1024]{1,0:T(8,128)(2,1)} %param.16) | copy-start | bytes 1572868
  15.0 2.0 %copy-start.6 = (bf16[256,1024]{1,0:T(8,128)(2,1)S(1)}, bf16[256,1024]{1,0:T(8,128)(2,1)}, u32[]{:S(2)}) copy-start(bf16[256,1024]{1,0:T(8,128)(2,1)} %param.20) | copy-start | bytes 1572868
  15.0 39.2 %copy-start.7 = (f32[1024]{0:T(1024)S(1)}, f32[1024]{0:T(1024)}, u32[]{:S(2)}) copy-start(f32[1024]{0:T(1024)} %param.21) | copy-start | bytes 12292
  17.0 40.0 %copy-start.10 = (f32[1024]{0:T(1024)S(1)}, f32[1024]{0:T(1024)}, u32[]{:S(2)}) copy-start(f32[1024]{0:T(1024)} %param.23) | copy-start | bytes 12292
  17.0 40.0 %copy-start.11 = (f32[1024]{0:T(1024)S(1)}, f32[1024]{0:T(1024)}, u32[]{:S(2)}) copy-start(f32[1024]{0:T(1024)} %param.22) | copy-start | bytes 12292
  18.2 39.2 %copy-start.15 = (f32[1024]{0:T(1024)S(1)}, f32[1024]{0:T(1024)}, u32[]{:S(2)}) copy-start(f32[1024]{0:T(1024)} %param.25) | copy-start | bytes 12292
  18.2 78.5 %all-reduce.6.cloned.1.call-start = ((), (), s32[]{:S(2)}) async-start(), calls=%async_computation.1 | async-start | bytes 1048576 | tf_op jit(solution)/shard_map/psum | solution.py:30
  54.2 2.8 %copy-start.3 = (bf16[256,1024]{1,0:T(8,128)(2,1)S(1)}, bf16[256,1024]{1,0:T(8,128)(2,1)}, u32[]{:S(2)}) copy-start(bf16[256,1024]{1,0:T(8,128)(2,1)} %all-reduce.4.cloned.1.call-done) | copy-start | bytes 1572868
  57.4 6.0 %copy-start.9 = (s32[128,64]{0,1:T(8,128)S(1)}, s32[128,64]{0,1:T(8,128)}, u32[]{:S(2)}) copy-start(s32[128,64]{0,1:T(8,128)} %param.31) | copy-start | bytes 98308
  57.4 39.3 %copy-start.8 = (f32[1024]{0:T(1024)S(1)}, f32[1024]{0:T(1024)}, u32[]{:S(2)}) copy-start(f32[1024]{0:T(1024)} %param.27) | copy-start | bytes 12292
  63.3 36.2 %copy-start.12 = (f32[1024]{0:T(1024)S(1)}, f32[1024]{0:T(1024)}, u32[]{:S(2)}) copy-start(f32[1024]{0:T(1024)} %param.29) | copy-start | bytes 12292
  63.3 36.2 %copy-start.13 = (f32[1024]{0:T(1024)S(1)}, f32[1024]{0:T(1024)}, u32[]{:S(2)}) copy-start(f32[1024]{0:T(1024)} %param.28) | copy-start | bytes 12292
  96.7 2.8 %copy-start.2 = (bf16[256,1024]{1,0:T(8,128)(2,1)S(1)}, bf16[256,1024]{1,0:T(8,128)(2,1)}, u32[]{:S(2)}) copy-start(bf16[256,1024]{1,0:T(8,128)(2,1)} %all-reduce.6.cloned.1.call-done) | copy-start | bytes 1572868
  96.7 34.1 %copy-start.5 = (bf16[2048,256]{1,0:T(8,128)(2,1)S(1)}, bf16[2048,256]{1,0:T(8,128)(2,1)}, u32[]{:S(2)}) copy-start(bf16[2048,256]{1,0:T(8,128)(2,1)} %param.30) | copy-start | bytes 3145732
  99.8 87.3 %copy-start.4 = (bf16[256,1024]{1,0:T(8,128)(2,1)}, bf16[256,1024]{1,0:T(8,128)(2,1)S(1)}, u32[]{:S(2)}) copy-start(bf16[256,1024]{1,0:T(8,128)(2,1)S(1)} %add_convert_fusion) | copy-start | bytes 1572868
Sparse Core Ops, SparseCore 0:
  18.3 35.8 all-reduce.3
  63.4 33.1 all-reduce.5
where the time goes:
time: 195 us; the launch traced here: 194 us
  blocking collectives  74.8 us (38%)
  waiting for transfers between devices  69.2 us (35%)
  other arithmetic  17.6 us (9%)
  matrix products  16.2 us (8%)
  between operations  14.3 us (7%)
    unnamed x1, blocking collectives  38.8 us
    psum x1, waiting for transfers between devices, settle_attention(): lax.psum(partial_value.astype(jnp.bfloat16), 'tensor').astype(jnp.float32)  36 us
    psum x1, waiting for transfers between devices, settle_forward(): lax.psum(partial_value.astype(jnp.bfloat16), 'tensor').astype(jnp.float32)  33.2 us
    all_gather x1, blocking collectives, body(): gathered = lax.all_gather(unit_quarter, 'dp', axis=0, tiled=True)  30.6 us
    reduce_sum x1, other arithmetic, score_block(): return jnp.sum(jnp.where(chosen, tile[:, None, :], 0.0), axis=2)  10.9 us
    dot_general x1, matrix products, body(): jnp.dot(activated, w_down, preferred_element_type=jnp.float32)  5.9 us
    all_gather x1, blocking collectives, body(): scores = lax.all_gather(slice_scores, 'tensor', axis=0, tiled=True)  5.43 us
    dot_general x3, matrix products, body(): jnp.dot(hidden, w_qkv[j], preferred_element_type=jnp.float32) + b_qkv[j]  4.58 us
  transfers between devices with their start and end apart: 2, of which 2 were waited for; matrix products, arithmetic and copies ran while one was open for 0% of the time, Pallas kernels for 0%

commit v1 on v0

--- a/solution.py
+++ b/solution.py
@@ -21,14 +21,60 @@
     return jnp.sum((position[:, None] >= ends[None, :]).astype(jnp.int32), axis=1)
 
 
-def settle_attention(partial_value, residual, bias, gain, shift):
-    total = lax.psum(partial_value.astype(jnp.bfloat16), "tensor").astype(jnp.float32)
-    return layer_norm(total + bias + residual.astype(jnp.float32), gain, shift).astype(jnp.bfloat16)
-
-
-def settle_forward(partial_value, residual, bias, gain, shift):
-    total = lax.psum(partial_value.astype(jnp.bfloat16), "tensor").astype(jnp.float32)
-    return layer_norm(total + bias + residual.astype(jnp.float32), gain, shift).astype(jnp.bfloat16)
+def is_power_of_two(n):
+    return n >= 1 and (n & (n - 1)) == 0
+
+
+def xor_pairs(n, k):
+    return [(i, i ^ k) for i in range(n)]
+
+
+def levels_of(n):
+    return [1 << j for j in range(int(math.log2(n)))] if n > 1 else []
+
+
+def reduce_scatter_xor(value, axis, n, levels):
+    index = lax.axis_index(axis)
+    acc = value
+    block = 0
+    count = 1
+    for k in levels:
+        half = acc.shape[0] // 2
+        bit = (index // k) % 2
+        mine = lax.dynamic_slice_in_dim(acc, bit * half, half, 0)
+        theirs = lax.dynamic_slice_in_dim(acc, (1 - bit) * half, half, 0)
+        wire = jnp.float32 if value.dtype == jnp.float32 else jnp.bfloat16
+        got = lax.ppermute(theirs.astype(wire), axis, xor_pairs(n, k))
+        acc = mine.astype(jnp.float32) + got.astype(jnp.float32)
+        count *= 2
+        block = block * 2 + bit
+    return acc, block
+
+
+def all_gather_xor(value, axis, n, levels):
+    index = lax.axis_index(axis)
+    cur = value
+    for k in levels:
+        other = lax.ppermute(cur, axis, xor_pairs(n, k))
+        bit = (index // k) % 2
+        cur = jnp.where(bit == 0, jnp.concatenate([cur, other]), jnp.concatenate([other, cur]))
+    return cur
+
+
+def settle(partial_value, residual, bias, gain, shift, n_tensor):
+    if not is_power_of_two(n_tensor) or partial_value.shape[0] % n_tensor:
+        total = lax.psum(partial_value.astype(jnp.bfloat16), "tensor").astype(jnp.float32)
+        return layer_norm(total + bias + residual.astype(jnp.float32), gain, shift).astype(
+            jnp.bfloat16
+        )
+    levels = levels_of(n_tensor)
+    total, block = reduce_scatter_xor(partial_value.astype(jnp.bfloat16), "tensor", n_tensor, levels)
+    rows = total.shape[0]
+    own_residual = lax.dynamic_slice_in_dim(residual, block * rows, rows, 0)
+    normed = layer_norm(total + bias + own_residual.astype(jnp.float32), gain, shift).astype(
+        jnp.bfloat16
+    )
+    return all_gather_xor(normed, "tensor", n_tensor, levels[::-1])
 
 
 def body(
@@ -48,6 +94,8 @@
     second_shift,
     index,
     candidates,
+    n_dp,
+    n_tensor,
 ):
     tokens_here = hidden.shape[0]
     local_width = w_qkv.shape[2]
@@ -68,12 +116,12 @@
     context = jnp.einsum("hts,shd->thd", weights, values, preferred_element_type=jnp.float32)
     context = context.astype(jnp.bfloat16).reshape(tokens_here, local_width)
     partial_value = jnp.dot(context, w_output, preferred_element_type=jnp.float32)
-    attended = settle_attention(partial_value, hidden, b_output, first_gain, first_shift)
+    attended = settle(partial_value, hidden, b_output, first_gain, first_shift, n_tensor)
     activated = jax.nn.gelu(
         jnp.dot(attended, w_up, preferred_element_type=jnp.float32) + b_up, approximate=False
     ).astype(jnp.bfloat16)
     partial_value = jnp.dot(activated, w_down, preferred_element_type=jnp.float32)
-    states = settle_forward(partial_value, attended, b_down, second_gain, second_shift)
+    states = settle(partial_value, attended, b_down, second_gain, second_shift, n_tensor)
     texts_here = lengths.shape[1]
     member = (segment[None, :] == jnp.arange(texts_here, dtype=jnp.int32)[:, None]).astype(
         jnp.bfloat16
@@ -88,7 +136,15 @@
         unit, lax.axis_index("tensor") * quarter, quarter, 1
     ).astype(jnp.bfloat16)
     row_base = lax.axis_index("dp") * index.shape[0]
-    gathered = lax.all_gather(unit_quarter, "dp", axis=0, tiled=True)
+    xor_ok = (
+        is_power_of_two(n_dp)
+        and is_power_of_two(n_tensor)
+        and candidates.shape[0] % n_dp == 0
+    )
+    if xor_ok:
+        gathered = all_gather_xor(unit_quarter, "dp", n_dp, levels_of(n_dp))
+    else:
+        gathered = lax.all_gather(unit_quarter, "dp", axis=0, tiled=True)
     all_texts = candidates.shape[0]
     cand_count = candidates.shape[1]
     shard_rows = index.shape[0]
@@ -113,11 +169,16 @@
         ),
     )
     partial_scores = partial_scores.reshape(all_texts, cand_count)
-    slice_scores = lax.psum_scatter(
-        partial_scores, ("dp", "tensor"), scatter_dimension=0, tiled=True
-    )
-    scores = lax.all_gather(slice_scores, "tensor", axis=0, tiled=True)
-    return (states, scores)
+    if not xor_ok:
+        slice_scores = lax.psum_scatter(
+            partial_scores, ("dp", "tensor"), scatter_dimension=0, tiled=True
+        )
+        scores = lax.all_gather(slice_scores, "tensor", axis=0, tiled=True)
+        return (states, scores)
+    text_scores, _ = reduce_scatter_xor(partial_scores, "dp", n_dp, levels_of(n_dp)[::-1])
+    for k in levels_of(n_tensor):
+        text_scores = text_scores + lax.ppermute(text_scores, "tensor", xor_pairs(n_tensor, k))
+    return (states, text_scores)
 
 
 def solution(mesh):
@@ -139,6 +200,12 @@
         P("dp", "tensor"),
         P(),
     )
+    n_dp = mesh.shape["dp"]
+    n_tensor = mesh.shape["tensor"]
+
+    def run(*args):
+        return body(*args, n_dp=n_dp, n_tensor=n_tensor)
+
     return jax.shard_map(
-        body, mesh=mesh, in_specs=placed, out_specs=(P("dp", None), P("dp", None)), check_vma=False
-    )
+        run, mesh=mesh, in_specs=placed, out_specs=(P("dp", None), P("dp", None)), check_vma=False
+    )

time: 195 us -> 89.5 us (0.46)
  blocking collectives: 74.8 us -> 0 us
  waiting for transfers between devices: 69.2 us -> 34.7 us
  starting transfers between devices: 0.08 us -> 23.5 us
  between operations: 14.3 us -> 1.03 us
  other arithmetic: 17.6 us -> 14.4 us
    psum x2 -> x0, waiting for transfers between devices: 69.2 us -> none  [the longest x1 36 us: settle_attention(): lax.psum(partial_value.astype(jnp.bfloat16), 'tensor').astype(jnp.float32)]
    unnamed x1 -> x0, blocking collectives: 38.8 us -> none
    all_gather x2 -> x0, blocking collectives: 36 us -> none  [the longest x1 30.6 us: body(): gathered = lax.all_gather(unit_quarter, 'dp', axis=0, tiled=True)]
    ppermute x0 -> x16, waiting for transfers between devices: none -> 34.7 us  [the longest x7 16.1 us: reduce_scatter_xor(): got = lax.ppermute(theirs.astype(wire), axis, xor_pairs(n, k))]
    ppermute x0 -> x16, starting transfers between devices: none -> 23.5 us  [the longest x7 11.8 us: reduce_scatter_xor(): got = lax.ppermute(theirs.astype(wire), axis, xor_pairs(n, k))]
    reduce_sum x2, other arithmetic: 2.74 us -> 0.39 us  [layer_norm(): spread = jnp.mean(centred * centred, axis=-1, keepdims=True)]
  transfers between devices with their start and end apart: 2 -> 16, of which waited for: 2 -> 16; matrix products, arithmetic and copies ran while one was open for 0% -> 0% of each run, Pallas kernels for 0% -> 0%
where the time goes in v1:
time: 89.5 us; the launch traced here: 89.2 us
  waiting for transfers between devices  34.7 us (39%)
  starting transfers between devices  23.5 us (26%)
  matrix products  14.4 us (16%)
  other arithmetic  14.4 us (16%)
  local copies, waits for them, and re-layouts  1.23 us (1%)
  between operations  1.03 us (1%)
    ppermute x7, waiting for transfers between devices, reduce_scatter_xor(): got = lax.ppermute(theirs.astype(wire), axis, xor_pairs(n, k))  16.1 us
    ppermute x7, waiting for transfers between devices, all_gather_xor(): other = lax.ppermute(cur, axis, xor_pairs(n, k))  15.4 us
    ppermute x7, starting transfers between devices, reduce_scatter_xor(): got = lax.ppermute(theirs.astype(wire), axis, xor_pairs(n, k))  11.8 us
    reduce_sum x1, other arithmetic, score_block(): return jnp.sum(jnp.where(chosen, tile[:, None, :], 0.0), axis=2)  10.9 us
    ppermute x7, starting transfers between devices, all_gather_xor(): other = lax.ppermute(cur, axis, xor_pairs(n, k))  10 us
    dot_general x1, matrix products, body(): jnp.dot(activated, w_down, preferred_element_type=jnp.float32)  5.11 us
    dot_general x3, matrix products, body(): jnp.dot(hidden, w_qkv[j], preferred_element_type=jnp.float32) + b_qkv[j]  4.68 us
    ppermute x2, waiting for transfers between devices, body(): lax.ppermute(text_scores, 'tensor', xor_pairs(n_tensor, k))  3.15 us
  transfers between devices with their start and end apart: 16, of which 16 were waited for; matrix products, arithmetic and copies ran while one was open for 0% of the time, Pallas kernels for 0%

profile of v1, /device:TPU:0, one launch (start us, length us, event | category | flops | bytes accessed | tf_op | source)
XLA Modules:
  0.0 89.2 jit_solution(11546857113439211476)
XLA Ops:
  11.2 2.9 %collective-permute-start.1 = (bf16[64,1024]{1,0:T(8,128)(2,1)S(1)}, bf16[64,1024]{1,0:T(8,128)(2,1)S(1)}, u32[]{:S(2)}, u32[]{:S(2)}) collective-permute-start(bf16[64,1024]{1,0:T(8,128)(2,1)S(1)} %dynamic-slice_convert_fusion.1), channel_id=1, source_target_pairs={{0,2},{1,3},{2,0},{3,1},{4,6},{5,7},{6,4},{7,5},{8,10},{9,11},{10,... | collective-permute-start | bytes 393224 | tf_op jit(solution)/shard_map/ppermute | solution.py:47
  14.1 3.8 %collective-permute-done.1 = bf16[64,1024]{1,0:T(8,128)(2,1)S(1)} collective-permute-done((bf16[64,1024]{1,0:T(8,128)(2,1)S(1)}, bf16[64,1024]{1,0:T(8,128)(2,1)S(1)}, u32[]{:S(2)}, u32[]{:S(2)}) %collective-permute-start.1) | collective-permute-done | bytes 131104 | tf_op jit(solution)/shard_map/ppermute | solution.py:47
  19.3 1.8 %collective-permute-start.2 = (bf16[64,1024]{1,0:T(8,128)(2,1)S(1)}, bf16[64,1024]{1,0:T(8,128)(2,1)S(1)}, u32[]{:S(2)}, u32[]{:S(2)}) collective-permute-start(bf16[64,1024]{1,0:T(8,128)(2,1)S(1)} %add_convert_fusion.1), channel_id=1, source_target_pairs={{0,2},{1,3},{2,0},{3,1},{4,6},{5,7},{6,4},{7,5},{8,10},{9,11},{10,... | collective-permute-start | bytes 393224 | tf_op jit(solution)/shard_map/ppermute | solution.py:58
  21.1 3.3 %collective-permute-done.2 = bf16[64,1024]{1,0:T(8,128)(2,1)S(1)} collective-permute-done((bf16[64,1024]{1,0:T(8,128)(2,1)S(1)}, bf16[64,1024]{1,0:T(8,128)(2,1)S(1)}, u32[]{:S(2)}, u32[]{:S(2)}) %collective-permute-start.2) | collective-permute-done | bytes 131104 | tf_op jit(solution)/shard_map/ppermute | solution.py:58
  26.3 5.1 %convolution_convert_fusion.1 = bf16[256,1024]{1,0:T(8,128)(2,1)S(1)} fusion(bf16[1024,1024]{1,0:T(8,128)(2,1)S(1)} %copy-done, bf16[256,1024]{1,0:T(8,128)(2,1)S(1)} %maximum_select_fusion, bf16[1024,1024]{1,0:T(8,128)(2,1)} %param.24, f32[1024]{0:T(1024)S(1)} %copy-done.10), kind=kOutput, calls=%fused_computation.9 | convolution fusion | flops 1091305472 | bytes 5246976 | tf_op jit(solution)/shard_map/dot_general | solution.py:123
  33.2 1.8 %collective-permute-start.5 = (bf16[64,1024]{1,0:T(8,128)(2,1)S(1)}, bf16[64,1024]{1,0:T(8,128)(2,1)S(1)}, u32[]{:S(2)}, u32[]{:S(2)}) collective-permute-start(bf16[64,1024]{1,0:T(8,128)(2,1)S(1)} %dynamic-slice_convert_fusion), channel_id=1, source_target_pairs={{0,2},{1,3},{2,0},{3,1},{4,6},{5,7},{6,4},{7,5},{8,10},{9,11},{10,... | collective-permute-start | bytes 393224 | tf_op jit(solution)/shard_map/ppermute | solution.py:47
  34.9 3.9 %collective-permute-done.5 = bf16[64,1024]{1,0:T(8,128)(2,1)S(1)} collective-permute-done((bf16[64,1024]{1,0:T(8,128)(2,1)S(1)}, bf16[64,1024]{1,0:T(8,128)(2,1)S(1)}, u32[]{:S(2)}, u32[]{:S(2)}) %collective-permute-start.5) | collective-permute-done | bytes 131104 | tf_op jit(solution)/shard_map/ppermute | solution.py:47
  39.3 1.7 %collective-permute-start.6 = (bf16[64,1024]{1,0:T(8,128)(2,1)S(1)}, bf16[64,1024]{1,0:T(8,128)(2,1)S(1)}, u32[]{:S(2)}, u32[]{:S(2)}) collective-permute-start(bf16[64,1024]{1,0:T(8,128)(2,1)S(1)} %add_convert_fusion), channel_id=1, source_target_pairs={{0,2},{1,3},{2,0},{3,1},{4,6},{5,7},{6,4},{7,5},{8,10},{9,11},{10,... | collective-permute-start | bytes 393224 | tf_op jit(solution)/shard_map/ppermute | solution.py:58
  41.0 3.3 %collective-permute-done.6 = bf16[64,1024]{1,0:T(8,128)(2,1)S(1)} collective-permute-done((bf16[64,1024]{1,0:T(8,128)(2,1)S(1)}, bf16[64,1024]{1,0:T(8,128)(2,1)S(1)}, u32[]{:S(2)}, u32[]{:S(2)}) %collective-permute-start.6) | collective-permute-done | bytes 131104 | tf_op jit(solution)/shard_map/ppermute | solution.py:58
  46.5 1.7 %collective-permute-start.8 = (bf16[16,256]{1,0:T(8,128)(2,1)S(1)}, bf16[16,256]{1,0:T(8,128)(2,1)S(1)}, u32[]{:S(2)}, u32[]{:S(2)}) collective-permute-start(bf16[16,256]{1,0:T(8,128)(2,1)S(1)} %fusion.61), channel_id=1, source_target_pairs={{0,4},{4,0},{8,12},{12,8},{16,20},{20,16},{24,28},{28,24},{1,5},{5... | collective-permute-start | bytes 24584 | tf_op jit(solution)/shard_map/ppermute | solution.py:58
  48.2 1.9 %collective-permute-done.8 = bf16[16,256]{1,0:T(8,128)(2,1)S(1)} collective-permute-done((bf16[16,256]{1,0:T(8,128)(2,1)S(1)}, bf16[16,256]{1,0:T(8,128)(2,1)S(1)}, u32[]{:S(2)}, u32[]{:S(2)}) %collective-permute-start.8) | collective-permute-done | bytes 8224 | tf_op jit(solution)/shard_map/ppermute | solution.py:58
  50.2 1.8 %collective-permute-start.9 = (bf16[32,256]{1,0:T(8,128)(2,1)S(1)}, bf16[32,256]{1,0:T(8,128)(2,1)S(1)}, u32[]{:S(2)}, u32[]{:S(2)}) collective-permute-start(bf16[32,256]{1,0:T(8,128)(2,1)S(1)} %maximum_select_fusion.7), channel_id=1, source_target_pairs={{0,8},{4,12},{8,0},{12,4},{16,24},{20,28},{24,16},{28,20},{1,9},{5... | collective-permute-start | bytes 49160 | tf_op jit(solution)/shard_map/ppermute | solution.py:58
  51.9 2.0 %collective-permute-done.9 = bf16[32,256]{1,0:T(8,128)(2,1)S(1)} collective-permute-done((bf16[32,256]{1,0:T(8,128)(2,1)S(1)}, bf16[32,256]{1,0:T(8,128)(2,1)S(1)}, u32[]{:S(2)}, u32[]{:S(2)}) %collective-permute-start.9) | collective-permute-done | bytes 16416 | tf_op jit(solution)/shard_map/ppermute | solution.py:58
  53.9 2.8 %collective-permute-start.10 = (bf16[64,256]{1,0:T(8,128)(2,1)S(1)}, bf16[64,256]{1,0:T(8,128)(2,1)S(1)}, u32[]{:S(2)}, u32[]{:S(2)}) collective-permute-start(bf16[64,256]{1,0:T(8,128)(2,1)S(1)} %maximum_select_fusion.6), channel_id=1, source_target_pairs={{0,16},{4,20},{8,24},{12,28},{16,0},{20,4},{24,8},{28,12},{1,17},{... | collective-permute-start | bytes 98312 | tf_op jit(solution)/shard_map/ppermute | solution.py:58
  56.9 1.9 %collective-permute-done.10 = bf16[64,256]{1,0:T(8,128)(2,1)S(1)} collective-permute-done((bf16[64,256]{1,0:T(8,128)(2,1)S(1)}, bf16[64,256]{1,0:T(8,128)(2,1)S(1)}, u32[]{:S(2)}, u32[]{:S(2)}) %collective-permute-start.10) | collective-permute-done | bytes 32800 | tf_op jit(solution)/shard_map/ppermute | solution.py:58
  58.8 1.7 %fusion.54 = f32[128,2048]{1,0:T(8,128)S(1)} fusion(bf16[2048,256]{1,0:T(8,128)(2,1)} %param.30, bf16[64,256]{1,0:T(8,128)(2,1)S(1)} %collective-permute-done.10, bf16[64,256]{1,0:T(8,128)(2,1)S(1)} %maximum_select_fusion.6, pred[]{:T(512)S(6)} %eq.90), kind=kOutput, calls=%fused_computation.91 | convolution fusion | flops 134512640 | bytes 2162689 | tf_op jit(solution)/shard_map/while/body/eval_jaxpr/dot_general | solution.py:158
  60.5 10.9 %select_reduce_fusion = f32[128,64]{1,0:T(8,128)S(1)} fusion(f32[128,2048]{1,0:T(8,128)S(1)} %fusion.54, s32[128,64]{1,0:T(8,128)S(1)} %copy.26), kind=kLoop, calls=%fused_computation.1 | loop fusion | flops 50323456 | bytes 1114112 | tf_op jit(solution)/shard_map/while/body/eval_jaxpr/reduce_sum | solution.py:162
  71.5 2.9 %collective-permute-start.11 = (f32[64,64]{1,0:T(8,128)S(1)}, f32[64,64]{1,0:T(8,128)S(1)}, u32[]{:S(2)}, u32[]{:S(2)}) collective-permute-start(f32[64,64]{1,0:T(8,128)S(1)} %constant_dynamic-slice_fusion.1), channel_id=1, source_target_pairs={{0,16},{4,20},{8,24},{12,28},{16,0},{20,4},{24,8},{28,12},{1,17},{... | collective-permute-start | bytes 49160 | tf_op jit(solution)/shard_map/ppermute | solution.py:47
  74.3 2.0 %collective-permute-done.11 = f32[64,64]{1,0:T(8,128)S(1)} collective-permute-done((f32[64,64]{1,0:T(8,128)S(1)}, f32[64,64]{1,0:T(8,128)S(1)}, u32[]{:S(2)}, u32[]{:S(2)}) %collective-permute-start.11) | collective-permute-done | bytes 16416 | tf_op jit(solution)/shard_map/ppermute | solution.py:47
  76.3 1.8 %collective-permute-start.12 = (f32[32,64]{1,0:T(8,128)S(1)}, f32[32,64]{1,0:T(8,128)S(1)}, u32[]{:S(2)}, u32[]{:S(2)}) collective-permute-start(f32[32,64]{1,0:T(8,128)S(1)} %constant_dynamic-slice_fusion), channel_id=1, source_target_pairs={{0,8},{4,12},{8,0},{12,4},{16,24},{20,28},{24,16},{28,20},{1,9},{5... | collective-permute-start | bytes 24584 | tf_op jit(solution)/shard_map/ppermute | solution.py:47
  78.2 2.0 %collective-permute-done.12 = f32[32,64]{1,0:T(8,128)S(1)} collective-permute-done((f32[32,64]{1,0:T(8,128)S(1)}, f32[32,64]{1,0:T(8,128)S(1)}, u32[]{:S(2)}, u32[]{:S(2)}) %collective-permute-start.12) | collective-permute-done | bytes 8224 | tf_op jit(solution)/shard_map/ppermute | solution.py:47
  80.2 1.7 %collective-permute-start.13 = (f32[16,64]{1,0:T(8,128)S(1)}, f32[16,64]{1,0:T(8,128)S(1)}, u32[]{:S(2)}, u32[]{:S(2)}) collective-permute-start(f32[16,64]{1,0:T(8,128)S(1)} %constant_dynamic-slice_fusion.3), channel_id=1, source_target_pairs={{0,4},{4,0},{8,12},{12,8},{16,20},{20,16},{24,28},{28,24},{1,5},{5... | collective-permute-start | bytes 12296 | tf_op jit(solution)/shard_map/ppermute | solution.py:47
  81.9 1.9 %collective-permute-done.13 = f32[16,64]{1,0:T(8,128)S(1)} collective-permute-done((f32[16,64]{1,0:T(8,128)S(1)}, f32[16,64]{1,0:T(8,128)S(1)}, u32[]{:S(2)}, u32[]{:S(2)}) %collective-permute-start.13) | collective-permute-done | bytes 4128 | tf_op jit(solution)/shard_map/ppermute | solution.py:47
  86.7 2.0 %collective-permute-done.15 = f32[16,64]{1,0:T(8,128)S(1)} collective-permute-done((f32[16,64]{1,0:T(8,128)S(1)}, f32[16,64]{1,0:T(8,128)S(1)}, u32[]{:S(2)}, u32[]{:S(2)}) %collective-permute-start.15) | collective-permute-done | bytes 4128 | tf_op jit(solution)/shard_map/ppermute | solution.py:180
  (82 shorter events, 21.5 us)
Async XLA Ops:
  0.6 25.6 %copy-start = (bf16[1024,1024]{1,0:T(8,128)(2,1)S(1)}, bf16[1024,1024]{1,0:T(8,128)(2,1)}, u32[]{:S(2)}) copy-start(bf16[1024,1024]{1,0:T(8,128)(2,1)} %param.26) | copy-start | bytes 6291460
  8.0 10.0 %copy-start.3 = (f32[1024]{0:T(1024)S(1)}, f32[1024]{0:T(1024)}, u32[]{:S(2)}) copy-start(f32[1024]{0:T(1024)} %param.21) | copy-start | bytes 12292
  8.0 11.2 %copy-start.4 = (f32[1024]{0:T(1024)S(1)}, f32[1024]{0:T(1024)}, u32[]{:S(2)}) copy-start(f32[1024]{0:T(1024)} %param.23) | copy-start | bytes 12292
  8.0 11.2 %copy-start.5 = (f32[1024]{0:T(1024)S(1)}, f32[1024]{0:T(1024)}, u32[]{:S(2)}) copy-start(f32[1024]{0:T(1024)} %param.22) | copy-start | bytes 12292
  9.4 1.7 %collective-permute-start = (bf16[128,1024]{1,0:T(8,128)(2,1)S(1)}, bf16[128,1024]{1,0:T(8,128)(2,1)S(1)}, u32[]{:S(2)}, u32[]{:S(2)}) collective-permute-start(bf16[128,1024]{1,0:T(8,128)(2,1)S(1)} %constant_dynamic-slice_fusion.4), channel_id=1, source_target_pairs={{0,1},{1,0},{2,3},{3,2},{4,5},{5,4},{6,7},{7,6},{8,9},{9,8},{10,11... | collective-permute-start | bytes 786440 | tf_op jit(solution)/shard_map/ppermute | solution.py:47
  9.9 16.3 %copy-start.10 = (f32[1024]{0:T(1024)S(1)}, f32[1024]{0:T(1024)}, u32[]{:S(2)}) copy-start(f32[1024]{0:T(1024)} %param.25) | copy-start | bytes 12292
  11.2 6.7 %collective-permute-start.1 = (bf16[64,1024]{1,0:T(8,128)(2,1)S(1)}, bf16[64,1024]{1,0:T(8,128)(2,1)S(1)}, u32[]{:S(2)}, u32[]{:S(2)}) collective-permute-start(bf16[64,1024]{1,0:T(8,128)(2,1)S(1)} %dynamic-slice_convert_fusion.1), channel_id=1, source_target_pairs={{0,2},{1,3},{2,0},{3,1},{4,6},{5,7},{6,4},{7,5},{8,10},{9,11},{10,... | collective-permute-start | bytes 393224 | tf_op jit(solution)/shard_map/ppermute | solution.py:47
  19.3 5.1 %collective-permute-start.2 = (bf16[64,1024]{1,0:T(8,128)(2,1)S(1)}, bf16[64,1024]{1,0:T(8,128)(2,1)S(1)}, u32[]{:S(2)}, u32[]{:S(2)}) collective-permute-start(bf16[64,1024]{1,0:T(8,128)(2,1)S(1)} %add_convert_fusion.1), channel_id=1, source_target_pairs={{0,2},{1,3},{2,0},{3,1},{4,6},{5,7},{6,4},{7,5},{8,10},{9,11},{10,... | collective-permute-start | bytes 393224 | tf_op jit(solution)/shard_map/ppermute | solution.py:58
  24.5 1.6 %collective-permute-start.3 = (bf16[128,1024]{1,0:T(8,128)(2,1)S(1)}, bf16[128,1024]{1,0:T(8,128)(2,1)S(1)}, u32[]{:S(2)}, u32[]{:S(2)}) collective-permute-start(bf16[128,1024]{1,0:T(8,128)(2,1)S(1)} %maximum_select_fusion.2), channel_id=1, source_target_pairs={{0,1},{1,0},{2,3},{3,2},{4,5},{5,4},{6,7},{7,6},{8,9},{9,8},{10,11... | collective-permute-start | bytes 786440 | tf_op jit(solution)/shard_map/ppermute | solution.py:58
  26.3 12.5 %copy-start.6 = (f32[1024]{0:T(1024)S(1)}, f32[1024]{0:T(1024)}, u32[]{:S(2)}) copy-start(f32[1024]{0:T(1024)} %param.27) | copy-start | bytes 12292
  31.4 1.6 %collective-permute-start.4 = (bf16[128,1024]{1,0:T(8,128)(2,1)S(1)}, bf16[128,1024]{1,0:T(8,128)(2,1)S(1)}, u32[]{:S(2)}, u32[]{:S(2)}) collective-permute-start(bf16[128,1024]{1,0:T(8,128)(2,1)S(1)} %constant_dynamic-slice_fusion.2), channel_id=1, source_target_pairs={{0,1},{1,0},{2,3},{3,2},{4,5},{5,4},{6,7},{7,6},{8,9},{9,8},{10,11... | collective-permute-start | bytes 786440 | tf_op jit(solution)/shard_map/ppermute | solution.py:47
  33.1 23.7 %copy-start.2 = (s32[128,64]{0,1:T(8,128)S(1)}, s32[128,64]{0,1:T(8,128)}, u32[]{:S(2)}) copy-start(s32[128,64]{0,1:T(8,128)} %param.31) | copy-start | bytes 98308
  33.2 5.6 %collective-permute-start.5 = (bf16[64,1024]{1,0:T(8,128)(2,1)S(1)}, bf16[64,1024]{1,0:T(8,128)(2,1)S(1)}, u32[]{:S(2)}, u32[]{:S(2)}) collective-permute-start(bf16[64,1024]{1,0:T(8,128)(2,1)S(1)} %dynamic-slice_convert_fusion), channel_id=1, source_target_pairs={{0,2},{1,3},{2,0},{3,1},{4,6},{5,7},{6,4},{7,5},{8,10},{9,11},{10,... | collective-permute-start | bytes 393224 | tf_op jit(solution)/shard_map/ppermute | solution.py:47
  39.3 5.0 %collective-permute-start.6 = (bf16[64,1024]{1,0:T(8,128)(2,1)S(1)}, bf16[64,1024]{1,0:T(8,128)(2,1)S(1)}, u32[]{:S(2)}, u32[]{:S(2)}) collective-permute-start(bf16[64,1024]{1,0:T(8,128)(2,1)S(1)} %add_convert_fusion), channel_id=1, source_target_pairs={{0,2},{1,3},{2,0},{3,1},{4,6},{5,7},{6,4},{7,5},{8,10},{9,11},{10,... | collective-permute-start | bytes 393224 | tf_op jit(solution)/shard_map/ppermute | solution.py:58
  44.4 1.6 %collective-permute-start.7 = (bf16[128,1024]{1,0:T(8,128)(2,1)S(1)}, bf16[128,1024]{1,0:T(8,128)(2,1)S(1)}, u32[]{:S(2)}, u32[]{:S(2)}) collective-permute-start(bf16[128,1024]{1,0:T(8,128)(2,1)S(1)} %maximum_select_fusion.3), channel_id=1, source_target_pairs={{0,1},{1,0},{2,3},{3,2},{4,5},{5,4},{6,7},{7,6},{8,9},{9,8},{10,11... | collective-permute-start | bytes 786440 | tf_op jit(solution)/shard_map/ppermute | solution.py:58
  46.1 25.3 %copy-start.1 = (bf16[256,1024]{1,0:T(8,128)(2,1)}, bf16[256,1024]{1,0:T(8,128)(2,1)S(1)}, u32[]{:S(2)}) copy-start(bf16[256,1024]{1,0:T(8,128)(2,1)S(1)} %maximum_select_fusion.1) | copy-start | bytes 1572868
  46.5 3.7 %collective-permute-start.8 = (bf16[16,256]{1,0:T(8,128)(2,1)S(1)}, bf16[16,256]{1,0:T(8,128)(2,1)S(1)}, u32[]{:S(2)}, u32[]{:S(2)}) collective-permute-start(bf16[16,256]{1,0:T(8,128)(2,1)S(1)} %fusion.61), channel_id=1, source_target_pairs={{0,4},{4,0},{8,12},{12,8},{16,20},{20,16},{24,28},{28,24},{1,5},{5... | collective-permute-start | bytes 24584 | tf_op jit(solution)/shard_map/ppermute | solution.py:58
  50.2 3.7 %collective-permute-start.9 = (bf16[32,256]{1,0:T(8,128)(2,1)S(1)}, bf16[32,256]{1,0:T(8,128)(2,1)S(1)}, u32[]{:S(2)}, u32[]{:S(2)}) collective-permute-start(bf16[32,256]{1,0:T(8,128)(2,1)S(1)} %maximum_select_fusion.7), channel_id=1, source_target_pairs={{0,8},{4,12},{8,0},{12,4},{16,24},{20,28},{24,16},{28,20},{1,9},{5... | collective-permute-start | bytes 49160 | tf_op jit(solution)/shard_map/ppermute | solution.py:58
  53.9 4.9 %collective-permute-start.10 = (bf16[64,256]{1,0:T(8,128)(2,1)S(1)}, bf16[64,256]{1,0:T(8,128)(2,1)S(1)}, u32[]{:S(2)}, u32[]{:S(2)}) collective-permute-start(bf16[64,256]{1,0:T(8,128)(2,1)S(1)} %maximum_select_fusion.6), channel_id=1, source_target_pairs={{0,16},{4,20},{8,24},{12,28},{16,0},{20,4},{24,8},{28,12},{1,17},{... | collective-permute-start | bytes 98312 | tf_op jit(solution)/shard_map/ppermute | solution.py:58
  71.5 4.9 %collective-permute-start.11 = (f32[64,64]{1,0:T(8,128)S(1)}, f32[64,64]{1,0:T(8,128)S(1)}, u32[]{:S(2)}, u32[]{:S(2)}) collective-permute-start(f32[64,64]{1,0:T(8,128)S(1)} %constant_dynamic-slice_fusion.1), channel_id=1, source_target_pairs={{0,16},{4,20},{8,24},{12,28},{16,0},{20,4},{24,8},{28,12},{1,17},{... | collective-permute-start | bytes 49160 | tf_op jit(solution)/shard_map/ppermute | solution.py:47
  76.3 3.8 %collective-permute-start.12 = (f32[32,64]{1,0:T(8,128)S(1)}, f32[32,64]{1,0:T(8,128)S(1)}, u32[]{:S(2)}, u32[]{:S(2)}) collective-permute-start(f32[32,64]{1,0:T(8,128)S(1)} %constant_dynamic-slice_fusion), channel_id=1, source_target_pairs={{0,8},{4,12},{8,0},{12,4},{16,24},{20,28},{24,16},{28,20},{1,9},{5... | collective-permute-start | bytes 24584 | tf_op jit(solution)/shard_map/ppermute | solution.py:47
  80.2 3.7 %collective-permute-start.13 = (f32[16,64]{1,0:T(8,128)S(1)}, f32[16,64]{1,0:T(8,128)S(1)}, u32[]{:S(2)}, u32[]{:S(2)}) collective-permute-start(f32[16,64]{1,0:T(8,128)S(1)} %constant_dynamic-slice_fusion.3), channel_id=1, source_target_pairs={{0,4},{4,0},{8,12},{12,8},{16,20},{20,16},{24,28},{28,24},{1,5},{5... | collective-permute-start | bytes 12296 | tf_op jit(solution)/shard_map/ppermute | solution.py:47
  83.8 1.2 %collective-permute-start.14 = (f32[16,64]{1,0:T(8,128)S(1)}, f32[16,64]{1,0:T(8,128)S(1)}, u32[]{:S(2)}, u32[]{:S(2)}) collective-permute-start(f32[16,64]{1,0:T(8,128)S(1)} %dynamic-slice_add_fusion.2), channel_id=1, source_target_pairs={{0,1},{1,0},{2,3},{3,2},{4,5},{5,4},{6,7},{7,6},{8,9},{9,8},{10,11... | collective-permute-start | bytes 12296 | tf_op jit(solution)/shard_map/ppermute | solution.py:180
  85.0 3.7 %collective-permute-start.15 = (f32[16,64]{1,0:T(8,128)S(1)}, f32[16,64]{1,0:T(8,128)S(1)}, u32[]{:S(2)}, u32[]{:S(2)}) collective-permute-start(f32[16,64]{1,0:T(8,128)S(1)} %add.253), channel_id=1, source_target_pairs={{0,2},{1,3},{2,0},{3,1},{4,6},{5,7},{6,4},{7,5},{8,10},{9,11},{10,... | collective-permute-start | bytes 12296 | tf_op jit(solution)/shard_map/ppermute | solution.py:180
  (3 other events, 19.5 us)

commit v2 on v1

--- a/solution.py
+++ b/solution.py
@@ -146,29 +146,14 @@
     else:
         gathered = lax.all_gather(unit_quarter, "dp", axis=0, tiled=True)
     all_texts = candidates.shape[0]
-    cand_count = candidates.shape[1]
     shard_rows = index.shape[0]
-    block_rows = math.gcd(all_texts, 128)
-    block_count = all_texts // block_rows
     local_rows = candidates - row_base
-    row_ids = jnp.arange(shard_rows, dtype=jnp.int32)
-
-    def score_block(packed):
-        query_block, wanted = packed
-        tile = lax.dot_general(
-            query_block, index, (((1,), (1,)), ((), ())), preferred_element_type=jnp.float32
-        )
-        chosen = wanted[:, :, None] == row_ids[None, None, :]
-        return jnp.sum(jnp.where(chosen, tile[:, None, :], 0.0), axis=2)
-
-    partial_scores = lax.map(
-        score_block,
-        (
-            gathered.reshape(block_count, block_rows, quarter),
-            local_rows.reshape(block_count, block_rows, cand_count),
-        ),
+    held = (local_rows >= 0) & (local_rows < shard_rows)
+    tile = lax.dot_general(
+        gathered, index, (((1,), (1,)), ((), ())), preferred_element_type=jnp.float32
     )
-    partial_scores = partial_scores.reshape(all_texts, cand_count)
+    picked = jnp.take_along_axis(tile, jnp.clip(local_rows, 0, shard_rows - 1), axis=1)
+    partial_scores = jnp.where(held, picked, 0.0)
     if not xor_ok:
         slice_scores = lax.psum_scatter(
             partial_scores, ("dp", "tensor"), scatter_dimension=0, tiled=True

time: 89.5 us -> 145 us (1.62)
  local copies, waits for them, and re-layouts: 1.23 us -> 67.2 us
  other arithmetic: 14.4 us -> 3.5 us
    gather x0 -> x3, local copies, waits for them, and re-layouts: none -> 65.2 us  [body(): jnp.take_along_axis(tile, jnp.clip(local_rows, 0, shard_rows - 1), axis=1)]
    reduce_sum x1 -> x0, other arithmetic: 10.9 us -> none  [score_block(): return jnp.sum(jnp.where(chosen, tile[:, None, :], 0.0), axis=2)]
where the time goes in v2:
time: 145 us; the launch traced here: 144 us
  local copies, waits for them, and re-layouts  67.2 us (46%)
  waiting for transfers between devices  34.6 us (24%)
  starting transfers between devices  23.5 us (16%)
  matrix products  14.4 us (10%)
  other arithmetic  3.5 us (2%)
    gather x3, local copies, waits for them, and re-layouts, body(): jnp.take_along_axis(tile, jnp.clip(local_rows, 0, shard_rows - 1), axis=1)  65.2 us
    ppermute x7, waiting for transfers between devices, reduce_scatter_xor(): got = lax.ppermute(theirs.astype(wire), axis, xor_pairs(n, k))  16.1 us
    ppermute x7, waiting for transfers between devices, all_gather_xor(): other = lax.ppermute(cur, axis, xor_pairs(n, k))  15.3 us
    ppermute x7, starting transfers between devices, reduce_scatter_xor(): got = lax.ppermute(theirs.astype(wire), axis, xor_pairs(n, k))  11.8 us
    ppermute x7, starting transfers between devices, all_gather_xor(): other = lax.ppermute(cur, axis, xor_pairs(n, k))  10 us
    dot_general x1, matrix products, body(): jnp.dot(activated, w_down, preferred_element_type=jnp.float32)  5.11 us
    dot_general x3, matrix products, body(): jnp.dot(hidden, w_qkv[j], preferred_element_type=jnp.float32) + b_qkv[j]  4.68 us
    ppermute x2, waiting for transfers between devices, body(): lax.ppermute(text_scores, 'tensor', xor_pairs(n_tensor, k))  3.15 us
  transfers between devices with their start and end apart: 16, of which 16 were waited for; matrix products, arithmetic and copies ran while one was open for 0% of the time, Pallas kernels for 0%

profile of v2, /device:TPU:0, one launch (start us, length us, event | category | flops | bytes accessed | tf_op | source)
XLA Modules:
  0.0 144.2 jit_solution(12468167625964096696)
XLA Ops:
  11.2 2.9 %collective-permute-start.1 = (bf16[64,1024]{1,0:T(8,128)(2,1)S(1)}, bf16[64,1024]{1,0:T(8,128)(2,1)S(1)}, u32[]{:S(2)}, u32[]{:S(2)}) collective-permute-start(bf16[64,1024]{1,0:T(8,128)(2,1)S(1)} %dynamic-slice_convert_fusion.1), channel_id=1, source_target_pairs={{0,2},{1,3},{2,0},{3,1},{4,6},{5,7},{6,4},{7,5},{8,10},{9,11},{10,... | collective-permute-start | bytes 393224 | tf_op jit(solution)/shard_map/ppermute | solution.py:47
  14.1 3.8 %collective-permute-done.1 = bf16[64,1024]{1,0:T(8,128)(2,1)S(1)} collective-permute-done((bf16[64,1024]{1,0:T(8,128)(2,1)S(1)}, bf16[64,1024]{1,0:T(8,128)(2,1)S(1)}, u32[]{:S(2)}, u32[]{:S(2)}) %collective-permute-start.1) | collective-permute-done | bytes 131104 | tf_op jit(solution)/shard_map/ppermute | solution.py:47
  19.3 1.8 %collective-permute-start.2 = (bf16[64,1024]{1,0:T(8,128)(2,1)S(1)}, bf16[64,1024]{1,0:T(8,128)(2,1)S(1)}, u32[]{:S(2)}, u32[]{:S(2)}) collective-permute-start(bf16[64,1024]{1,0:T(8,128)(2,1)S(1)} %add_convert_fusion.1), channel_id=1, source_target_pairs={{0,2},{1,3},{2,0},{3,1},{4,6},{5,7},{6,4},{7,5},{8,10},{9,11},{10,... | collective-permute-start | bytes 393224 | tf_op jit(solution)/shard_map/ppermute | solution.py:58
  21.1 3.3 %collective-permute-done.2 = bf16[64,1024]{1,0:T(8,128)(2,1)S(1)} collective-permute-done((bf16[64,1024]{1,0:T(8,128)(2,1)S(1)}, bf16[64,1024]{1,0:T(8,128)(2,1)S(1)}, u32[]{:S(2)}, u32[]{:S(2)}) %collective-permute-start.2) | collective-permute-done | bytes 131104 | tf_op jit(solution)/shard_map/ppermute | solution.py:58
  26.3 5.1 %convolution_convert_fusion.1 = bf16[256,1024]{1,0:T(8,128)(2,1)S(1)} fusion(bf16[1024,1024]{1,0:T(8,128)(2,1)S(1)} %copy-done, bf16[256,1024]{1,0:T(8,128)(2,1)S(1)} %maximum_select_fusion, bf16[1024,1024]{1,0:T(8,128)(2,1)} %param.24, f32[1024]{0:T(1024)S(1)} %copy-done.10), kind=kOutput, calls=%fused_computation.8 | convolution fusion | flops 1091305472 | bytes 5246976 | tf_op jit(solution)/shard_map/dot_general | solution.py:123
  33.2 1.8 %collective-permute-start.5 = (bf16[64,1024]{1,0:T(8,128)(2,1)S(1)}, bf16[64,1024]{1,0:T(8,128)(2,1)S(1)}, u32[]{:S(2)}, u32[]{:S(2)}) collective-permute-start(bf16[64,1024]{1,0:T(8,128)(2,1)S(1)} %dynamic-slice_convert_fusion), channel_id=1, source_target_pairs={{0,2},{1,3},{2,0},{3,1},{4,6},{5,7},{6,4},{7,5},{8,10},{9,11},{10,... | collective-permute-start | bytes 393224 | tf_op jit(solution)/shard_map/ppermute | solution.py:47
  34.9 3.9 %collective-permute-done.5 = bf16[64,1024]{1,0:T(8,128)(2,1)S(1)} collective-permute-done((bf16[64,1024]{1,0:T(8,128)(2,1)S(1)}, bf16[64,1024]{1,0:T(8,128)(2,1)S(1)}, u32[]{:S(2)}, u32[]{:S(2)}) %collective-permute-start.5) | collective-permute-done | bytes 131104 | tf_op jit(solution)/shard_map/ppermute | solution.py:47
  39.3 1.7 %collective-permute-start.6 = (bf16[64,1024]{1,0:T(8,128)(2,1)S(1)}, bf16[64,1024]{1,0:T(8,128)(2,1)S(1)}, u32[]{:S(2)}, u32[]{:S(2)}) collective-permute-start(bf16[64,1024]{1,0:T(8,128)(2,1)S(1)} %add_convert_fusion), channel_id=1, source_target_pairs={{0,2},{1,3},{2,0},{3,1},{4,6},{5,7},{6,4},{7,5},{8,10},{9,11},{10,... | collective-permute-start | bytes 393224 | tf_op jit(solution)/shard_map/ppermute | solution.py:58
  41.0 3.3 %collective-permute-done.6 = bf16[64,1024]{1,0:T(8,128)(2,1)S(1)} collective-permute-done((bf16[64,1024]{1,0:T(8,128)(2,1)S(1)}, bf16[64,1024]{1,0:T(8,128)(2,1)S(1)}, u32[]{:S(2)}, u32[]{:S(2)}) %collective-permute-start.6) | collective-permute-done | bytes 131104 | tf_op jit(solution)/shard_map/ppermute | solution.py:58
  47.3 1.7 %collective-permute-start.8 = (bf16[16,256]{1,0:T(8,128)(2,1)S(1)}, bf16[16,256]{1,0:T(8,128)(2,1)S(1)}, u32[]{:S(2)}, u32[]{:S(2)}) collective-permute-start(bf16[16,256]{1,0:T(8,128)(2,1)S(1)} %fusion.61), channel_id=1, source_target_pairs={{0,4},{4,0},{8,12},{12,8},{16,20},{20,16},{24,28},{28,24},{1,5},{5... | collective-permute-start | bytes 24584 | tf_op jit(solution)/shard_map/ppermute | solution.py:58
  49.0 1.9 %collective-permute-done.8 = bf16[16,256]{1,0:T(8,128)(2,1)S(1)} collective-permute-done((bf16[16,256]{1,0:T(8,128)(2,1)S(1)}, bf16[16,256]{1,0:T(8,128)(2,1)S(1)}, u32[]{:S(2)}, u32[]{:S(2)}) %collective-permute-start.8) | collective-permute-done | bytes 8224 | tf_op jit(solution)/shard_map/ppermute | solution.py:58
  51.0 1.8 %collective-permute-start.9 = (bf16[32,256]{1,0:T(8,128)(2,1)S(1)}, bf16[32,256]{1,0:T(8,128)(2,1)S(1)}, u32[]{:S(2)}, u32[]{:S(2)}) collective-permute-start(bf16[32,256]{1,0:T(8,128)(2,1)S(1)} %maximum_select_fusion.7), channel_id=1, source_target_pairs={{0,8},{4,12},{8,0},{12,4},{16,24},{20,28},{24,16},{28,20},{1,9},{5... | collective-permute-start | bytes 49160 | tf_op jit(solution)/shard_map/ppermute | solution.py:58
  52.8 1.9 %collective-permute-done.9 = bf16[32,256]{1,0:T(8,128)(2,1)S(1)} collective-permute-done((bf16[32,256]{1,0:T(8,128)(2,1)S(1)}, bf16[32,256]{1,0:T(8,128)(2,1)S(1)}, u32[]{:S(2)}, u32[]{:S(2)}) %collective-permute-start.9) | collective-permute-done | bytes 16416 | tf_op jit(solution)/shard_map/ppermute | solution.py:58
  54.7 2.8 %collective-permute-start.10 = (bf16[64,256]{1,0:T(8,128)(2,1)S(1)}, bf16[64,256]{1,0:T(8,128)(2,1)S(1)}, u32[]{:S(2)}, u32[]{:S(2)}) collective-permute-start(bf16[64,256]{1,0:T(8,128)(2,1)S(1)} %maximum_select_fusion.6), channel_id=1, source_target_pairs={{0,16},{4,20},{8,24},{12,28},{16,0},{20,4},{24,8},{28,12},{1,17},{... | collective-permute-start | bytes 98312 | tf_op jit(solution)/shard_map/ppermute | solution.py:58
  57.7 1.9 %collective-permute-done.10 = bf16[64,256]{1,0:T(8,128)(2,1)S(1)} collective-permute-done((bf16[64,256]{1,0:T(8,128)(2,1)S(1)}, bf16[64,256]{1,0:T(8,128)(2,1)S(1)}, u32[]{:S(2)}, u32[]{:S(2)}) %collective-permute-start.10) | collective-permute-done | bytes 32800 | tf_op jit(solution)/shard_map/ppermute | solution.py:58
  59.6 1.7 %fusion.54 = f32[128,2048]{1,0:T(8,128)S(1)} fusion(bf16[2048,256]{1,0:T(8,128)(2,1)} %param.30, bf16[64,256]{1,0:T(8,128)(2,1)S(1)} %collective-permute-done.10, bf16[64,256]{1,0:T(8,128)(2,1)S(1)} %maximum_select_fusion.6, pred[]{:T(512)S(6)} %eq.67), kind=kOutput, calls=%fused_computation.91 | convolution fusion | flops 134512640 | bytes 2162689 | tf_op jit(solution)/shard_map/dot_general | solution.py:152
  61.3 65.0 %gather_fusion = f32[8192]{0:T(1024)S(1)} fusion(f32[128,2048]{1,0:T(8,128)S(1)} %fusion.54, s32[8192]{0:T(1024)S(1)} %reshape.128), kind=kCustom, calls=%fused_computation | custom fusion | bytes 131072 | tf_op jit(solution)/shard_map/jit(take_along_axis)/gather | solution.py:155
  126.4 2.9 %collective-permute-start.11 = (f32[64,64]{1,0:T(8,128)S(1)}, f32[64,64]{1,0:T(8,128)S(1)}, u32[]{:S(2)}, u32[]{:S(2)}) collective-permute-start(f32[64,64]{1,0:T(8,128)S(1)} %constant_dynamic-slice_fusion.2), channel_id=1, source_target_pairs={{0,16},{4,20},{8,24},{12,28},{16,0},{20,4},{24,8},{28,12},{1,17},{... | collective-permute-start | bytes 49160 | tf_op jit(solution)/shard_map/ppermute | solution.py:47
  129.3 2.0 %collective-permute-done.11 = f32[64,64]{1,0:T(8,128)S(1)} collective-permute-done((f32[64,64]{1,0:T(8,128)S(1)}, f32[64,64]{1,0:T(8,128)S(1)}, u32[]{:S(2)}, u32[]{:S(2)}) %collective-permute-start.11) | collective-permute-done | bytes 16416 | tf_op jit(solution)/shard_map/ppermute | solution.py:47
  131.3 1.8 %collective-permute-start.12 = (f32[32,64]{1,0:T(8,128)S(1)}, f32[32,64]{1,0:T(8,128)S(1)}, u32[]{:S(2)}, u32[]{:S(2)}) collective-permute-start(f32[32,64]{1,0:T(8,128)S(1)} %constant_dynamic-slice_fusion.1), channel_id=1, source_target_pairs={{0,8},{4,12},{8,0},{12,4},{16,24},{20,28},{24,16},{28,20},{1,9},{5... | collective-permute-start | bytes 24584 | tf_op jit(solution)/shard_map/ppermute | solution.py:47
  133.2 2.0 %collective-permute-done.12 = f32[32,64]{1,0:T(8,128)S(1)} collective-permute-done((f32[32,64]{1,0:T(8,128)S(1)}, f32[32,64]{1,0:T(8,128)S(1)}, u32[]{:S(2)}, u32[]{:S(2)}) %collective-permute-start.12) | collective-permute-done | bytes 8224 | tf_op jit(solution)/shard_map/ppermute | solution.py:47
  135.1 1.7 %collective-permute-start.13 = (f32[16,64]{1,0:T(8,128)S(1)}, f32[16,64]{1,0:T(8,128)S(1)}, u32[]{:S(2)}, u32[]{:S(2)}) collective-permute-start(f32[16,64]{1,0:T(8,128)S(1)} %constant_dynamic-slice_fusion), channel_id=1, source_target_pairs={{0,4},{4,0},{8,12},{12,8},{16,20},{20,16},{24,28},{28,24},{1,5},{5... | collective-permute-start | bytes 12296 | tf_op jit(solution)/shard_map/ppermute | solution.py:47
  136.8 1.9 %collective-permute-done.13 = f32[16,64]{1,0:T(8,128)S(1)} collective-permute-done((f32[16,64]{1,0:T(8,128)S(1)}, f32[16,64]{1,0:T(8,128)S(1)}, u32[]{:S(2)}, u32[]{:S(2)}) %collective-permute-start.13) | collective-permute-done | bytes 4128 | tf_op jit(solution)/shard_map/ppermute | solution.py:47
  141.7 2.0 %collective-permute-done.15 = f32[16,64]{1,0:T(8,128)S(1)} collective-permute-done((f32[16,64]{1,0:T(8,128)S(1)}, f32[16,64]{1,0:T(8,128)S(1)}, u32[]{:S(2)}, u32[]{:S(2)}) %collective-permute-start.15) | collective-permute-done | bytes 4128 | tf_op jit(solution)/shard_map/ppermute | solution.py:165
  (85 shorter events, 22.5 us)
Async XLA Ops:
  0.6 25.6 %copy-start = (bf16[1024,1024]{1,0:T(8,128)(2,1)S(1)}, bf16[1024,1024]{1,0:T(8,128)(2,1)}, u32[]{:S(2)}) copy-start(bf16[1024,1024]{1,0:T(8,128)(2,1)} %param.26) | copy-start | bytes 6291460
  8.0 10.0 %copy-start.3 = (f32[1024]{0:T(1024)S(1)}, f32[1024]{0:T(1024)}, u32[]{:S(2)}) copy-start(f32[1024]{0:T(1024)} %param.21) | copy-start | bytes 12292
  8.0 11.2 %copy-start.4 = (f32[1024]{0:T(1024)S(1)}, f32[1024]{0:T(1024)}, u32[]{:S(2)}) copy-start(f32[1024]{0:T(1024)} %param.23) | copy-start | bytes 12292
  8.0 11.2 %copy-start.5 = (f32[1024]{0:T(1024)S(1)}, f32[1024]{0:T(1024)}, u32[]{:S(2)}) copy-start(f32[1024]{0:T(1024)} %param.22) | copy-start | bytes 12292
  9.4 1.7 %collective-permute-start = (bf16[128,1024]{1,0:T(8,128)(2,1)S(1)}, bf16[128,1024]{1,0:T(8,128)(2,1)S(1)}, u32[]{:S(2)}, u32[]{:S(2)}) collective-permute-start(bf16[128,1024]{1,0:T(8,128)(2,1)S(1)} %constant_dynamic-slice_fusion.4), channel_id=1, source_target_pairs={{0,1},{1,0},{2,3},{3,2},{4,5},{5,4},{6,7},{7,6},{8,9},{9,8},{10,11... | collective-permute-start | bytes 786440 | tf_op jit(solution)/shard_map/ppermute | solution.py:47
  9.9 16.3 %copy-start.10 = (f32[1024]{0:T(1024)S(1)}, f32[1024]{0:T(1024)}, u32[]{:S(2)}) copy-start(f32[1024]{0:T(1024)} %param.25) | copy-start | bytes 12292
  11.2 6.7 %collective-permute-start.1 = (bf16[64,1024]{1,0:T(8,128)(2,1)S(1)}, bf16[64,1024]{1,0:T(8,128)(2,1)S(1)}, u32[]{:S(2)}, u32[]{:S(2)}) collective-permute-start(bf16[64,1024]{1,0:T(8,128)(2,1)S(1)} %dynamic-slice_convert_fusion.1), channel_id=1, source_target_pairs={{0,2},{1,3},{2,0},{3,1},{4,6},{5,7},{6,4},{7,5},{8,10},{9,11},{10,... | collective-permute-start | bytes 393224 | tf_op jit(solution)/shard_map/ppermute | solution.py:47
  19.3 5.1 %collective-permute-start.2 = (bf16[64,1024]{1,0:T(8,128)(2,1)S(1)}, bf16[64,1024]{1,0:T(8,128)(2,1)S(1)}, u32[]{:S(2)}, u32[]{:S(2)}) collective-permute-start(bf16[64,1024]{1,0:T(8,128)(2,1)S(1)} %add_convert_fusion.1), channel_id=1, source_target_pairs={{0,2},{1,3},{2,0},{3,1},{4,6},{5,7},{6,4},{7,5},{8,10},{9,11},{10,... | collective-permute-start | bytes 393224 | tf_op jit(solution)/shard_map/ppermute | solution.py:58
  24.5 1.6 %collective-permute-start.3 = (bf16[128,1024]{1,0:T(8,128)(2,1)S(1)}, bf16[128,1024]{1,0:T(8,128)(2,1)S(1)}, u32[]{:S(2)}, u32[]{:S(2)}) collective-permute-start(bf16[128,1024]{1,0:T(8,128)(2,1)S(1)} %maximum_select_fusion.2), channel_id=1, source_target_pairs={{0,1},{1,0},{2,3},{3,2},{4,5},{5,4},{6,7},{7,6},{8,9},{9,8},{10,11... | collective-permute-start | bytes 786440 | tf_op jit(solution)/shard_map/ppermute | solution.py:58
  26.3 12.5 %copy-start.6 = (f32[1024]{0:T(1024)S(1)}, f32[1024]{0:T(1024)}, u32[]{:S(2)}) copy-start(f32[1024]{0:T(1024)} %param.27) | copy-start | bytes 12292
  31.4 7.8 %copy-start.7 = (f32[1024]{0:T(1024)S(1)}, f32[1024]{0:T(1024)}, u32[]{:S(2)}) copy-start(f32[1024]{0:T(1024)} %param.29) | copy-start | bytes 12292
  31.4 1.6 %collective-permute-start.4 = (bf16[128,1024]{1,0:T(8,128)(2,1)S(1)}, bf16[128,1024]{1,0:T(8,128)(2,1)S(1)}, u32[]{:S(2)}, u32[]{:S(2)}) collective-permute-start(bf16[128,1024]{1,0:T(8,128)(2,1)S(1)} %constant_dynamic-slice_fusion.3), channel_id=1, source_target_pairs={{0,1},{1,0},{2,3},{3,2},{4,5},{5,4},{6,7},{7,6},{8,9},{9,8},{10,11... | collective-permute-start | bytes 786440 | tf_op jit(solution)/shard_map/ppermute | solution.py:47
  33.1 19.6 %copy-start.2 = (s32[128,64]{0,1:T(8,128)S(1)}, s32[128,64]{0,1:T(8,128)}, u32[]{:S(2)}) copy-start(s32[128,64]{0,1:T(8,128)} %param.31) | copy-start | bytes 98308
  33.2 5.6 %collective-permute-start.5 = (bf16[64,1024]{1,0:T(8,128)(2,1)S(1)}, bf16[64,1024]{1,0:T(8,128)(2,1)S(1)}, u32[]{:S(2)}, u32[]{:S(2)}) collective-permute-start(bf16[64,1024]{1,0:T(8,128)(2,1)S(1)} %dynamic-slice_convert_fusion), channel_id=1, source_target_pairs={{0,2},{1,3},{2,0},{3,1},{4,6},{5,7},{6,4},{7,5},{8,10},{9,11},{10,... | collective-permute-start | bytes 393224 | tf_op jit(solution)/shard_map/ppermute | solution.py:47
  39.3 5.0 %collective-permute-start.6 = (bf16[64,1024]{1,0:T(8,128)(2,1)S(1)}, bf16[64,1024]{1,0:T(8,128)(2,1)S(1)}, u32[]{:S(2)}, u32[]{:S(2)}) collective-permute-start(bf16[64,1024]{1,0:T(8,128)(2,1)S(1)} %add_convert_fusion), channel_id=1, source_target_pairs={{0,2},{1,3},{2,0},{3,1},{4,6},{5,7},{6,4},{7,5},{8,10},{9,11},{10,... | collective-permute-start | bytes 393224 | tf_op jit(solution)/shard_map/ppermute | solution.py:58
  44.4 1.6 %collective-permute-start.7 = (bf16[128,1024]{1,0:T(8,128)(2,1)S(1)}, bf16[128,1024]{1,0:T(8,128)(2,1)S(1)}, u32[]{:S(2)}, u32[]{:S(2)}) collective-permute-start(bf16[128,1024]{1,0:T(8,128)(2,1)S(1)} %maximum_select_fusion.3), channel_id=1, source_target_pairs={{0,1},{1,0},{2,3},{3,2},{4,5},{5,4},{6,7},{7,6},{8,9},{9,8},{10,11... | collective-permute-start | bytes 786440 | tf_op jit(solution)/shard_map/ppermute | solution.py:58
  47.3 3.7 %collective-permute-start.8 = (bf16[16,256]{1,0:T(8,128)(2,1)S(1)}, bf16[16,256]{1,0:T(8,128)(2,1)S(1)}, u32[]{:S(2)}, u32[]{:S(2)}) collective-permute-start(bf16[16,256]{1,0:T(8,128)(2,1)S(1)} %fusion.61), channel_id=1, source_target_pairs={{0,4},{4,0},{8,12},{12,8},{16,20},{20,16},{24,28},{28,24},{1,5},{5... | collective-permute-start | bytes 24584 | tf_op jit(solution)/shard_map/ppermute | solution.py:58
  51.0 3.7 %collective-permute-start.9 = (bf16[32,256]{1,0:T(8,128)(2,1)S(1)}, bf16[32,256]{1,0:T(8,128)(2,1)S(1)}, u32[]{:S(2)}, u32[]{:S(2)}) collective-permute-start(bf16[32,256]{1,0:T(8,128)(2,1)S(1)} %maximum_select_fusion.7), channel_id=1, source_target_pairs={{0,8},{4,12},{8,0},{12,4},{16,24},{20,28},{24,16},{28,20},{1,9},{5... | collective-permute-start | bytes 49160 | tf_op jit(solution)/shard_map/ppermute | solution.py:58
  54.7 4.9 %collective-permute-start.10 = (bf16[64,256]{1,0:T(8,128)(2,1)S(1)}, bf16[64,256]{1,0:T(8,128)(2,1)S(1)}, u32[]{:S(2)}, u32[]{:S(2)}) collective-permute-start(bf16[64,256]{1,0:T(8,128)(2,1)S(1)} %maximum_select_fusion.6), channel_id=1, source_target_pairs={{0,16},{4,20},{8,24},{12,28},{16,0},{20,4},{24,8},{28,12},{1,17},{... | collective-permute-start | bytes 98312 | tf_op jit(solution)/shard_map/ppermute | solution.py:58
  126.4 4.9 %collective-permute-start.11 = (f32[64,64]{1,0:T(8,128)S(1)}, f32[64,64]{1,0:T(8,128)S(1)}, u32[]{:S(2)}, u32[]{:S(2)}) collective-permute-start(f32[64,64]{1,0:T(8,128)S(1)} %constant_dynamic-slice_fusion.2), channel_id=1, source_target_pairs={{0,16},{4,20},{8,24},{12,28},{16,0},{20,4},{24,8},{28,12},{1,17},{... | collective-permute-start | bytes 49160 | tf_op jit(solution)/shard_map/ppermute | solution.py:47
  131.3 3.8 %collective-permute-start.12 = (f32[32,64]{1,0:T(8,128)S(1)}, f32[32,64]{1,0:T(8,128)S(1)}, u32[]{:S(2)}, u32[]{:S(2)}) collective-permute-start(f32[32,64]{1,0:T(8,128)S(1)} %constant_dynamic-slice_fusion.1), channel_id=1, source_target_pairs={{0,8},{4,12},{8,0},{12,4},{16,24},{20,28},{24,16},{28,20},{1,9},{5... | collective-permute-start | bytes 24584 | tf_op jit(solution)/shard_map/ppermute | solution.py:47
  135.1 3.7 %collective-permute-start.13 = (f32[16,64]{1,0:T(8,128)S(1)}, f32[16,64]{1,0:T(8,128)S(1)}, u32[]{:S(2)}, u32[]{:S(2)}) collective-permute-start(f32[16,64]{1,0:T(8,128)S(1)} %constant_dynamic-slice_fusion), channel_id=1, source_target_pairs={{0,4},{4,0},{8,12},{12,8},{16,20},{20,16},{24,28},{28,24},{1,5},{5... | collective-permute-start | bytes 12296 | tf_op jit(solution)/shard_map/ppermute | solution.py:47
  138.8 1.2 collective-permute-start.14
  140.0 3.7 %collective-permute-start.15 = (f32[16,64]{1,0:T(8,128)S(1)}, f32[16,64]{1,0:T(8,128)S(1)}, u32[]{:S(2)}, u32[]{:S(2)}) collective-permute-start(f32[16,64]{1,0:T(8,128)S(1)} %add.258), channel_id=1, source_target_pairs={{0,2},{1,3},{2,0},{3,1},{4,6},{5,7},{6,4},{7,5},{8,10},{9,11},{10,... | collective-permute-start | bytes 12296 | tf_op jit(solution)/shard_map/ppermute | solution.py:165
  (3 other events, 12.6 us)

commit v3 on v2

--- a/solution.py
+++ b/solution.py
@@ -152,7 +152,26 @@
     tile = lax.dot_general(
         gathered, index, (((1,), (1,)), ((), ())), preferred_element_type=jnp.float32
     )
-    picked = jnp.take_along_axis(tile, jnp.clip(local_rows, 0, shard_rows - 1), axis=1)
+    wanted = jnp.clip(local_rows, 0, shard_rows - 1)
+    minor = 16
+    if shard_rows % minor == 0:
+        major = shard_rows // minor
+        major_hot = (
+            (wanted // minor)[:, :, None] == jnp.arange(major, dtype=jnp.int32)[None, None, :]
+        ).astype(jnp.float32)
+        rows_of = jnp.einsum(
+            "tca,tab->tcb",
+            major_hot,
+            tile.reshape(all_texts, major, minor),
+            precision=lax.Precision.HIGHEST,
+            preferred_element_type=jnp.float32,
+        )
+        minor_hot = (wanted % minor)[:, :, None] == jnp.arange(minor, dtype=jnp.int32)[None, None, :]
+        picked = jnp.sum(jnp.where(minor_hot, rows_of, 0.0), axis=2)
+    else:
+        row_ids = jnp.arange(shard_rows, dtype=jnp.int32)
+        chosen = wanted[:, :, None] == row_ids[None, None, :]
+        picked = jnp.sum(jnp.where(chosen, tile[:, None, :], 0.0), axis=2)
     partial_scores = jnp.where(held, picked, 0.0)
     if not xor_ok:
         slice_scores = lax.psum_scatter(

time: 145 us -> 85.9 us (0.59)
  local copies, waits for them, and re-layouts: 67.2 us -> 3.62 us
  matrix products: 14.4 us -> 19.3 us
    gather x3 -> x0, local copies, waits for them, and re-layouts: 65.2 us -> none  [body(): jnp.take_along_axis(tile, jnp.clip(local_rows, 0, shard_rows - 1), axis=1)]
    dot_general x0 -> x1, matrix products: none -> 4.92 us  [body(): jnp.einsum('tca,tab->tcb', major_hot, tile.reshape(all_texts, major, mino...]
    reshape x0 -> x1, local copies, waits for them, and re-layouts: none -> 1.61 us  [body(): tile.reshape(all_texts, major, minor)]
where the time goes in v3:
time: 85.9 us; the launch traced here: 85.6 us
  waiting for transfers between devices  34.6 us (40%)
  starting transfers between devices  23.5 us (27%)
  matrix products  19.3 us (22%)
  local copies, waits for them, and re-layouts  3.62 us (4%)
  other arithmetic  3.51 us (4%)
  between operations  1.09 us (1%)
    ppermute x7, waiting for transfers between devices, reduce_scatter_xor(): got = lax.ppermute(theirs.astype(wire), axis, xor_pairs(n, k))  16.1 us
    ppermute x7, waiting for transfers between devices, all_gather_xor(): other = lax.ppermute(cur, axis, xor_pairs(n, k))  15.3 us
    ppermute x7, starting transfers between devices, reduce_scatter_xor(): got = lax.ppermute(theirs.astype(wire), axis, xor_pairs(n, k))  11.8 us
    ppermute x7, starting transfers between devices, all_gather_xor(): other = lax.ppermute(cur, axis, xor_pairs(n, k))  10 us
    dot_general x1, matrix products, body(): jnp.dot(activated, w_down, preferred_element_type=jnp.float32)  5.11 us
    dot_general x1, matrix products, body(): jnp.einsum('tca,tab->tcb', major_hot, tile.reshape(all_texts, major, mino...  4.92 us
    dot_general x3, matrix products, body(): jnp.dot(hidden, w_qkv[j], preferred_element_type=jnp.float32) + b_qkv[j]  4.68 us
    ppermute x2, waiting for transfers between devices, body(): lax.ppermute(text_scores, 'tensor', xor_pairs(n_tensor, k))  3.15 us
  transfers between devices with their start and end apart: 16, of which 16 were waited for; matrix products, arithmetic and copies ran while one was open for 0% of the time, Pallas kernels for 0%

profile of v3, /device:TPU:0, one launch (start us, length us, event | category | flops | bytes accessed | tf_op | source)
XLA Modules:
  0.0 85.6 jit_solution(16147970987222288727)
XLA Ops:
  11.2 2.9 %collective-permute-start.1 = (bf16[64,1024]{1,0:T(8,128)(2,1)S(1)}, bf16[64,1024]{1,0:T(8,128)(2,1)S(1)}, u32[]{:S(2)}, u32[]{:S(2)}) collective-permute-start(bf16[64,1024]{1,0:T(8,128)(2,1)S(1)} %dynamic-slice_convert_fusion.1), channel_id=1, source_target_pairs={{0,2},{1,3},{2,0},{3,1},{4,6},{5,7},{6,4},{7,5},{8,10},{9,11},{10,... | collective-permute-start | bytes 393224 | tf_op jit(solution)/shard_map/ppermute | solution.py:47
  14.1 3.8 %collective-permute-done.1 = bf16[64,1024]{1,0:T(8,128)(2,1)S(1)} collective-permute-done((bf16[64,1024]{1,0:T(8,128)(2,1)S(1)}, bf16[64,1024]{1,0:T(8,128)(2,1)S(1)}, u32[]{:S(2)}, u32[]{:S(2)}) %collective-permute-start.1) | collective-permute-done | bytes 131104 | tf_op jit(solution)/shard_map/ppermute | solution.py:47
  19.3 1.8 %collective-permute-start.2 = (bf16[64,1024]{1,0:T(8,128)(2,1)S(1)}, bf16[64,1024]{1,0:T(8,128)(2,1)S(1)}, u32[]{:S(2)}, u32[]{:S(2)}) collective-permute-start(bf16[64,1024]{1,0:T(8,128)(2,1)S(1)} %add_convert_fusion.1), channel_id=1, source_target_pairs={{0,2},{1,3},{2,0},{3,1},{4,6},{5,7},{6,4},{7,5},{8,10},{9,11},{10,... | collective-permute-start | bytes 393224 | tf_op jit(solution)/shard_map/ppermute | solution.py:58
  21.1 3.3 %collective-permute-done.2 = bf16[64,1024]{1,0:T(8,128)(2,1)S(1)} collective-permute-done((bf16[64,1024]{1,0:T(8,128)(2,1)S(1)}, bf16[64,1024]{1,0:T(8,128)(2,1)S(1)}, u32[]{:S(2)}, u32[]{:S(2)}) %collective-permute-start.2) | collective-permute-done | bytes 131104 | tf_op jit(solution)/shard_map/ppermute | solution.py:58
  26.3 5.1 %convolution_convert_fusion.1 = bf16[256,1024]{1,0:T(8,128)(2,1)S(1)} fusion(bf16[1024,1024]{1,0:T(8,128)(2,1)S(1)} %copy-done, bf16[256,1024]{1,0:T(8,128)(2,1)S(1)} %maximum_select_fusion, bf16[1024,1024]{1,0:T(8,128)(2,1)} %param.24, f32[1024]{0:T(1024)S(1)} %copy-done.10), kind=kOutput, calls=%fused_computation.11 | convolution fusion | flops 1091305472 | bytes 5246976 | tf_op jit(solution)/shard_map/dot_general | solution.py:123
  33.2 1.8 %collective-permute-start.5 = (bf16[64,1024]{1,0:T(8,128)(2,1)S(1)}, bf16[64,1024]{1,0:T(8,128)(2,1)S(1)}, u32[]{:S(2)}, u32[]{:S(2)}) collective-permute-start(bf16[64,1024]{1,0:T(8,128)(2,1)S(1)} %dynamic-slice_convert_fusion), channel_id=1, source_target_pairs={{0,2},{1,3},{2,0},{3,1},{4,6},{5,7},{6,4},{7,5},{8,10},{9,11},{10,... | collective-permute-start | bytes 393224 | tf_op jit(solution)/shard_map/ppermute | solution.py:47
  34.9 3.9 %collective-permute-done.5 = bf16[64,1024]{1,0:T(8,128)(2,1)S(1)} collective-permute-done((bf16[64,1024]{1,0:T(8,128)(2,1)S(1)}, bf16[64,1024]{1,0:T(8,128)(2,1)S(1)}, u32[]{:S(2)}, u32[]{:S(2)}) %collective-permute-start.5) | collective-permute-done | bytes 131104 | tf_op jit(solution)/shard_map/ppermute | solution.py:47
  39.3 1.7 %collective-permute-start.6 = (bf16[64,1024]{1,0:T(8,128)(2,1)S(1)}, bf16[64,1024]{1,0:T(8,128)(2,1)S(1)}, u32[]{:S(2)}, u32[]{:S(2)}) collective-permute-start(bf16[64,1024]{1,0:T(8,128)(2,1)S(1)} %add_convert_fusion), channel_id=1, source_target_pairs={{0,2},{1,3},{2,0},{3,1},{4,6},{5,7},{6,4},{7,5},{8,10},{9,11},{10,... | collective-permute-start | bytes 393224 | tf_op jit(solution)/shard_map/ppermute | solution.py:58
  41.0 3.3 %collective-permute-done.6 = bf16[64,1024]{1,0:T(8,128)(2,1)S(1)} collective-permute-done((bf16[64,1024]{1,0:T(8,128)(2,1)S(1)}, bf16[64,1024]{1,0:T(8,128)(2,1)S(1)}, u32[]{:S(2)}, u32[]{:S(2)}) %collective-permute-start.6) | collective-permute-done | bytes 131104 | tf_op jit(solution)/shard_map/ppermute | solution.py:58
  47.3 1.7 %collective-permute-start.8 = (bf16[16,256]{1,0:T(8,128)(2,1)S(1)}, bf16[16,256]{1,0:T(8,128)(2,1)S(1)}, u32[]{:S(2)}, u32[]{:S(2)}) collective-permute-start(bf16[16,256]{1,0:T(8,128)(2,1)S(1)} %fusion.67), channel_id=1, source_target_pairs={{0,4},{4,0},{8,12},{12,8},{16,20},{20,16},{24,28},{28,24},{1,5},{5... | collective-permute-start | bytes 24584 | tf_op jit(solution)/shard_map/ppermute | solution.py:58
  49.0 1.9 %collective-permute-done.8 = bf16[16,256]{1,0:T(8,128)(2,1)S(1)} collective-permute-done((bf16[16,256]{1,0:T(8,128)(2,1)S(1)}, bf16[16,256]{1,0:T(8,128)(2,1)S(1)}, u32[]{:S(2)}, u32[]{:S(2)}) %collective-permute-start.8) | collective-permute-done | bytes 8224 | tf_op jit(solution)/shard_map/ppermute | solution.py:58
  51.0 1.8 %collective-permute-start.9 = (bf16[32,256]{1,0:T(8,128)(2,1)S(1)}, bf16[32,256]{1,0:T(8,128)(2,1)S(1)}, u32[]{:S(2)}, u32[]{:S(2)}) collective-permute-start(bf16[32,256]{1,0:T(8,128)(2,1)S(1)} %maximum_select_fusion.7), channel_id=1, source_target_pairs={{0,8},{4,12},{8,0},{12,4},{16,24},{20,28},{24,16},{28,20},{1,9},{5... | collective-permute-start | bytes 49160 | tf_op jit(solution)/shard_map/ppermute | solution.py:58
  52.8 1.9 %collective-permute-done.9 = bf16[32,256]{1,0:T(8,128)(2,1)S(1)} collective-permute-done((bf16[32,256]{1,0:T(8,128)(2,1)S(1)}, bf16[32,256]{1,0:T(8,128)(2,1)S(1)}, u32[]{:S(2)}, u32[]{:S(2)}) %collective-permute-start.9) | collective-permute-done | bytes 16416 | tf_op jit(solution)/shard_map/ppermute | solution.py:58
  54.7 2.8 %collective-permute-start.10 = (bf16[64,256]{1,0:T(8,128)(2,1)S(1)}, bf16[64,256]{1,0:T(8,128)(2,1)S(1)}, u32[]{:S(2)}, u32[]{:S(2)}) collective-permute-start(bf16[64,256]{1,0:T(8,128)(2,1)S(1)} %maximum_select_fusion.6), channel_id=1, source_target_pairs={{0,16},{4,20},{8,24},{12,28},{16,0},{20,4},{24,8},{28,12},{1,17},{... | collective-permute-start | bytes 98312 | tf_op jit(solution)/shard_map/ppermute | solution.py:58
  57.7 1.9 %collective-permute-done.10 = bf16[64,256]{1,0:T(8,128)(2,1)S(1)} collective-permute-done((bf16[64,256]{1,0:T(8,128)(2,1)S(1)}, bf16[64,256]{1,0:T(8,128)(2,1)S(1)}, u32[]{:S(2)}, u32[]{:S(2)}) %collective-permute-start.10) | collective-permute-done | bytes 32800 | tf_op jit(solution)/shard_map/ppermute | solution.py:58
  62.8 4.9 %fusion.6 = f32[128,64]{1,0:T(8,128)S(1)} fusion(f32[128,128,16]{1,2,0:T(8,128)} %copy.31, s32[128,64]{1,0:T(8,128)S(1)} %get-tuple-element.7, s32[128,64]{1,0:T(8,128)S(1)} %get-tuple-element.6), kind=kOutput, calls=%fused_computation.12 | convolution fusion | flops 202760192 | bytes 1146880 | tf_op jit(solution)/shard_map/tca,tab->tcb/dot_general | solution.py:162
  67.8 2.9 %collective-permute-start.11 = (f32[64,64]{1,0:T(8,128)S(1)}, f32[64,64]{1,0:T(8,128)S(1)}, u32[]{:S(2)}, u32[]{:S(2)}) collective-permute-start(f32[64,64]{1,0:T(8,128)S(1)} %constant_dynamic-slice_fusion.1), channel_id=1, source_target_pairs={{0,16},{4,20},{8,24},{12,28},{16,0},{20,4},{24,8},{28,12},{1,17},{... | collective-permute-start | bytes 49160 | tf_op jit(solution)/shard_map/ppermute | solution.py:47
  70.7 2.0 %collective-permute-done.11 = f32[64,64]{1,0:T(8,128)S(1)} collective-permute-done((f32[64,64]{1,0:T(8,128)S(1)}, f32[64,64]{1,0:T(8,128)S(1)}, u32[]{:S(2)}, u32[]{:S(2)}) %collective-permute-start.11) | collective-permute-done | bytes 16416 | tf_op jit(solution)/shard_map/ppermute | solution.py:47
  72.7 1.8 %collective-permute-start.12 = (f32[32,64]{1,0:T(8,128)S(1)}, f32[32,64]{1,0:T(8,128)S(1)}, u32[]{:S(2)}, u32[]{:S(2)}) collective-permute-start(f32[32,64]{1,0:T(8,128)S(1)} %constant_dynamic-slice_fusion), channel_id=1, source_target_pairs={{0,8},{4,12},{8,0},{12,4},{16,24},{20,28},{24,16},{28,20},{1,9},{5... | collective-permute-start | bytes 24584 | tf_op jit(solution)/shard_map/ppermute | solution.py:47
  74.5 2.0 %collective-permute-done.12 = f32[32,64]{1,0:T(8,128)S(1)} collective-permute-done((f32[32,64]{1,0:T(8,128)S(1)}, f32[32,64]{1,0:T(8,128)S(1)}, u32[]{:S(2)}, u32[]{:S(2)}) %collective-permute-start.12) | collective-permute-done | bytes 8224 | tf_op jit(solution)/shard_map/ppermute | solution.py:47
  76.5 1.7 %collective-permute-start.13 = (f32[16,64]{1,0:T(8,128)S(1)}, f32[16,64]{1,0:T(8,128)S(1)}, u32[]{:S(2)}, u32[]{:S(2)}) collective-permute-start(f32[16,64]{1,0:T(8,128)S(1)} %constant_dynamic-slice_fusion.3), channel_id=1, source_target_pairs={{0,4},{4,0},{8,12},{12,8},{16,20},{20,16},{24,28},{28,24},{1,5},{5... | collective-permute-start | bytes 12296 | tf_op jit(solution)/shard_map/ppermute | solution.py:47
  78.2 1.9 %collective-permute-done.13 = f32[16,64]{1,0:T(8,128)S(1)} collective-permute-done((f32[16,64]{1,0:T(8,128)S(1)}, f32[16,64]{1,0:T(8,128)S(1)}, u32[]{:S(2)}, u32[]{:S(2)}) %collective-permute-start.13) | collective-permute-done | bytes 4128 | tf_op jit(solution)/shard_map/ppermute | solution.py:47
  81.4 1.7 %collective-permute-start.15 = (f32[16,64]{1,0:T(8,128)S(1)}, f32[16,64]{1,0:T(8,128)S(1)}, u32[]{:S(2)}, u32[]{:S(2)}) collective-permute-start(f32[16,64]{1,0:T(8,128)S(1)} %add.259), channel_id=1, source_target_pairs={{0,2},{1,3},{2,0},{3,1},{4,6},{5,7},{6,4},{7,5},{8,10},{9,11},{10,... | collective-permute-start | bytes 12296 | tf_op jit(solution)/shard_map/ppermute | solution.py:184
  83.0 2.0 %collective-permute-done.15 = f32[16,64]{1,0:T(8,128)S(1)} collective-permute-done((f32[16,64]{1,0:T(8,128)S(1)}, f32[16,64]{1,0:T(8,128)S(1)}, u32[]{:S(2)}, u32[]{:S(2)}) %collective-permute-start.15) | collective-permute-done | bytes 4128 | tf_op jit(solution)/shard_map/ppermute | solution.py:184
  (84 shorter events, 24.0 us)
Async XLA Ops:
  0.6 25.6 %copy-start = (bf16[1024,1024]{1,0:T(8,128)(2,1)S(1)}, bf16[1024,1024]{1,0:T(8,128)(2,1)}, u32[]{:S(2)}) copy-start(bf16[1024,1024]{1,0:T(8,128)(2,1)} %param.26) | copy-start | bytes 6291460
  8.0 10.0 %copy-start.3 = (f32[1024]{0:T(1024)S(1)}, f32[1024]{0:T(1024)}, u32[]{:S(2)}) copy-start(f32[1024]{0:T(1024)} %param.21) | copy-start | bytes 12292
  8.0 11.2 %copy-start.4 = (f32[1024]{0:T(1024)S(1)}, f32[1024]{0:T(1024)}, u32[]{:S(2)}) copy-start(f32[1024]{0:T(1024)} %param.23) | copy-start | bytes 12292
  8.0 11.2 %copy-start.5 = (f32[1024]{0:T(1024)S(1)}, f32[1024]{0:T(1024)}, u32[]{:S(2)}) copy-start(f32[1024]{0:T(1024)} %param.22) | copy-start | bytes 12292
  9.4 1.7 %collective-permute-start = (bf16[128,1024]{1,0:T(8,128)(2,1)S(1)}, bf16[128,1024]{1,0:T(8,128)(2,1)S(1)}, u32[]{:S(2)}, u32[]{:S(2)}) collective-permute-start(bf16[128,1024]{1,0:T(8,128)(2,1)S(1)} %constant_dynamic-slice_fusion.4), channel_id=1, source_target_pairs={{0,1},{1,0},{2,3},{3,2},{4,5},{5,4},{6,7},{7,6},{8,9},{9,8},{10,11... | collective-permute-start | bytes 786440 | tf_op jit(solution)/shard_map/ppermute | solution.py:47
  9.9 16.3 %copy-start.10 = (f32[1024]{0:T(1024)S(1)}, f32[1024]{0:T(1024)}, u32[]{:S(2)}) copy-start(f32[1024]{0:T(1024)} %param.25) | copy-start | bytes 12292
  11.2 6.7 %collective-permute-start.1 = (bf16[64,1024]{1,0:T(8,128)(2,1)S(1)}, bf16[64,1024]{1,0:T(8,128)(2,1)S(1)}, u32[]{:S(2)}, u32[]{:S(2)}) collective-permute-start(bf16[64,1024]{1,0:T(8,128)(2,1)S(1)} %dynamic-slice_convert_fusion.1), channel_id=1, source_target_pairs={{0,2},{1,3},{2,0},{3,1},{4,6},{5,7},{6,4},{7,5},{8,10},{9,11},{10,... | collective-permute-start | bytes 393224 | tf_op jit(solution)/shard_map/ppermute | solution.py:47
  19.3 5.1 %collective-permute-start.2 = (bf16[64,1024]{1,0:T(8,128)(2,1)S(1)}, bf16[64,1024]{1,0:T(8,128)(2,1)S(1)}, u32[]{:S(2)}, u32[]{:S(2)}) collective-permute-start(bf16[64,1024]{1,0:T(8,128)(2,1)S(1)} %add_convert_fusion.1), channel_id=1, source_target_pairs={{0,2},{1,3},{2,0},{3,1},{4,6},{5,7},{6,4},{7,5},{8,10},{9,11},{10,... | collective-permute-start | bytes 393224 | tf_op jit(solution)/shard_map/ppermute | solution.py:58
  24.5 1.6 %collective-permute-start.3 = (bf16[128,1024]{1,0:T(8,128)(2,1)S(1)}, bf16[128,1024]{1,0:T(8,128)(2,1)S(1)}, u32[]{:S(2)}, u32[]{:S(2)}) collective-permute-start(bf16[128,1024]{1,0:T(8,128)(2,1)S(1)} %maximum_select_fusion.2), channel_id=1, source_target_pairs={{0,1},{1,0},{2,3},{3,2},{4,5},{5,4},{6,7},{7,6},{8,9},{9,8},{10,11... | collective-permute-start | bytes 786440 | tf_op jit(solution)/shard_map/ppermute | solution.py:58
  26.3 12.5 %copy-start.6 = (f32[1024]{0:T(1024)S(1)}, f32[1024]{0:T(1024)}, u32[]{:S(2)}) copy-start(f32[1024]{0:T(1024)} %param.27) | copy-start | bytes 12292
  31.4 7.8 %copy-start.7 = (f32[1024]{0:T(1024)S(1)}, f32[1024]{0:T(1024)}, u32[]{:S(2)}) copy-start(f32[1024]{0:T(1024)} %param.29) | copy-start | bytes 12292
  31.4 1.6 %collective-permute-start.4 = (bf16[128,1024]{1,0:T(8,128)(2,1)S(1)}, bf16[128,1024]{1,0:T(8,128)(2,1)S(1)}, u32[]{:S(2)}, u32[]{:S(2)}) collective-permute-start(bf16[128,1024]{1,0:T(8,128)(2,1)S(1)} %constant_dynamic-slice_fusion.2), channel_id=1, source_target_pairs={{0,1},{1,0},{2,3},{3,2},{4,5},{5,4},{6,7},{7,6},{8,9},{9,8},{10,11... | collective-permute-start | bytes 786440 | tf_op jit(solution)/shard_map/ppermute | solution.py:47
  33.1 19.6 %copy-start.2 = (s32[128,64]{0,1:T(8,128)S(1)}, s32[128,64]{0,1:T(8,128)}, u32[]{:S(2)}) copy-start(s32[128,64]{0,1:T(8,128)} %param.31) | copy-start | bytes 98308
  33.2 5.6 %collective-permute-start.5 = (bf16[64,1024]{1,0:T(8,128)(2,1)S(1)}, bf16[64,1024]{1,0:T(8,128)(2,1)S(1)}, u32[]{:S(2)}, u32[]{:S(2)}) collective-permute-start(bf16[64,1024]{1,0:T(8,128)(2,1)S(1)} %dynamic-slice_convert_fusion), channel_id=1, source_target_pairs={{0,2},{1,3},{2,0},{3,1},{4,6},{5,7},{6,4},{7,5},{8,10},{9,11},{10,... | collective-permute-start | bytes 393224 | tf_op jit(solution)/shard_map/ppermute | solution.py:47
  39.3 5.0 %collective-permute-start.6 = (bf16[64,1024]{1,0:T(8,128)(2,1)S(1)}, bf16[64,1024]{1,0:T(8,128)(2,1)S(1)}, u32[]{:S(2)}, u32[]{:S(2)}) collective-permute-start(bf16[64,1024]{1,0:T(8,128)(2,1)S(1)} %add_convert_fusion), channel_id=1, source_target_pairs={{0,2},{1,3},{2,0},{3,1},{4,6},{5,7},{6,4},{7,5},{8,10},{9,11},{10,... | collective-permute-start | bytes 393224 | tf_op jit(solution)/shard_map/ppermute | solution.py:58
  44.4 1.6 %collective-permute-start.7 = (bf16[128,1024]{1,0:T(8,128)(2,1)S(1)}, bf16[128,1024]{1,0:T(8,128)(2,1)S(1)}, u32[]{:S(2)}, u32[]{:S(2)}) collective-permute-start(bf16[128,1024]{1,0:T(8,128)(2,1)S(1)} %maximum_select_fusion.3), channel_id=1, source_target_pairs={{0,1},{1,0},{2,3},{3,2},{4,5},{5,4},{6,7},{7,6},{8,9},{9,8},{10,11... | collective-permute-start | bytes 786440 | tf_op jit(solution)/shard_map/ppermute | solution.py:58
  47.3 3.7 %collective-permute-start.8 = (bf16[16,256]{1,0:T(8,128)(2,1)S(1)}, bf16[16,256]{1,0:T(8,128)(2,1)S(1)}, u32[]{:S(2)}, u32[]{:S(2)}) collective-permute-start(bf16[16,256]{1,0:T(8,128)(2,1)S(1)} %fusion.67), channel_id=1, source_target_pairs={{0,4},{4,0},{8,12},{12,8},{16,20},{20,16},{24,28},{28,24},{1,5},{5... | collective-permute-start | bytes 24584 | tf_op jit(solution)/shard_map/ppermute | solution.py:58
  51.0 3.7 %collective-permute-start.9 = (bf16[32,256]{1,0:T(8,128)(2,1)S(1)}, bf16[32,256]{1,0:T(8,128)(2,1)S(1)}, u32[]{:S(2)}, u32[]{:S(2)}) collective-permute-start(bf16[32,256]{1,0:T(8,128)(2,1)S(1)} %maximum_select_fusion.7), channel_id=1, source_target_pairs={{0,8},{4,12},{8,0},{12,4},{16,24},{20,28},{24,16},{28,20},{1,9},{5... | collective-permute-start | bytes 49160 | tf_op jit(solution)/shard_map/ppermute | solution.py:58
  54.7 4.9 %collective-permute-start.10 = (bf16[64,256]{1,0:T(8,128)(2,1)S(1)}, bf16[64,256]{1,0:T(8,128)(2,1)S(1)}, u32[]{:S(2)}, u32[]{:S(2)}) collective-permute-start(bf16[64,256]{1,0:T(8,128)(2,1)S(1)} %maximum_select_fusion.6), channel_id=1, source_target_pairs={{0,16},{4,20},{8,24},{12,28},{16,0},{20,4},{24,8},{28,12},{1,17},{... | collective-permute-start | bytes 98312 | tf_op jit(solution)/shard_map/ppermute | solution.py:58
  67.8 4.9 %collective-permute-start.11 = (f32[64,64]{1,0:T(8,128)S(1)}, f32[64,64]{1,0:T(8,128)S(1)}, u32[]{:S(2)}, u32[]{:S(2)}) collective-permute-start(f32[64,64]{1,0:T(8,128)S(1)} %constant_dynamic-slice_fusion.1), channel_id=1, source_target_pairs={{0,16},{4,20},{8,24},{12,28},{16,0},{20,4},{24,8},{28,12},{1,17},{... | collective-permute-start | bytes 49160 | tf_op jit(solution)/shard_map/ppermute | solution.py:47
  72.7 3.8 %collective-permute-start.12 = (f32[32,64]{1,0:T(8,128)S(1)}, f32[32,64]{1,0:T(8,128)S(1)}, u32[]{:S(2)}, u32[]{:S(2)}) collective-permute-start(f32[32,64]{1,0:T(8,128)S(1)} %constant_dynamic-slice_fusion), channel_id=1, source_target_pairs={{0,8},{4,12},{8,0},{12,4},{16,24},{20,28},{24,16},{28,20},{1,9},{5... | collective-permute-start | bytes 24584 | tf_op jit(solution)/shard_map/ppermute | solution.py:47
  76.5 3.7 %collective-permute-start.13 = (f32[16,64]{1,0:T(8,128)S(1)}, f32[16,64]{1,0:T(8,128)S(1)}, u32[]{:S(2)}, u32[]{:S(2)}) collective-permute-start(f32[16,64]{1,0:T(8,128)S(1)} %constant_dynamic-slice_fusion.3), channel_id=1, source_target_pairs={{0,4},{4,0},{8,12},{12,8},{16,20},{20,16},{24,28},{28,24},{1,5},{5... | collective-permute-start | bytes 12296 | tf_op jit(solution)/shard_map/ppermute | solution.py:47
  80.2 1.2 %collective-permute-start.14 = (f32[16,64]{1,0:T(8,128)S(1)}, f32[16,64]{1,0:T(8,128)S(1)}, u32[]{:S(2)}, u32[]{:S(2)}) collective-permute-start(f32[16,64]{1,0:T(8,128)S(1)} %dynamic-slice_add_fusion.2), channel_id=1, source_target_pairs={{0,1},{1,0},{2,3},{3,2},{4,5},{5,4},{6,7},{7,6},{8,9},{9,8},{10,11... | collective-permute-start | bytes 12296 | tf_op jit(solution)/shard_map/ppermute | solution.py:184
  81.4 3.7 %collective-permute-start.15 = (f32[16,64]{1,0:T(8,128)S(1)}, f32[16,64]{1,0:T(8,128)S(1)}, u32[]{:S(2)}, u32[]{:S(2)}) collective-permute-start(f32[16,64]{1,0:T(8,128)S(1)} %add.259), channel_id=1, source_target_pairs={{0,2},{1,3},{2,0},{3,1},{4,6},{5,7},{6,4},{7,5},{8,10},{9,11},{10,... | collective-permute-start | bytes 12296 | tf_op jit(solution)/shard_map/ppermute | solution.py:184
  (3 other events, 12.6 us)

commit v4 on v3

--- a/solution.py
+++ b/solution.py
@@ -158,14 +158,20 @@
         major = shard_rows // minor
         major_hot = (
             (wanted // minor)[:, :, None] == jnp.arange(major, dtype=jnp.int32)[None, None, :]
-        ).astype(jnp.float32)
-        rows_of = jnp.einsum(
-            "tca,tab->tcb",
-            major_hot,
-            tile.reshape(all_texts, major, minor),
-            precision=lax.Precision.HIGHEST,
-            preferred_element_type=jnp.float32,
-        )
+        ).astype(jnp.bfloat16)
+        high = tile.astype(jnp.bfloat16)
+        rest = tile - high.astype(jnp.float32)
+        middle = rest.astype(jnp.bfloat16)
+        low = (rest - middle.astype(jnp.float32)).astype(jnp.bfloat16)
+        parts = jnp.concatenate(
+            [p.reshape(all_texts, major, minor) for p in (high, middle, low)], axis=2
+        )
+        chosen_parts = jnp.einsum(
+            "tca,tab->tcb", major_hot, parts, preferred_element_type=jnp.float32
+        )
+        rows_of = (
+            chosen_parts[:, :, :minor] + chosen_parts[:, :, minor : 2 * minor]
+        ) + chosen_parts[:, :, 2 * minor :]
         minor_hot = (wanted % minor)[:, :, None] == jnp.arange(minor, dtype=jnp.int32)[None, None, :]
         picked = jnp.sum(jnp.where(minor_hot, rows_of, 0.0), axis=2)
     else:

time: 85.9 us -> 92.8 us (1.080)
  local copies, waits for them, and re-layouts: 3.62 us -> 7.96 us
  matrix products: 19.3 us -> 21 us
    convert_element_type x0 -> x3, local copies, waits for them, and re-layouts: none -> 2.94 us  [the longest x1 1.37 us: body(): middle = rest.astype(jnp.bfloat16)]
    reshape x1 -> x3, local copies, waits for them, and re-layouts: 1.61 us -> 3.78 us  [body(): p.reshape(all_texts, major, minor)]
    dot_general x1, matrix products: 1.65 us -> 2.89 us  [body(): lax.dot_general(gathered, index, (((1,), (1,)), ((), ())), preferred_elem...]
where the time goes in v4:
time: 92.8 us; the launch traced here: 92.2 us
  waiting for transfers between devices  34.6 us (37%)
  starting transfers between devices  23.5 us (25%)
  matrix products  21 us (23%)
  local copies, waits for them, and re-layouts  7.96 us (9%)
  other arithmetic  3.96 us (4%)
  between operations  1.12 us (1%)
    ppermute x7, waiting for transfers between devices, reduce_scatter_xor(): got = lax.ppermute(theirs.astype(wire), axis, xor_pairs(n, k))  16.1 us
    ppermute x7, waiting for transfers between devices, all_gather_xor(): other = lax.ppermute(cur, axis, xor_pairs(n, k))  15.3 us
    ppermute x7, starting transfers between devices, reduce_scatter_xor(): got = lax.ppermute(theirs.astype(wire), axis, xor_pairs(n, k))  11.8 us
    ppermute x7, starting transfers between devices, all_gather_xor(): other = lax.ppermute(cur, axis, xor_pairs(n, k))  10 us
    dot_general x1, matrix products, body(): jnp.einsum('tca,tab->tcb', major_hot, parts, preferred_element_type=jnp.f...  5.39 us
    dot_general x1, matrix products, body(): jnp.dot(activated, w_down, preferred_element_type=jnp.float32)  5.11 us
    dot_general x3, matrix products, body(): jnp.dot(hidden, w_qkv[j], preferred_element_type=jnp.float32) + b_qkv[j]  4.68 us
    reshape x3, local copies, waits for them, and re-layouts, body(): p.reshape(all_texts, major, minor)  3.78 us
  transfers between devices with their start and end apart: 16, of which 16 were waited for; matrix products, arithmetic and copies ran while one was open for 0% of the time, Pallas kernels for 0%

profile of v4, /device:TPU:0, one launch (start us, length us, event | category | flops | bytes accessed | tf_op | source)
XLA Modules:
  0.0 92.2 jit_solution(6440244110573084030)
XLA Ops:
  11.2 2.9 %collective-permute-start.1 = (bf16[64,1024]{1,0:T(8,128)(2,1)S(1)}, bf16[64,1024]{1,0:T(8,128)(2,1)S(1)}, u32[]{:S(2)}, u32[]{:S(2)}) collective-permute-start(bf16[64,1024]{1,0:T(8,128)(2,1)S(1)} %dynamic-slice_convert_fusion.1), channel_id=1, source_target_pairs={{0,2},{1,3},{2,0},{3,1},{4,6},{5,7},{6,4},{7,5},{8,10},{9,11},{10,... | collective-permute-start | bytes 393224 | tf_op jit(solution)/shard_map/ppermute | solution.py:47
  14.1 3.8 %collective-permute-done.1 = bf16[64,1024]{1,0:T(8,128)(2,1)S(1)} collective-permute-done((bf16[64,1024]{1,0:T(8,128)(2,1)S(1)}, bf16[64,1024]{1,0:T(8,128)(2,1)S(1)}, u32[]{:S(2)}, u32[]{:S(2)}) %collective-permute-start.1) | collective-permute-done | bytes 131104 | tf_op jit(solution)/shard_map/ppermute | solution.py:47
  19.3 1.8 %collective-permute-start.2 = (bf16[64,1024]{1,0:T(8,128)(2,1)S(1)}, bf16[64,1024]{1,0:T(8,128)(2,1)S(1)}, u32[]{:S(2)}, u32[]{:S(2)}) collective-permute-start(bf16[64,1024]{1,0:T(8,128)(2,1)S(1)} %add_convert_fusion.1), channel_id=1, source_target_pairs={{0,2},{1,3},{2,0},{3,1},{4,6},{5,7},{6,4},{7,5},{8,10},{9,11},{10,... | collective-permute-start | bytes 393224 | tf_op jit(solution)/shard_map/ppermute | solution.py:58
  21.1 3.3 %collective-permute-done.2 = bf16[64,1024]{1,0:T(8,128)(2,1)S(1)} collective-permute-done((bf16[64,1024]{1,0:T(8,128)(2,1)S(1)}, bf16[64,1024]{1,0:T(8,128)(2,1)S(1)}, u32[]{:S(2)}, u32[]{:S(2)}) %collective-permute-start.2) | collective-permute-done | bytes 131104 | tf_op jit(solution)/shard_map/ppermute | solution.py:58
  26.3 5.1 %convolution_convert_fusion.1 = bf16[256,1024]{1,0:T(8,128)(2,1)S(1)} fusion(bf16[1024,1024]{1,0:T(8,128)(2,1)S(1)} %copy-done, bf16[256,1024]{1,0:T(8,128)(2,1)S(1)} %maximum_select_fusion, bf16[1024,1024]{1,0:T(8,128)(2,1)} %param.24, f32[1024]{0:T(1024)S(1)} %copy-done.11), kind=kOutput, calls=%fused_computation.15 | convolution fusion | flops 1091305472 | bytes 5246976 | tf_op jit(solution)/shard_map/dot_general | solution.py:123
  33.2 1.8 %collective-permute-start.5 = (bf16[64,1024]{1,0:T(8,128)(2,1)S(1)}, bf16[64,1024]{1,0:T(8,128)(2,1)S(1)}, u32[]{:S(2)}, u32[]{:S(2)}) collective-permute-start(bf16[64,1024]{1,0:T(8,128)(2,1)S(1)} %dynamic-slice_convert_fusion), channel_id=1, source_target_pairs={{0,2},{1,3},{2,0},{3,1},{4,6},{5,7},{6,4},{7,5},{8,10},{9,11},{10,... | collective-permute-start | bytes 393224 | tf_op jit(solution)/shard_map/ppermute | solution.py:47
  34.9 3.9 %collective-permute-done.5 = bf16[64,1024]{1,0:T(8,128)(2,1)S(1)} collective-permute-done((bf16[64,1024]{1,0:T(8,128)(2,1)S(1)}, bf16[64,1024]{1,0:T(8,128)(2,1)S(1)}, u32[]{:S(2)}, u32[]{:S(2)}) %collective-permute-start.5) | collective-permute-done | bytes 131104 | tf_op jit(solution)/shard_map/ppermute | solution.py:47
  39.3 1.7 %collective-permute-start.6 = (bf16[64,1024]{1,0:T(8,128)(2,1)S(1)}, bf16[64,1024]{1,0:T(8,128)(2,1)S(1)}, u32[]{:S(2)}, u32[]{:S(2)}) collective-permute-start(bf16[64,1024]{1,0:T(8,128)(2,1)S(1)} %add_convert_fusion), channel_id=1, source_target_pairs={{0,2},{1,3},{2,0},{3,1},{4,6},{5,7},{6,4},{7,5},{8,10},{9,11},{10,... | collective-permute-start | bytes 393224 | tf_op jit(solution)/shard_map/ppermute | solution.py:58
  41.0 3.3 %collective-permute-done.6 = bf16[64,1024]{1,0:T(8,128)(2,1)S(1)} collective-permute-done((bf16[64,1024]{1,0:T(8,128)(2,1)S(1)}, bf16[64,1024]{1,0:T(8,128)(2,1)S(1)}, u32[]{:S(2)}, u32[]{:S(2)}) %collective-permute-start.6) | collective-permute-done | bytes 131104 | tf_op jit(solution)/shard_map/ppermute | solution.py:58
  46.5 1.7 %collective-permute-start.8 = (bf16[16,256]{1,0:T(8,128)(2,1)S(1)}, bf16[16,256]{1,0:T(8,128)(2,1)S(1)}, u32[]{:S(2)}, u32[]{:S(2)}) collective-permute-start(bf16[16,256]{1,0:T(8,128)(2,1)S(1)} %fusion.73), channel_id=1, source_target_pairs={{0,4},{4,0},{8,12},{12,8},{16,20},{20,16},{24,28},{28,24},{1,5},{5... | collective-permute-start | bytes 24584 | tf_op jit(solution)/shard_map/ppermute | solution.py:58
  48.2 1.9 %collective-permute-done.8 = bf16[16,256]{1,0:T(8,128)(2,1)S(1)} collective-permute-done((bf16[16,256]{1,0:T(8,128)(2,1)S(1)}, bf16[16,256]{1,0:T(8,128)(2,1)S(1)}, u32[]{:S(2)}, u32[]{:S(2)}) %collective-permute-start.8) | collective-permute-done | bytes 8224 | tf_op jit(solution)/shard_map/ppermute | solution.py:58
  50.2 1.8 %collective-permute-start.9 = (bf16[32,256]{1,0:T(8,128)(2,1)S(1)}, bf16[32,256]{1,0:T(8,128)(2,1)S(1)}, u32[]{:S(2)}, u32[]{:S(2)}) collective-permute-start(bf16[32,256]{1,0:T(8,128)(2,1)S(1)} %maximum_select_fusion.7), channel_id=1, source_target_pairs={{0,8},{4,12},{8,0},{12,4},{16,24},{20,28},{24,16},{28,20},{1,9},{5... | collective-permute-start | bytes 49160 | tf_op jit(solution)/shard_map/ppermute | solution.py:58
  52.0 1.9 %collective-permute-done.9 = bf16[32,256]{1,0:T(8,128)(2,1)S(1)} collective-permute-done((bf16[32,256]{1,0:T(8,128)(2,1)S(1)}, bf16[32,256]{1,0:T(8,128)(2,1)S(1)}, u32[]{:S(2)}, u32[]{:S(2)}) %collective-permute-start.9) | collective-permute-done | bytes 16416 | tf_op jit(solution)/shard_map/ppermute | solution.py:58
  53.9 2.8 %collective-permute-start.10 = (bf16[64,256]{1,0:T(8,128)(2,1)S(1)}, bf16[64,256]{1,0:T(8,128)(2,1)S(1)}, u32[]{:S(2)}, u32[]{:S(2)}) collective-permute-start(bf16[64,256]{1,0:T(8,128)(2,1)S(1)} %maximum_select_fusion.6), channel_id=1, source_target_pairs={{0,16},{4,20},{8,24},{12,28},{16,0},{20,4},{24,8},{28,12},{1,17},{... | collective-permute-start | bytes 98312 | tf_op jit(solution)/shard_map/ppermute | solution.py:58
  56.9 1.9 %collective-permute-done.10 = bf16[64,256]{1,0:T(8,128)(2,1)S(1)} collective-permute-done((bf16[64,256]{1,0:T(8,128)(2,1)S(1)}, bf16[64,256]{1,0:T(8,128)(2,1)S(1)}, u32[]{:S(2)}, u32[]{:S(2)}) %collective-permute-start.10) | collective-permute-done | bytes 32800 | tf_op jit(solution)/shard_map/ppermute | solution.py:58
  58.8 2.9 %fusion.111 = (bf16[128,2048]{1,0:T(8,128)(2,1)}, bf16[128,2048]{1,0:T(8,128)(2,1)}, bf16[128,2048]{1,0:T(8,128)(2,1)}) fusion(bf16[2048,256]{1,0:T(8,128)(2,1)} %param.30, bf16[64,256]{1,0:T(8,128)(2,1)S(1)} %collective-permute-done.10, bf16[64,256]{1,0:T(8,128)(2,1)S(1)} %maximum_select_fusion.6, pred[]{:T(512)S(6)} %eq.101), kind=kOutput, calls=%fused_computation.182 | convolution fusion | flops 136347648 | bytes 2686977 | tf_op jit(solution)/shard_map/dot_general | solution.py:152
  68.5 5.4 %fusion.1 = f32[128,64,48]{1,2,0:T(8,128)S(1)} fusion(s32[128,64]{1,0:T(8,128)S(1)} %get-tuple-element.10, bf16[128,128,16]{1,2,0:T(8,128)(2,1)S(1)} %copy.41, bf16[128,128,16]{1,2,0:T(8,128)(2,1)} %copy.40, bf16[128,128,16]{1,2,0:T(8,128)(2,1)} %copy.39), kind=kOutput, calls=%fused_computation.2 | convolution fusion | flops 106430464 | bytes 3178496 | tf_op jit(solution)/shard_map/tca,tab->tcb/dot_general | solution.py:169
  74.4 2.9 %collective-permute-start.11 = (f32[64,64]{1,0:T(8,128)S(1)}, f32[64,64]{1,0:T(8,128)S(1)}, u32[]{:S(2)}, u32[]{:S(2)}) collective-permute-start(f32[64,64]{1,0:T(8,128)S(1)} %constant_dynamic-slice_fusion.1), channel_id=1, source_target_pairs={{0,16},{4,20},{8,24},{12,28},{16,0},{20,4},{24,8},{28,12},{1,17},{... | collective-permute-start | bytes 49160 | tf_op jit(solution)/shard_map/ppermute | solution.py:47
  77.2 2.0 %collective-permute-done.11 = f32[64,64]{1,0:T(8,128)S(1)} collective-permute-done((f32[64,64]{1,0:T(8,128)S(1)}, f32[64,64]{1,0:T(8,128)S(1)}, u32[]{:S(2)}, u32[]{:S(2)}) %collective-permute-start.11) | collective-permute-done | bytes 16416 | tf_op jit(solution)/shard_map/ppermute | solution.py:47
  79.3 1.8 %collective-permute-start.12 = (f32[32,64]{1,0:T(8,128)S(1)}, f32[32,64]{1,0:T(8,128)S(1)}, u32[]{:S(2)}, u32[]{:S(2)}) collective-permute-start(f32[32,64]{1,0:T(8,128)S(1)} %constant_dynamic-slice_fusion), channel_id=1, source_target_pairs={{0,8},{4,12},{8,0},{12,4},{16,24},{20,28},{24,16},{28,20},{1,9},{5... | collective-permute-start | bytes 24584 | tf_op jit(solution)/shard_map/ppermute | solution.py:47
  81.1 2.0 %collective-permute-done.12 = f32[32,64]{1,0:T(8,128)S(1)} collective-permute-done((f32[32,64]{1,0:T(8,128)S(1)}, f32[32,64]{1,0:T(8,128)S(1)}, u32[]{:S(2)}, u32[]{:S(2)}) %collective-permute-start.12) | collective-permute-done | bytes 8224 | tf_op jit(solution)/shard_map/ppermute | solution.py:47
  83.1 1.7 %collective-permute-start.13 = (f32[16,64]{1,0:T(8,128)S(1)}, f32[16,64]{1,0:T(8,128)S(1)}, u32[]{:S(2)}, u32[]{:S(2)}) collective-permute-start(f32[16,64]{1,0:T(8,128)S(1)} %constant_dynamic-slice_fusion.3), channel_id=1, source_target_pairs={{0,4},{4,0},{8,12},{12,8},{16,20},{20,16},{24,28},{28,24},{1,5},{5... | collective-permute-start | bytes 12296 | tf_op jit(solution)/shard_map/ppermute | solution.py:47
  84.8 1.9 %collective-permute-done.13 = f32[16,64]{1,0:T(8,128)S(1)} collective-permute-done((f32[16,64]{1,0:T(8,128)S(1)}, f32[16,64]{1,0:T(8,128)S(1)}, u32[]{:S(2)}, u32[]{:S(2)}) %collective-permute-start.13) | collective-permute-done | bytes 4128 | tf_op jit(solution)/shard_map/ppermute | solution.py:47
  89.6 2.0 %collective-permute-done.15 = f32[16,64]{1,0:T(8,128)S(1)} collective-permute-done((f32[16,64]{1,0:T(8,128)S(1)}, f32[16,64]{1,0:T(8,128)S(1)}, u32[]{:S(2)}, u32[]{:S(2)}) %collective-permute-start.15) | collective-permute-done | bytes 4128 | tf_op jit(solution)/shard_map/ppermute | solution.py:190
  (92 shorter events, 28.8 us)
Async XLA Ops:
  0.6 25.6 %copy-start = (bf16[1024,1024]{1,0:T(8,128)(2,1)S(1)}, bf16[1024,1024]{1,0:T(8,128)(2,1)}, u32[]{:S(2)}) copy-start(bf16[1024,1024]{1,0:T(8,128)(2,1)} %param.26) | copy-start | bytes 6291460
  8.0 10.0 %copy-start.4 = (f32[1024]{0:T(1024)S(1)}, f32[1024]{0:T(1024)}, u32[]{:S(2)}) copy-start(f32[1024]{0:T(1024)} %param.21) | copy-start | bytes 12292
  8.0 11.2 %copy-start.5 = (f32[1024]{0:T(1024)S(1)}, f32[1024]{0:T(1024)}, u32[]{:S(2)}) copy-start(f32[1024]{0:T(1024)} %param.23) | copy-start | bytes 12292
  8.0 11.2 %copy-start.6 = (f32[1024]{0:T(1024)S(1)}, f32[1024]{0:T(1024)}, u32[]{:S(2)}) copy-start(f32[1024]{0:T(1024)} %param.22) | copy-start | bytes 12292
  9.4 1.7 %collective-permute-start = (bf16[128,1024]{1,0:T(8,128)(2,1)S(1)}, bf16[128,1024]{1,0:T(8,128)(2,1)S(1)}, u32[]{:S(2)}, u32[]{:S(2)}) collective-permute-start(bf16[128,1024]{1,0:T(8,128)(2,1)S(1)} %constant_dynamic-slice_fusion.4), channel_id=1, source_target_pairs={{0,1},{1,0},{2,3},{3,2},{4,5},{5,4},{6,7},{7,6},{8,9},{9,8},{10,11... | collective-permute-start | bytes 786440 | tf_op jit(solution)/shard_map/ppermute | solution.py:47
  9.9 16.3 %copy-start.11 = (f32[1024]{0:T(1024)S(1)}, f32[1024]{0:T(1024)}, u32[]{:S(2)}) copy-start(f32[1024]{0:T(1024)} %param.25) | copy-start | bytes 12292
  11.2 6.7 %collective-permute-start.1 = (bf16[64,1024]{1,0:T(8,128)(2,1)S(1)}, bf16[64,1024]{1,0:T(8,128)(2,1)S(1)}, u32[]{:S(2)}, u32[]{:S(2)}) collective-permute-start(bf16[64,1024]{1,0:T(8,128)(2,1)S(1)} %dynamic-slice_convert_fusion.1), channel_id=1, source_target_pairs={{0,2},{1,3},{2,0},{3,1},{4,6},{5,7},{6,4},{7,5},{8,10},{9,11},{10,... | collective-permute-start | bytes 393224 | tf_op jit(solution)/shard_map/ppermute | solution.py:47
  19.3 5.1 %collective-permute-start.2 = (bf16[64,1024]{1,0:T(8,128)(2,1)S(1)}, bf16[64,1024]{1,0:T(8,128)(2,1)S(1)}, u32[]{:S(2)}, u32[]{:S(2)}) collective-permute-start(bf16[64,1024]{1,0:T(8,128)(2,1)S(1)} %add_convert_fusion.1), channel_id=1, source_target_pairs={{0,2},{1,3},{2,0},{3,1},{4,6},{5,7},{6,4},{7,5},{8,10},{9,11},{10,... | collective-permute-start | bytes 393224 | tf_op jit(solution)/shard_map/ppermute | solution.py:58
  24.5 1.6 %collective-permute-start.3 = (bf16[128,1024]{1,0:T(8,128)(2,1)S(1)}, bf16[128,1024]{1,0:T(8,128)(2,1)S(1)}, u32[]{:S(2)}, u32[]{:S(2)}) collective-permute-start(bf16[128,1024]{1,0:T(8,128)(2,1)S(1)} %maximum_select_fusion.2), channel_id=1, source_target_pairs={{0,1},{1,0},{2,3},{3,2},{4,5},{5,4},{6,7},{7,6},{8,9},{9,8},{10,11... | collective-permute-start | bytes 786440 | tf_op jit(solution)/shard_map/ppermute | solution.py:58
  26.3 12.5 %copy-start.7 = (f32[1024]{0:T(1024)S(1)}, f32[1024]{0:T(1024)}, u32[]{:S(2)}) copy-start(f32[1024]{0:T(1024)} %param.27) | copy-start | bytes 12292
  31.4 1.6 %collective-permute-start.4 = (bf16[128,1024]{1,0:T(8,128)(2,1)S(1)}, bf16[128,1024]{1,0:T(8,128)(2,1)S(1)}, u32[]{:S(2)}, u32[]{:S(2)}) collective-permute-start(bf16[128,1024]{1,0:T(8,128)(2,1)S(1)} %constant_dynamic-slice_fusion.2), channel_id=1, source_target_pairs={{0,1},{1,0},{2,3},{3,2},{4,5},{5,4},{6,7},{7,6},{8,9},{9,8},{10,11... | collective-permute-start | bytes 786440 | tf_op jit(solution)/shard_map/ppermute | solution.py:47
  33.1 18.8 %copy-start.3 = (s32[128,64]{0,1:T(8,128)S(1)}, s32[128,64]{0,1:T(8,128)}, u32[]{:S(2)}) copy-start(s32[128,64]{0,1:T(8,128)} %param.31) | copy-start | bytes 98308
  33.2 5.6 %collective-permute-start.5 = (bf16[64,1024]{1,0:T(8,128)(2,1)S(1)}, bf16[64,1024]{1,0:T(8,128)(2,1)S(1)}, u32[]{:S(2)}, u32[]{:S(2)}) collective-permute-start(bf16[64,1024]{1,0:T(8,128)(2,1)S(1)} %dynamic-slice_convert_fusion), channel_id=1, source_target_pairs={{0,2},{1,3},{2,0},{3,1},{4,6},{5,7},{6,4},{7,5},{8,10},{9,11},{10,... | collective-permute-start | bytes 393224 | tf_op jit(solution)/shard_map/ppermute | solution.py:47
  39.3 5.0 %collective-permute-start.6 = (bf16[64,1024]{1,0:T(8,128)(2,1)S(1)}, bf16[64,1024]{1,0:T(8,128)(2,1)S(1)}, u32[]{:S(2)}, u32[]{:S(2)}) collective-permute-start(bf16[64,1024]{1,0:T(8,128)(2,1)S(1)} %add_convert_fusion), channel_id=1, source_target_pairs={{0,2},{1,3},{2,0},{3,1},{4,6},{5,7},{6,4},{7,5},{8,10},{9,11},{10,... | collective-permute-start | bytes 393224 | tf_op jit(solution)/shard_map/ppermute | solution.py:58
  44.4 1.6 %collective-permute-start.7 = (bf16[128,1024]{1,0:T(8,128)(2,1)S(1)}, bf16[128,1024]{1,0:T(8,128)(2,1)S(1)}, u32[]{:S(2)}, u32[]{:S(2)}) collective-permute-start(bf16[128,1024]{1,0:T(8,128)(2,1)S(1)} %maximum_select_fusion.3), channel_id=1, source_target_pairs={{0,1},{1,0},{2,3},{3,2},{4,5},{5,4},{6,7},{7,6},{8,9},{9,8},{10,11... | collective-permute-start | bytes 786440 | tf_op jit(solution)/shard_map/ppermute | solution.py:58
  46.1 16.9 %copy-start.1 = (bf16[256,1024]{1,0:T(8,128)(2,1)}, bf16[256,1024]{1,0:T(8,128)(2,1)S(1)}, u32[]{:S(2)}) copy-start(bf16[256,1024]{1,0:T(8,128)(2,1)S(1)} %maximum_select_fusion.1) | copy-start | bytes 1572868
  46.5 3.7 %collective-permute-start.8 = (bf16[16,256]{1,0:T(8,128)(2,1)S(1)}, bf16[16,256]{1,0:T(8,128)(2,1)S(1)}, u32[]{:S(2)}, u32[]{:S(2)}) collective-permute-start(bf16[16,256]{1,0:T(8,128)(2,1)S(1)} %fusion.73), channel_id=1, source_target_pairs={{0,4},{4,0},{8,12},{12,8},{16,20},{20,16},{24,28},{28,24},{1,5},{5... | collective-permute-start | bytes 24584 | tf_op jit(solution)/shard_map/ppermute | solution.py:58
  50.2 3.7 %collective-permute-start.9 = (bf16[32,256]{1,0:T(8,128)(2,1)S(1)}, bf16[32,256]{1,0:T(8,128)(2,1)S(1)}, u32[]{:S(2)}, u32[]{:S(2)}) collective-permute-start(bf16[32,256]{1,0:T(8,128)(2,1)S(1)} %maximum_select_fusion.7), channel_id=1, source_target_pairs={{0,8},{4,12},{8,0},{12,4},{16,24},{20,28},{24,16},{28,20},{1,9},{5... | collective-permute-start | bytes 49160 | tf_op jit(solution)/shard_map/ppermute | solution.py:58
  53.9 4.9 %collective-permute-start.10 = (bf16[64,256]{1,0:T(8,128)(2,1)S(1)}, bf16[64,256]{1,0:T(8,128)(2,1)S(1)}, u32[]{:S(2)}, u32[]{:S(2)}) collective-permute-start(bf16[64,256]{1,0:T(8,128)(2,1)S(1)} %maximum_select_fusion.6), channel_id=1, source_target_pairs={{0,16},{4,20},{8,24},{12,28},{16,0},{20,4},{24,8},{28,12},{1,17},{... | collective-permute-start | bytes 98312 | tf_op jit(solution)/shard_map/ppermute | solution.py:58
  74.4 4.9 %collective-permute-start.11 = (f32[64,64]{1,0:T(8,128)S(1)}, f32[64,64]{1,0:T(8,128)S(1)}, u32[]{:S(2)}, u32[]{:S(2)}) collective-permute-start(f32[64,64]{1,0:T(8,128)S(1)} %constant_dynamic-slice_fusion.1), channel_id=1, source_target_pairs={{0,16},{4,20},{8,24},{12,28},{16,0},{20,4},{24,8},{28,12},{1,17},{... | collective-permute-start | bytes 49160 | tf_op jit(solution)/shard_map/ppermute | solution.py:47
  79.3 3.8 %collective-permute-start.12 = (f32[32,64]{1,0:T(8,128)S(1)}, f32[32,64]{1,0:T(8,128)S(1)}, u32[]{:S(2)}, u32[]{:S(2)}) collective-permute-start(f32[32,64]{1,0:T(8,128)S(1)} %constant_dynamic-slice_fusion), channel_id=1, source_target_pairs={{0,8},{4,12},{8,0},{12,4},{16,24},{20,28},{24,16},{28,20},{1,9},{5... | collective-permute-start | bytes 24584 | tf_op jit(solution)/shard_map/ppermute | solution.py:47
  83.1 3.7 %collective-permute-start.13 = (f32[16,64]{1,0:T(8,128)S(1)}, f32[16,64]{1,0:T(8,128)S(1)}, u32[]{:S(2)}, u32[]{:S(2)}) collective-permute-start(f32[16,64]{1,0:T(8,128)S(1)} %constant_dynamic-slice_fusion.3), channel_id=1, source_target_pairs={{0,4},{4,0},{8,12},{12,8},{16,20},{20,16},{24,28},{28,24},{1,5},{5... | collective-permute-start | bytes 12296 | tf_op jit(solution)/shard_map/ppermute | solution.py:47
  86.7 1.2 %collective-permute-start.14 = (f32[16,64]{1,0:T(8,128)S(1)}, f32[16,64]{1,0:T(8,128)S(1)}, u32[]{:S(2)}, u32[]{:S(2)}) collective-permute-start(f32[16,64]{1,0:T(8,128)S(1)} %dynamic-slice_add_fusion.2), channel_id=1, source_target_pairs={{0,1},{1,0},{2,3},{3,2},{4,5},{5,4},{6,7},{7,6},{8,9},{9,8},{10,11... | collective-permute-start | bytes 12296 | tf_op jit(solution)/shard_map/ppermute | solution.py:190
  87.9 3.7 %collective-permute-start.15 = (f32[16,64]{1,0:T(8,128)S(1)}, f32[16,64]{1,0:T(8,128)S(1)}, u32[]{:S(2)}, u32[]{:S(2)}) collective-permute-start(f32[16,64]{1,0:T(8,128)S(1)} %add.267), channel_id=1, source_target_pairs={{0,2},{1,3},{2,0},{3,1},{4,6},{5,7},{6,4},{7,5},{8,10},{9,11},{10,... | collective-permute-start | bytes 12296 | tf_op jit(solution)/shard_map/ppermute | solution.py:190
  (4 other events, 22.4 us)

commit v5 on v3

--- a/solution.py
+++ b/solution.py
@@ -153,7 +153,7 @@
         gathered, index, (((1,), (1,)), ((), ())), preferred_element_type=jnp.float32
     )
     wanted = jnp.clip(local_rows, 0, shard_rows - 1)
-    minor = 16
+    minor = 128
     if shard_rows % minor == 0:
         major = shard_rows // minor
         major_hot = (

time: 85.9 us -> 84.7 us (0.986)
  local copies, waits for them, and re-layouts: 3.62 us -> 1.42 us
  matrix products: 19.3 us -> 20.3 us
    reshape x1 -> x0, local copies, waits for them, and re-layouts: 1.61 us -> none  [body(): tile.reshape(all_texts, major, minor)]
    dot_general x1, matrix products: 4.92 us -> 5.86 us  [body(): jnp.einsum('tca,tab->tcb', major_hot, tile.reshape(all_texts, major, mino...]
where the time goes in v5:
time: 84.7 us; the launch traced here: 84.4 us
  waiting for transfers between devices  34.6 us (41%)
  starting transfers between devices  23.5 us (28%)
  matrix products  20.3 us (24%)
  other arithmetic  3.51 us (4%)
  local copies, waits for them, and re-layouts  1.42 us (2%)
  between operations  1.1 us (1%)
    ppermute x7, waiting for transfers between devices, reduce_scatter_xor(): got = lax.ppermute(theirs.astype(wire), axis, xor_pairs(n, k))  16.1 us
    ppermute x7, waiting for transfers between devices, all_gather_xor(): other = lax.ppermute(cur, axis, xor_pairs(n, k))  15.3 us
    ppermute x7, starting transfers between devices, reduce_scatter_xor(): got = lax.ppermute(theirs.astype(wire), axis, xor_pairs(n, k))  11.8 us
    ppermute x7, starting transfers between devices, all_gather_xor(): other = lax.ppermute(cur, axis, xor_pairs(n, k))  10 us
    dot_general x1, matrix products, body(): jnp.einsum('tca,tab->tcb', major_hot, tile.reshape(all_texts, major, mino...  5.86 us
    dot_general x1, matrix products, body(): jnp.dot(activated, w_down, preferred_element_type=jnp.float32)  5.11 us
    dot_general x3, matrix products, body(): jnp.dot(hidden, w_qkv[j], preferred_element_type=jnp.float32) + b_qkv[j]  4.68 us
    ppermute x2, waiting for transfers between devices, body(): lax.ppermute(text_scores, 'tensor', xor_pairs(n_tensor, k))  3.15 us
  transfers between devices with their start and end apart: 16, of which 16 were waited for; matrix products, arithmetic and copies ran while one was open for 0% of the time, Pallas kernels for 0%

profile of v5, /device:TPU:0, one launch (start us, length us, event | category | flops | bytes accessed | tf_op | source)
XLA Modules:
  0.0 84.4 jit_solution(10249236360549875259)
XLA Ops:
  11.2 2.9 %collective-permute-start.1 = (bf16[64,1024]{1,0:T(8,128)(2,1)S(1)}, bf16[64,1024]{1,0:T(8,128)(2,1)S(1)}, u32[]{:S(2)}, u32[]{:S(2)}) collective-permute-start(bf16[64,1024]{1,0:T(8,128)(2,1)S(1)} %dynamic-slice_convert_fusion.1), channel_id=1, source_target_pairs={{0,2},{1,3},{2,0},{3,1},{4,6},{5,7},{6,4},{7,5},{8,10},{9,11},{10,... | collective-permute-start | bytes 393224 | tf_op jit(solution)/shard_map/ppermute | solution.py:47
  14.1 3.8 %collective-permute-done.1 = bf16[64,1024]{1,0:T(8,128)(2,1)S(1)} collective-permute-done((bf16[64,1024]{1,0:T(8,128)(2,1)S(1)}, bf16[64,1024]{1,0:T(8,128)(2,1)S(1)}, u32[]{:S(2)}, u32[]{:S(2)}) %collective-permute-start.1) | collective-permute-done | bytes 131104 | tf_op jit(solution)/shard_map/ppermute | solution.py:47
  19.3 1.8 %collective-permute-start.2 = (bf16[64,1024]{1,0:T(8,128)(2,1)S(1)}, bf16[64,1024]{1,0:T(8,128)(2,1)S(1)}, u32[]{:S(2)}, u32[]{:S(2)}) collective-permute-start(bf16[64,1024]{1,0:T(8,128)(2,1)S(1)} %add_convert_fusion.1), channel_id=1, source_target_pairs={{0,2},{1,3},{2,0},{3,1},{4,6},{5,7},{6,4},{7,5},{8,10},{9,11},{10,... | collective-permute-start | bytes 393224 | tf_op jit(solution)/shard_map/ppermute | solution.py:58
  21.1 3.3 %collective-permute-done.2 = bf16[64,1024]{1,0:T(8,128)(2,1)S(1)} collective-permute-done((bf16[64,1024]{1,0:T(8,128)(2,1)S(1)}, bf16[64,1024]{1,0:T(8,128)(2,1)S(1)}, u32[]{:S(2)}, u32[]{:S(2)}) %collective-permute-start.2) | collective-permute-done | bytes 131104 | tf_op jit(solution)/shard_map/ppermute | solution.py:58
  26.3 5.1 %convolution_convert_fusion.1 = bf16[256,1024]{1,0:T(8,128)(2,1)S(1)} fusion(bf16[1024,1024]{1,0:T(8,128)(2,1)S(1)} %copy-done, bf16[256,1024]{1,0:T(8,128)(2,1)S(1)} %maximum_select_fusion, bf16[1024,1024]{1,0:T(8,128)(2,1)} %param.24, f32[1024]{0:T(1024)S(1)} %copy-done.10), kind=kOutput, calls=%fused_computation.10 | convolution fusion | flops 1091305472 | bytes 5246976 | tf_op jit(solution)/shard_map/dot_general | solution.py:123
  33.2 1.8 %collective-permute-start.5 = (bf16[64,1024]{1,0:T(8,128)(2,1)S(1)}, bf16[64,1024]{1,0:T(8,128)(2,1)S(1)}, u32[]{:S(2)}, u32[]{:S(2)}) collective-permute-start(bf16[64,1024]{1,0:T(8,128)(2,1)S(1)} %dynamic-slice_convert_fusion), channel_id=1, source_target_pairs={{0,2},{1,3},{2,0},{3,1},{4,6},{5,7},{6,4},{7,5},{8,10},{9,11},{10,... | collective-permute-start | bytes 393224 | tf_op jit(solution)/shard_map/ppermute | solution.py:47
  34.9 3.9 %collective-permute-done.5 = bf16[64,1024]{1,0:T(8,128)(2,1)S(1)} collective-permute-done((bf16[64,1024]{1,0:T(8,128)(2,1)S(1)}, bf16[64,1024]{1,0:T(8,128)(2,1)S(1)}, u32[]{:S(2)}, u32[]{:S(2)}) %collective-permute-start.5) | collective-permute-done | bytes 131104 | tf_op jit(solution)/shard_map/ppermute | solution.py:47
  39.3 1.7 %collective-permute-start.6 = (bf16[64,1024]{1,0:T(8,128)(2,1)S(1)}, bf16[64,1024]{1,0:T(8,128)(2,1)S(1)}, u32[]{:S(2)}, u32[]{:S(2)}) collective-permute-start(bf16[64,1024]{1,0:T(8,128)(2,1)S(1)} %add_convert_fusion), channel_id=1, source_target_pairs={{0,2},{1,3},{2,0},{3,1},{4,6},{5,7},{6,4},{7,5},{8,10},{9,11},{10,... | collective-permute-start | bytes 393224 | tf_op jit(solution)/shard_map/ppermute | solution.py:58
  41.0 3.3 %collective-permute-done.6 = bf16[64,1024]{1,0:T(8,128)(2,1)S(1)} collective-permute-done((bf16[64,1024]{1,0:T(8,128)(2,1)S(1)}, bf16[64,1024]{1,0:T(8,128)(2,1)S(1)}, u32[]{:S(2)}, u32[]{:S(2)}) %collective-permute-start.6) | collective-permute-done | bytes 131104 | tf_op jit(solution)/shard_map/ppermute | solution.py:58
  46.5 1.7 %collective-permute-start.8 = (bf16[16,256]{1,0:T(8,128)(2,1)S(1)}, bf16[16,256]{1,0:T(8,128)(2,1)S(1)}, u32[]{:S(2)}, u32[]{:S(2)}) collective-permute-start(bf16[16,256]{1,0:T(8,128)(2,1)S(1)} %fusion.63), channel_id=1, source_target_pairs={{0,4},{4,0},{8,12},{12,8},{16,20},{20,16},{24,28},{28,24},{1,5},{5... | collective-permute-start | bytes 24584 | tf_op jit(solution)/shard_map/ppermute | solution.py:58
  48.2 1.9 %collective-permute-done.8 = bf16[16,256]{1,0:T(8,128)(2,1)S(1)} collective-permute-done((bf16[16,256]{1,0:T(8,128)(2,1)S(1)}, bf16[16,256]{1,0:T(8,128)(2,1)S(1)}, u32[]{:S(2)}, u32[]{:S(2)}) %collective-permute-start.8) | collective-permute-done | bytes 8224 | tf_op jit(solution)/shard_map/ppermute | solution.py:58
  50.2 1.8 %collective-permute-start.9 = (bf16[32,256]{1,0:T(8,128)(2,1)S(1)}, bf16[32,256]{1,0:T(8,128)(2,1)S(1)}, u32[]{:S(2)}, u32[]{:S(2)}) collective-permute-start(bf16[32,256]{1,0:T(8,128)(2,1)S(1)} %maximum_select_fusion.7), channel_id=1, source_target_pairs={{0,8},{4,12},{8,0},{12,4},{16,24},{20,28},{24,16},{28,20},{1,9},{5... | collective-permute-start | bytes 49160 | tf_op jit(solution)/shard_map/ppermute | solution.py:58
  52.0 1.9 %collective-permute-done.9 = bf16[32,256]{1,0:T(8,128)(2,1)S(1)} collective-permute-done((bf16[32,256]{1,0:T(8,128)(2,1)S(1)}, bf16[32,256]{1,0:T(8,128)(2,1)S(1)}, u32[]{:S(2)}, u32[]{:S(2)}) %collective-permute-start.9) | collective-permute-done | bytes 16416 | tf_op jit(solution)/shard_map/ppermute | solution.py:58
  53.9 2.8 %collective-permute-start.10 = (bf16[64,256]{1,0:T(8,128)(2,1)S(1)}, bf16[64,256]{1,0:T(8,128)(2,1)S(1)}, u32[]{:S(2)}, u32[]{:S(2)}) collective-permute-start(bf16[64,256]{1,0:T(8,128)(2,1)S(1)} %maximum_select_fusion.6), channel_id=1, source_target_pairs={{0,16},{4,20},{8,24},{12,28},{16,0},{20,4},{24,8},{28,12},{1,17},{... | collective-permute-start | bytes 98312 | tf_op jit(solution)/shard_map/ppermute | solution.py:58
  56.9 1.9 %collective-permute-done.10 = bf16[64,256]{1,0:T(8,128)(2,1)S(1)} collective-permute-done((bf16[64,256]{1,0:T(8,128)(2,1)S(1)}, bf16[64,256]{1,0:T(8,128)(2,1)S(1)}, u32[]{:S(2)}, u32[]{:S(2)}) %collective-permute-start.10) | collective-permute-done | bytes 32800 | tf_op jit(solution)/shard_map/ppermute | solution.py:58
  58.8 1.7 %convolution_bitcast_fusion = f32[16,8,16,128]{3,1,2,0:T(8,128)S(1)} fusion(bf16[2048,256]{1,0:T(8,128)(2,1)} %param.30, bf16[64,256]{1,0:T(8,128)(2,1)S(1)} %collective-permute-done.10, bf16[64,256]{1,0:T(8,128)(2,1)S(1)} %maximum_select_fusion.6, pred[]{:T(512)S(6)} %eq.101), kind=kOutput, calls=%fused_computation.6 | convolution fusion | flops 134512640 | bytes 2162689 | tf_op jit(solution)/shard_map/dot_general | solution.py:152
  60.7 5.9 %select_reduce_fusion = f32[128,64]{1,0:T(8,128)S(1)} fusion(f32[128,16,128]{2,1,0:T(8,128)S(1)} %bitcast.41, s32[128,64]{1,0:T(8,128)S(1)} %get-tuple-element.7, s32[128,64]{1,0:T(8,128)S(1)} %get-tuple-element.6), kind=kOutput, calls=%fused_computation.1 | convolution fusion | flops 204595200 | bytes 1146880 | tf_op jit(solution)/shard_map/tca,tab->tcb/dot_general | solution.py:162
  66.6 2.9 %collective-permute-start.11 = (f32[64,64]{1,0:T(8,128)S(1)}, f32[64,64]{1,0:T(8,128)S(1)}, u32[]{:S(2)}, u32[]{:S(2)}) collective-permute-start(f32[64,64]{1,0:T(8,128)S(1)} %constant_dynamic-slice_fusion.1), channel_id=1, source_target_pairs={{0,16},{4,20},{8,24},{12,28},{16,0},{20,4},{24,8},{28,12},{1,17},{... | collective-permute-start | bytes 49160 | tf_op jit(solution)/shard_map/ppermute | solution.py:47
  69.5 2.0 %collective-permute-done.11 = f32[64,64]{1,0:T(8,128)S(1)} collective-permute-done((f32[64,64]{1,0:T(8,128)S(1)}, f32[64,64]{1,0:T(8,128)S(1)}, u32[]{:S(2)}, u32[]{:S(2)}) %collective-permute-start.11) | collective-permute-done | bytes 16416 | tf_op jit(solution)/shard_map/ppermute | solution.py:47
  71.5 1.8 %collective-permute-start.12 = (f32[32,64]{1,0:T(8,128)S(1)}, f32[32,64]{1,0:T(8,128)S(1)}, u32[]{:S(2)}, u32[]{:S(2)}) collective-permute-start(f32[32,64]{1,0:T(8,128)S(1)} %constant_dynamic-slice_fusion), channel_id=1, source_target_pairs={{0,8},{4,12},{8,0},{12,4},{16,24},{20,28},{24,16},{28,20},{1,9},{5... | collective-permute-start | bytes 24584 | tf_op jit(solution)/shard_map/ppermute | solution.py:47
  73.3 2.0 %collective-permute-done.12 = f32[32,64]{1,0:T(8,128)S(1)} collective-permute-done((f32[32,64]{1,0:T(8,128)S(1)}, f32[32,64]{1,0:T(8,128)S(1)}, u32[]{:S(2)}, u32[]{:S(2)}) %collective-permute-start.12) | collective-permute-done | bytes 8224 | tf_op jit(solution)/shard_map/ppermute | solution.py:47
  75.3 1.7 %collective-permute-start.13 = (f32[16,64]{1,0:T(8,128)S(1)}, f32[16,64]{1,0:T(8,128)S(1)}, u32[]{:S(2)}, u32[]{:S(2)}) collective-permute-start(f32[16,64]{1,0:T(8,128)S(1)} %constant_dynamic-slice_fusion.3), channel_id=1, source_target_pairs={{0,4},{4,0},{8,12},{12,8},{16,20},{20,16},{24,28},{28,24},{1,5},{5... | collective-permute-start | bytes 12296 | tf_op jit(solution)/shard_map/ppermute | solution.py:47
  77.0 1.9 %collective-permute-done.13 = f32[16,64]{1,0:T(8,128)S(1)} collective-permute-done((f32[16,64]{1,0:T(8,128)S(1)}, f32[16,64]{1,0:T(8,128)S(1)}, u32[]{:S(2)}, u32[]{:S(2)}) %collective-permute-start.13) | collective-permute-done | bytes 4128 | tf_op jit(solution)/shard_map/ppermute | solution.py:47
  81.8 2.0 %collective-permute-done.15 = f32[16,64]{1,0:T(8,128)S(1)} collective-permute-done((f32[16,64]{1,0:T(8,128)S(1)}, f32[16,64]{1,0:T(8,128)S(1)}, u32[]{:S(2)}, u32[]{:S(2)}) %collective-permute-start.15) | collective-permute-done | bytes 4128 | tf_op jit(solution)/shard_map/ppermute | solution.py:184
  (84 shorter events, 21.8 us)
Async XLA Ops:
  0.6 25.6 %copy-start = (bf16[1024,1024]{1,0:T(8,128)(2,1)S(1)}, bf16[1024,1024]{1,0:T(8,128)(2,1)}, u32[]{:S(2)}) copy-start(bf16[1024,1024]{1,0:T(8,128)(2,1)} %param.26) | copy-start | bytes 6291460
  8.0 10.0 %copy-start.3 = (f32[1024]{0:T(1024)S(1)}, f32[1024]{0:T(1024)}, u32[]{:S(2)}) copy-start(f32[1024]{0:T(1024)} %param.21) | copy-start | bytes 12292
  8.0 11.2 %copy-start.4 = (f32[1024]{0:T(1024)S(1)}, f32[1024]{0:T(1024)}, u32[]{:S(2)}) copy-start(f32[1024]{0:T(1024)} %param.23) | copy-start | bytes 12292
  8.0 11.2 %copy-start.5 = (f32[1024]{0:T(1024)S(1)}, f32[1024]{0:T(1024)}, u32[]{:S(2)}) copy-start(f32[1024]{0:T(1024)} %param.22) | copy-start | bytes 12292
  9.4 1.7 %collective-permute-start = (bf16[128,1024]{1,0:T(8,128)(2,1)S(1)}, bf16[128,1024]{1,0:T(8,128)(2,1)S(1)}, u32[]{:S(2)}, u32[]{:S(2)}) collective-permute-start(bf16[128,1024]{1,0:T(8,128)(2,1)S(1)} %constant_dynamic-slice_fusion.4), channel_id=1, source_target_pairs={{0,1},{1,0},{2,3},{3,2},{4,5},{5,4},{6,7},{7,6},{8,9},{9,8},{10,11... | collective-permute-start | bytes 786440 | tf_op jit(solution)/shard_map/ppermute | solution.py:47
  9.9 16.3 %copy-start.10 = (f32[1024]{0:T(1024)S(1)}, f32[1024]{0:T(1024)}, u32[]{:S(2)}) copy-start(f32[1024]{0:T(1024)} %param.25) | copy-start | bytes 12292
  11.2 6.7 %collective-permute-start.1 = (bf16[64,1024]{1,0:T(8,128)(2,1)S(1)}, bf16[64,1024]{1,0:T(8,128)(2,1)S(1)}, u32[]{:S(2)}, u32[]{:S(2)}) collective-permute-start(bf16[64,1024]{1,0:T(8,128)(2,1)S(1)} %dynamic-slice_convert_fusion.1), channel_id=1, source_target_pairs={{0,2},{1,3},{2,0},{3,1},{4,6},{5,7},{6,4},{7,5},{8,10},{9,11},{10,... | collective-permute-start | bytes 393224 | tf_op jit(solution)/shard_map/ppermute | solution.py:47
  19.3 5.1 %collective-permute-start.2 = (bf16[64,1024]{1,0:T(8,128)(2,1)S(1)}, bf16[64,1024]{1,0:T(8,128)(2,1)S(1)}, u32[]{:S(2)}, u32[]{:S(2)}) collective-permute-start(bf16[64,1024]{1,0:T(8,128)(2,1)S(1)} %add_convert_fusion.1), channel_id=1, source_target_pairs={{0,2},{1,3},{2,0},{3,1},{4,6},{5,7},{6,4},{7,5},{8,10},{9,11},{10,... | collective-permute-start | bytes 393224 | tf_op jit(solution)/shard_map/ppermute | solution.py:58
  24.5 1.6 %collective-permute-start.3 = (bf16[128,1024]{1,0:T(8,128)(2,1)S(1)}, bf16[128,1024]{1,0:T(8,128)(2,1)S(1)}, u32[]{:S(2)}, u32[]{:S(2)}) collective-permute-start(bf16[128,1024]{1,0:T(8,128)(2,1)S(1)} %maximum_select_fusion.2), channel_id=1, source_target_pairs={{0,1},{1,0},{2,3},{3,2},{4,5},{5,4},{6,7},{7,6},{8,9},{9,8},{10,11... | collective-permute-start | bytes 786440 | tf_op jit(solution)/shard_map/ppermute | solution.py:58
  26.3 12.5 %copy-start.6 = (f32[1024]{0:T(1024)S(1)}, f32[1024]{0:T(1024)}, u32[]{:S(2)}) copy-start(f32[1024]{0:T(1024)} %param.27) | copy-start | bytes 12292
  31.4 1.6 %collective-permute-start.4 = (bf16[128,1024]{1,0:T(8,128)(2,1)S(1)}, bf16[128,1024]{1,0:T(8,128)(2,1)S(1)}, u32[]{:S(2)}, u32[]{:S(2)}) collective-permute-start(bf16[128,1024]{1,0:T(8,128)(2,1)S(1)} %constant_dynamic-slice_fusion.2), channel_id=1, source_target_pairs={{0,1},{1,0},{2,3},{3,2},{4,5},{5,4},{6,7},{7,6},{8,9},{9,8},{10,11... | collective-permute-start | bytes 786440 | tf_op jit(solution)/shard_map/ppermute | solution.py:47
  33.1 18.8 %copy-start.2 = (s32[128,64]{0,1:T(8,128)S(1)}, s32[128,64]{0,1:T(8,128)}, u32[]{:S(2)}) copy-start(s32[128,64]{0,1:T(8,128)} %param.31) | copy-start | bytes 98308
  33.2 5.6 %collective-permute-start.5 = (bf16[64,1024]{1,0:T(8,128)(2,1)S(1)}, bf16[64,1024]{1,0:T(8,128)(2,1)S(1)}, u32[]{:S(2)}, u32[]{:S(2)}) collective-permute-start(bf16[64,1024]{1,0:T(8,128)(2,1)S(1)} %dynamic-slice_convert_fusion), channel_id=1, source_target_pairs={{0,2},{1,3},{2,0},{3,1},{4,6},{5,7},{6,4},{7,5},{8,10},{9,11},{10,... | collective-permute-start | bytes 393224 | tf_op jit(solution)/shard_map/ppermute | solution.py:47
  39.3 5.0 %collective-permute-start.6 = (bf16[64,1024]{1,0:T(8,128)(2,1)S(1)}, bf16[64,1024]{1,0:T(8,128)(2,1)S(1)}, u32[]{:S(2)}, u32[]{:S(2)}) collective-permute-start(bf16[64,1024]{1,0:T(8,128)(2,1)S(1)} %add_convert_fusion), channel_id=1, source_target_pairs={{0,2},{1,3},{2,0},{3,1},{4,6},{5,7},{6,4},{7,5},{8,10},{9,11},{10,... | collective-permute-start | bytes 393224 | tf_op jit(solution)/shard_map/ppermute | solution.py:58
  44.4 1.6 %collective-permute-start.7 = (bf16[128,1024]{1,0:T(8,128)(2,1)S(1)}, bf16[128,1024]{1,0:T(8,128)(2,1)S(1)}, u32[]{:S(2)}, u32[]{:S(2)}) collective-permute-start(bf16[128,1024]{1,0:T(8,128)(2,1)S(1)} %maximum_select_fusion.3), channel_id=1, source_target_pairs={{0,1},{1,0},{2,3},{3,2},{4,5},{5,4},{6,7},{7,6},{8,9},{9,8},{10,11... | collective-permute-start | bytes 786440 | tf_op jit(solution)/shard_map/ppermute | solution.py:58
  46.1 14.6 %copy-start.1 = (bf16[256,1024]{1,0:T(8,128)(2,1)}, bf16[256,1024]{1,0:T(8,128)(2,1)S(1)}, u32[]{:S(2)}) copy-start(bf16[256,1024]{1,0:T(8,128)(2,1)S(1)} %maximum_select_fusion.1) | copy-start | bytes 1572868
  46.5 3.7 %collective-permute-start.8 = (bf16[16,256]{1,0:T(8,128)(2,1)S(1)}, bf16[16,256]{1,0:T(8,128)(2,1)S(1)}, u32[]{:S(2)}, u32[]{:S(2)}) collective-permute-start(bf16[16,256]{1,0:T(8,128)(2,1)S(1)} %fusion.63), channel_id=1, source_target_pairs={{0,4},{4,0},{8,12},{12,8},{16,20},{20,16},{24,28},{28,24},{1,5},{5... | collective-permute-start | bytes 24584 | tf_op jit(solution)/shard_map/ppermute | solution.py:58
  50.2 3.7 %collective-permute-start.9 = (bf16[32,256]{1,0:T(8,128)(2,1)S(1)}, bf16[32,256]{1,0:T(8,128)(2,1)S(1)}, u32[]{:S(2)}, u32[]{:S(2)}) collective-permute-start(bf16[32,256]{1,0:T(8,128)(2,1)S(1)} %maximum_select_fusion.7), channel_id=1, source_target_pairs={{0,8},{4,12},{8,0},{12,4},{16,24},{20,28},{24,16},{28,20},{1,9},{5... | collective-permute-start | bytes 49160 | tf_op jit(solution)/shard_map/ppermute | solution.py:58
  53.9 4.9 %collective-permute-start.10 = (bf16[64,256]{1,0:T(8,128)(2,1)S(1)}, bf16[64,256]{1,0:T(8,128)(2,1)S(1)}, u32[]{:S(2)}, u32[]{:S(2)}) collective-permute-start(bf16[64,256]{1,0:T(8,128)(2,1)S(1)} %maximum_select_fusion.6), channel_id=1, source_target_pairs={{0,16},{4,20},{8,24},{12,28},{16,0},{20,4},{24,8},{28,12},{1,17},{... | collective-permute-start | bytes 98312 | tf_op jit(solution)/shard_map/ppermute | solution.py:58
  66.6 4.9 %collective-permute-start.11 = (f32[64,64]{1,0:T(8,128)S(1)}, f32[64,64]{1,0:T(8,128)S(1)}, u32[]{:S(2)}, u32[]{:S(2)}) collective-permute-start(f32[64,64]{1,0:T(8,128)S(1)} %constant_dynamic-slice_fusion.1), channel_id=1, source_target_pairs={{0,16},{4,20},{8,24},{12,28},{16,0},{20,4},{24,8},{28,12},{1,17},{... | collective-permute-start | bytes 49160 | tf_op jit(solution)/shard_map/ppermute | solution.py:47
  71.5 3.8 %collective-permute-start.12 = (f32[32,64]{1,0:T(8,128)S(1)}, f32[32,64]{1,0:T(8,128)S(1)}, u32[]{:S(2)}, u32[]{:S(2)}) collective-permute-start(f32[32,64]{1,0:T(8,128)S(1)} %constant_dynamic-slice_fusion), channel_id=1, source_target_pairs={{0,8},{4,12},{8,0},{12,4},{16,24},{20,28},{24,16},{28,20},{1,9},{5... | collective-permute-start | bytes 24584 | tf_op jit(solution)/shard_map/ppermute | solution.py:47
  75.3 3.7 %collective-permute-start.13 = (f32[16,64]{1,0:T(8,128)S(1)}, f32[16,64]{1,0:T(8,128)S(1)}, u32[]{:S(2)}, u32[]{:S(2)}) collective-permute-start(f32[16,64]{1,0:T(8,128)S(1)} %constant_dynamic-slice_fusion.3), channel_id=1, source_target_pairs={{0,4},{4,0},{8,12},{12,8},{16,20},{20,16},{24,28},{28,24},{1,5},{5... | collective-permute-start | bytes 12296 | tf_op jit(solution)/shard_map/ppermute | solution.py:47
  79.0 1.2 %collective-permute-start.14 = (f32[16,64]{1,0:T(8,128)S(1)}, f32[16,64]{1,0:T(8,128)S(1)}, u32[]{:S(2)}, u32[]{:S(2)}) collective-permute-start(f32[16,64]{1,0:T(8,128)S(1)} %dynamic-slice_add_fusion.2), channel_id=1, source_target_pairs={{0,1},{1,0},{2,3},{3,2},{4,5},{5,4},{6,7},{7,6},{8,9},{9,8},{10,11... | collective-permute-start | bytes 12296 | tf_op jit(solution)/shard_map/ppermute | solution.py:184
  80.2 3.7 %collective-permute-start.15 = (f32[16,64]{1,0:T(8,128)S(1)}, f32[16,64]{1,0:T(8,128)S(1)}, u32[]{:S(2)}, u32[]{:S(2)}) collective-permute-start(f32[16,64]{1,0:T(8,128)S(1)} %add.259), channel_id=1, source_target_pairs={{0,2},{1,3},{2,0},{3,1},{4,6},{5,7},{6,4},{7,5},{8,10},{9,11},{10,... | collective-permute-start | bytes 12296 | tf_op jit(solution)/shard_map/ppermute | solution.py:184
  (3 other events, 19.5 us)

commit v6 on v5

--- a/solution.py
+++ b/solution.py
@@ -100,9 +100,10 @@
     tokens_here = hidden.shape[0]
     local_width = w_qkv.shape[2]
     local_heads = local_width // HEAD
-    projected = [
-        jnp.dot(hidden, w_qkv[j], preferred_element_type=jnp.float32) + b_qkv[j] for j in range(3)
-    ]
+    projected = (
+        jnp.einsum("td,jdf->jtf", hidden, w_qkv, preferred_element_type=jnp.float32)
+        + b_qkv[:, None, :]
+    )
     queries = (projected[0] * 0.125).astype(jnp.bfloat16).reshape(tokens_here, local_heads, HEAD)
     keys = projected[1].astype(jnp.bfloat16).reshape(tokens_here, local_heads, HEAD)
     values = projected[2].astype(jnp.bfloat16).reshape(tokens_here, local_heads, HEAD)

time: 84.7 us -> 83 us (0.980)
  matrix products: 20.3 us -> 18.8 us
    dot_general x3 -> x1, matrix products: 4.68 us -> 2.34 us  [body(): jnp.einsum('td,jdf->jtf', hidden, w_qkv, preferred_element_type=jnp.float32)]
    dot_general x1, matrix products: 0.38 us -> 1.29 us  [body(): jnp.einsum('hts,shd->thd', weights, values, preferred_element_type=jnp.fl...]
where the time goes in v6:
time: 83 us; the launch traced here: 82.8 us
  waiting for transfers between devices  34.7 us (42%)
  starting transfers between devices  23.4 us (28%)
  matrix products  18.8 us (23%)
  other arithmetic  3.53 us (4%)
  local copies, waits for them, and re-layouts  1.22 us (1%)
  between operations  1.09 us (1%)
    ppermute x7, waiting for transfers between devices, reduce_scatter_xor(): got = lax.ppermute(theirs.astype(wire), axis, xor_pairs(n, k))  16.2 us
    ppermute x7, waiting for transfers between devices, all_gather_xor(): other = lax.ppermute(cur, axis, xor_pairs(n, k))  15.4 us
    ppermute x7, starting transfers between devices, reduce_scatter_xor(): got = lax.ppermute(theirs.astype(wire), axis, xor_pairs(n, k))  11.8 us
    ppermute x7, starting transfers between devices, all_gather_xor(): other = lax.ppermute(cur, axis, xor_pairs(n, k))  9.98 us
    dot_general x1, matrix products, body(): jnp.einsum('tca,tab->tcb', major_hot, tile.reshape(all_texts, major, mino...  5.86 us
    dot_general x1, matrix products, body(): jnp.dot(activated, w_down, preferred_element_type=jnp.float32)  5.11 us
    ppermute x2, waiting for transfers between devices, body(): lax.ppermute(text_scores, 'tensor', xor_pairs(n_tensor, k))  3.15 us
    dot_general x1, matrix products, body(): jnp.einsum('td,jdf->jtf', hidden, w_qkv, preferred_element_type=jnp.float32)  2.34 us
  transfers between devices with their start and end apart: 16, of which 16 were waited for; matrix products, arithmetic and copies ran while one was open for 0% of the time, Pallas kernels for 0%

profile of v6, /device:TPU:0, one launch (start us, length us, event | category | flops | bytes accessed | tf_op | source)
XLA Modules:
  0.0 82.8 jit_solution(9486054277146200453)
XLA Ops:
  0.7 2.3 %fusion.94 = (bf16[3,256,256]{1,2,0:T(8,128)(2,1)S(1)}, f32[3,256,256]{1,2,0:T(8,128)S(1)}) fusion(f32[3,256]{1,0:T(4,128)} %param.19, bf16[3,1024,256]{2,1,0:T(8,128)(2,1)} %param.18, bf16[256,1024]{1,0:T(8,128)(2,1)} %param.16), kind=kOutput, calls=%fused_computation.162 | convolution fusion | flops 403046400 | bytes 3279872 | tf_op jit(solution)/shard_map/td,jdf->jtf/dot_general | solution.py:104
  9.6 2.9 %collective-permute-start.1 = (bf16[64,1024]{1,0:T(8,128)(2,1)S(1)}, bf16[64,1024]{1,0:T(8,128)(2,1)S(1)}, u32[]{:S(2)}, u32[]{:S(2)}) collective-permute-start(bf16[64,1024]{1,0:T(8,128)(2,1)S(1)} %dynamic-slice_convert_fusion.1), channel_id=1, source_target_pairs={{0,2},{1,3},{2,0},{3,1},{4,6},{5,7},{6,4},{7,5},{8,10},{9,11},{10,... | collective-permute-start | bytes 393224 | tf_op jit(solution)/shard_map/ppermute | solution.py:47
  12.5 3.8 %collective-permute-done.1 = bf16[64,1024]{1,0:T(8,128)(2,1)S(1)} collective-permute-done((bf16[64,1024]{1,0:T(8,128)(2,1)S(1)}, bf16[64,1024]{1,0:T(8,128)(2,1)S(1)}, u32[]{:S(2)}, u32[]{:S(2)}) %collective-permute-start.1) | collective-permute-done | bytes 131104 | tf_op jit(solution)/shard_map/ppermute | solution.py:47
  17.7 1.8 %collective-permute-start.2 = (bf16[64,1024]{1,0:T(8,128)(2,1)S(1)}, bf16[64,1024]{1,0:T(8,128)(2,1)S(1)}, u32[]{:S(2)}, u32[]{:S(2)}) collective-permute-start(bf16[64,1024]{1,0:T(8,128)(2,1)S(1)} %add_convert_fusion.1), channel_id=1, source_target_pairs={{0,2},{1,3},{2,0},{3,1},{4,6},{5,7},{6,4},{7,5},{8,10},{9,11},{10,... | collective-permute-start | bytes 393224 | tf_op jit(solution)/shard_map/ppermute | solution.py:58
  19.5 3.3 %collective-permute-done.2 = bf16[64,1024]{1,0:T(8,128)(2,1)S(1)} collective-permute-done((bf16[64,1024]{1,0:T(8,128)(2,1)S(1)}, bf16[64,1024]{1,0:T(8,128)(2,1)S(1)}, u32[]{:S(2)}, u32[]{:S(2)}) %collective-permute-start.2) | collective-permute-done | bytes 131104 | tf_op jit(solution)/shard_map/ppermute | solution.py:58
  24.6 5.1 %convolution_convert_fusion.1 = bf16[256,1024]{1,0:T(8,128)(2,1)S(1)} fusion(bf16[1024,1024]{1,0:T(8,128)(2,1)S(1)} %copy-done, bf16[256,1024]{1,0:T(8,128)(2,1)S(1)} %maximum_select_fusion, bf16[1024,1024]{1,0:T(8,128)(2,1)} %param.24, f32[1024]{0:T(1024)S(1)} %copy-done.10), kind=kOutput, calls=%fused_computation.10 | convolution fusion | flops 1091305472 | bytes 5246976 | tf_op jit(solution)/shard_map/dot_general | solution.py:124
  31.5 1.7 %collective-permute-start.5 = (bf16[64,1024]{1,0:T(8,128)(2,1)S(1)}, bf16[64,1024]{1,0:T(8,128)(2,1)S(1)}, u32[]{:S(2)}, u32[]{:S(2)}) collective-permute-start(bf16[64,1024]{1,0:T(8,128)(2,1)S(1)} %dynamic-slice_convert_fusion), channel_id=1, source_target_pairs={{0,2},{1,3},{2,0},{3,1},{4,6},{5,7},{6,4},{7,5},{8,10},{9,11},{10,... | collective-permute-start | bytes 393224 | tf_op jit(solution)/shard_map/ppermute | solution.py:47
  33.3 3.9 %collective-permute-done.5 = bf16[64,1024]{1,0:T(8,128)(2,1)S(1)} collective-permute-done((bf16[64,1024]{1,0:T(8,128)(2,1)S(1)}, bf16[64,1024]{1,0:T(8,128)(2,1)S(1)}, u32[]{:S(2)}, u32[]{:S(2)}) %collective-permute-start.5) | collective-permute-done | bytes 131104 | tf_op jit(solution)/shard_map/ppermute | solution.py:47
  37.6 1.7 %collective-permute-start.6 = (bf16[64,1024]{1,0:T(8,128)(2,1)S(1)}, bf16[64,1024]{1,0:T(8,128)(2,1)S(1)}, u32[]{:S(2)}, u32[]{:S(2)}) collective-permute-start(bf16[64,1024]{1,0:T(8,128)(2,1)S(1)} %add_convert_fusion), channel_id=1, source_target_pairs={{0,2},{1,3},{2,0},{3,1},{4,6},{5,7},{6,4},{7,5},{8,10},{9,11},{10,... | collective-permute-start | bytes 393224 | tf_op jit(solution)/shard_map/ppermute | solution.py:58
  39.4 3.3 %collective-permute-done.6 = bf16[64,1024]{1,0:T(8,128)(2,1)S(1)} collective-permute-done((bf16[64,1024]{1,0:T(8,128)(2,1)S(1)}, bf16[64,1024]{1,0:T(8,128)(2,1)S(1)}, u32[]{:S(2)}, u32[]{:S(2)}) %collective-permute-start.6) | collective-permute-done | bytes 131104 | tf_op jit(solution)/shard_map/ppermute | solution.py:58
  44.9 1.7 %collective-permute-start.8 = (bf16[16,256]{1,0:T(8,128)(2,1)S(1)}, bf16[16,256]{1,0:T(8,128)(2,1)S(1)}, u32[]{:S(2)}, u32[]{:S(2)}) collective-permute-start(bf16[16,256]{1,0:T(8,128)(2,1)S(1)} %fusion.56), channel_id=1, source_target_pairs={{0,4},{4,0},{8,12},{12,8},{16,20},{20,16},{24,28},{28,24},{1,5},{5... | collective-permute-start | bytes 24584 | tf_op jit(solution)/shard_map/ppermute | solution.py:58
  46.6 2.0 %collective-permute-done.8 = bf16[16,256]{1,0:T(8,128)(2,1)S(1)} collective-permute-done((bf16[16,256]{1,0:T(8,128)(2,1)S(1)}, bf16[16,256]{1,0:T(8,128)(2,1)S(1)}, u32[]{:S(2)}, u32[]{:S(2)}) %collective-permute-start.8) | collective-permute-done | bytes 8224 | tf_op jit(solution)/shard_map/ppermute | solution.py:58
  48.5 1.8 %collective-permute-start.9 = (bf16[32,256]{1,0:T(8,128)(2,1)S(1)}, bf16[32,256]{1,0:T(8,128)(2,1)S(1)}, u32[]{:S(2)}, u32[]{:S(2)}) collective-permute-start(bf16[32,256]{1,0:T(8,128)(2,1)S(1)} %maximum_select_fusion.7), channel_id=1, source_target_pairs={{0,8},{4,12},{8,0},{12,4},{16,24},{20,28},{24,16},{28,20},{1,9},{5... | collective-permute-start | bytes 49160 | tf_op jit(solution)/shard_map/ppermute | solution.py:58
  50.4 1.9 %collective-permute-done.9 = bf16[32,256]{1,0:T(8,128)(2,1)S(1)} collective-permute-done((bf16[32,256]{1,0:T(8,128)(2,1)S(1)}, bf16[32,256]{1,0:T(8,128)(2,1)S(1)}, u32[]{:S(2)}, u32[]{:S(2)}) %collective-permute-start.9) | collective-permute-done | bytes 16416 | tf_op jit(solution)/shard_map/ppermute | solution.py:58
  52.3 2.8 %collective-permute-start.10 = (bf16[64,256]{1,0:T(8,128)(2,1)S(1)}, bf16[64,256]{1,0:T(8,128)(2,1)S(1)}, u32[]{:S(2)}, u32[]{:S(2)}) collective-permute-start(bf16[64,256]{1,0:T(8,128)(2,1)S(1)} %maximum_select_fusion.6), channel_id=1, source_target_pairs={{0,16},{4,20},{8,24},{12,28},{16,0},{20,4},{24,8},{28,12},{1,17},{... | collective-permute-start | bytes 98312 | tf_op jit(solution)/shard_map/ppermute | solution.py:58
  55.2 1.9 %collective-permute-done.10 = bf16[64,256]{1,0:T(8,128)(2,1)S(1)} collective-permute-done((bf16[64,256]{1,0:T(8,128)(2,1)S(1)}, bf16[64,256]{1,0:T(8,128)(2,1)S(1)}, u32[]{:S(2)}, u32[]{:S(2)}) %collective-permute-start.10) | collective-permute-done | bytes 32800 | tf_op jit(solution)/shard_map/ppermute | solution.py:58
  59.1 5.9 %select_reduce_fusion = f32[128,64]{1,0:T(8,128)S(1)} fusion(f32[128,16,128]{2,1,0:T(8,128)S(1)} %bitcast.34, s32[128,64]{1,0:T(8,128)S(1)} %get-tuple-element.9, s32[128,64]{1,0:T(8,128)S(1)} %get-tuple-element.8), kind=kOutput, calls=%fused_computation.1 | convolution fusion | flops 204595200 | bytes 1146880 | tf_op jit(solution)/shard_map/tca,tab->tcb/dot_general | solution.py:163
  65.0 2.9 %collective-permute-start.11 = (f32[64,64]{1,0:T(8,128)S(1)}, f32[64,64]{1,0:T(8,128)S(1)}, u32[]{:S(2)}, u32[]{:S(2)}) collective-permute-start(f32[64,64]{1,0:T(8,128)S(1)} %constant_dynamic-slice_fusion.1), channel_id=1, source_target_pairs={{0,16},{4,20},{8,24},{12,28},{16,0},{20,4},{24,8},{28,12},{1,17},{... | collective-permute-start | bytes 49160 | tf_op jit(solution)/shard_map/ppermute | solution.py:47
  67.8 2.0 %collective-permute-done.11 = f32[64,64]{1,0:T(8,128)S(1)} collective-permute-done((f32[64,64]{1,0:T(8,128)S(1)}, f32[64,64]{1,0:T(8,128)S(1)}, u32[]{:S(2)}, u32[]{:S(2)}) %collective-permute-start.11) | collective-permute-done | bytes 16416 | tf_op jit(solution)/shard_map/ppermute | solution.py:47
  69.9 1.8 %collective-permute-start.12 = (f32[32,64]{1,0:T(8,128)S(1)}, f32[32,64]{1,0:T(8,128)S(1)}, u32[]{:S(2)}, u32[]{:S(2)}) collective-permute-start(f32[32,64]{1,0:T(8,128)S(1)} %constant_dynamic-slice_fusion), channel_id=1, source_target_pairs={{0,8},{4,12},{8,0},{12,4},{16,24},{20,28},{24,16},{28,20},{1,9},{5... | collective-permute-start | bytes 24584 | tf_op jit(solution)/shard_map/ppermute | solution.py:47
  71.7 2.0 %collective-permute-done.12 = f32[32,64]{1,0:T(8,128)S(1)} collective-permute-done((f32[32,64]{1,0:T(8,128)S(1)}, f32[32,64]{1,0:T(8,128)S(1)}, u32[]{:S(2)}, u32[]{:S(2)}) %collective-permute-start.12) | collective-permute-done | bytes 8224 | tf_op jit(solution)/shard_map/ppermute | solution.py:47
  73.7 1.7 %collective-permute-start.13 = (f32[16,64]{1,0:T(8,128)S(1)}, f32[16,64]{1,0:T(8,128)S(1)}, u32[]{:S(2)}, u32[]{:S(2)}) collective-permute-start(f32[16,64]{1,0:T(8,128)S(1)} %constant_dynamic-slice_fusion.3), channel_id=1, source_target_pairs={{0,4},{4,0},{8,12},{12,8},{16,20},{20,16},{24,28},{28,24},{1,5},{5... | collective-permute-start | bytes 12296 | tf_op jit(solution)/shard_map/ppermute | solution.py:47
  75.4 1.9 %collective-permute-done.13 = f32[16,64]{1,0:T(8,128)S(1)} collective-permute-done((f32[16,64]{1,0:T(8,128)S(1)}, f32[16,64]{1,0:T(8,128)S(1)}, u32[]{:S(2)}, u32[]{:S(2)}) %collective-permute-start.13) | collective-permute-done | bytes 4128 | tf_op jit(solution)/shard_map/ppermute | solution.py:47
  80.2 2.0 %collective-permute-done.15 = f32[16,64]{1,0:T(8,128)S(1)} collective-permute-done((f32[16,64]{1,0:T(8,128)S(1)}, f32[16,64]{1,0:T(8,128)S(1)}, u32[]{:S(2)}, u32[]{:S(2)}) %collective-permute-start.15) | collective-permute-done | bytes 4128 | tf_op jit(solution)/shard_map/ppermute | solution.py:185
  (83 shorter events, 19.6 us)
Async XLA Ops:
  0.6 24.0 %copy-start = (bf16[1024,1024]{1,0:T(8,128)(2,1)S(1)}, bf16[1024,1024]{1,0:T(8,128)(2,1)}, u32[]{:S(2)}) copy-start(bf16[1024,1024]{1,0:T(8,128)(2,1)} %param.26) | copy-start | bytes 6291460
  6.3 10.0 %copy-start.3 = (f32[1024]{0:T(1024)S(1)}, f32[1024]{0:T(1024)}, u32[]{:S(2)}) copy-start(f32[1024]{0:T(1024)} %param.21) | copy-start | bytes 12292
  6.3 11.2 %copy-start.4 = (f32[1024]{0:T(1024)S(1)}, f32[1024]{0:T(1024)}, u32[]{:S(2)}) copy-start(f32[1024]{0:T(1024)} %param.23) | copy-start | bytes 12292
  6.3 11.2 %copy-start.5 = (f32[1024]{0:T(1024)S(1)}, f32[1024]{0:T(1024)}, u32[]{:S(2)}) copy-start(f32[1024]{0:T(1024)} %param.22) | copy-start | bytes 12292
  7.8 1.7 %collective-permute-start = (bf16[128,1024]{1,0:T(8,128)(2,1)S(1)}, bf16[128,1024]{1,0:T(8,128)(2,1)S(1)}, u32[]{:S(2)}, u32[]{:S(2)}) collective-permute-start(bf16[128,1024]{1,0:T(8,128)(2,1)S(1)} %constant_dynamic-slice_fusion.4), channel_id=1, source_target_pairs={{0,1},{1,0},{2,3},{3,2},{4,5},{5,4},{6,7},{7,6},{8,9},{9,8},{10,11... | collective-permute-start | bytes 786440 | tf_op jit(solution)/shard_map/ppermute | solution.py:47
  8.3 16.3 %copy-start.10 = (f32[1024]{0:T(1024)S(1)}, f32[1024]{0:T(1024)}, u32[]{:S(2)}) copy-start(f32[1024]{0:T(1024)} %param.25) | copy-start | bytes 12292
  9.6 6.7 %collective-permute-start.1 = (bf16[64,1024]{1,0:T(8,128)(2,1)S(1)}, bf16[64,1024]{1,0:T(8,128)(2,1)S(1)}, u32[]{:S(2)}, u32[]{:S(2)}) collective-permute-start(bf16[64,1024]{1,0:T(8,128)(2,1)S(1)} %dynamic-slice_convert_fusion.1), channel_id=1, source_target_pairs={{0,2},{1,3},{2,0},{3,1},{4,6},{5,7},{6,4},{7,5},{8,10},{9,11},{10,... | collective-permute-start | bytes 393224 | tf_op jit(solution)/shard_map/ppermute | solution.py:47
  17.7 5.1 %collective-permute-start.2 = (bf16[64,1024]{1,0:T(8,128)(2,1)S(1)}, bf16[64,1024]{1,0:T(8,128)(2,1)S(1)}, u32[]{:S(2)}, u32[]{:S(2)}) collective-permute-start(bf16[64,1024]{1,0:T(8,128)(2,1)S(1)} %add_convert_fusion.1), channel_id=1, source_target_pairs={{0,2},{1,3},{2,0},{3,1},{4,6},{5,7},{6,4},{7,5},{8,10},{9,11},{10,... | collective-permute-start | bytes 393224 | tf_op jit(solution)/shard_map/ppermute | solution.py:58
  22.9 1.6 %collective-permute-start.3 = (bf16[128,1024]{1,0:T(8,128)(2,1)S(1)}, bf16[128,1024]{1,0:T(8,128)(2,1)S(1)}, u32[]{:S(2)}, u32[]{:S(2)}) collective-permute-start(bf16[128,1024]{1,0:T(8,128)(2,1)S(1)} %maximum_select_fusion.2), channel_id=1, source_target_pairs={{0,1},{1,0},{2,3},{3,2},{4,5},{5,4},{6,7},{7,6},{8,9},{9,8},{10,11... | collective-permute-start | bytes 786440 | tf_op jit(solution)/shard_map/ppermute | solution.py:58
  24.6 12.5 %copy-start.6 = (f32[1024]{0:T(1024)S(1)}, f32[1024]{0:T(1024)}, u32[]{:S(2)}) copy-start(f32[1024]{0:T(1024)} %param.27) | copy-start | bytes 12292
  29.8 1.6 %collective-permute-start.4 = (bf16[128,1024]{1,0:T(8,128)(2,1)S(1)}, bf16[128,1024]{1,0:T(8,128)(2,1)S(1)}, u32[]{:S(2)}, u32[]{:S(2)}) collective-permute-start(bf16[128,1024]{1,0:T(8,128)(2,1)S(1)} %constant_dynamic-slice_fusion.2), channel_id=1, source_target_pairs={{0,1},{1,0},{2,3},{3,2},{4,5},{5,4},{6,7},{7,6},{8,9},{9,8},{10,11... | collective-permute-start | bytes 786440 | tf_op jit(solution)/shard_map/ppermute | solution.py:47
  31.5 18.8 %copy-start.2 = (s32[128,64]{0,1:T(8,128)S(1)}, s32[128,64]{0,1:T(8,128)}, u32[]{:S(2)}) copy-start(s32[128,64]{0,1:T(8,128)} %param.31) | copy-start | bytes 98308
  31.5 5.6 %collective-permute-start.5 = (bf16[64,1024]{1,0:T(8,128)(2,1)S(1)}, bf16[64,1024]{1,0:T(8,128)(2,1)S(1)}, u32[]{:S(2)}, u32[]{:S(2)}) collective-permute-start(bf16[64,1024]{1,0:T(8,128)(2,1)S(1)} %dynamic-slice_convert_fusion), channel_id=1, source_target_pairs={{0,2},{1,3},{2,0},{3,1},{4,6},{5,7},{6,4},{7,5},{8,10},{9,11},{10,... | collective-permute-start | bytes 393224 | tf_op jit(solution)/shard_map/ppermute | solution.py:47
  37.6 5.0 %collective-permute-start.6 = (bf16[64,1024]{1,0:T(8,128)(2,1)S(1)}, bf16[64,1024]{1,0:T(8,128)(2,1)S(1)}, u32[]{:S(2)}, u32[]{:S(2)}) collective-permute-start(bf16[64,1024]{1,0:T(8,128)(2,1)S(1)} %add_convert_fusion), channel_id=1, source_target_pairs={{0,2},{1,3},{2,0},{3,1},{4,6},{5,7},{6,4},{7,5},{8,10},{9,11},{10,... | collective-permute-start | bytes 393224 | tf_op jit(solution)/shard_map/ppermute | solution.py:58
  42.7 1.6 %collective-permute-start.7 = (bf16[128,1024]{1,0:T(8,128)(2,1)S(1)}, bf16[128,1024]{1,0:T(8,128)(2,1)S(1)}, u32[]{:S(2)}, u32[]{:S(2)}) collective-permute-start(bf16[128,1024]{1,0:T(8,128)(2,1)S(1)} %maximum_select_fusion.3), channel_id=1, source_target_pairs={{0,1},{1,0},{2,3},{3,2},{4,5},{5,4},{6,7},{7,6},{8,9},{9,8},{10,11... | collective-permute-start | bytes 786440 | tf_op jit(solution)/shard_map/ppermute | solution.py:58
  44.5 14.6 %copy-start.1 = (bf16[256,1024]{1,0:T(8,128)(2,1)}, bf16[256,1024]{1,0:T(8,128)(2,1)S(1)}, u32[]{:S(2)}) copy-start(bf16[256,1024]{1,0:T(8,128)(2,1)S(1)} %maximum_select_fusion.1) | copy-start | bytes 1572868
  44.9 3.7 %collective-permute-start.8 = (bf16[16,256]{1,0:T(8,128)(2,1)S(1)}, bf16[16,256]{1,0:T(8,128)(2,1)S(1)}, u32[]{:S(2)}, u32[]{:S(2)}) collective-permute-start(bf16[16,256]{1,0:T(8,128)(2,1)S(1)} %fusion.56), channel_id=1, source_target_pairs={{0,4},{4,0},{8,12},{12,8},{16,20},{20,16},{24,28},{28,24},{1,5},{5... | collective-permute-start | bytes 24584 | tf_op jit(solution)/shard_map/ppermute | solution.py:58
  48.5 3.7 %collective-permute-start.9 = (bf16[32,256]{1,0:T(8,128)(2,1)S(1)}, bf16[32,256]{1,0:T(8,128)(2,1)S(1)}, u32[]{:S(2)}, u32[]{:S(2)}) collective-permute-start(bf16[32,256]{1,0:T(8,128)(2,1)S(1)} %maximum_select_fusion.7), channel_id=1, source_target_pairs={{0,8},{4,12},{8,0},{12,4},{16,24},{20,28},{24,16},{28,20},{1,9},{5... | collective-permute-start | bytes 49160 | tf_op jit(solution)/shard_map/ppermute | solution.py:58
  52.3 4.9 %collective-permute-start.10 = (bf16[64,256]{1,0:T(8,128)(2,1)S(1)}, bf16[64,256]{1,0:T(8,128)(2,1)S(1)}, u32[]{:S(2)}, u32[]{:S(2)}) collective-permute-start(bf16[64,256]{1,0:T(8,128)(2,1)S(1)} %maximum_select_fusion.6), channel_id=1, source_target_pairs={{0,16},{4,20},{8,24},{12,28},{16,0},{20,4},{24,8},{28,12},{1,17},{... | collective-permute-start | bytes 98312 | tf_op jit(solution)/shard_map/ppermute | solution.py:58
  65.0 4.9 %collective-permute-start.11 = (f32[64,64]{1,0:T(8,128)S(1)}, f32[64,64]{1,0:T(8,128)S(1)}, u32[]{:S(2)}, u32[]{:S(2)}) collective-permute-start(f32[64,64]{1,0:T(8,128)S(1)} %constant_dynamic-slice_fusion.1), channel_id=1, source_target_pairs={{0,16},{4,20},{8,24},{12,28},{16,0},{20,4},{24,8},{28,12},{1,17},{... | collective-permute-start | bytes 49160 | tf_op jit(solution)/shard_map/ppermute | solution.py:47
  69.9 3.8 %collective-permute-start.12 = (f32[32,64]{1,0:T(8,128)S(1)}, f32[32,64]{1,0:T(8,128)S(1)}, u32[]{:S(2)}, u32[]{:S(2)}) collective-permute-start(f32[32,64]{1,0:T(8,128)S(1)} %constant_dynamic-slice_fusion), channel_id=1, source_target_pairs={{0,8},{4,12},{8,0},{12,4},{16,24},{20,28},{24,16},{28,20},{1,9},{5... | collective-permute-start | bytes 24584 | tf_op jit(solution)/shard_map/ppermute | solution.py:47
  73.7 3.7 %collective-permute-start.13 = (f32[16,64]{1,0:T(8,128)S(1)}, f32[16,64]{1,0:T(8,128)S(1)}, u32[]{:S(2)}, u32[]{:S(2)}) collective-permute-start(f32[16,64]{1,0:T(8,128)S(1)} %constant_dynamic-slice_fusion.3), channel_id=1, source_target_pairs={{0,4},{4,0},{8,12},{12,8},{16,20},{20,16},{24,28},{28,24},{1,5},{5... | collective-permute-start | bytes 12296 | tf_op jit(solution)/shard_map/ppermute | solution.py:47
  77.4 1.2 %collective-permute-start.14 = (f32[16,64]{1,0:T(8,128)S(1)}, f32[16,64]{1,0:T(8,128)S(1)}, u32[]{:S(2)}, u32[]{:S(2)}) collective-permute-start(f32[16,64]{1,0:T(8,128)S(1)} %dynamic-slice_add_fusion.2), channel_id=1, source_target_pairs={{0,1},{1,0},{2,3},{3,2},{4,5},{5,4},{6,7},{7,6},{8,9},{9,8},{10,11... | collective-permute-start | bytes 12296 | tf_op jit(solution)/shard_map/ppermute | solution.py:185
  78.5 3.7 %collective-permute-start.15 = (f32[16,64]{1,0:T(8,128)S(1)}, f32[16,64]{1,0:T(8,128)S(1)}, u32[]{:S(2)}, u32[]{:S(2)}) collective-permute-start(f32[16,64]{1,0:T(8,128)S(1)} %add.234), channel_id=1, source_target_pairs={{0,2},{1,3},{2,0},{3,1},{4,6},{5,7},{6,4},{7,5},{8,10},{9,11},{10,... | collective-permute-start | bytes 12296 | tf_op jit(solution)/shard_map/ppermute | solution.py:185
  (3 other events, 18.6 us)

commit v7 on v6

--- a/solution.py
+++ b/solution.py
@@ -75,6 +75,38 @@
         jnp.bfloat16
     )
     return all_gather_xor(normed, "tensor", n_tensor, levels[::-1])
+
+
+def in_order(first_bit, mine, other):
+    return jnp.where(first_bit == 0, jnp.concatenate([mine, other]), jnp.concatenate([other, mine]))
+
+
+def overlapped_layer(
+    partial_value, hidden, b_output, first_gain, first_shift, feed_forward, b_down, second_gain,
+    second_shift,
+):
+    index = lax.axis_index("tensor")
+    low = index % 2
+    high = (index // 2) % 2
+    total, block = reduce_scatter_xor(partial_value.astype(jnp.bfloat16), "tensor", 4, [1, 2])
+    rows = total.shape[0]
+    own_residual = lax.dynamic_slice_in_dim(hidden, block * rows, rows, 0)
+    own = layer_norm(total + b_output + own_residual.astype(jnp.float32), first_gain, first_shift)
+    own = own.astype(jnp.bfloat16)
+    cross = lax.ppermute(own, "tensor", xor_pairs(4, 2))
+    own_out = feed_forward(own)
+    half = in_order(high, own, cross)
+    other_half = lax.ppermute(half, "tensor", xor_pairs(4, 1))
+    cross_out = feed_forward(cross)
+    other_out = feed_forward(other_half)
+    got = lax.ppermute(other_out.astype(jnp.bfloat16), "tensor", xor_pairs(4, 1))
+    half_sum = in_order(high, own_out, cross_out) + got.astype(jnp.float32)
+    keep = lax.dynamic_slice_in_dim(half_sum, high * rows, rows, 0)
+    send = lax.dynamic_slice_in_dim(half_sum, (1 - high) * rows, rows, 0)
+    got = lax.ppermute(send.astype(jnp.bfloat16), "tensor", xor_pairs(4, 2))
+    total = keep + got.astype(jnp.float32)
+    normed = layer_norm(total + b_down + own.astype(jnp.float32), second_gain, second_shift)
+    return all_gather_xor(normed.astype(jnp.bfloat16), "tensor", 4, [2, 1])
 
 
 def body(
@@ -117,12 +149,29 @@
     context = jnp.einsum("hts,shd->thd", weights, values, preferred_element_type=jnp.float32)
     context = context.astype(jnp.bfloat16).reshape(tokens_here, local_width)
     partial_value = jnp.dot(context, w_output, preferred_element_type=jnp.float32)
-    attended = settle(partial_value, hidden, b_output, first_gain, first_shift, n_tensor)
-    activated = jax.nn.gelu(
-        jnp.dot(attended, w_up, preferred_element_type=jnp.float32) + b_up, approximate=False
-    ).astype(jnp.bfloat16)
-    partial_value = jnp.dot(activated, w_down, preferred_element_type=jnp.float32)
-    states = settle(partial_value, attended, b_down, second_gain, second_shift, n_tensor)
+    def feed_forward(rows):
+        activated = jax.nn.gelu(
+            jnp.dot(rows, w_up, preferred_element_type=jnp.float32) + b_up, approximate=False
+        ).astype(jnp.bfloat16)
+        return jnp.dot(activated, w_down, preferred_element_type=jnp.float32)
+
+    if n_tensor == 4 and tokens_here % 4 == 0:
+        states = overlapped_layer(
+            partial_value,
+            hidden,
+            b_output,
+            first_gain,
+            first_shift,
+            feed_forward,
+            b_down,
+            second_gain,
+            second_shift,
+        )
+    else:
+        attended = settle(partial_value, hidden, b_output, first_gain, first_shift, n_tensor)
+        states = settle(
+            feed_forward(attended), attended, b_down, second_gain, second_shift, n_tensor
+        )
     texts_here = lengths.shape[1]
     member = (segment[None, :] == jnp.arange(texts_here, dtype=jnp.int32)[:, None]).astype(
         jnp.bfloat16

time: 83 us -> 85.3 us (1.028)
  matrix products: 18.8 us -> 23.9 us
  waiting for transfers between devices: 34.7 us -> 31.6 us
    ppermute x0 -> x4, waiting for transfers between devices: none -> 7.04 us  [the longest x1 3.75 us: overlapped_layer(): got = lax.ppermute(send.astype(jnp.bfloat16), 'tensor', xor_pairs(4, 2))]
    ppermute x7 -> x5, waiting for transfers between devices: 16.2 us -> 10.9 us  [reduce_scatter_xor(): got = lax.ppermute(theirs.astype(wire), axis, xor_pairs(n, k))]
    dot_general x1 -> x3, matrix products: 5.11 us -> 10.1 us  [feed_forward(): return jnp.dot(activated, w_down, preferred_element_type=jnp.float32)]
    ppermute x7 -> x5, waiting for transfers between devices: 15.4 us -> 10.5 us  [all_gather_xor(): other = lax.ppermute(cur, axis, xor_pairs(n, k))]
    ppermute x0 -> x4, starting transfers between devices: none -> 4.11 us  [the longest x1 1.81 us: overlapped_layer(): cross = lax.ppermute(own, 'tensor', xor_pairs(4, 2))]
    ppermute x7 -> x5, starting transfers between devices: 11.8 us -> 9.85 us  [reduce_scatter_xor(): got = lax.ppermute(theirs.astype(wire), axis, xor_pairs(n, k))]
    ppermute x7 -> x5, starting transfers between devices: 9.98 us -> 8.15 us  [all_gather_xor(): other = lax.ppermute(cur, axis, xor_pairs(n, k))]
  transfers between devices with their start and end apart: 16 -> 16, of which waited for: 16 -> 14; matrix products, arithmetic and copies ran while one was open for 0% -> 7% of each run, Pallas kernels for 0% -> 0%
where the time goes in v7:
time: 85.3 us; the launch traced here: 85 us
  waiting for transfers between devices  31.6 us (37%)
  matrix products  23.9 us (28%)
  starting transfers between devices  23.8 us (28%)
  other arithmetic  3.47 us (4%)
  local copies, waits for them, and re-layouts  1.2 us (1%)
  between operations  1.09 us (1%)
    ppermute x5, waiting for transfers between devices, reduce_scatter_xor(): got = lax.ppermute(theirs.astype(wire), axis, xor_pairs(n, k))  10.9 us
    ppermute x5, waiting for transfers between devices, all_gather_xor(): other = lax.ppermute(cur, axis, xor_pairs(n, k))  10.5 us
    dot_general x3, matrix products, feed_forward(): return jnp.dot(activated, w_down, preferred_element_type=jnp.float32)  10.1 us
    ppermute x5, starting transfers between devices, reduce_scatter_xor(): got = lax.ppermute(theirs.astype(wire), axis, xor_pairs(n, k))  9.85 us
    ppermute x5, starting transfers between devices, all_gather_xor(): other = lax.ppermute(cur, axis, xor_pairs(n, k))  8.15 us
    dot_general x1, matrix products, body(): jnp.einsum('tca,tab->tcb', major_hot, tile.reshape(all_texts, major, mino...  5.86 us
    ppermute x1, waiting for transfers between devices, overlapped_layer(): got = lax.ppermute(send.astype(jnp.bfloat16), 'tensor', xor_pairs(4, 2))  3.75 us
    ppermute x1, waiting for transfers between devices, overlapped_layer(): cross = lax.ppermute(own, 'tensor', xor_pairs(4, 2))  3.29 us
  transfers between devices with their start and end apart: 16, of which 14 were waited for; matrix products, arithmetic and copies ran while one was open for 7% of the time, Pallas kernels for 0%

profile of v7, /device:TPU:0, one launch (start us, length us, event | category | flops | bytes accessed | tf_op | source)
XLA Modules:
  0.0 85.0 jit_solution(6823796160432230503)
XLA Ops:
  0.7 2.3 %fusion.239 = (bf16[3,256,256]{1,2,0:T(8,128)(2,1)S(1)}, f32[3,256,256]{1,2,0:T(8,128)S(1)}) fusion(f32[3,256]{1,0:T(4,128)} %param.19, bf16[3,1024,256]{2,1,0:T(8,128)(2,1)} %param.18, bf16[256,1024]{1,0:T(8,128)(2,1)} %param.16), kind=kOutput, calls=%fused_computation.325 | convolution fusion | flops 403046400 | bytes 3279872 | tf_op jit(solution)/shard_map/td,jdf->jtf/dot_general | solution.py:136
  9.6 2.9 %collective-permute-start.1 = (bf16[64,1024]{1,0:T(8,128)(2,1)S(1)}, bf16[64,1024]{1,0:T(8,128)(2,1)S(1)}, u32[]{:S(2)}, u32[]{:S(2)}) collective-permute-start(bf16[64,1024]{1,0:T(8,128)(2,1)S(1)} %dynamic-slice_convert_fusion.1), channel_id=1, source_target_pairs={{0,2},{1,3},{2,0},{3,1},{4,6},{5,7},{6,4},{7,5},{8,10},{9,11},{10,... | collective-permute-start | bytes 393224 | tf_op jit(solution)/shard_map/ppermute | solution.py:47
  12.5 3.8 %collective-permute-done.1 = bf16[64,1024]{1,0:T(8,128)(2,1)S(1)} collective-permute-done((bf16[64,1024]{1,0:T(8,128)(2,1)S(1)}, bf16[64,1024]{1,0:T(8,128)(2,1)S(1)}, u32[]{:S(2)}, u32[]{:S(2)}) %collective-permute-start.1) | collective-permute-done | bytes 131104 | tf_op jit(solution)/shard_map/ppermute | solution.py:47
  17.7 1.8 %collective-permute-start.2 = (bf16[64,1024]{1,0:T(8,128)(2,1)S(1)}, bf16[64,1024]{1,0:T(8,128)(2,1)S(1)}, u32[]{:S(2)}, u32[]{:S(2)}) collective-permute-start(bf16[64,1024]{1,0:T(8,128)(2,1)S(1)} %add_convert_fusion.1), channel_id=1, source_target_pairs={{0,2},{1,3},{2,0},{3,1},{4,6},{5,7},{6,4},{7,5},{8,10},{9,11},{10,... | collective-permute-start | bytes 393224 | tf_op jit(solution)/shard_map/ppermute | solution.py:96
  19.5 3.3 %collective-permute-done.2 = bf16[64,1024]{1,0:T(8,128)(2,1)S(1)} collective-permute-done((bf16[64,1024]{1,0:T(8,128)(2,1)S(1)}, bf16[64,1024]{1,0:T(8,128)(2,1)S(1)}, u32[]{:S(2)}, u32[]{:S(2)}) %collective-permute-start.2) | collective-permute-done | bytes 131104 | tf_op jit(solution)/shard_map/ppermute | solution.py:96
  23.0 3.0 %fusion.70 = f32[64,1024]{1,0:T(8,128)S(1)} fusion(bf16[1024,1024]{1,0:T(8,128)(2,1)S(1)} %copy-done, bf16[64,1024]{1,0:T(8,128)(2,1)S(1)} %add_convert_fusion.1, bf16[1024,1024]{1,0:T(8,128)(2,1)} %param.24, f32[1024]{0:T(1024)S(1)} %copy-done.10), kind=kOutput, calls=%fused_computation.125 | convolution fusion | flops 272760832 | bytes 4591616 | tf_op jit(solution)/shard_map/dot_general | solution.py:156
  26.0 4.2 %convolution_convert_fusion.1 = bf16[128,1024]{1,0:T(8,128)(2,1)} fusion(bf16[1024,1024]{1,0:T(8,128)(2,1)S(1)} %copy-done, bf16[128,1024]{1,0:T(8,128)(2,1)S(1)} %collective-permute-done.3, bf16[1024,1024]{1,0:T(8,128)(2,1)} %param.24, f32[1024]{0:T(1024)S(1)} %copy-done.10), kind=kOutput, calls=%fused_computation.11 | convolution fusion | flops 545652736 | bytes 4722688 | tf_op jit(solution)/shard_map/dot_general | solution.py:156
  30.6 3.0 %fusion.68 = f32[64,1024]{1,0:T(8,128)S(1)} fusion(bf16[1024,1024]{1,0:T(8,128)(2,1)S(1)} %copy-done, bf16[64,1024]{1,0:T(8,128)(2,1)S(1)} %collective-permute-done.2, bf16[1024,1024]{1,0:T(8,128)(2,1)} %param.24, f32[1024]{0:T(1024)S(1)} %copy-done.10), kind=kOutput, calls=%fused_computation.122 | convolution fusion | flops 272760832 | bytes 4591616 | tf_op jit(solution)/shard_map/dot_general | solution.py:156
  33.8 1.7 %collective-permute-start.5 = (bf16[64,1024]{1,0:T(8,128)(2,1)S(1)}, bf16[64,1024]{1,0:T(8,128)(2,1)S(1)}, u32[]{:S(2)}, u32[]{:S(2)}) collective-permute-start(bf16[64,1024]{1,0:T(8,128)(2,1)S(1)} %dynamic-slice_convert_fusion), channel_id=1, source_target_pairs={{0,2},{1,3},{2,0},{3,1},{4,6},{5,7},{6,4},{7,5},{8,10},{9,11},{10,... | collective-permute-start | bytes 393224 | tf_op jit(solution)/shard_map/ppermute | solution.py:106
  35.5 3.7 %collective-permute-done.5 = bf16[64,1024]{1,0:T(8,128)(2,1)S(1)} collective-permute-done((bf16[64,1024]{1,0:T(8,128)(2,1)S(1)}, bf16[64,1024]{1,0:T(8,128)(2,1)S(1)}, u32[]{:S(2)}, u32[]{:S(2)}) %collective-permute-start.5) | collective-permute-done | bytes 131104 | tf_op jit(solution)/shard_map/ppermute | solution.py:106
  39.9 1.7 %collective-permute-start.6 = (bf16[64,1024]{1,0:T(8,128)(2,1)S(1)}, bf16[64,1024]{1,0:T(8,128)(2,1)S(1)}, u32[]{:S(2)}, u32[]{:S(2)}) collective-permute-start(bf16[64,1024]{1,0:T(8,128)(2,1)S(1)} %add_convert_fusion), channel_id=1, source_target_pairs={{0,2},{1,3},{2,0},{3,1},{4,6},{5,7},{6,4},{7,5},{8,10},{9,11},{10,... | collective-permute-start | bytes 393224 | tf_op jit(solution)/shard_map/ppermute | solution.py:58
  41.6 3.3 %collective-permute-done.6 = bf16[64,1024]{1,0:T(8,128)(2,1)S(1)} collective-permute-done((bf16[64,1024]{1,0:T(8,128)(2,1)S(1)}, bf16[64,1024]{1,0:T(8,128)(2,1)S(1)}, u32[]{:S(2)}, u32[]{:S(2)}) %collective-permute-start.6) | collective-permute-done | bytes 131104 | tf_op jit(solution)/shard_map/ppermute | solution.py:58
  48.8 1.9 %collective-permute-done.8 = bf16[16,256]{1,0:T(8,128)(2,1)S(1)} collective-permute-done((bf16[16,256]{1,0:T(8,128)(2,1)S(1)}, bf16[16,256]{1,0:T(8,128)(2,1)S(1)}, u32[]{:S(2)}, u32[]{:S(2)}) %collective-permute-start.8) | collective-permute-done | bytes 8224 | tf_op jit(solution)/shard_map/ppermute | solution.py:58
  50.8 1.8 %collective-permute-start.9 = (bf16[32,256]{1,0:T(8,128)(2,1)S(1)}, bf16[32,256]{1,0:T(8,128)(2,1)S(1)}, u32[]{:S(2)}, u32[]{:S(2)}) collective-permute-start(bf16[32,256]{1,0:T(8,128)(2,1)S(1)} %maximum_select_fusion.7), channel_id=1, source_target_pairs={{0,8},{4,12},{8,0},{12,4},{16,24},{20,28},{24,16},{28,20},{1,9},{5... | collective-permute-start | bytes 49160 | tf_op jit(solution)/shard_map/ppermute | solution.py:58
  52.6 1.9 %collective-permute-done.9 = bf16[32,256]{1,0:T(8,128)(2,1)S(1)} collective-permute-done((bf16[32,256]{1,0:T(8,128)(2,1)S(1)}, bf16[32,256]{1,0:T(8,128)(2,1)S(1)}, u32[]{:S(2)}, u32[]{:S(2)}) %collective-permute-start.9) | collective-permute-done | bytes 16416 | tf_op jit(solution)/shard_map/ppermute | solution.py:58
  54.5 2.8 %collective-permute-start.10 = (bf16[64,256]{1,0:T(8,128)(2,1)S(1)}, bf16[64,256]{1,0:T(8,128)(2,1)S(1)}, u32[]{:S(2)}, u32[]{:S(2)}) collective-permute-start(bf16[64,256]{1,0:T(8,128)(2,1)S(1)} %maximum_select_fusion.6), channel_id=1, source_target_pairs={{0,16},{4,20},{8,24},{12,28},{16,0},{20,4},{24,8},{28,12},{1,17},{... | collective-permute-start | bytes 98312 | tf_op jit(solution)/shard_map/ppermute | solution.py:58
  57.5 1.9 %collective-permute-done.10 = bf16[64,256]{1,0:T(8,128)(2,1)S(1)} collective-permute-done((bf16[64,256]{1,0:T(8,128)(2,1)S(1)}, bf16[64,256]{1,0:T(8,128)(2,1)S(1)}, u32[]{:S(2)}, u32[]{:S(2)}) %collective-permute-start.10) | collective-permute-done | bytes 32800 | tf_op jit(solution)/shard_map/ppermute | solution.py:58
  61.3 5.9 %select_reduce_fusion = f32[128,64]{1,0:T(8,128)S(1)} fusion(f32[128,16,128]{2,1,0:T(8,128)S(1)} %bitcast.40, s32[128,64]{1,0:T(8,128)S(1)} %get-tuple-element.9, s32[128,64]{1,0:T(8,128)S(1)} %get-tuple-element.8), kind=kOutput, calls=%fused_computation.1 | convolution fusion | flops 204595200 | bytes 1146880 | tf_op jit(solution)/shard_map/tca,tab->tcb/dot_general | solution.py:212
  67.2 2.9 %collective-permute-start.11 = (f32[64,64]{1,0:T(8,128)S(1)}, f32[64,64]{1,0:T(8,128)S(1)}, u32[]{:S(2)}, u32[]{:S(2)}) collective-permute-start(f32[64,64]{1,0:T(8,128)S(1)} %constant_dynamic-slice_fusion.2), channel_id=1, source_target_pairs={{0,16},{4,20},{8,24},{12,28},{16,0},{20,4},{24,8},{28,12},{1,17},{... | collective-permute-start | bytes 49160 | tf_op jit(solution)/shard_map/ppermute | solution.py:47
  70.1 2.0 %collective-permute-done.11 = f32[64,64]{1,0:T(8,128)S(1)} collective-permute-done((f32[64,64]{1,0:T(8,128)S(1)}, f32[64,64]{1,0:T(8,128)S(1)}, u32[]{:S(2)}, u32[]{:S(2)}) %collective-permute-start.11) | collective-permute-done | bytes 16416 | tf_op jit(solution)/shard_map/ppermute | solution.py:47
  72.1 1.8 %collective-permute-start.12 = (f32[32,64]{1,0:T(8,128)S(1)}, f32[32,64]{1,0:T(8,128)S(1)}, u32[]{:S(2)}, u32[]{:S(2)}) collective-permute-start(f32[32,64]{1,0:T(8,128)S(1)} %constant_dynamic-slice_fusion.1), channel_id=1, source_target_pairs={{0,8},{4,12},{8,0},{12,4},{16,24},{20,28},{24,16},{28,20},{1,9},{5... | collective-permute-start | bytes 24584 | tf_op jit(solution)/shard_map/ppermute | solution.py:47
  73.9 2.0 %collective-permute-done.12 = f32[32,64]{1,0:T(8,128)S(1)} collective-permute-done((f32[32,64]{1,0:T(8,128)S(1)}, f32[32,64]{1,0:T(8,128)S(1)}, u32[]{:S(2)}, u32[]{:S(2)}) %collective-permute-start.12) | collective-permute-done | bytes 8224 | tf_op jit(solution)/shard_map/ppermute | solution.py:47
  77.6 1.9 %collective-permute-done.13 = f32[16,64]{1,0:T(8,128)S(1)} collective-permute-done((f32[16,64]{1,0:T(8,128)S(1)}, f32[16,64]{1,0:T(8,128)S(1)}, u32[]{:S(2)}, u32[]{:S(2)}) %collective-permute-start.13) | collective-permute-done | bytes 4128 | tf_op jit(solution)/shard_map/ppermute | solution.py:47
  82.4 2.0 %collective-permute-done.15 = f32[16,64]{1,0:T(8,128)S(1)} collective-permute-done((f32[16,64]{1,0:T(8,128)S(1)}, f32[16,64]{1,0:T(8,128)S(1)}, u32[]{:S(2)}, u32[]{:S(2)}) %collective-permute-start.15) | collective-permute-done | bytes 4128 | tf_op jit(solution)/shard_map/ppermute | solution.py:234
  (83 shorter events, 20.3 us)
Async XLA Ops:
  0.6 22.3 %copy-start = (bf16[1024,1024]{1,0:T(8,128)(2,1)S(1)}, bf16[1024,1024]{1,0:T(8,128)(2,1)}, u32[]{:S(2)}) copy-start(bf16[1024,1024]{1,0:T(8,128)(2,1)} %param.26) | copy-start | bytes 6291460
  6.3 10.0 %copy-start.5 = (f32[1024]{0:T(1024)S(1)}, f32[1024]{0:T(1024)}, u32[]{:S(2)}) copy-start(f32[1024]{0:T(1024)} %param.21) | copy-start | bytes 12292
  6.3 11.3 %copy-start.3 = (f32[1024]{0:T(1024)S(1)}, f32[1024]{0:T(1024)}, u32[]{:S(2)}) copy-start(f32[1024]{0:T(1024)} %param.23) | copy-start | bytes 12292
  6.3 11.2 %copy-start.4 = (f32[1024]{0:T(1024)S(1)}, f32[1024]{0:T(1024)}, u32[]{:S(2)}) copy-start(f32[1024]{0:T(1024)} %param.22) | copy-start | bytes 12292
  7.7 15.2 %copy-start.10 = (f32[1024]{0:T(1024)S(1)}, f32[1024]{0:T(1024)}, u32[]{:S(2)}) copy-start(f32[1024]{0:T(1024)} %param.25) | copy-start | bytes 12292
  7.8 1.7 %collective-permute-start = (bf16[128,1024]{1,0:T(8,128)(2,1)S(1)}, bf16[128,1024]{1,0:T(8,128)(2,1)S(1)}, u32[]{:S(2)}, u32[]{:S(2)}) collective-permute-start(bf16[128,1024]{1,0:T(8,128)(2,1)S(1)} %constant_dynamic-slice_fusion.3), channel_id=1, source_target_pairs={{0,1},{1,0},{2,3},{3,2},{4,5},{5,4},{6,7},{7,6},{8,9},{9,8},{10,11... | collective-permute-start | bytes 786440 | tf_op jit(solution)/shard_map/ppermute | solution.py:47
  9.6 6.7 %collective-permute-start.1 = (bf16[64,1024]{1,0:T(8,128)(2,1)S(1)}, bf16[64,1024]{1,0:T(8,128)(2,1)S(1)}, u32[]{:S(2)}, u32[]{:S(2)}) collective-permute-start(bf16[64,1024]{1,0:T(8,128)(2,1)S(1)} %dynamic-slice_convert_fusion.1), channel_id=1, source_target_pairs={{0,2},{1,3},{2,0},{3,1},{4,6},{5,7},{6,4},{7,5},{8,10},{9,11},{10,... | collective-permute-start | bytes 393224 | tf_op jit(solution)/shard_map/ppermute | solution.py:47
  17.7 5.1 %collective-permute-start.2 = (bf16[64,1024]{1,0:T(8,128)(2,1)S(1)}, bf16[64,1024]{1,0:T(8,128)(2,1)S(1)}, u32[]{:S(2)}, u32[]{:S(2)}) collective-permute-start(bf16[64,1024]{1,0:T(8,128)(2,1)S(1)} %add_convert_fusion.1), channel_id=1, source_target_pairs={{0,2},{1,3},{2,0},{3,1},{4,6},{5,7},{6,4},{7,5},{8,10},{9,11},{10,... | collective-permute-start | bytes 393224 | tf_op jit(solution)/shard_map/ppermute | solution.py:96
  22.9 3.1 %collective-permute-start.3 = (bf16[128,1024]{1,0:T(8,128)(2,1)S(1)}, bf16[128,1024]{1,0:T(8,128)(2,1)S(1)}, u32[]{:S(2)}, u32[]{:S(2)}) collective-permute-start(bf16[128,1024]{1,0:T(8,128)(2,1)S(1)} %maximum_select_fusion.2), channel_id=1, source_target_pairs={{0,1},{1,0},{2,3},{3,2},{4,5},{5,4},{6,7},{7,6},{8,9},{9,8},{10,11... | collective-permute-start | bytes 786440 | tf_op jit(solution)/shard_map/ppermute | solution.py:99
  30.2 9.1 %copy-start.6 = (f32[1024]{0:T(1024)S(1)}, f32[1024]{0:T(1024)}, u32[]{:S(2)}) copy-start(f32[1024]{0:T(1024)} %param.27) | copy-start | bytes 12292
  30.2 3.5 %collective-permute-start.4 = (bf16[128,1024]{1,0:T(8,128)(2,1)}, bf16[128,1024]{1,0:T(8,128)(2,1)S(1)}, u32[]{:S(2)}, u32[]{:S(2)}) collective-permute-start(bf16[128,1024]{1,0:T(8,128)(2,1)} %convolution_convert_fusion.1), channel_id=1, source_target_pairs={{0,1},{1,0},{2,3},{3,2},{4,5},{5,4},{6,7},{7,6},{8,9},{9,8},{10,11... | collective-permute-start | bytes 786440 | tf_op jit(solution)/shard_map/ppermute | solution.py:102
  33.7 18.8 %copy-start.2 = (s32[128,64]{0,1:T(8,128)S(1)}, s32[128,64]{0,1:T(8,128)}, u32[]{:S(2)}) copy-start(s32[128,64]{0,1:T(8,128)} %param.31) | copy-start | bytes 98308
  33.8 5.5 %collective-permute-start.5 = (bf16[64,1024]{1,0:T(8,128)(2,1)S(1)}, bf16[64,1024]{1,0:T(8,128)(2,1)S(1)}, u32[]{:S(2)}, u32[]{:S(2)}) collective-permute-start(bf16[64,1024]{1,0:T(8,128)(2,1)S(1)} %dynamic-slice_convert_fusion), channel_id=1, source_target_pairs={{0,2},{1,3},{2,0},{3,1},{4,6},{5,7},{6,4},{7,5},{8,10},{9,11},{10,... | collective-permute-start | bytes 393224 | tf_op jit(solution)/shard_map/ppermute | solution.py:106
  39.9 5.0 %collective-permute-start.6 = (bf16[64,1024]{1,0:T(8,128)(2,1)S(1)}, bf16[64,1024]{1,0:T(8,128)(2,1)S(1)}, u32[]{:S(2)}, u32[]{:S(2)}) collective-permute-start(bf16[64,1024]{1,0:T(8,128)(2,1)S(1)} %add_convert_fusion), channel_id=1, source_target_pairs={{0,2},{1,3},{2,0},{3,1},{4,6},{5,7},{6,4},{7,5},{8,10},{9,11},{10,... | collective-permute-start | bytes 393224 | tf_op jit(solution)/shard_map/ppermute | solution.py:58
  44.9 1.6 %collective-permute-start.7 = (bf16[128,1024]{1,0:T(8,128)(2,1)S(1)}, bf16[128,1024]{1,0:T(8,128)(2,1)S(1)}, u32[]{:S(2)}, u32[]{:S(2)}) collective-permute-start(bf16[128,1024]{1,0:T(8,128)(2,1)S(1)} %maximum_select_fusion.3), channel_id=1, source_target_pairs={{0,1},{1,0},{2,3},{3,2},{4,5},{5,4},{6,7},{7,6},{8,9},{9,8},{10,11... | collective-permute-start | bytes 786440 | tf_op jit(solution)/shard_map/ppermute | solution.py:58
  46.7 14.6 %copy-start.1 = (bf16[256,1024]{1,0:T(8,128)(2,1)}, bf16[256,1024]{1,0:T(8,128)(2,1)S(1)}, u32[]{:S(2)}) copy-start(bf16[256,1024]{1,0:T(8,128)(2,1)S(1)} %maximum_select_fusion.1) | copy-start | bytes 1572868
  47.1 3.7 %collective-permute-start.8 = (bf16[16,256]{1,0:T(8,128)(2,1)S(1)}, bf16[16,256]{1,0:T(8,128)(2,1)S(1)}, u32[]{:S(2)}, u32[]{:S(2)}) collective-permute-start(bf16[16,256]{1,0:T(8,128)(2,1)S(1)} %fusion.141), channel_id=1, source_target_pairs={{0,4},{4,0},{8,12},{12,8},{16,20},{20,16},{24,28},{28,24},{1,5},{5... | collective-permute-start | bytes 24584 | tf_op jit(solution)/shard_map/ppermute | solution.py:58
  50.8 3.7 %collective-permute-start.9 = (bf16[32,256]{1,0:T(8,128)(2,1)S(1)}, bf16[32,256]{1,0:T(8,128)(2,1)S(1)}, u32[]{:S(2)}, u32[]{:S(2)}) collective-permute-start(bf16[32,256]{1,0:T(8,128)(2,1)S(1)} %maximum_select_fusion.7), channel_id=1, source_target_pairs={{0,8},{4,12},{8,0},{12,4},{16,24},{20,28},{24,16},{28,20},{1,9},{5... | collective-permute-start | bytes 49160 | tf_op jit(solution)/shard_map/ppermute | solution.py:58
  54.5 4.9 %collective-permute-start.10 = (bf16[64,256]{1,0:T(8,128)(2,1)S(1)}, bf16[64,256]{1,0:T(8,128)(2,1)S(1)}, u32[]{:S(2)}, u32[]{:S(2)}) collective-permute-start(bf16[64,256]{1,0:T(8,128)(2,1)S(1)} %maximum_select_fusion.6), channel_id=1, source_target_pairs={{0,16},{4,20},{8,24},{12,28},{16,0},{20,4},{24,8},{28,12},{1,17},{... | collective-permute-start | bytes 98312 | tf_op jit(solution)/shard_map/ppermute | solution.py:58
  67.2 4.9 %collective-permute-start.11 = (f32[64,64]{1,0:T(8,128)S(1)}, f32[64,64]{1,0:T(8,128)S(1)}, u32[]{:S(2)}, u32[]{:S(2)}) collective-permute-start(f32[64,64]{1,0:T(8,128)S(1)} %constant_dynamic-slice_fusion.2), channel_id=1, source_target_pairs={{0,16},{4,20},{8,24},{12,28},{16,0},{20,4},{24,8},{28,12},{1,17},{... | collective-permute-start | bytes 49160 | tf_op jit(solution)/shard_map/ppermute | solution.py:47
  72.1 3.8 %collective-permute-start.12 = (f32[32,64]{1,0:T(8,128)S(1)}, f32[32,64]{1,0:T(8,128)S(1)}, u32[]{:S(2)}, u32[]{:S(2)}) collective-permute-start(f32[32,64]{1,0:T(8,128)S(1)} %constant_dynamic-slice_fusion.1), channel_id=1, source_target_pairs={{0,8},{4,12},{8,0},{12,4},{16,24},{20,28},{24,16},{28,20},{1,9},{5... | collective-permute-start | bytes 24584 | tf_op jit(solution)/shard_map/ppermute | solution.py:47
  75.9 3.7 %collective-permute-start.13 = (f32[16,64]{1,0:T(8,128)S(1)}, f32[16,64]{1,0:T(8,128)S(1)}, u32[]{:S(2)}, u32[]{:S(2)}) collective-permute-start(f32[16,64]{1,0:T(8,128)S(1)} %constant_dynamic-slice_fusion), channel_id=1, source_target_pairs={{0,4},{4,0},{8,12},{12,8},{16,20},{20,16},{24,28},{28,24},{1,5},{5... | collective-permute-start | bytes 12296 | tf_op jit(solution)/shard_map/ppermute | solution.py:47
  79.6 1.2 %collective-permute-start.14 = (f32[16,64]{1,0:T(8,128)S(1)}, f32[16,64]{1,0:T(8,128)S(1)}, u32[]{:S(2)}, u32[]{:S(2)}) collective-permute-start(f32[16,64]{1,0:T(8,128)S(1)} %dynamic-slice_add_fusion.2), channel_id=1, source_target_pairs={{0,1},{1,0},{2,3},{3,2},{4,5},{5,4},{6,7},{7,6},{8,9},{9,8},{10,11... | collective-permute-start | bytes 12296 | tf_op jit(solution)/shard_map/ppermute | solution.py:234
  80.7 3.7 %collective-permute-start.15 = (f32[16,64]{1,0:T(8,128)S(1)}, f32[16,64]{1,0:T(8,128)S(1)}, u32[]{:S(2)}, u32[]{:S(2)}) collective-permute-start(f32[16,64]{1,0:T(8,128)S(1)} %add.244), channel_id=1, source_target_pairs={{0,2},{1,3},{2,0},{3,1},{4,6},{5,7},{6,4},{7,5},{8,10},{9,11},{10,... | collective-permute-start | bytes 12296 | tf_op jit(solution)/shard_map/ppermute | solution.py:234
  (3 other events, 15.2 us)

commit v8 on v6

--- a/solution.py
+++ b/solution.py
@@ -164,7 +164,7 @@
             "tca,tab->tcb",
             major_hot,
             tile.reshape(all_texts, major, minor),
-            precision=lax.Precision.HIGHEST,
+            precision=lax.Precision.HIGH,
             preferred_element_type=jnp.float32,
         )
         minor_hot = (wanted % minor)[:, :, None] == jnp.arange(minor, dtype=jnp.int32)[None, None, :]

time: 83 us -> 82 us (0.988)
  matrix products: 18.8 us -> 17.7 us
    dot_general x1, matrix products: 5.86 us -> 4.79 us  [body(): jnp.einsum('tca,tab->tcb', major_hot, tile.reshape(all_texts, major, mino...]
where the time goes in v8:
time: 82 us; the launch traced here: 81.7 us
  waiting for transfers between devices  34.7 us (42%)
  starting transfers between devices  23.4 us (29%)
  matrix products  17.7 us (22%)
  other arithmetic  3.53 us (4%)
  local copies, waits for them, and re-layouts  1.22 us (1%)
  between operations  1.09 us (1%)
    ppermute x7, waiting for transfers between devices, reduce_scatter_xor(): got = lax.ppermute(theirs.astype(wire), axis, xor_pairs(n, k))  16.2 us
    ppermute x7, waiting for transfers between devices, all_gather_xor(): other = lax.ppermute(cur, axis, xor_pairs(n, k))  15.4 us
    ppermute x7, starting transfers between devices, reduce_scatter_xor(): got = lax.ppermute(theirs.astype(wire), axis, xor_pairs(n, k))  11.8 us
    ppermute x7, starting transfers between devices, all_gather_xor(): other = lax.ppermute(cur, axis, xor_pairs(n, k))  9.98 us
    dot_general x1, matrix products, body(): jnp.dot(activated, w_down, preferred_element_type=jnp.float32)  5.11 us
    dot_general x1, matrix products, body(): jnp.einsum('tca,tab->tcb', major_hot, tile.reshape(all_texts, major, mino...  4.79 us
    ppermute x2, waiting for transfers between devices, body(): lax.ppermute(text_scores, 'tensor', xor_pairs(n_tensor, k))  3.15 us
    dot_general x1, matrix products, body(): jnp.einsum('td,jdf->jtf', hidden, w_qkv, preferred_element_type=jnp.float32)  2.34 us
  transfers between devices with their start and end apart: 16, of which 16 were waited for; matrix products, arithmetic and copies ran while one was open for 0% of the time, Pallas kernels for 0%

profile of v8, /device:TPU:0, one launch (start us, length us, event | category | flops | bytes accessed | tf_op | source)
XLA Modules:
  0.0 81.7 jit_solution(13619792444213948587)
XLA Ops:
  0.7 2.3 %fusion.94 = (bf16[3,256,256]{1,2,0:T(8,128)(2,1)S(1)}, f32[3,256,256]{1,2,0:T(8,128)S(1)}) fusion(f32[3,256]{1,0:T(4,128)} %param.19, bf16[3,1024,256]{2,1,0:T(8,128)(2,1)} %param.18, bf16[256,1024]{1,0:T(8,128)(2,1)} %param.16), kind=kOutput, calls=%fused_computation.162 | convolution fusion | flops 403046400 | bytes 3279872 | tf_op jit(solution)/shard_map/td,jdf->jtf/dot_general | solution.py:104
  9.6 2.9 %collective-permute-start.1 = (bf16[64,1024]{1,0:T(8,128)(2,1)S(1)}, bf16[64,1024]{1,0:T(8,128)(2,1)S(1)}, u32[]{:S(2)}, u32[]{:S(2)}) collective-permute-start(bf16[64,1024]{1,0:T(8,128)(2,1)S(1)} %dynamic-slice_convert_fusion.1), channel_id=1, source_target_pairs={{0,2},{1,3},{2,0},{3,1},{4,6},{5,7},{6,4},{7,5},{8,10},{9,11},{10,... | collective-permute-start | bytes 393224 | tf_op jit(solution)/shard_map/ppermute | solution.py:47
  12.5 3.8 %collective-permute-done.1 = bf16[64,1024]{1,0:T(8,128)(2,1)S(1)} collective-permute-done((bf16[64,1024]{1,0:T(8,128)(2,1)S(1)}, bf16[64,1024]{1,0:T(8,128)(2,1)S(1)}, u32[]{:S(2)}, u32[]{:S(2)}) %collective-permute-start.1) | collective-permute-done | bytes 131104 | tf_op jit(solution)/shard_map/ppermute | solution.py:47
  17.7 1.8 %collective-permute-start.2 = (bf16[64,1024]{1,0:T(8,128)(2,1)S(1)}, bf16[64,1024]{1,0:T(8,128)(2,1)S(1)}, u32[]{:S(2)}, u32[]{:S(2)}) collective-permute-start(bf16[64,1024]{1,0:T(8,128)(2,1)S(1)} %add_convert_fusion.1), channel_id=1, source_target_pairs={{0,2},{1,3},{2,0},{3,1},{4,6},{5,7},{6,4},{7,5},{8,10},{9,11},{10,... | collective-permute-start | bytes 393224 | tf_op jit(solution)/shard_map/ppermute | solution.py:58
  19.5 3.3 %collective-permute-done.2 = bf16[64,1024]{1,0:T(8,128)(2,1)S(1)} collective-permute-done((bf16[64,1024]{1,0:T(8,128)(2,1)S(1)}, bf16[64,1024]{1,0:T(8,128)(2,1)S(1)}, u32[]{:S(2)}, u32[]{:S(2)}) %collective-permute-start.2) | collective-permute-done | bytes 131104 | tf_op jit(solution)/shard_map/ppermute | solution.py:58
  24.6 5.1 %convolution_convert_fusion.1 = bf16[256,1024]{1,0:T(8,128)(2,1)S(1)} fusion(bf16[1024,1024]{1,0:T(8,128)(2,1)S(1)} %copy-done, bf16[256,1024]{1,0:T(8,128)(2,1)S(1)} %maximum_select_fusion, bf16[1024,1024]{1,0:T(8,128)(2,1)} %param.24, f32[1024]{0:T(1024)S(1)} %copy-done.10), kind=kOutput, calls=%fused_computation.10 | convolution fusion | flops 1091305472 | bytes 5246976 | tf_op jit(solution)/shard_map/dot_general | solution.py:124
  31.5 1.7 %collective-permute-start.5 = (bf16[64,1024]{1,0:T(8,128)(2,1)S(1)}, bf16[64,1024]{1,0:T(8,128)(2,1)S(1)}, u32[]{:S(2)}, u32[]{:S(2)}) collective-permute-start(bf16[64,1024]{1,0:T(8,128)(2,1)S(1)} %dynamic-slice_convert_fusion), channel_id=1, source_target_pairs={{0,2},{1,3},{2,0},{3,1},{4,6},{5,7},{6,4},{7,5},{8,10},{9,11},{10,... | collective-permute-start | bytes 393224 | tf_op jit(solution)/shard_map/ppermute | solution.py:47
  33.3 3.9 %collective-permute-done.5 = bf16[64,1024]{1,0:T(8,128)(2,1)S(1)} collective-permute-done((bf16[64,1024]{1,0:T(8,128)(2,1)S(1)}, bf16[64,1024]{1,0:T(8,128)(2,1)S(1)}, u32[]{:S(2)}, u32[]{:S(2)}) %collective-permute-start.5) | collective-permute-done | bytes 131104 | tf_op jit(solution)/shard_map/ppermute | solution.py:47
  37.6 1.7 %collective-permute-start.6 = (bf16[64,1024]{1,0:T(8,128)(2,1)S(1)}, bf16[64,1024]{1,0:T(8,128)(2,1)S(1)}, u32[]{:S(2)}, u32[]{:S(2)}) collective-permute-start(bf16[64,1024]{1,0:T(8,128)(2,1)S(1)} %add_convert_fusion), channel_id=1, source_target_pairs={{0,2},{1,3},{2,0},{3,1},{4,6},{5,7},{6,4},{7,5},{8,10},{9,11},{10,... | collective-permute-start | bytes 393224 | tf_op jit(solution)/shard_map/ppermute | solution.py:58
  39.4 3.3 %collective-permute-done.6 = bf16[64,1024]{1,0:T(8,128)(2,1)S(1)} collective-permute-done((bf16[64,1024]{1,0:T(8,128)(2,1)S(1)}, bf16[64,1024]{1,0:T(8,128)(2,1)S(1)}, u32[]{:S(2)}, u32[]{:S(2)}) %collective-permute-start.6) | collective-permute-done | bytes 131104 | tf_op jit(solution)/shard_map/ppermute | solution.py:58
  44.9 1.7 %collective-permute-start.8 = (bf16[16,256]{1,0:T(8,128)(2,1)S(1)}, bf16[16,256]{1,0:T(8,128)(2,1)S(1)}, u32[]{:S(2)}, u32[]{:S(2)}) collective-permute-start(bf16[16,256]{1,0:T(8,128)(2,1)S(1)} %fusion.56), channel_id=1, source_target_pairs={{0,4},{4,0},{8,12},{12,8},{16,20},{20,16},{24,28},{28,24},{1,5},{5... | collective-permute-start | bytes 24584 | tf_op jit(solution)/shard_map/ppermute | solution.py:58
  46.6 2.0 %collective-permute-done.8 = bf16[16,256]{1,0:T(8,128)(2,1)S(1)} collective-permute-done((bf16[16,256]{1,0:T(8,128)(2,1)S(1)}, bf16[16,256]{1,0:T(8,128)(2,1)S(1)}, u32[]{:S(2)}, u32[]{:S(2)}) %collective-permute-start.8) | collective-permute-done | bytes 8224 | tf_op jit(solution)/shard_map/ppermute | solution.py:58
  48.5 1.8 %collective-permute-start.9 = (bf16[32,256]{1,0:T(8,128)(2,1)S(1)}, bf16[32,256]{1,0:T(8,128)(2,1)S(1)}, u32[]{:S(2)}, u32[]{:S(2)}) collective-permute-start(bf16[32,256]{1,0:T(8,128)(2,1)S(1)} %maximum_select_fusion.7), channel_id=1, source_target_pairs={{0,8},{4,12},{8,0},{12,4},{16,24},{20,28},{24,16},{28,20},{1,9},{5... | collective-permute-start | bytes 49160 | tf_op jit(solution)/shard_map/ppermute | solution.py:58
  50.4 1.9 %collective-permute-done.9 = bf16[32,256]{1,0:T(8,128)(2,1)S(1)} collective-permute-done((bf16[32,256]{1,0:T(8,128)(2,1)S(1)}, bf16[32,256]{1,0:T(8,128)(2,1)S(1)}, u32[]{:S(2)}, u32[]{:S(2)}) %collective-permute-start.9) | collective-permute-done | bytes 16416 | tf_op jit(solution)/shard_map/ppermute | solution.py:58
  52.3 2.8 %collective-permute-start.10 = (bf16[64,256]{1,0:T(8,128)(2,1)S(1)}, bf16[64,256]{1,0:T(8,128)(2,1)S(1)}, u32[]{:S(2)}, u32[]{:S(2)}) collective-permute-start(bf16[64,256]{1,0:T(8,128)(2,1)S(1)} %maximum_select_fusion.6), channel_id=1, source_target_pairs={{0,16},{4,20},{8,24},{12,28},{16,0},{20,4},{24,8},{28,12},{1,17},{... | collective-permute-start | bytes 98312 | tf_op jit(solution)/shard_map/ppermute | solution.py:58
  55.2 1.9 %collective-permute-done.10 = bf16[64,256]{1,0:T(8,128)(2,1)S(1)} collective-permute-done((bf16[64,256]{1,0:T(8,128)(2,1)S(1)}, bf16[64,256]{1,0:T(8,128)(2,1)S(1)}, u32[]{:S(2)}, u32[]{:S(2)}) %collective-permute-start.10) | collective-permute-done | bytes 32800 | tf_op jit(solution)/shard_map/ppermute | solution.py:58
  59.1 4.8 %select_reduce_fusion = f32[128,64]{1,0:T(8,128)S(1)} fusion(f32[128,16,128]{2,1,0:T(8,128)S(1)} %bitcast.34, s32[128,64]{1,0:T(8,128)S(1)} %get-tuple-element.9, s32[128,64]{1,0:T(8,128)S(1)} %get-tuple-element.8), kind=kOutput, calls=%fused_computation.1 | convolution fusion | flops 103931904 | bytes 1146880 | tf_op jit(solution)/shard_map/tca,tab->tcb/dot_general | solution.py:163
  63.9 2.9 %collective-permute-start.11 = (f32[64,64]{1,0:T(8,128)S(1)}, f32[64,64]{1,0:T(8,128)S(1)}, u32[]{:S(2)}, u32[]{:S(2)}) collective-permute-start(f32[64,64]{1,0:T(8,128)S(1)} %constant_dynamic-slice_fusion.1), channel_id=1, source_target_pairs={{0,16},{4,20},{8,24},{12,28},{16,0},{20,4},{24,8},{28,12},{1,17},{... | collective-permute-start | bytes 49160 | tf_op jit(solution)/shard_map/ppermute | solution.py:47
  66.8 2.0 %collective-permute-done.11 = f32[64,64]{1,0:T(8,128)S(1)} collective-permute-done((f32[64,64]{1,0:T(8,128)S(1)}, f32[64,64]{1,0:T(8,128)S(1)}, u32[]{:S(2)}, u32[]{:S(2)}) %collective-permute-start.11) | collective-permute-done | bytes 16416 | tf_op jit(solution)/shard_map/ppermute | solution.py:47
  68.8 1.8 %collective-permute-start.12 = (f32[32,64]{1,0:T(8,128)S(1)}, f32[32,64]{1,0:T(8,128)S(1)}, u32[]{:S(2)}, u32[]{:S(2)}) collective-permute-start(f32[32,64]{1,0:T(8,128)S(1)} %constant_dynamic-slice_fusion), channel_id=1, source_target_pairs={{0,8},{4,12},{8,0},{12,4},{16,24},{20,28},{24,16},{28,20},{1,9},{5... | collective-permute-start | bytes 24584 | tf_op jit(solution)/shard_map/ppermute | solution.py:47
  70.6 2.0 %collective-permute-done.12 = f32[32,64]{1,0:T(8,128)S(1)} collective-permute-done((f32[32,64]{1,0:T(8,128)S(1)}, f32[32,64]{1,0:T(8,128)S(1)}, u32[]{:S(2)}, u32[]{:S(2)}) %collective-permute-start.12) | collective-permute-done | bytes 8224 | tf_op jit(solution)/shard_map/ppermute | solution.py:47
  72.6 1.7 %collective-permute-start.13 = (f32[16,64]{1,0:T(8,128)S(1)}, f32[16,64]{1,0:T(8,128)S(1)}, u32[]{:S(2)}, u32[]{:S(2)}) collective-permute-start(f32[16,64]{1,0:T(8,128)S(1)} %constant_dynamic-slice_fusion.3), channel_id=1, source_target_pairs={{0,4},{4,0},{8,12},{12,8},{16,20},{20,16},{24,28},{28,24},{1,5},{5... | collective-permute-start | bytes 12296 | tf_op jit(solution)/shard_map/ppermute | solution.py:47
  74.3 1.9 %collective-permute-done.13 = f32[16,64]{1,0:T(8,128)S(1)} collective-permute-done((f32[16,64]{1,0:T(8,128)S(1)}, f32[16,64]{1,0:T(8,128)S(1)}, u32[]{:S(2)}, u32[]{:S(2)}) %collective-permute-start.13) | collective-permute-done | bytes 4128 | tf_op jit(solution)/shard_map/ppermute | solution.py:47
  79.1 2.0 %collective-permute-done.15 = f32[16,64]{1,0:T(8,128)S(1)} collective-permute-done((f32[16,64]{1,0:T(8,128)S(1)}, f32[16,64]{1,0:T(8,128)S(1)}, u32[]{:S(2)}, u32[]{:S(2)}) %collective-permute-start.15) | collective-permute-done | bytes 4128 | tf_op jit(solution)/shard_map/ppermute | solution.py:185
  (83 shorter events, 19.6 us)
Async XLA Ops:
  0.6 24.0 %copy-start = (bf16[1024,1024]{1,0:T(8,128)(2,1)S(1)}, bf16[1024,1024]{1,0:T(8,128)(2,1)}, u32[]{:S(2)}) copy-start(bf16[1024,1024]{1,0:T(8,128)(2,1)} %param.26) | copy-start | bytes 6291460
  6.3 10.0 %copy-start.3 = (f32[1024]{0:T(1024)S(1)}, f32[1024]{0:T(1024)}, u32[]{:S(2)}) copy-start(f32[1024]{0:T(1024)} %param.21) | copy-start | bytes 12292
  6.3 11.2 %copy-start.4 = (f32[1024]{0:T(1024)S(1)}, f32[1024]{0:T(1024)}, u32[]{:S(2)}) copy-start(f32[1024]{0:T(1024)} %param.23) | copy-start | bytes 12292
  6.3 11.2 %copy-start.5 = (f32[1024]{0:T(1024)S(1)}, f32[1024]{0:T(1024)}, u32[]{:S(2)}) copy-start(f32[1024]{0:T(1024)} %param.22) | copy-start | bytes 12292
  7.8 1.7 %collective-permute-start = (bf16[128,1024]{1,0:T(8,128)(2,1)S(1)}, bf16[128,1024]{1,0:T(8,128)(2,1)S(1)}, u32[]{:S(2)}, u32[]{:S(2)}) collective-permute-start(bf16[128,1024]{1,0:T(8,128)(2,1)S(1)} %constant_dynamic-slice_fusion.4), channel_id=1, source_target_pairs={{0,1},{1,0},{2,3},{3,2},{4,5},{5,4},{6,7},{7,6},{8,9},{9,8},{10,11... | collective-permute-start | bytes 786440 | tf_op jit(solution)/shard_map/ppermute | solution.py:47
  8.3 16.3 %copy-start.10 = (f32[1024]{0:T(1024)S(1)}, f32[1024]{0:T(1024)}, u32[]{:S(2)}) copy-start(f32[1024]{0:T(1024)} %param.25) | copy-start | bytes 12292
  9.6 6.7 %collective-permute-start.1 = (bf16[64,1024]{1,0:T(8,128)(2,1)S(1)}, bf16[64,1024]{1,0:T(8,128)(2,1)S(1)}, u32[]{:S(2)}, u32[]{:S(2)}) collective-permute-start(bf16[64,1024]{1,0:T(8,128)(2,1)S(1)} %dynamic-slice_convert_fusion.1), channel_id=1, source_target_pairs={{0,2},{1,3},{2,0},{3,1},{4,6},{5,7},{6,4},{7,5},{8,10},{9,11},{10,... | collective-permute-start | bytes 393224 | tf_op jit(solution)/shard_map/ppermute | solution.py:47
  17.7 5.1 %collective-permute-start.2 = (bf16[64,1024]{1,0:T(8,128)(2,1)S(1)}, bf16[64,1024]{1,0:T(8,128)(2,1)S(1)}, u32[]{:S(2)}, u32[]{:S(2)}) collective-permute-start(bf16[64,1024]{1,0:T(8,128)(2,1)S(1)} %add_convert_fusion.1), channel_id=1, source_target_pairs={{0,2},{1,3},{2,0},{3,1},{4,6},{5,7},{6,4},{7,5},{8,10},{9,11},{10,... | collective-permute-start | bytes 393224 | tf_op jit(solution)/shard_map/ppermute | solution.py:58
  22.9 1.6 %collective-permute-start.3 = (bf16[128,1024]{1,0:T(8,128)(2,1)S(1)}, bf16[128,1024]{1,0:T(8,128)(2,1)S(1)}, u32[]{:S(2)}, u32[]{:S(2)}) collective-permute-start(bf16[128,1024]{1,0:T(8,128)(2,1)S(1)} %maximum_select_fusion.2), channel_id=1, source_target_pairs={{0,1},{1,0},{2,3},{3,2},{4,5},{5,4},{6,7},{7,6},{8,9},{9,8},{10,11... | collective-permute-start | bytes 786440 | tf_op jit(solution)/shard_map/ppermute | solution.py:58
  24.6 12.5 %copy-start.6 = (f32[1024]{0:T(1024)S(1)}, f32[1024]{0:T(1024)}, u32[]{:S(2)}) copy-start(f32[1024]{0:T(1024)} %param.27) | copy-start | bytes 12292
  29.8 1.6 %collective-permute-start.4 = (bf16[128,1024]{1,0:T(8,128)(2,1)S(1)}, bf16[128,1024]{1,0:T(8,128)(2,1)S(1)}, u32[]{:S(2)}, u32[]{:S(2)}) collective-permute-start(bf16[128,1024]{1,0:T(8,128)(2,1)S(1)} %constant_dynamic-slice_fusion.2), channel_id=1, source_target_pairs={{0,1},{1,0},{2,3},{3,2},{4,5},{5,4},{6,7},{7,6},{8,9},{9,8},{10,11... | collective-permute-start | bytes 786440 | tf_op jit(solution)/shard_map/ppermute | solution.py:47
  31.5 18.8 %copy-start.2 = (s32[128,64]{0,1:T(8,128)S(1)}, s32[128,64]{0,1:T(8,128)}, u32[]{:S(2)}) copy-start(s32[128,64]{0,1:T(8,128)} %param.31) | copy-start | bytes 98308
  31.5 5.6 %collective-permute-start.5 = (bf16[64,1024]{1,0:T(8,128)(2,1)S(1)}, bf16[64,1024]{1,0:T(8,128)(2,1)S(1)}, u32[]{:S(2)}, u32[]{:S(2)}) collective-permute-start(bf16[64,1024]{1,0:T(8,128)(2,1)S(1)} %dynamic-slice_convert_fusion), channel_id=1, source_target_pairs={{0,2},{1,3},{2,0},{3,1},{4,6},{5,7},{6,4},{7,5},{8,10},{9,11},{10,... | collective-permute-start | bytes 393224 | tf_op jit(solution)/shard_map/ppermute | solution.py:47
  37.6 5.0 %collective-permute-start.6 = (bf16[64,1024]{1,0:T(8,128)(2,1)S(1)}, bf16[64,1024]{1,0:T(8,128)(2,1)S(1)}, u32[]{:S(2)}, u32[]{:S(2)}) collective-permute-start(bf16[64,1024]{1,0:T(8,128)(2,1)S(1)} %add_convert_fusion), channel_id=1, source_target_pairs={{0,2},{1,3},{2,0},{3,1},{4,6},{5,7},{6,4},{7,5},{8,10},{9,11},{10,... | collective-permute-start | bytes 393224 | tf_op jit(solution)/shard_map/ppermute | solution.py:58
  42.7 1.6 %collective-permute-start.7 = (bf16[128,1024]{1,0:T(8,128)(2,1)S(1)}, bf16[128,1024]{1,0:T(8,128)(2,1)S(1)}, u32[]{:S(2)}, u32[]{:S(2)}) collective-permute-start(bf16[128,1024]{1,0:T(8,128)(2,1)S(1)} %maximum_select_fusion.3), channel_id=1, source_target_pairs={{0,1},{1,0},{2,3},{3,2},{4,5},{5,4},{6,7},{7,6},{8,9},{9,8},{10,11... | collective-permute-start | bytes 786440 | tf_op jit(solution)/shard_map/ppermute | solution.py:58
  44.5 14.6 %copy-start.1 = (bf16[256,1024]{1,0:T(8,128)(2,1)}, bf16[256,1024]{1,0:T(8,128)(2,1)S(1)}, u32[]{:S(2)}) copy-start(bf16[256,1024]{1,0:T(8,128)(2,1)S(1)} %maximum_select_fusion.1) | copy-start | bytes 1572868
  44.9 3.7 %collective-permute-start.8 = (bf16[16,256]{1,0:T(8,128)(2,1)S(1)}, bf16[16,256]{1,0:T(8,128)(2,1)S(1)}, u32[]{:S(2)}, u32[]{:S(2)}) collective-permute-start(bf16[16,256]{1,0:T(8,128)(2,1)S(1)} %fusion.56), channel_id=1, source_target_pairs={{0,4},{4,0},{8,12},{12,8},{16,20},{20,16},{24,28},{28,24},{1,5},{5... | collective-permute-start | bytes 24584 | tf_op jit(solution)/shard_map/ppermute | solution.py:58
  48.5 3.7 %collective-permute-start.9 = (bf16[32,256]{1,0:T(8,128)(2,1)S(1)}, bf16[32,256]{1,0:T(8,128)(2,1)S(1)}, u32[]{:S(2)}, u32[]{:S(2)}) collective-permute-start(bf16[32,256]{1,0:T(8,128)(2,1)S(1)} %maximum_select_fusion.7), channel_id=1, source_target_pairs={{0,8},{4,12},{8,0},{12,4},{16,24},{20,28},{24,16},{28,20},{1,9},{5... | collective-permute-start | bytes 49160 | tf_op jit(solution)/shard_map/ppermute | solution.py:58
  52.3 4.9 %collective-permute-start.10 = (bf16[64,256]{1,0:T(8,128)(2,1)S(1)}, bf16[64,256]{1,0:T(8,128)(2,1)S(1)}, u32[]{:S(2)}, u32[]{:S(2)}) collective-permute-start(bf16[64,256]{1,0:T(8,128)(2,1)S(1)} %maximum_select_fusion.6), channel_id=1, source_target_pairs={{0,16},{4,20},{8,24},{12,28},{16,0},{20,4},{24,8},{28,12},{1,17},{... | collective-permute-start | bytes 98312 | tf_op jit(solution)/shard_map/ppermute | solution.py:58
  63.9 4.9 %collective-permute-start.11 = (f32[64,64]{1,0:T(8,128)S(1)}, f32[64,64]{1,0:T(8,128)S(1)}, u32[]{:S(2)}, u32[]{:S(2)}) collective-permute-start(f32[64,64]{1,0:T(8,128)S(1)} %constant_dynamic-slice_fusion.1), channel_id=1, source_target_pairs={{0,16},{4,20},{8,24},{12,28},{16,0},{20,4},{24,8},{28,12},{1,17},{... | collective-permute-start | bytes 49160 | tf_op jit(solution)/shard_map/ppermute | solution.py:47
  68.8 3.8 %collective-permute-start.12 = (f32[32,64]{1,0:T(8,128)S(1)}, f32[32,64]{1,0:T(8,128)S(1)}, u32[]{:S(2)}, u32[]{:S(2)}) collective-permute-start(f32[32,64]{1,0:T(8,128)S(1)} %constant_dynamic-slice_fusion), channel_id=1, source_target_pairs={{0,8},{4,12},{8,0},{12,4},{16,24},{20,28},{24,16},{28,20},{1,9},{5... | collective-permute-start | bytes 24584 | tf_op jit(solution)/shard_map/ppermute | solution.py:47
  72.6 3.7 %collective-permute-start.13 = (f32[16,64]{1,0:T(8,128)S(1)}, f32[16,64]{1,0:T(8,128)S(1)}, u32[]{:S(2)}, u32[]{:S(2)}) collective-permute-start(f32[16,64]{1,0:T(8,128)S(1)} %constant_dynamic-slice_fusion.3), channel_id=1, source_target_pairs={{0,4},{4,0},{8,12},{12,8},{16,20},{20,16},{24,28},{28,24},{1,5},{5... | collective-permute-start | bytes 12296 | tf_op jit(solution)/shard_map/ppermute | solution.py:47
  76.3 1.2 %collective-permute-start.14 = (f32[16,64]{1,0:T(8,128)S(1)}, f32[16,64]{1,0:T(8,128)S(1)}, u32[]{:S(2)}, u32[]{:S(2)}) collective-permute-start(f32[16,64]{1,0:T(8,128)S(1)} %dynamic-slice_add_fusion.2), channel_id=1, source_target_pairs={{0,1},{1,0},{2,3},{3,2},{4,5},{5,4},{6,7},{7,6},{8,9},{9,8},{10,11... | collective-permute-start | bytes 12296 | tf_op jit(solution)/shard_map/ppermute | solution.py:185
  77.5 3.7 %collective-permute-start.15 = (f32[16,64]{1,0:T(8,128)S(1)}, f32[16,64]{1,0:T(8,128)S(1)}, u32[]{:S(2)}, u32[]{:S(2)}) collective-permute-start(f32[16,64]{1,0:T(8,128)S(1)} %add.234), channel_id=1, source_target_pairs={{0,2},{1,3},{2,0},{3,1},{4,6},{5,7},{6,4},{7,5},{8,10},{9,11},{10,... | collective-permute-start | bytes 12296 | tf_op jit(solution)/shard_map/ppermute | solution.py:185
  (3 other events, 18.6 us)

commit v9 on v8

--- a/solution.py
+++ b/solution.py
@@ -62,6 +62,8 @@
 
 
 def settle(partial_value, residual, bias, gain, shift, n_tensor):
+    if n_tensor == 4 and partial_value.shape[0] % 2 == 0:
+        return settle_by_chip(partial_value, residual, bias, gain, shift)
     if not is_power_of_two(n_tensor) or partial_value.shape[0] % n_tensor:
         total = lax.psum(partial_value.astype(jnp.bfloat16), "tensor").astype(jnp.float32)
         return layer_norm(total + bias + residual.astype(jnp.float32), gain, shift).astype(
@@ -75,6 +77,25 @@
         jnp.bfloat16
     )
     return all_gather_xor(normed, "tensor", n_tensor, levels[::-1])
+
+
+def settle_by_chip(partial_value, residual, bias, gain, shift):
+    index = lax.axis_index("tensor")
+    low = index % 2
+    half = partial_value.shape[0] // 2
+    rounded = partial_value.astype(jnp.bfloat16)
+    mine = lax.dynamic_slice_in_dim(rounded, low * half, half, 0)
+    theirs = lax.dynamic_slice_in_dim(rounded, (1 - low) * half, half, 0)
+    got = lax.ppermute(theirs, "tensor", xor_pairs(4, 1))
+    chip_sum = (mine.astype(jnp.float32) + got.astype(jnp.float32)).astype(jnp.bfloat16)
+    across = lax.ppermute(chip_sum, "tensor", xor_pairs(4, 2))
+    total = chip_sum.astype(jnp.float32) + across.astype(jnp.float32)
+    own_residual = lax.dynamic_slice_in_dim(residual, low * half, half, 0)
+    normed = layer_norm(total + bias + own_residual.astype(jnp.float32), gain, shift).astype(
+        jnp.bfloat16
+    )
+    other = lax.ppermute(normed, "tensor", xor_pairs(4, 1))
+    return jnp.where(low == 0, jnp.concatenate([normed, other]), jnp.concatenate([other, normed]))
 
 
 def body(

time: 82 us -> 77.9 us (0.950)
  starting transfers between devices: 23.4 us -> 20.4 us
  waiting for transfers between devices: 34.7 us -> 33.3 us
    ppermute x0 -> x6, waiting for transfers between devices: none -> 18.9 us  [the longest x2 13.2 us: settle_by_chip(): across = lax.ppermute(chip_sum, 'tensor', xor_pairs(4, 2))]
    ppermute x7 -> x3, waiting for transfers between devices: 16.2 us -> 5.74 us  [reduce_scatter_xor(): got = lax.ppermute(theirs.astype(wire), axis, xor_pairs(n, k))]
    ppermute x7 -> x3, waiting for transfers between devices: 15.4 us -> 5.57 us  [all_gather_xor(): other = lax.ppermute(cur, axis, xor_pairs(n, k))]
    ppermute x0 -> x6, starting transfers between devices: none -> 5.59 us  [the longest x2 4.74 us: settle_by_chip(): across = lax.ppermute(chip_sum, 'tensor', xor_pairs(4, 2))]
    ppermute x7 -> x3, starting transfers between devices: 11.8 us -> 6.59 us  [reduce_scatter_xor(): got = lax.ppermute(theirs.astype(wire), axis, xor_pairs(n, k))]
    ppermute x7 -> x3, starting transfers between devices: 9.98 us -> 6.5 us  [all_gather_xor(): other = lax.ppermute(cur, axis, xor_pairs(n, k))]
    convert_element_type x2 -> x4, other arithmetic: 0.23 us -> 1.5 us  [the longest x2 1.08 us: settle_by_chip(): (mine.astype(jnp.float32) + got.astype(jnp.float32)).astype(jnp.bfloat16)]
  transfers between devices with their start and end apart: 16 -> 14, of which waited for: 16 -> 14; matrix products, arithmetic and copies ran while one was open for 0% -> 0% of each run, Pallas kernels for 0% -> 0%
where the time goes in v9:
time: 77.9 us; the launch traced here: 77.6 us
  waiting for transfers between devices  33.3 us (43%)
  starting transfers between devices  20.4 us (26%)
  matrix products  17.8 us (23%)
  other arithmetic  3.86 us (5%)
  local copies, waits for them, and re-layouts  1.18 us (2%)
  between operations  1.04 us (1%)
    ppermute x2, waiting for transfers between devices, settle_by_chip(): across = lax.ppermute(chip_sum, 'tensor', xor_pairs(4, 2))  13.2 us
    ppermute x3, starting transfers between devices, reduce_scatter_xor(): got = lax.ppermute(theirs.astype(wire), axis, xor_pairs(n, k))  6.59 us
    ppermute x3, starting transfers between devices, all_gather_xor(): other = lax.ppermute(cur, axis, xor_pairs(n, k))  6.5 us
    ppermute x3, waiting for transfers between devices, reduce_scatter_xor(): got = lax.ppermute(theirs.astype(wire), axis, xor_pairs(n, k))  5.74 us
    ppermute x3, waiting for transfers between devices, all_gather_xor(): other = lax.ppermute(cur, axis, xor_pairs(n, k))  5.57 us
    dot_general x1, matrix products, body(): jnp.dot(activated, w_down, preferred_element_type=jnp.float32)  5.11 us
    dot_general x1, matrix products, body(): jnp.einsum('tca,tab->tcb', major_hot, tile.reshape(all_texts, major, mino...  4.79 us
    ppermute x2, starting transfers between devices, settle_by_chip(): across = lax.ppermute(chip_sum, 'tensor', xor_pairs(4, 2))  4.74 us
  transfers between devices with their start and end apart: 14, of which 14 were waited for; matrix products, arithmetic and copies ran while one was open for 0% of the time, Pallas kernels for 0%

profile of v9, /device:TPU:0, one launch (start us, length us, event | category | flops | bytes accessed | tf_op | source)
XLA Modules:
  0.0 77.6 jit_solution(15936293298222097461)
XLA Ops:
  0.7 2.3 %fusion.94 = (bf16[3,256,256]{1,2,0:T(8,128)(2,1)S(1)}, f32[3,256,256]{1,2,0:T(8,128)S(1)}) fusion(f32[3,256]{1,0:T(4,128)} %param.19, bf16[3,1024,256]{2,1,0:T(8,128)(2,1)} %param.18, bf16[256,1024]{1,0:T(8,128)(2,1)} %param.16), kind=kOutput, calls=%fused_computation.158 | convolution fusion | flops 403046400 | bytes 3279872 | tf_op jit(solution)/shard_map/td,jdf->jtf/dot_general | solution.py:125
  10.7 2.9 %collective-permute-start.1 = (bf16[128,1024]{1,0:T(8,128)(2,1)S(1)}, bf16[128,1024]{1,0:T(8,128)(2,1)S(1)}, u32[]{:S(2)}, u32[]{:S(2)}) collective-permute-start(bf16[128,1024]{1,0:T(8,128)(2,1)S(1)} %add_convert_fusion.3), channel_id=1, source_target_pairs={{0,2},{1,3},{2,0},{3,1},{4,6},{5,7},{6,4},{7,5},{8,10},{9,11},{10,... | collective-permute-start | bytes 786440 | tf_op jit(solution)/shard_map/ppermute | solution.py:91
  13.6 6.6 %collective-permute-done.1 = bf16[128,1024]{1,0:T(8,128)(2,1)S(1)} collective-permute-done((bf16[128,1024]{1,0:T(8,128)(2,1)S(1)}, bf16[128,1024]{1,0:T(8,128)(2,1)S(1)}, u32[]{:S(2)}, u32[]{:S(2)}) %collective-permute-start.1) | collective-permute-done | bytes 262176 | tf_op jit(solution)/shard_map/ppermute | solution.py:91
  21.0 1.5 %collective-permute-done.2 = bf16[128,1024]{1,0:T(8,128)(2,1)S(1)} collective-permute-done((bf16[128,1024]{1,0:T(8,128)(2,1)S(1)}, bf16[128,1024]{1,0:T(8,128)(2,1)S(1)}, u32[]{:S(2)}, u32[]{:S(2)}) %collective-permute-start.2) | collective-permute-done | bytes 262176 | tf_op jit(solution)/shard_map/ppermute | solution.py:97
  22.7 5.1 %convolution_convert_fusion.1 = bf16[256,1024]{1,0:T(8,128)(2,1)S(1)} fusion(bf16[1024,1024]{1,0:T(8,128)(2,1)S(1)} %copy-done, bf16[256,1024]{1,0:T(8,128)(2,1)S(1)} %maximum_select_fusion, bf16[1024,1024]{1,0:T(8,128)(2,1)} %param.24, f32[1024]{0:T(1024)S(1)} %copy-done.11), kind=kOutput, calls=%fused_computation.10 | convolution fusion | flops 1091305472 | bytes 5246976 | tf_op jit(solution)/shard_map/dot_general | solution.py:145
  29.5 1.8 %collective-permute-start.4 = (bf16[128,1024]{1,0:T(8,128)(2,1)S(1)}, bf16[128,1024]{1,0:T(8,128)(2,1)S(1)}, u32[]{:S(2)}, u32[]{:S(2)}) collective-permute-start(bf16[128,1024]{1,0:T(8,128)(2,1)S(1)} %add_convert_fusion.1), channel_id=1, source_target_pairs={{0,2},{1,3},{2,0},{3,1},{4,6},{5,7},{6,4},{7,5},{8,10},{9,11},{10,... | collective-permute-start | bytes 786440 | tf_op jit(solution)/shard_map/ppermute | solution.py:91
  31.3 6.6 %collective-permute-done.4 = bf16[128,1024]{1,0:T(8,128)(2,1)S(1)} collective-permute-done((bf16[128,1024]{1,0:T(8,128)(2,1)S(1)}, bf16[128,1024]{1,0:T(8,128)(2,1)S(1)}, u32[]{:S(2)}, u32[]{:S(2)}) %collective-permute-start.4) | collective-permute-done | bytes 262176 | tf_op jit(solution)/shard_map/ppermute | solution.py:91
  38.7 1.5 %collective-permute-done.5 = bf16[128,1024]{1,0:T(8,128)(2,1)S(1)} collective-permute-done((bf16[128,1024]{1,0:T(8,128)(2,1)S(1)}, bf16[128,1024]{1,0:T(8,128)(2,1)S(1)}, u32[]{:S(2)}, u32[]{:S(2)}) %collective-permute-start.5) | collective-permute-done | bytes 262176 | tf_op jit(solution)/shard_map/ppermute | solution.py:97
  40.8 1.8 %collective-permute-start.6 = (bf16[16,256]{1,0:T(8,128)(2,1)S(1)}, bf16[16,256]{1,0:T(8,128)(2,1)S(1)}, u32[]{:S(2)}, u32[]{:S(2)}) collective-permute-start(bf16[16,256]{1,0:T(8,128)(2,1)S(1)} %fusion.56), channel_id=1, source_target_pairs={{0,4},{4,0},{8,12},{12,8},{16,20},{20,16},{24,28},{28,24},{1,5},{5... | collective-permute-start | bytes 24584 | tf_op jit(solution)/shard_map/ppermute | solution.py:58
  42.6 1.9 %collective-permute-done.6 = bf16[16,256]{1,0:T(8,128)(2,1)S(1)} collective-permute-done((bf16[16,256]{1,0:T(8,128)(2,1)S(1)}, bf16[16,256]{1,0:T(8,128)(2,1)S(1)}, u32[]{:S(2)}, u32[]{:S(2)}) %collective-permute-start.6) | collective-permute-done | bytes 8224 | tf_op jit(solution)/shard_map/ppermute | solution.py:58
  44.4 1.8 %collective-permute-start.7 = (bf16[32,256]{1,0:T(8,128)(2,1)S(1)}, bf16[32,256]{1,0:T(8,128)(2,1)S(1)}, u32[]{:S(2)}, u32[]{:S(2)}) collective-permute-start(bf16[32,256]{1,0:T(8,128)(2,1)S(1)} %maximum_select_fusion.5), channel_id=1, source_target_pairs={{0,8},{4,12},{8,0},{12,4},{16,24},{20,28},{24,16},{28,20},{1,9},{5... | collective-permute-start | bytes 49160 | tf_op jit(solution)/shard_map/ppermute | solution.py:58
  46.4 1.8 %collective-permute-done.7 = bf16[32,256]{1,0:T(8,128)(2,1)S(1)} collective-permute-done((bf16[32,256]{1,0:T(8,128)(2,1)S(1)}, bf16[32,256]{1,0:T(8,128)(2,1)S(1)}, u32[]{:S(2)}, u32[]{:S(2)}) %collective-permute-start.7) | collective-permute-done | bytes 16416 | tf_op jit(solution)/shard_map/ppermute | solution.py:58
  48.2 2.9 %collective-permute-start.8 = (bf16[64,256]{1,0:T(8,128)(2,1)S(1)}, bf16[64,256]{1,0:T(8,128)(2,1)S(1)}, u32[]{:S(2)}, u32[]{:S(2)}) collective-permute-start(bf16[64,256]{1,0:T(8,128)(2,1)S(1)} %maximum_select_fusion.4), channel_id=1, source_target_pairs={{0,16},{4,20},{8,24},{12,28},{16,0},{20,4},{24,8},{28,12},{1,17},{... | collective-permute-start | bytes 98312 | tf_op jit(solution)/shard_map/ppermute | solution.py:58
  51.2 1.9 %collective-permute-done.8 = bf16[64,256]{1,0:T(8,128)(2,1)S(1)} collective-permute-done((bf16[64,256]{1,0:T(8,128)(2,1)S(1)}, bf16[64,256]{1,0:T(8,128)(2,1)S(1)}, u32[]{:S(2)}, u32[]{:S(2)}) %collective-permute-start.8) | collective-permute-done | bytes 32800 | tf_op jit(solution)/shard_map/ppermute | solution.py:58
  53.1 1.7 %convolution_bitcast_fusion = f32[16,8,16,128]{3,1,2,0:T(8,128)S(1)} fusion(bf16[2048,256]{1,0:T(8,128)(2,1)} %param.30, bf16[64,256]{1,0:T(8,128)(2,1)S(1)} %collective-permute-done.8, bf16[64,256]{1,0:T(8,128)(2,1)S(1)} %maximum_select_fusion.4, pred[]{:T(512)S(6)} %eq.90), kind=kOutput, calls=%fused_computation.6 | convolution fusion | flops 134512640 | bytes 2162689 | tf_op jit(solution)/shard_map/dot_general | solution.py:174
  55.0 4.8 %select_reduce_fusion = f32[128,64]{1,0:T(8,128)S(1)} fusion(f32[128,16,128]{2,1,0:T(8,128)S(1)} %bitcast.34, s32[128,64]{1,0:T(8,128)S(1)} %get-tuple-element.5, s32[128,64]{1,0:T(8,128)S(1)} %get-tuple-element.4), kind=kOutput, calls=%fused_computation.1 | convolution fusion | flops 103931904 | bytes 1146880 | tf_op jit(solution)/shard_map/tca,tab->tcb/dot_general | solution.py:184
  59.8 2.9 %collective-permute-start.9 = (f32[64,64]{1,0:T(8,128)S(1)}, f32[64,64]{1,0:T(8,128)S(1)}, u32[]{:S(2)}, u32[]{:S(2)}) collective-permute-start(f32[64,64]{1,0:T(8,128)S(1)} %constant_dynamic-slice_fusion.2), channel_id=1, source_target_pairs={{0,16},{4,20},{8,24},{12,28},{16,0},{20,4},{24,8},{28,12},{1,17},{... | collective-permute-start | bytes 49160 | tf_op jit(solution)/shard_map/ppermute | solution.py:47
  62.7 1.9 %collective-permute-done.9 = f32[64,64]{1,0:T(8,128)S(1)} collective-permute-done((f32[64,64]{1,0:T(8,128)S(1)}, f32[64,64]{1,0:T(8,128)S(1)}, u32[]{:S(2)}, u32[]{:S(2)}) %collective-permute-start.9) | collective-permute-done | bytes 16416 | tf_op jit(solution)/shard_map/ppermute | solution.py:47
  64.7 1.9 %collective-permute-start.10 = (f32[32,64]{1,0:T(8,128)S(1)}, f32[32,64]{1,0:T(8,128)S(1)}, u32[]{:S(2)}, u32[]{:S(2)}) collective-permute-start(f32[32,64]{1,0:T(8,128)S(1)} %constant_dynamic-slice_fusion.1), channel_id=1, source_target_pairs={{0,8},{4,12},{8,0},{12,4},{16,24},{20,28},{24,16},{28,20},{1,9},{5... | collective-permute-start | bytes 24584 | tf_op jit(solution)/shard_map/ppermute | solution.py:47
  66.6 1.9 %collective-permute-done.10 = f32[32,64]{1,0:T(8,128)S(1)} collective-permute-done((f32[32,64]{1,0:T(8,128)S(1)}, f32[32,64]{1,0:T(8,128)S(1)}, u32[]{:S(2)}, u32[]{:S(2)}) %collective-permute-start.10) | collective-permute-done | bytes 8224 | tf_op jit(solution)/shard_map/ppermute | solution.py:47
  68.5 1.8 %collective-permute-start.11 = (f32[16,64]{1,0:T(8,128)S(1)}, f32[16,64]{1,0:T(8,128)S(1)}, u32[]{:S(2)}, u32[]{:S(2)}) collective-permute-start(f32[16,64]{1,0:T(8,128)S(1)} %constant_dynamic-slice_fusion), channel_id=1, source_target_pairs={{0,4},{4,0},{8,12},{12,8},{16,20},{20,16},{24,28},{28,24},{1,5},{5... | collective-permute-start | bytes 12296 | tf_op jit(solution)/shard_map/ppermute | solution.py:47
  70.3 1.9 %collective-permute-done.11 = f32[16,64]{1,0:T(8,128)S(1)} collective-permute-done((f32[16,64]{1,0:T(8,128)S(1)}, f32[16,64]{1,0:T(8,128)S(1)}, u32[]{:S(2)}, u32[]{:S(2)}) %collective-permute-start.11) | collective-permute-done | bytes 4128 | tf_op jit(solution)/shard_map/ppermute | solution.py:47
  73.4 1.7 %collective-permute-start.13 = (f32[16,64]{1,0:T(8,128)S(1)}, f32[16,64]{1,0:T(8,128)S(1)}, u32[]{:S(2)}, u32[]{:S(2)}) collective-permute-start(f32[16,64]{1,0:T(8,128)S(1)} %add.205), channel_id=1, source_target_pairs={{0,2},{1,3},{2,0},{3,1},{4,6},{5,7},{6,4},{7,5},{8,10},{9,11},{10,... | collective-permute-start | bytes 12296 | tf_op jit(solution)/shard_map/ppermute | solution.py:206
  75.1 1.9 %collective-permute-done.13 = f32[16,64]{1,0:T(8,128)S(1)} collective-permute-done((f32[16,64]{1,0:T(8,128)S(1)}, f32[16,64]{1,0:T(8,128)S(1)}, u32[]{:S(2)}, u32[]{:S(2)}) %collective-permute-start.13) | collective-permute-done | bytes 4128 | tf_op jit(solution)/shard_map/ppermute | solution.py:206
  (77 shorter events, 13.6 us)
Async XLA Ops:
  0.6 22.0 %copy-start = (bf16[1024,1024]{1,0:T(8,128)(2,1)S(1)}, bf16[1024,1024]{1,0:T(8,128)(2,1)}, u32[]{:S(2)}) copy-start(bf16[1024,1024]{1,0:T(8,128)(2,1)} %param.26) | copy-start | bytes 6291460
  6.3 13.9 %copy-start.1 = (bf16[256,1024]{1,0:T(8,128)(2,1)S(1)}, bf16[256,1024]{1,0:T(8,128)(2,1)}, u32[]{:S(2)}) copy-start(bf16[256,1024]{1,0:T(8,128)(2,1)} %param.16) | copy-start | bytes 1572868
  6.3 13.9 %copy-start.3 = (f32[1024]{0:T(1024)S(1)}, f32[1024]{0:T(1024)}, u32[]{:S(2)}) copy-start(f32[1024]{0:T(1024)} %param.21) | copy-start | bytes 12292
  6.3 14.3 %copy-start.6 = (f32[1024]{0:T(1024)S(1)}, f32[1024]{0:T(1024)}, u32[]{:S(2)}) copy-start(f32[1024]{0:T(1024)} %param.23) | copy-start | bytes 12292
  6.4 14.3 %copy-start.7 = (f32[1024]{0:T(1024)S(1)}, f32[1024]{0:T(1024)}, u32[]{:S(2)}) copy-start(f32[1024]{0:T(1024)} %param.22) | copy-start | bytes 12292
  7.8 1.8 %collective-permute-start = (bf16[128,1024]{1,0:T(8,128)(2,1)S(1)}, bf16[128,1024]{1,0:T(8,128)(2,1)}, u32[]{:S(2)}, u32[]{:S(2)}) collective-permute-start(bf16[128,1024]{1,0:T(8,128)(2,1)S(1)} %constant_dynamic-slice_fusion.4), channel_id=1, source_target_pairs={{0,1},{1,0},{2,3},{3,2},{4,5},{5,4},{6,7},{7,6},{8,9},{9,8},{10,11... | collective-permute-start | bytes 786440 | tf_op jit(solution)/shard_map/ppermute | solution.py:89
  8.3 14.3 %copy-start.11 = (f32[1024]{0:T(1024)S(1)}, f32[1024]{0:T(1024)}, u32[]{:S(2)}) copy-start(f32[1024]{0:T(1024)} %param.25) | copy-start | bytes 12292
  10.7 9.5 %collective-permute-start.1 = (bf16[128,1024]{1,0:T(8,128)(2,1)S(1)}, bf16[128,1024]{1,0:T(8,128)(2,1)S(1)}, u32[]{:S(2)}, u32[]{:S(2)}) collective-permute-start(bf16[128,1024]{1,0:T(8,128)(2,1)S(1)} %add_convert_fusion.3), channel_id=1, source_target_pairs={{0,2},{1,3},{2,0},{3,1},{4,6},{5,7},{6,4},{7,5},{8,10},{9,11},{10,... | collective-permute-start | bytes 786440 | tf_op jit(solution)/shard_map/ppermute | solution.py:91
  20.9 1.6 %collective-permute-start.2 = (bf16[128,1024]{1,0:T(8,128)(2,1)S(1)}, bf16[128,1024]{1,0:T(8,128)(2,1)S(1)}, u32[]{:S(2)}, u32[]{:S(2)}) collective-permute-start(bf16[128,1024]{1,0:T(8,128)(2,1)S(1)} %add_convert_fusion.2), channel_id=1, source_target_pairs={{0,1},{1,0},{2,3},{3,2},{4,5},{5,4},{6,7},{7,6},{8,9},{9,8},{10,11... | collective-permute-start | bytes 786440 | tf_op jit(solution)/shard_map/ppermute | solution.py:97
  22.6 15.3 %copy-start.4 = (f32[1024]{0:T(1024)S(1)}, f32[1024]{0:T(1024)}, u32[]{:S(2)}) copy-start(f32[1024]{0:T(1024)} %param.27) | copy-start | bytes 12292
  27.8 10.6 %copy-start.8 = (f32[1024]{0:T(1024)S(1)}, f32[1024]{0:T(1024)}, u32[]{:S(2)}) copy-start(f32[1024]{0:T(1024)} %param.29) | copy-start | bytes 12292
  27.8 1.6 %collective-permute-start.3 = (bf16[128,1024]{1,0:T(8,128)(2,1)S(1)}, bf16[128,1024]{1,0:T(8,128)(2,1)S(1)}, u32[]{:S(2)}, u32[]{:S(2)}) collective-permute-start(bf16[128,1024]{1,0:T(8,128)(2,1)S(1)} %constant_dynamic-slice_fusion.3), channel_id=1, source_target_pairs={{0,1},{1,0},{2,3},{3,2},{4,5},{5,4},{6,7},{7,6},{8,9},{9,8},{10,11... | collective-permute-start | bytes 786440 | tf_op jit(solution)/shard_map/ppermute | solution.py:89
  29.5 16.8 %copy-start.5 = (s32[128,64]{0,1:T(8,128)S(1)}, s32[128,64]{0,1:T(8,128)}, u32[]{:S(2)}) copy-start(s32[128,64]{0,1:T(8,128)} %param.31) | copy-start | bytes 98308
  29.5 8.4 %collective-permute-start.4 = (bf16[128,1024]{1,0:T(8,128)(2,1)S(1)}, bf16[128,1024]{1,0:T(8,128)(2,1)S(1)}, u32[]{:S(2)}, u32[]{:S(2)}) collective-permute-start(bf16[128,1024]{1,0:T(8,128)(2,1)S(1)} %add_convert_fusion.1), channel_id=1, source_target_pairs={{0,2},{1,3},{2,0},{3,1},{4,6},{5,7},{6,4},{7,5},{8,10},{9,11},{10,... | collective-permute-start | bytes 786440 | tf_op jit(solution)/shard_map/ppermute | solution.py:91
  38.6 1.6 %collective-permute-start.5 = (bf16[128,1024]{1,0:T(8,128)(2,1)S(1)}, bf16[128,1024]{1,0:T(8,128)(2,1)S(1)}, u32[]{:S(2)}, u32[]{:S(2)}) collective-permute-start(bf16[128,1024]{1,0:T(8,128)(2,1)S(1)} %add_convert_fusion), channel_id=1, source_target_pairs={{0,1},{1,0},{2,3},{3,2},{4,5},{5,4},{6,7},{7,6},{8,9},{9,8},{10,11... | collective-permute-start | bytes 786440 | tf_op jit(solution)/shard_map/ppermute | solution.py:97
  40.4 14.6 %copy-start.2 = (bf16[256,1024]{1,0:T(8,128)(2,1)}, bf16[256,1024]{1,0:T(8,128)(2,1)S(1)}, u32[]{:S(2)}) copy-start(bf16[256,1024]{1,0:T(8,128)(2,1)S(1)} %maximum_select_fusion.1) | copy-start | bytes 1572868
  40.8 3.7 %collective-permute-start.6 = (bf16[16,256]{1,0:T(8,128)(2,1)S(1)}, bf16[16,256]{1,0:T(8,128)(2,1)S(1)}, u32[]{:S(2)}, u32[]{:S(2)}) collective-permute-start(bf16[16,256]{1,0:T(8,128)(2,1)S(1)} %fusion.56), channel_id=1, source_target_pairs={{0,4},{4,0},{8,12},{12,8},{16,20},{20,16},{24,28},{28,24},{1,5},{5... | collective-permute-start | bytes 24584 | tf_op jit(solution)/shard_map/ppermute | solution.py:58
  44.4 3.7 %collective-permute-start.7 = (bf16[32,256]{1,0:T(8,128)(2,1)S(1)}, bf16[32,256]{1,0:T(8,128)(2,1)S(1)}, u32[]{:S(2)}, u32[]{:S(2)}) collective-permute-start(bf16[32,256]{1,0:T(8,128)(2,1)S(1)} %maximum_select_fusion.5), channel_id=1, source_target_pairs={{0,8},{4,12},{8,0},{12,4},{16,24},{20,28},{24,16},{28,20},{1,9},{5... | collective-permute-start | bytes 49160 | tf_op jit(solution)/shard_map/ppermute | solution.py:58
  48.2 4.9 %collective-permute-start.8 = (bf16[64,256]{1,0:T(8,128)(2,1)S(1)}, bf16[64,256]{1,0:T(8,128)(2,1)S(1)}, u32[]{:S(2)}, u32[]{:S(2)}) collective-permute-start(bf16[64,256]{1,0:T(8,128)(2,1)S(1)} %maximum_select_fusion.4), channel_id=1, source_target_pairs={{0,16},{4,20},{8,24},{12,28},{16,0},{20,4},{24,8},{28,12},{1,17},{... | collective-permute-start | bytes 98312 | tf_op jit(solution)/shard_map/ppermute | solution.py:58
  59.8 4.9 %collective-permute-start.9 = (f32[64,64]{1,0:T(8,128)S(1)}, f32[64,64]{1,0:T(8,128)S(1)}, u32[]{:S(2)}, u32[]{:S(2)}) collective-permute-start(f32[64,64]{1,0:T(8,128)S(1)} %constant_dynamic-slice_fusion.2), channel_id=1, source_target_pairs={{0,16},{4,20},{8,24},{12,28},{16,0},{20,4},{24,8},{28,12},{1,17},{... | collective-permute-start | bytes 49160 | tf_op jit(solution)/shard_map/ppermute | solution.py:47
  64.7 3.8 %collective-permute-start.10 = (f32[32,64]{1,0:T(8,128)S(1)}, f32[32,64]{1,0:T(8,128)S(1)}, u32[]{:S(2)}, u32[]{:S(2)}) collective-permute-start(f32[32,64]{1,0:T(8,128)S(1)} %constant_dynamic-slice_fusion.1), channel_id=1, source_target_pairs={{0,8},{4,12},{8,0},{12,4},{16,24},{20,28},{24,16},{28,20},{1,9},{5... | collective-permute-start | bytes 24584 | tf_op jit(solution)/shard_map/ppermute | solution.py:47
  68.5 3.7 %collective-permute-start.11 = (f32[16,64]{1,0:T(8,128)S(1)}, f32[16,64]{1,0:T(8,128)S(1)}, u32[]{:S(2)}, u32[]{:S(2)}) collective-permute-start(f32[16,64]{1,0:T(8,128)S(1)} %constant_dynamic-slice_fusion), channel_id=1, source_target_pairs={{0,4},{4,0},{8,12},{12,8},{16,20},{20,16},{24,28},{28,24},{1,5},{5... | collective-permute-start | bytes 12296 | tf_op jit(solution)/shard_map/ppermute | solution.py:47
  72.2 1.2 %collective-permute-start.12 = (f32[16,64]{1,0:T(8,128)S(1)}, f32[16,64]{1,0:T(8,128)S(1)}, u32[]{:S(2)}, u32[]{:S(2)}) collective-permute-start(f32[16,64]{1,0:T(8,128)S(1)} %dynamic-slice_add_fusion.2), channel_id=1, source_target_pairs={{0,1},{1,0},{2,3},{3,2},{4,5},{5,4},{6,7},{7,6},{8,9},{9,8},{10,11... | collective-permute-start | bytes 12296 | tf_op jit(solution)/shard_map/ppermute | solution.py:206
  73.4 3.7 %collective-permute-start.13 = (f32[16,64]{1,0:T(8,128)S(1)}, f32[16,64]{1,0:T(8,128)S(1)}, u32[]{:S(2)}, u32[]{:S(2)}) collective-permute-start(f32[16,64]{1,0:T(8,128)S(1)} %add.205), channel_id=1, source_target_pairs={{0,2},{1,3},{2,0},{3,1},{4,6},{5,7},{6,4},{7,5},{8,10},{9,11},{10,... | collective-permute-start | bytes 12296 | tf_op jit(solution)/shard_map/ppermute | solution.py:206
  (2 other events, 13.7 us)

commit v10 on v9

--- a/solution.py
+++ b/solution.py
@@ -88,7 +88,13 @@
     theirs = lax.dynamic_slice_in_dim(rounded, (1 - low) * half, half, 0)
     got = lax.ppermute(theirs, "tensor", xor_pairs(4, 1))
     chip_sum = (mine.astype(jnp.float32) + got.astype(jnp.float32)).astype(jnp.bfloat16)
-    across = lax.ppermute(chip_sum, "tensor", xor_pairs(4, 2))
+    split = half // 2
+    across = jnp.concatenate(
+        [
+            lax.ppermute(chip_sum[:split], "tensor", xor_pairs(4, 2)),
+            lax.ppermute(chip_sum[split:], "tensor", xor_pairs(4, 2)),
+        ]
+    )
     total = chip_sum.astype(jnp.float32) + across.astype(jnp.float32)
     own_residual = lax.dynamic_slice_in_dim(residual, low * half, half, 0)
     normed = layer_norm(total + bias + own_residual.astype(jnp.float32), gain, shift).astype(

time: 77.9 us -> 77.9 us (level)
    ppermute x2 -> x4, waiting for transfers between devices: 13.2 us -> 12.9 us  [the longest x2 8.52 us: settle_by_chip(): lax.ppermute(chip_sum[:split], 'tensor', xor_pairs(4, 2))]
    ppermute x2 -> x4, starting transfers between devices: 4.74 us -> 5.09 us  [the longest x2 4.74 us: settle_by_chip(): lax.ppermute(chip_sum[:split], 'tensor', xor_pairs(4, 2))]
  transfers between devices with their start and end apart: 14 -> 16, of which waited for: 14 -> 16; matrix products, arithmetic and copies ran while one was open for 0% -> 0% of each run, Pallas kernels for 0% -> 0%
where the time goes in v10:
time: 77.9 us; the launch traced here: 77.7 us
  waiting for transfers between devices  33 us (42%)
  starting transfers between devices  20.7 us (27%)
  matrix products  17.8 us (23%)
  other arithmetic  3.86 us (5%)
  local copies, waits for them, and re-layouts  1.22 us (2%)
  between operations  1.06 us (1%)
    ppermute x2, waiting for transfers between devices, settle_by_chip(): lax.ppermute(chip_sum[:split], 'tensor', xor_pairs(4, 2))  8.52 us
    ppermute x3, starting transfers between devices, reduce_scatter_xor(): got = lax.ppermute(theirs.astype(wire), axis, xor_pairs(n, k))  6.56 us
    ppermute x3, starting transfers between devices, all_gather_xor(): other = lax.ppermute(cur, axis, xor_pairs(n, k))  6.48 us
    ppermute x3, waiting for transfers between devices, reduce_scatter_xor(): got = lax.ppermute(theirs.astype(wire), axis, xor_pairs(n, k))  5.78 us
    ppermute x3, waiting for transfers between devices, all_gather_xor(): other = lax.ppermute(cur, axis, xor_pairs(n, k))  5.59 us
    dot_general x1, matrix products, body(): jnp.dot(activated, w_down, preferred_element_type=jnp.float32)  5.11 us
    dot_general x1, matrix products, body(): jnp.einsum('tca,tab->tcb', major_hot, tile.reshape(all_texts, major, mino...  4.79 us
    ppermute x2, starting transfers between devices, settle_by_chip(): lax.ppermute(chip_sum[:split], 'tensor', xor_pairs(4, 2))  4.74 us
  transfers between devices with their start and end apart: 16, of which 16 were waited for; matrix products, arithmetic and copies ran while one was open for 0% of the time, Pallas kernels for 0%

profile of v10, /device:TPU:0, one launch (start us, length us, event | category | flops | bytes accessed | tf_op | source)
XLA Modules:
  0.0 77.7 jit_solution(10096845998327977018)
XLA Ops:
  0.7 2.3 %fusion.96 = (bf16[3,256,256]{1,2,0:T(8,128)(2,1)S(1)}, f32[3,256,256]{1,2,0:T(8,128)S(1)}) fusion(f32[3,256]{1,0:T(4,128)} %param.19, bf16[3,1024,256]{2,1,0:T(8,128)(2,1)} %param.18, bf16[256,1024]{1,0:T(8,128)(2,1)} %param.16), kind=kOutput, calls=%fused_computation.160 | convolution fusion | flops 403046400 | bytes 3279872 | tf_op jit(solution)/shard_map/td,jdf->jtf/dot_general | solution.py:131
  10.7 2.9 %collective-permute-start.1 = (bf16[64,1024]{1,0:T(8,128)(2,1)S(1)}, bf16[64,1024]{1,0:T(8,128)(2,1)S(1)}, u32[]{:S(2)}, u32[]{:S(2)}) collective-permute-start(bf16[64,1024]{1,0:T(8,128)(2,1)S(1)} %get-tuple-element.6), channel_id=1, source_target_pairs={{0,2},{1,3},{2,0},{3,1},{4,6},{5,7},{6,4},{7,5},{8,10},{9,11},{10,... | collective-permute-start | bytes 393224 | tf_op jit(solution)/shard_map/ppermute | solution.py:94
  13.7 4.2 %collective-permute-done.1 = bf16[64,1024]{1,0:T(8,128)(2,1)S(1)} collective-permute-done((bf16[64,1024]{1,0:T(8,128)(2,1)S(1)}, bf16[64,1024]{1,0:T(8,128)(2,1)S(1)}, u32[]{:S(2)}, u32[]{:S(2)}) %collective-permute-start.1) | collective-permute-done | bytes 131104 | tf_op jit(solution)/shard_map/ppermute | solution.py:94
  17.9 2.3 %collective-permute-done.2 = bf16[64,1024]{1,0:T(8,128)(2,1)S(1)} collective-permute-done((bf16[64,1024]{1,0:T(8,128)(2,1)S(1)}, bf16[64,1024]{1,0:T(8,128)(2,1)S(1)}, u32[]{:S(2)}, u32[]{:S(2)}) %collective-permute-start.2) | collective-permute-done | bytes 131104 | tf_op jit(solution)/shard_map/ppermute | solution.py:95
  22.7 5.1 %convolution_convert_fusion.1 = bf16[256,1024]{1,0:T(8,128)(2,1)S(1)} fusion(bf16[1024,1024]{1,0:T(8,128)(2,1)S(1)} %copy-done, bf16[256,1024]{1,0:T(8,128)(2,1)S(1)} %maximum_select_fusion, bf16[1024,1024]{1,0:T(8,128)(2,1)} %param.24, f32[1024]{0:T(1024)S(1)} %copy-done.11), kind=kOutput, calls=%fused_computation.10 | convolution fusion | flops 1091305472 | bytes 5246976 | tf_op jit(solution)/shard_map/dot_general | solution.py:151
  29.6 1.8 %collective-permute-start.5 = (bf16[64,1024]{1,0:T(8,128)(2,1)S(1)}, bf16[64,1024]{1,0:T(8,128)(2,1)S(1)}, u32[]{:S(2)}, u32[]{:S(2)}) collective-permute-start(bf16[64,1024]{1,0:T(8,128)(2,1)S(1)} %get-tuple-element.4), channel_id=1, source_target_pairs={{0,2},{1,3},{2,0},{3,1},{4,6},{5,7},{6,4},{7,5},{8,10},{9,11},{10,... | collective-permute-start | bytes 393224 | tf_op jit(solution)/shard_map/ppermute | solution.py:94
  31.7 4.3 %collective-permute-done.5 = bf16[64,1024]{1,0:T(8,128)(2,1)S(1)} collective-permute-done((bf16[64,1024]{1,0:T(8,128)(2,1)S(1)}, bf16[64,1024]{1,0:T(8,128)(2,1)S(1)}, u32[]{:S(2)}, u32[]{:S(2)}) %collective-permute-start.5) | collective-permute-done | bytes 131104 | tf_op jit(solution)/shard_map/ppermute | solution.py:94
  36.0 2.0 %collective-permute-done.6 = bf16[64,1024]{1,0:T(8,128)(2,1)S(1)} collective-permute-done((bf16[64,1024]{1,0:T(8,128)(2,1)S(1)}, bf16[64,1024]{1,0:T(8,128)(2,1)S(1)}, u32[]{:S(2)}, u32[]{:S(2)}) %collective-permute-start.6) | collective-permute-done | bytes 131104 | tf_op jit(solution)/shard_map/ppermute | solution.py:95
  40.8 1.8 %collective-permute-start.8 = (bf16[16,256]{1,0:T(8,128)(2,1)S(1)}, bf16[16,256]{1,0:T(8,128)(2,1)S(1)}, u32[]{:S(2)}, u32[]{:S(2)}) collective-permute-start(bf16[16,256]{1,0:T(8,128)(2,1)S(1)} %fusion.56), channel_id=1, source_target_pairs={{0,4},{4,0},{8,12},{12,8},{16,20},{20,16},{24,28},{28,24},{1,5},{5... | collective-permute-start | bytes 24584 | tf_op jit(solution)/shard_map/ppermute | solution.py:58
  42.6 1.9 %collective-permute-done.8 = bf16[16,256]{1,0:T(8,128)(2,1)S(1)} collective-permute-done((bf16[16,256]{1,0:T(8,128)(2,1)S(1)}, bf16[16,256]{1,0:T(8,128)(2,1)S(1)}, u32[]{:S(2)}, u32[]{:S(2)}) %collective-permute-start.8) | collective-permute-done | bytes 8224 | tf_op jit(solution)/shard_map/ppermute | solution.py:58
  44.5 1.8 %collective-permute-start.9 = (bf16[32,256]{1,0:T(8,128)(2,1)S(1)}, bf16[32,256]{1,0:T(8,128)(2,1)S(1)}, u32[]{:S(2)}, u32[]{:S(2)}) collective-permute-start(bf16[32,256]{1,0:T(8,128)(2,1)S(1)} %maximum_select_fusion.5), channel_id=1, source_target_pairs={{0,8},{4,12},{8,0},{12,4},{16,24},{20,28},{24,16},{28,20},{1,9},{5... | collective-permute-start | bytes 49160 | tf_op jit(solution)/shard_map/ppermute | solution.py:58
  46.4 1.8 %collective-permute-done.9 = bf16[32,256]{1,0:T(8,128)(2,1)S(1)} collective-permute-done((bf16[32,256]{1,0:T(8,128)(2,1)S(1)}, bf16[32,256]{1,0:T(8,128)(2,1)S(1)}, u32[]{:S(2)}, u32[]{:S(2)}) %collective-permute-start.9) | collective-permute-done | bytes 16416 | tf_op jit(solution)/shard_map/ppermute | solution.py:58
  48.2 2.9 %collective-permute-start.10 = (bf16[64,256]{1,0:T(8,128)(2,1)S(1)}, bf16[64,256]{1,0:T(8,128)(2,1)S(1)}, u32[]{:S(2)}, u32[]{:S(2)}) collective-permute-start(bf16[64,256]{1,0:T(8,128)(2,1)S(1)} %maximum_select_fusion.4), channel_id=1, source_target_pairs={{0,16},{4,20},{8,24},{12,28},{16,0},{20,4},{24,8},{28,12},{1,17},{... | collective-permute-start | bytes 98312 | tf_op jit(solution)/shard_map/ppermute | solution.py:58
  51.3 1.9 %collective-permute-done.10 = bf16[64,256]{1,0:T(8,128)(2,1)S(1)} collective-permute-done((bf16[64,256]{1,0:T(8,128)(2,1)S(1)}, bf16[64,256]{1,0:T(8,128)(2,1)S(1)}, u32[]{:S(2)}, u32[]{:S(2)}) %collective-permute-start.10) | collective-permute-done | bytes 32800 | tf_op jit(solution)/shard_map/ppermute | solution.py:58
  53.1 1.7 %convolution_bitcast_fusion = f32[16,8,16,128]{3,1,2,0:T(8,128)S(1)} fusion(bf16[2048,256]{1,0:T(8,128)(2,1)} %param.30, bf16[64,256]{1,0:T(8,128)(2,1)S(1)} %collective-permute-done.10, bf16[64,256]{1,0:T(8,128)(2,1)S(1)} %maximum_select_fusion.4, pred[]{:T(512)S(6)} %eq.90), kind=kOutput, calls=%fused_computation.6 | convolution fusion | flops 134512640 | bytes 2162689 | tf_op jit(solution)/shard_map/dot_general | solution.py:180
  55.0 4.8 %select_reduce_fusion = f32[128,64]{1,0:T(8,128)S(1)} fusion(f32[128,16,128]{2,1,0:T(8,128)S(1)} %bitcast.34, s32[128,64]{1,0:T(8,128)S(1)} %get-tuple-element.9, s32[128,64]{1,0:T(8,128)S(1)} %get-tuple-element.8), kind=kOutput, calls=%fused_computation.1 | convolution fusion | flops 103931904 | bytes 1146880 | tf_op jit(solution)/shard_map/tca,tab->tcb/dot_general | solution.py:190
  59.9 2.9 %collective-permute-start.11 = (f32[64,64]{1,0:T(8,128)S(1)}, f32[64,64]{1,0:T(8,128)S(1)}, u32[]{:S(2)}, u32[]{:S(2)}) collective-permute-start(f32[64,64]{1,0:T(8,128)S(1)} %constant_dynamic-slice_fusion.2), channel_id=1, source_target_pairs={{0,16},{4,20},{8,24},{12,28},{16,0},{20,4},{24,8},{28,12},{1,17},{... | collective-permute-start | bytes 49160 | tf_op jit(solution)/shard_map/ppermute | solution.py:47
  62.8 2.0 %collective-permute-done.11 = f32[64,64]{1,0:T(8,128)S(1)} collective-permute-done((f32[64,64]{1,0:T(8,128)S(1)}, f32[64,64]{1,0:T(8,128)S(1)}, u32[]{:S(2)}, u32[]{:S(2)}) %collective-permute-start.11) | collective-permute-done | bytes 16416 | tf_op jit(solution)/shard_map/ppermute | solution.py:47
  64.8 1.9 %collective-permute-start.12 = (f32[32,64]{1,0:T(8,128)S(1)}, f32[32,64]{1,0:T(8,128)S(1)}, u32[]{:S(2)}, u32[]{:S(2)}) collective-permute-start(f32[32,64]{1,0:T(8,128)S(1)} %constant_dynamic-slice_fusion.1), channel_id=1, source_target_pairs={{0,8},{4,12},{8,0},{12,4},{16,24},{20,28},{24,16},{28,20},{1,9},{5... | collective-permute-start | bytes 24584 | tf_op jit(solution)/shard_map/ppermute | solution.py:47
  66.6 1.9 %collective-permute-done.12 = f32[32,64]{1,0:T(8,128)S(1)} collective-permute-done((f32[32,64]{1,0:T(8,128)S(1)}, f32[32,64]{1,0:T(8,128)S(1)}, u32[]{:S(2)}, u32[]{:S(2)}) %collective-permute-start.12) | collective-permute-done | bytes 8224 | tf_op jit(solution)/shard_map/ppermute | solution.py:47
  68.6 1.8 %collective-permute-start.13 = (f32[16,64]{1,0:T(8,128)S(1)}, f32[16,64]{1,0:T(8,128)S(1)}, u32[]{:S(2)}, u32[]{:S(2)}) collective-permute-start(f32[16,64]{1,0:T(8,128)S(1)} %constant_dynamic-slice_fusion), channel_id=1, source_target_pairs={{0,4},{4,0},{8,12},{12,8},{16,20},{20,16},{24,28},{28,24},{1,5},{5... | collective-permute-start | bytes 12296 | tf_op jit(solution)/shard_map/ppermute | solution.py:47
  70.4 1.9 %collective-permute-done.13 = f32[16,64]{1,0:T(8,128)S(1)} collective-permute-done((f32[16,64]{1,0:T(8,128)S(1)}, f32[16,64]{1,0:T(8,128)S(1)}, u32[]{:S(2)}, u32[]{:S(2)}) %collective-permute-start.13) | collective-permute-done | bytes 4128 | tf_op jit(solution)/shard_map/ppermute | solution.py:47
  73.4 1.7 %collective-permute-start.15 = (f32[16,64]{1,0:T(8,128)S(1)}, f32[16,64]{1,0:T(8,128)S(1)}, u32[]{:S(2)}, u32[]{:S(2)}) collective-permute-start(f32[16,64]{1,0:T(8,128)S(1)} %add.205), channel_id=1, source_target_pairs={{0,2},{1,3},{2,0},{3,1},{4,6},{5,7},{6,4},{7,5},{8,10},{9,11},{10,... | collective-permute-start | bytes 12296 | tf_op jit(solution)/shard_map/ppermute | solution.py:212
  75.2 1.9 %collective-permute-done.15 = f32[16,64]{1,0:T(8,128)S(1)} collective-permute-done((f32[16,64]{1,0:T(8,128)S(1)}, f32[16,64]{1,0:T(8,128)S(1)}, u32[]{:S(2)}, u32[]{:S(2)}) %collective-permute-start.15) | collective-permute-done | bytes 4128 | tf_op jit(solution)/shard_map/ppermute | solution.py:212
  (83 shorter events, 17.0 us)
Async XLA Ops:
  0.6 22.0 %copy-start = (bf16[1024,1024]{1,0:T(8,128)(2,1)S(1)}, bf16[1024,1024]{1,0:T(8,128)(2,1)}, u32[]{:S(2)}) copy-start(bf16[1024,1024]{1,0:T(8,128)(2,1)} %param.26) | copy-start | bytes 6291460
  6.3 13.9 %copy-start.1 = (bf16[256,1024]{1,0:T(8,128)(2,1)S(1)}, bf16[256,1024]{1,0:T(8,128)(2,1)}, u32[]{:S(2)}) copy-start(bf16[256,1024]{1,0:T(8,128)(2,1)} %param.16) | copy-start | bytes 1572868
  6.3 13.9 %copy-start.3 = (f32[1024]{0:T(1024)S(1)}, f32[1024]{0:T(1024)}, u32[]{:S(2)}) copy-start(f32[1024]{0:T(1024)} %param.21) | copy-start | bytes 12292
  6.3 14.4 %copy-start.6 = (f32[1024]{0:T(1024)S(1)}, f32[1024]{0:T(1024)}, u32[]{:S(2)}) copy-start(f32[1024]{0:T(1024)} %param.23) | copy-start | bytes 12292
  6.4 14.4 %copy-start.7 = (f32[1024]{0:T(1024)S(1)}, f32[1024]{0:T(1024)}, u32[]{:S(2)}) copy-start(f32[1024]{0:T(1024)} %param.22) | copy-start | bytes 12292
  7.8 1.8 %collective-permute-start = (bf16[128,1024]{1,0:T(8,128)(2,1)S(1)}, bf16[128,1024]{1,0:T(8,128)(2,1)}, u32[]{:S(2)}, u32[]{:S(2)}) collective-permute-start(bf16[128,1024]{1,0:T(8,128)(2,1)S(1)} %constant_dynamic-slice_fusion.4), channel_id=1, source_target_pairs={{0,1},{1,0},{2,3},{3,2},{4,5},{5,4},{6,7},{7,6},{8,9},{9,8},{10,11... | collective-permute-start | bytes 786440 | tf_op jit(solution)/shard_map/ppermute | solution.py:89
  10.7 7.2 %collective-permute-start.1 = (bf16[64,1024]{1,0:T(8,128)(2,1)S(1)}, bf16[64,1024]{1,0:T(8,128)(2,1)S(1)}, u32[]{:S(2)}, u32[]{:S(2)}) collective-permute-start(bf16[64,1024]{1,0:T(8,128)(2,1)S(1)} %get-tuple-element.6), channel_id=1, source_target_pairs={{0,2},{1,3},{2,0},{3,1},{4,6},{5,7},{6,4},{7,5},{8,10},{9,11},{10,... | collective-permute-start | bytes 393224 | tf_op jit(solution)/shard_map/ppermute | solution.py:94
  13.6 6.6 %collective-permute-start.2 = (bf16[64,1024]{1,0:T(8,128)(2,1)S(1)}, bf16[64,1024]{1,0:T(8,128)(2,1)S(1)}, u32[]{:S(2)}, u32[]{:S(2)}) collective-permute-start(bf16[64,1024]{1,0:T(8,128)(2,1)S(1)} %get-tuple-element.7), channel_id=1, source_target_pairs={{0,2},{1,3},{2,0},{3,1},{4,6},{5,7},{6,4},{7,5},{8,10},{9,11},{10,... | collective-permute-start | bytes 393224 | tf_op jit(solution)/shard_map/ppermute | solution.py:95
  20.9 1.6 %collective-permute-start.3 = (bf16[128,1024]{1,0:T(8,128)(2,1)S(1)}, bf16[128,1024]{1,0:T(8,128)(2,1)S(1)}, u32[]{:S(2)}, u32[]{:S(2)}) collective-permute-start(bf16[128,1024]{1,0:T(8,128)(2,1)S(1)} %add_convert_fusion.2), channel_id=1, source_target_pairs={{0,1},{1,0},{2,3},{3,2},{4,5},{5,4},{6,7},{7,6},{8,9},{9,8},{10,11... | collective-permute-start | bytes 786440 | tf_op jit(solution)/shard_map/ppermute | solution.py:103
  22.7 15.3 %copy-start.4 = (f32[1024]{0:T(1024)S(1)}, f32[1024]{0:T(1024)}, u32[]{:S(2)}) copy-start(f32[1024]{0:T(1024)} %param.27) | copy-start | bytes 12292
  27.9 1.6 %collective-permute-start.4 = (bf16[128,1024]{1,0:T(8,128)(2,1)S(1)}, bf16[128,1024]{1,0:T(8,128)(2,1)S(1)}, u32[]{:S(2)}, u32[]{:S(2)}) collective-permute-start(bf16[128,1024]{1,0:T(8,128)(2,1)S(1)} %constant_dynamic-slice_fusion.3), channel_id=1, source_target_pairs={{0,1},{1,0},{2,3},{3,2},{4,5},{5,4},{6,7},{7,6},{8,9},{9,8},{10,11... | collective-permute-start | bytes 786440 | tf_op jit(solution)/shard_map/ppermute | solution.py:89
  29.6 6.4 %collective-permute-start.5 = (bf16[64,1024]{1,0:T(8,128)(2,1)S(1)}, bf16[64,1024]{1,0:T(8,128)(2,1)S(1)}, u32[]{:S(2)}, u32[]{:S(2)}) collective-permute-start(bf16[64,1024]{1,0:T(8,128)(2,1)S(1)} %get-tuple-element.4), channel_id=1, source_target_pairs={{0,2},{1,3},{2,0},{3,1},{4,6},{5,7},{6,4},{7,5},{8,10},{9,11},{10,... | collective-permute-start | bytes 393224 | tf_op jit(solution)/shard_map/ppermute | solution.py:94
  31.4 14.9 %copy-start.5 = (s32[128,64]{0,1:T(8,128)S(1)}, s32[128,64]{0,1:T(8,128)}, u32[]{:S(2)}) copy-start(s32[128,64]{0,1:T(8,128)} %param.31) | copy-start | bytes 98308
  31.4 6.6 %collective-permute-start.6 = (bf16[64,1024]{1,0:T(8,128)(2,1)S(1)}, bf16[64,1024]{1,0:T(8,128)(2,1)S(1)}, u32[]{:S(2)}, u32[]{:S(2)}) collective-permute-start(bf16[64,1024]{1,0:T(8,128)(2,1)S(1)} %get-tuple-element.5), channel_id=1, source_target_pairs={{0,2},{1,3},{2,0},{3,1},{4,6},{5,7},{6,4},{7,5},{8,10},{9,11},{10,... | collective-permute-start | bytes 393224 | tf_op jit(solution)/shard_map/ppermute | solution.py:95
  38.7 1.6 %collective-permute-start.7 = (bf16[128,1024]{1,0:T(8,128)(2,1)S(1)}, bf16[128,1024]{1,0:T(8,128)(2,1)S(1)}, u32[]{:S(2)}, u32[]{:S(2)}) collective-permute-start(bf16[128,1024]{1,0:T(8,128)(2,1)S(1)} %add_convert_fusion), channel_id=1, source_target_pairs={{0,1},{1,0},{2,3},{3,2},{4,5},{5,4},{6,7},{7,6},{8,9},{9,8},{10,11... | collective-permute-start | bytes 786440 | tf_op jit(solution)/shard_map/ppermute | solution.py:103
  40.4 14.6 %copy-start.2 = (bf16[256,1024]{1,0:T(8,128)(2,1)}, bf16[256,1024]{1,0:T(8,128)(2,1)S(1)}, u32[]{:S(2)}) copy-start(bf16[256,1024]{1,0:T(8,128)(2,1)S(1)} %maximum_select_fusion.1) | copy-start | bytes 1572868
  40.8 3.7 %collective-permute-start.8 = (bf16[16,256]{1,0:T(8,128)(2,1)S(1)}, bf16[16,256]{1,0:T(8,128)(2,1)S(1)}, u32[]{:S(2)}, u32[]{:S(2)}) collective-permute-start(bf16[16,256]{1,0:T(8,128)(2,1)S(1)} %fusion.56), channel_id=1, source_target_pairs={{0,4},{4,0},{8,12},{12,8},{16,20},{20,16},{24,28},{28,24},{1,5},{5... | collective-permute-start | bytes 24584 | tf_op jit(solution)/shard_map/ppermute | solution.py:58
  44.5 3.7 %collective-permute-start.9 = (bf16[32,256]{1,0:T(8,128)(2,1)S(1)}, bf16[32,256]{1,0:T(8,128)(2,1)S(1)}, u32[]{:S(2)}, u32[]{:S(2)}) collective-permute-start(bf16[32,256]{1,0:T(8,128)(2,1)S(1)} %maximum_select_fusion.5), channel_id=1, source_target_pairs={{0,8},{4,12},{8,0},{12,4},{16,24},{20,28},{24,16},{28,20},{1,9},{5... | collective-permute-start | bytes 49160 | tf_op jit(solution)/shard_map/ppermute | solution.py:58
  48.2 4.9 %collective-permute-start.10 = (bf16[64,256]{1,0:T(8,128)(2,1)S(1)}, bf16[64,256]{1,0:T(8,128)(2,1)S(1)}, u32[]{:S(2)}, u32[]{:S(2)}) collective-permute-start(bf16[64,256]{1,0:T(8,128)(2,1)S(1)} %maximum_select_fusion.4), channel_id=1, source_target_pairs={{0,16},{4,20},{8,24},{12,28},{16,0},{20,4},{24,8},{28,12},{1,17},{... | collective-permute-start | bytes 98312 | tf_op jit(solution)/shard_map/ppermute | solution.py:58
  59.9 4.9 %collective-permute-start.11 = (f32[64,64]{1,0:T(8,128)S(1)}, f32[64,64]{1,0:T(8,128)S(1)}, u32[]{:S(2)}, u32[]{:S(2)}) collective-permute-start(f32[64,64]{1,0:T(8,128)S(1)} %constant_dynamic-slice_fusion.2), channel_id=1, source_target_pairs={{0,16},{4,20},{8,24},{12,28},{16,0},{20,4},{24,8},{28,12},{1,17},{... | collective-permute-start | bytes 49160 | tf_op jit(solution)/shard_map/ppermute | solution.py:47
  64.8 3.8 %collective-permute-start.12 = (f32[32,64]{1,0:T(8,128)S(1)}, f32[32,64]{1,0:T(8,128)S(1)}, u32[]{:S(2)}, u32[]{:S(2)}) collective-permute-start(f32[32,64]{1,0:T(8,128)S(1)} %constant_dynamic-slice_fusion.1), channel_id=1, source_target_pairs={{0,8},{4,12},{8,0},{12,4},{16,24},{20,28},{24,16},{28,20},{1,9},{5... | collective-permute-start | bytes 24584 | tf_op jit(solution)/shard_map/ppermute | solution.py:47
  68.6 3.7 %collective-permute-start.13 = (f32[16,64]{1,0:T(8,128)S(1)}, f32[16,64]{1,0:T(8,128)S(1)}, u32[]{:S(2)}, u32[]{:S(2)}) collective-permute-start(f32[16,64]{1,0:T(8,128)S(1)} %constant_dynamic-slice_fusion), channel_id=1, source_target_pairs={{0,4},{4,0},{8,12},{12,8},{16,20},{20,16},{24,28},{28,24},{1,5},{5... | collective-permute-start | bytes 12296 | tf_op jit(solution)/shard_map/ppermute | solution.py:47
  72.2 1.2 %collective-permute-start.14 = (f32[16,64]{1,0:T(8,128)S(1)}, f32[16,64]{1,0:T(8,128)S(1)}, u32[]{:S(2)}, u32[]{:S(2)}) collective-permute-start(f32[16,64]{1,0:T(8,128)S(1)} %dynamic-slice_add_fusion.2), channel_id=1, source_target_pairs={{0,1},{1,0},{2,3},{3,2},{4,5},{5,4},{6,7},{7,6},{8,9},{9,8},{10,11... | collective-permute-start | bytes 12296 | tf_op jit(solution)/shard_map/ppermute | solution.py:212
  73.4 3.7 %collective-permute-start.15 = (f32[16,64]{1,0:T(8,128)S(1)}, f32[16,64]{1,0:T(8,128)S(1)}, u32[]{:S(2)}, u32[]{:S(2)}) collective-permute-start(f32[16,64]{1,0:T(8,128)S(1)} %add.205), channel_id=1, source_target_pairs={{0,2},{1,3},{2,0},{3,1},{4,6},{5,7},{6,4},{7,5},{8,10},{9,11},{10,... | collective-permute-start | bytes 12296 | tf_op jit(solution)/shard_map/ppermute | solution.py:212
  (4 other events, 36.4 us)

commit v11 on v9

--- a/solution.py
+++ b/solution.py
@@ -171,29 +171,48 @@
     shard_rows = index.shape[0]
     local_rows = candidates - row_base
     held = (local_rows >= 0) & (local_rows < shard_rows)
-    tile = lax.dot_general(
-        gathered, index, (((1,), (1,)), ((), ())), preferred_element_type=jnp.float32
-    )
-    wanted = jnp.clip(local_rows, 0, shard_rows - 1)
-    minor = 128
-    if shard_rows % minor == 0:
-        major = shard_rows // minor
-        major_hot = (
-            (wanted // minor)[:, :, None] == jnp.arange(major, dtype=jnp.int32)[None, None, :]
-        ).astype(jnp.float32)
-        rows_of = jnp.einsum(
-            "tca,tab->tcb",
-            major_hot,
-            tile.reshape(all_texts, major, minor),
-            precision=lax.Precision.HIGH,
-            preferred_element_type=jnp.float32,
+
+    def pick(packed):
+        units_block, wanted = packed
+        texts = units_block.shape[0]
+        tile = lax.dot_general(
+            units_block, index, (((1,), (1,)), ((), ())), preferred_element_type=jnp.float32
         )
-        minor_hot = (wanted % minor)[:, :, None] == jnp.arange(minor, dtype=jnp.int32)[None, None, :]
-        picked = jnp.sum(jnp.where(minor_hot, rows_of, 0.0), axis=2)
+        minor = 128
+        if shard_rows % minor == 0:
+            major = shard_rows // minor
+            major_hot = (
+                (wanted // minor)[:, :, None] == jnp.arange(major, dtype=jnp.int32)[None, None, :]
+            ).astype(jnp.bfloat16)
+            high = tile.astype(jnp.bfloat16)
+            low = (tile - high.astype(jnp.float32)).astype(jnp.bfloat16)
+            parts = jnp.concatenate(
+                [high.reshape(texts, major, minor), low.reshape(texts, major, minor)], axis=2
+            )
+            chosen_parts = jnp.einsum(
+                "tca,tab->tcb", major_hot, parts, preferred_element_type=jnp.float32
+            )
+            rows_of = chosen_parts[:, :, :minor] + chosen_parts[:, :, minor:]
+            minor_hot = (wanted % minor)[:, :, None] == jnp.arange(minor, dtype=jnp.int32)[None, None, :]
+            picked = jnp.sum(jnp.where(minor_hot, rows_of, 0.0), axis=2)
+        else:
+            row_ids = jnp.arange(shard_rows, dtype=jnp.int32)
+            chosen = wanted[:, :, None] == row_ids[None, None, :]
+            picked = jnp.sum(jnp.where(chosen, tile[:, None, :], 0.0), axis=2)
+        return picked
+
+    wanted_all = jnp.clip(local_rows, 0, shard_rows - 1)
+    block_rows = math.gcd(all_texts, 128)
+    if block_rows == all_texts:
+        picked = pick((gathered, wanted_all))
     else:
-        row_ids = jnp.arange(shard_rows, dtype=jnp.int32)
-        chosen = wanted[:, :, None] == row_ids[None, None, :]
-        picked = jnp.sum(jnp.where(chosen, tile[:, None, :], 0.0), axis=2)
+        picked = lax.map(
+            pick,
+            (
+                gathered.reshape(all_texts // block_rows, block_rows, -1),
+                wanted_all.reshape(all_texts // block_rows, block_rows, -1),
+            ),
+        ).reshape(all_texts, -1)
     partial_scores = jnp.where(held, picked, 0.0)
     if not xor_ok:
         slice_scores = lax.psum_scatter(

time: 77.9 us -> 77.1 us (0.990)
  matrix products: 17.8 us -> 14.3 us
  other arithmetic: 3.86 us -> 6.51 us
    dot_general x2, matrix products: 6.48 us -> 3 us  [the longest x1 1.69 us: pick(): lax.dot_general(units_block, index, (((1,), (1,)), ((), ())), preferred_e...]
    reduce_sum x0 -> x1, other arithmetic: none -> 2.66 us  [pick(): picked = jnp.sum(jnp.where(minor_hot, rows_of, 0.0), axis=2)]
where the time goes in v11:
time: 77.1 us; the launch traced here: 76.8 us
  waiting for transfers between devices  33.3 us (43%)
  starting transfers between devices  20.4 us (26%)
  matrix products  14.3 us (19%)
  other arithmetic  6.51 us (8%)
  local copies, waits for them, and re-layouts  1.22 us (2%)
  between operations  1.06 us (1%)
    ppermute x2, waiting for transfers between devices, settle_by_chip(): across = lax.ppermute(chip_sum, 'tensor', xor_pairs(4, 2))  13.2 us
    ppermute x3, starting transfers between devices, reduce_scatter_xor(): got = lax.ppermute(theirs.astype(wire), axis, xor_pairs(n, k))  6.59 us
    ppermute x3, starting transfers between devices, all_gather_xor(): other = lax.ppermute(cur, axis, xor_pairs(n, k))  6.5 us
    ppermute x3, waiting for transfers between devices, reduce_scatter_xor(): got = lax.ppermute(theirs.astype(wire), axis, xor_pairs(n, k))  5.74 us
    ppermute x3, waiting for transfers between devices, all_gather_xor(): other = lax.ppermute(cur, axis, xor_pairs(n, k))  5.57 us
    dot_general x1, matrix products, body(): jnp.dot(activated, w_down, preferred_element_type=jnp.float32)  5.11 us
    ppermute x2, starting transfers between devices, settle_by_chip(): across = lax.ppermute(chip_sum, 'tensor', xor_pairs(4, 2))  4.74 us
    ppermute x2, waiting for transfers between devices, body(): lax.ppermute(text_scores, 'tensor', xor_pairs(n_tensor, k))  3.08 us
  transfers between devices with their start and end apart: 14, of which 14 were waited for; matrix products, arithmetic and copies ran while one was open for 0% of the time, Pallas kernels for 0%

profile of v11, /device:TPU:0, one launch (start us, length us, event | category | flops | bytes accessed | tf_op | source)
XLA Modules:
  0.0 76.8 jit_solution(10137919450137700284)
XLA Ops:
  0.7 2.3 %fusion.103 = (bf16[3,256,256]{1,2,0:T(8,128)(2,1)S(1)}, f32[3,256,256]{1,2,0:T(8,128)S(1)}) fusion(f32[3,256]{1,0:T(4,128)} %param.19, bf16[3,1024,256]{2,1,0:T(8,128)(2,1)} %param.18, bf16[256,1024]{1,0:T(8,128)(2,1)} %param.16), kind=kOutput, calls=%fused_computation.168 | convolution fusion | flops 403046400 | bytes 3279872 | tf_op jit(solution)/shard_map/td,jdf->jtf/dot_general | solution.py:125
  10.7 2.9 %collective-permute-start.1 = (bf16[128,1024]{1,0:T(8,128)(2,1)S(1)}, bf16[128,1024]{1,0:T(8,128)(2,1)S(1)}, u32[]{:S(2)}, u32[]{:S(2)}) collective-permute-start(bf16[128,1024]{1,0:T(8,128)(2,1)S(1)} %add_convert_fusion.3), channel_id=1, source_target_pairs={{0,2},{1,3},{2,0},{3,1},{4,6},{5,7},{6,4},{7,5},{8,10},{9,11},{10,... | collective-permute-start | bytes 786440 | tf_op jit(solution)/shard_map/ppermute | solution.py:91
  13.6 6.6 %collective-permute-done.1 = bf16[128,1024]{1,0:T(8,128)(2,1)S(1)} collective-permute-done((bf16[128,1024]{1,0:T(8,128)(2,1)S(1)}, bf16[128,1024]{1,0:T(8,128)(2,1)S(1)}, u32[]{:S(2)}, u32[]{:S(2)}) %collective-permute-start.1) | collective-permute-done | bytes 262176 | tf_op jit(solution)/shard_map/ppermute | solution.py:91
  21.0 1.5 %collective-permute-done.2 = bf16[128,1024]{1,0:T(8,128)(2,1)S(1)} collective-permute-done((bf16[128,1024]{1,0:T(8,128)(2,1)S(1)}, bf16[128,1024]{1,0:T(8,128)(2,1)S(1)}, u32[]{:S(2)}, u32[]{:S(2)}) %collective-permute-start.2) | collective-permute-done | bytes 262176 | tf_op jit(solution)/shard_map/ppermute | solution.py:97
  22.7 5.1 %convolution_convert_fusion.1 = bf16[256,1024]{1,0:T(8,128)(2,1)S(1)} fusion(bf16[1024,1024]{1,0:T(8,128)(2,1)S(1)} %copy-done, bf16[256,1024]{1,0:T(8,128)(2,1)S(1)} %maximum_select_fusion, bf16[1024,1024]{1,0:T(8,128)(2,1)} %param.24, f32[1024]{0:T(1024)S(1)} %copy-done.11), kind=kOutput, calls=%fused_computation.11 | convolution fusion | flops 1091305472 | bytes 5246976 | tf_op jit(solution)/shard_map/dot_general | solution.py:145
  29.5 1.8 %collective-permute-start.4 = (bf16[128,1024]{1,0:T(8,128)(2,1)S(1)}, bf16[128,1024]{1,0:T(8,128)(2,1)S(1)}, u32[]{:S(2)}, u32[]{:S(2)}) collective-permute-start(bf16[128,1024]{1,0:T(8,128)(2,1)S(1)} %add_convert_fusion.1), channel_id=1, source_target_pairs={{0,2},{1,3},{2,0},{3,1},{4,6},{5,7},{6,4},{7,5},{8,10},{9,11},{10,... | collective-permute-start | bytes 786440 | tf_op jit(solution)/shard_map/ppermute | solution.py:91
  31.3 6.6 %collective-permute-done.4 = bf16[128,1024]{1,0:T(8,128)(2,1)S(1)} collective-permute-done((bf16[128,1024]{1,0:T(8,128)(2,1)S(1)}, bf16[128,1024]{1,0:T(8,128)(2,1)S(1)}, u32[]{:S(2)}, u32[]{:S(2)}) %collective-permute-start.4) | collective-permute-done | bytes 262176 | tf_op jit(solution)/shard_map/ppermute | solution.py:91
  38.7 1.5 %collective-permute-done.5 = bf16[128,1024]{1,0:T(8,128)(2,1)S(1)} collective-permute-done((bf16[128,1024]{1,0:T(8,128)(2,1)S(1)}, bf16[128,1024]{1,0:T(8,128)(2,1)S(1)}, u32[]{:S(2)}, u32[]{:S(2)}) %collective-permute-start.5) | collective-permute-done | bytes 262176 | tf_op jit(solution)/shard_map/ppermute | solution.py:97
  40.8 1.8 %collective-permute-start.6 = (bf16[16,256]{1,0:T(8,128)(2,1)S(1)}, bf16[16,256]{1,0:T(8,128)(2,1)S(1)}, u32[]{:S(2)}, u32[]{:S(2)}) collective-permute-start(bf16[16,256]{1,0:T(8,128)(2,1)S(1)} %fusion.64), channel_id=1, source_target_pairs={{0,4},{4,0},{8,12},{12,8},{16,20},{20,16},{24,28},{28,24},{1,5},{5... | collective-permute-start | bytes 24584 | tf_op jit(solution)/shard_map/ppermute | solution.py:58
  42.6 1.9 %collective-permute-done.6 = bf16[16,256]{1,0:T(8,128)(2,1)S(1)} collective-permute-done((bf16[16,256]{1,0:T(8,128)(2,1)S(1)}, bf16[16,256]{1,0:T(8,128)(2,1)S(1)}, u32[]{:S(2)}, u32[]{:S(2)}) %collective-permute-start.6) | collective-permute-done | bytes 8224 | tf_op jit(solution)/shard_map/ppermute | solution.py:58
  44.4 1.8 %collective-permute-start.7 = (bf16[32,256]{1,0:T(8,128)(2,1)S(1)}, bf16[32,256]{1,0:T(8,128)(2,1)S(1)}, u32[]{:S(2)}, u32[]{:S(2)}) collective-permute-start(bf16[32,256]{1,0:T(8,128)(2,1)S(1)} %maximum_select_fusion.5), channel_id=1, source_target_pairs={{0,8},{4,12},{8,0},{12,4},{16,24},{20,28},{24,16},{28,20},{1,9},{5... | collective-permute-start | bytes 49160 | tf_op jit(solution)/shard_map/ppermute | solution.py:58
  46.4 1.8 %collective-permute-done.7 = bf16[32,256]{1,0:T(8,128)(2,1)S(1)} collective-permute-done((bf16[32,256]{1,0:T(8,128)(2,1)S(1)}, bf16[32,256]{1,0:T(8,128)(2,1)S(1)}, u32[]{:S(2)}, u32[]{:S(2)}) %collective-permute-start.7) | collective-permute-done | bytes 16416 | tf_op jit(solution)/shard_map/ppermute | solution.py:58
  48.2 2.9 %collective-permute-start.8 = (bf16[64,256]{1,0:T(8,128)(2,1)S(1)}, bf16[64,256]{1,0:T(8,128)(2,1)S(1)}, u32[]{:S(2)}, u32[]{:S(2)}) collective-permute-start(bf16[64,256]{1,0:T(8,128)(2,1)S(1)} %maximum_select_fusion.4), channel_id=1, source_target_pairs={{0,16},{4,20},{8,24},{12,28},{16,0},{20,4},{24,8},{28,12},{1,17},{... | collective-permute-start | bytes 98312 | tf_op jit(solution)/shard_map/ppermute | solution.py:58
  51.2 1.9 %collective-permute-done.8 = bf16[64,256]{1,0:T(8,128)(2,1)S(1)} collective-permute-done((bf16[64,256]{1,0:T(8,128)(2,1)S(1)}, bf16[64,256]{1,0:T(8,128)(2,1)S(1)}, u32[]{:S(2)}, u32[]{:S(2)}) %collective-permute-start.8) | collective-permute-done | bytes 32800 | tf_op jit(solution)/shard_map/ppermute | solution.py:58
  53.1 1.7 %convert_bitcast_fusion = (bf16[16,8,16,128]{3,1,2,0:T(8,128)(2,1)S(1)}, bf16[16,8,16,128]{3,1,2,0:T(8,128)(2,1)S(1)}) fusion(bf16[2048,256]{1,0:T(8,128)(2,1)} %param.30, bf16[64,256]{1,0:T(8,128)(2,1)S(1)} %collective-permute-done.8, bf16[64,256]{1,0:T(8,128)(2,1)S(1)} %maximum_select_fusion.4, pred[]{:T(512)S(6)} %eq.90), kind=kOutput, calls=%fused_computation.87 | convolution fusion | flops 135561216 | bytes 2162689 | tf_op jit(solution)/shard_map/dot_general | solution.py:178
  56.3 2.7 %fusion.2 = f32[128,64]{1,0:T(8,128)S(1)} fusion(f32[128,64,256]{2,1,0:T(8,128)S(1)} %fusion.9, s32[128,64]{1,0:T(8,128)S(1)} %get-tuple-element.6), kind=kLoop, calls=%fused_computation.3 | loop fusion | flops 4186112 | bytes 8454144 | tf_op jit(solution)/shard_map/reduce_sum | solution.py:197
  59.0 2.9 %collective-permute-start.9 = (f32[64,64]{1,0:T(8,128)S(1)}, f32[64,64]{1,0:T(8,128)S(1)}, u32[]{:S(2)}, u32[]{:S(2)}) collective-permute-start(f32[64,64]{1,0:T(8,128)S(1)} %constant_dynamic-slice_fusion.2), channel_id=1, source_target_pairs={{0,16},{4,20},{8,24},{12,28},{16,0},{20,4},{24,8},{28,12},{1,17},{... | collective-permute-start | bytes 49160 | tf_op jit(solution)/shard_map/ppermute | solution.py:47
  62.0 1.9 %collective-permute-done.9 = f32[64,64]{1,0:T(8,128)S(1)} collective-permute-done((f32[64,64]{1,0:T(8,128)S(1)}, f32[64,64]{1,0:T(8,128)S(1)}, u32[]{:S(2)}, u32[]{:S(2)}) %collective-permute-start.9) | collective-permute-done | bytes 16416 | tf_op jit(solution)/shard_map/ppermute | solution.py:47
  63.9 1.9 %collective-permute-start.10 = (f32[32,64]{1,0:T(8,128)S(1)}, f32[32,64]{1,0:T(8,128)S(1)}, u32[]{:S(2)}, u32[]{:S(2)}) collective-permute-start(f32[32,64]{1,0:T(8,128)S(1)} %constant_dynamic-slice_fusion.1), channel_id=1, source_target_pairs={{0,8},{4,12},{8,0},{12,4},{16,24},{20,28},{24,16},{28,20},{1,9},{5... | collective-permute-start | bytes 24584 | tf_op jit(solution)/shard_map/ppermute | solution.py:47
  65.8 1.9 %collective-permute-done.10 = f32[32,64]{1,0:T(8,128)S(1)} collective-permute-done((f32[32,64]{1,0:T(8,128)S(1)}, f32[32,64]{1,0:T(8,128)S(1)}, u32[]{:S(2)}, u32[]{:S(2)}) %collective-permute-start.10) | collective-permute-done | bytes 8224 | tf_op jit(solution)/shard_map/ppermute | solution.py:47
  67.8 1.8 %collective-permute-start.11 = (f32[16,64]{1,0:T(8,128)S(1)}, f32[16,64]{1,0:T(8,128)S(1)}, u32[]{:S(2)}, u32[]{:S(2)}) collective-permute-start(f32[16,64]{1,0:T(8,128)S(1)} %constant_dynamic-slice_fusion), channel_id=1, source_target_pairs={{0,4},{4,0},{8,12},{12,8},{16,20},{20,16},{24,28},{28,24},{1,5},{5... | collective-permute-start | bytes 12296 | tf_op jit(solution)/shard_map/ppermute | solution.py:47
  69.5 1.9 %collective-permute-done.11 = f32[16,64]{1,0:T(8,128)S(1)} collective-permute-done((f32[16,64]{1,0:T(8,128)S(1)}, f32[16,64]{1,0:T(8,128)S(1)}, u32[]{:S(2)}, u32[]{:S(2)}) %collective-permute-start.11) | collective-permute-done | bytes 4128 | tf_op jit(solution)/shard_map/ppermute | solution.py:47
  72.6 1.7 %collective-permute-start.13 = (f32[16,64]{1,0:T(8,128)S(1)}, f32[16,64]{1,0:T(8,128)S(1)}, u32[]{:S(2)}, u32[]{:S(2)}) collective-permute-start(f32[16,64]{1,0:T(8,128)S(1)} %add.209), channel_id=1, source_target_pairs={{0,2},{1,3},{2,0},{3,1},{4,6},{5,7},{6,4},{7,5},{8,10},{9,11},{10,... | collective-permute-start | bytes 12296 | tf_op jit(solution)/shard_map/ppermute | solution.py:225
  74.3 1.9 %collective-permute-done.13 = f32[16,64]{1,0:T(8,128)S(1)} collective-permute-done((f32[16,64]{1,0:T(8,128)S(1)}, f32[16,64]{1,0:T(8,128)S(1)}, u32[]{:S(2)}, u32[]{:S(2)}) %collective-permute-start.13) | collective-permute-done | bytes 4128 | tf_op jit(solution)/shard_map/ppermute | solution.py:225
  (79 shorter events, 15.0 us)
Async XLA Ops:
  0.6 22.0 %copy-start = (bf16[1024,1024]{1,0:T(8,128)(2,1)S(1)}, bf16[1024,1024]{1,0:T(8,128)(2,1)}, u32[]{:S(2)}) copy-start(bf16[1024,1024]{1,0:T(8,128)(2,1)} %param.26) | copy-start | bytes 6291460
  6.3 13.9 %copy-start.1 = (bf16[256,1024]{1,0:T(8,128)(2,1)S(1)}, bf16[256,1024]{1,0:T(8,128)(2,1)}, u32[]{:S(2)}) copy-start(bf16[256,1024]{1,0:T(8,128)(2,1)} %param.16) | copy-start | bytes 1572868
  6.3 13.9 %copy-start.3 = (f32[1024]{0:T(1024)S(1)}, f32[1024]{0:T(1024)}, u32[]{:S(2)}) copy-start(f32[1024]{0:T(1024)} %param.21) | copy-start | bytes 12292
  6.3 14.3 %copy-start.6 = (f32[1024]{0:T(1024)S(1)}, f32[1024]{0:T(1024)}, u32[]{:S(2)}) copy-start(f32[1024]{0:T(1024)} %param.23) | copy-start | bytes 12292
  6.4 14.3 %copy-start.7 = (f32[1024]{0:T(1024)S(1)}, f32[1024]{0:T(1024)}, u32[]{:S(2)}) copy-start(f32[1024]{0:T(1024)} %param.22) | copy-start | bytes 12292
  7.8 1.8 %collective-permute-start = (bf16[128,1024]{1,0:T(8,128)(2,1)S(1)}, bf16[128,1024]{1,0:T(8,128)(2,1)}, u32[]{:S(2)}, u32[]{:S(2)}) collective-permute-start(bf16[128,1024]{1,0:T(8,128)(2,1)S(1)} %constant_dynamic-slice_fusion.4), channel_id=1, source_target_pairs={{0,1},{1,0},{2,3},{3,2},{4,5},{5,4},{6,7},{7,6},{8,9},{9,8},{10,11... | collective-permute-start | bytes 786440 | tf_op jit(solution)/shard_map/ppermute | solution.py:89
  8.3 14.3 %copy-start.11 = (f32[1024]{0:T(1024)S(1)}, f32[1024]{0:T(1024)}, u32[]{:S(2)}) copy-start(f32[1024]{0:T(1024)} %param.25) | copy-start | bytes 12292
  10.7 9.5 %collective-permute-start.1 = (bf16[128,1024]{1,0:T(8,128)(2,1)S(1)}, bf16[128,1024]{1,0:T(8,128)(2,1)S(1)}, u32[]{:S(2)}, u32[]{:S(2)}) collective-permute-start(bf16[128,1024]{1,0:T(8,128)(2,1)S(1)} %add_convert_fusion.3), channel_id=1, source_target_pairs={{0,2},{1,3},{2,0},{3,1},{4,6},{5,7},{6,4},{7,5},{8,10},{9,11},{10,... | collective-permute-start | bytes 786440 | tf_op jit(solution)/shard_map/ppermute | solution.py:91
  20.9 1.6 %collective-permute-start.2 = (bf16[128,1024]{1,0:T(8,128)(2,1)S(1)}, bf16[128,1024]{1,0:T(8,128)(2,1)S(1)}, u32[]{:S(2)}, u32[]{:S(2)}) collective-permute-start(bf16[128,1024]{1,0:T(8,128)(2,1)S(1)} %add_convert_fusion.2), channel_id=1, source_target_pairs={{0,1},{1,0},{2,3},{3,2},{4,5},{5,4},{6,7},{7,6},{8,9},{9,8},{10,11... | collective-permute-start | bytes 786440 | tf_op jit(solution)/shard_map/ppermute | solution.py:97
  22.6 15.3 %copy-start.4 = (f32[1024]{0:T(1024)S(1)}, f32[1024]{0:T(1024)}, u32[]{:S(2)}) copy-start(f32[1024]{0:T(1024)} %param.27) | copy-start | bytes 12292
  27.8 10.6 %copy-start.8 = (f32[1024]{0:T(1024)S(1)}, f32[1024]{0:T(1024)}, u32[]{:S(2)}) copy-start(f32[1024]{0:T(1024)} %param.29) | copy-start | bytes 12292
  27.8 1.6 %collective-permute-start.3 = (bf16[128,1024]{1,0:T(8,128)(2,1)S(1)}, bf16[128,1024]{1,0:T(8,128)(2,1)S(1)}, u32[]{:S(2)}, u32[]{:S(2)}) collective-permute-start(bf16[128,1024]{1,0:T(8,128)(2,1)S(1)} %constant_dynamic-slice_fusion.3), channel_id=1, source_target_pairs={{0,1},{1,0},{2,3},{3,2},{4,5},{5,4},{6,7},{7,6},{8,9},{9,8},{10,11... | collective-permute-start | bytes 786440 | tf_op jit(solution)/shard_map/ppermute | solution.py:89
  29.5 16.8 %copy-start.5 = (s32[128,64]{0,1:T(8,128)S(1)}, s32[128,64]{0,1:T(8,128)}, u32[]{:S(2)}) copy-start(s32[128,64]{0,1:T(8,128)} %param.31) | copy-start | bytes 98308
  29.5 8.4 %collective-permute-start.4 = (bf16[128,1024]{1,0:T(8,128)(2,1)S(1)}, bf16[128,1024]{1,0:T(8,128)(2,1)S(1)}, u32[]{:S(2)}, u32[]{:S(2)}) collective-permute-start(bf16[128,1024]{1,0:T(8,128)(2,1)S(1)} %add_convert_fusion.1), channel_id=1, source_target_pairs={{0,2},{1,3},{2,0},{3,1},{4,6},{5,7},{6,4},{7,5},{8,10},{9,11},{10,... | collective-permute-start | bytes 786440 | tf_op jit(solution)/shard_map/ppermute | solution.py:91
  38.6 1.6 %collective-permute-start.5 = (bf16[128,1024]{1,0:T(8,128)(2,1)S(1)}, bf16[128,1024]{1,0:T(8,128)(2,1)S(1)}, u32[]{:S(2)}, u32[]{:S(2)}) collective-permute-start(bf16[128,1024]{1,0:T(8,128)(2,1)S(1)} %add_convert_fusion), channel_id=1, source_target_pairs={{0,1},{1,0},{2,3},{3,2},{4,5},{5,4},{6,7},{7,6},{8,9},{9,8},{10,11... | collective-permute-start | bytes 786440 | tf_op jit(solution)/shard_map/ppermute | solution.py:97
  40.4 14.5 %copy-start.2 = (bf16[256,1024]{1,0:T(8,128)(2,1)}, bf16[256,1024]{1,0:T(8,128)(2,1)S(1)}, u32[]{:S(2)}) copy-start(bf16[256,1024]{1,0:T(8,128)(2,1)S(1)} %maximum_select_fusion.1) | copy-start | bytes 1572868
  40.8 3.7 %collective-permute-start.6 = (bf16[16,256]{1,0:T(8,128)(2,1)S(1)}, bf16[16,256]{1,0:T(8,128)(2,1)S(1)}, u32[]{:S(2)}, u32[]{:S(2)}) collective-permute-start(bf16[16,256]{1,0:T(8,128)(2,1)S(1)} %fusion.64), channel_id=1, source_target_pairs={{0,4},{4,0},{8,12},{12,8},{16,20},{20,16},{24,28},{28,24},{1,5},{5... | collective-permute-start | bytes 24584 | tf_op jit(solution)/shard_map/ppermute | solution.py:58
  44.4 3.7 %collective-permute-start.7 = (bf16[32,256]{1,0:T(8,128)(2,1)S(1)}, bf16[32,256]{1,0:T(8,128)(2,1)S(1)}, u32[]{:S(2)}, u32[]{:S(2)}) collective-permute-start(bf16[32,256]{1,0:T(8,128)(2,1)S(1)} %maximum_select_fusion.5), channel_id=1, source_target_pairs={{0,8},{4,12},{8,0},{12,4},{16,24},{20,28},{24,16},{28,20},{1,9},{5... | collective-permute-start | bytes 49160 | tf_op jit(solution)/shard_map/ppermute | solution.py:58
  48.2 4.9 %collective-permute-start.8 = (bf16[64,256]{1,0:T(8,128)(2,1)S(1)}, bf16[64,256]{1,0:T(8,128)(2,1)S(1)}, u32[]{:S(2)}, u32[]{:S(2)}) collective-permute-start(bf16[64,256]{1,0:T(8,128)(2,1)S(1)} %maximum_select_fusion.4), channel_id=1, source_target_pairs={{0,16},{4,20},{8,24},{12,28},{16,0},{20,4},{24,8},{28,12},{1,17},{... | collective-permute-start | bytes 98312 | tf_op jit(solution)/shard_map/ppermute | solution.py:58
  59.0 4.9 %collective-permute-start.9 = (f32[64,64]{1,0:T(8,128)S(1)}, f32[64,64]{1,0:T(8,128)S(1)}, u32[]{:S(2)}, u32[]{:S(2)}) collective-permute-start(f32[64,64]{1,0:T(8,128)S(1)} %constant_dynamic-slice_fusion.2), channel_id=1, source_target_pairs={{0,16},{4,20},{8,24},{12,28},{16,0},{20,4},{24,8},{28,12},{1,17},{... | collective-permute-start | bytes 49160 | tf_op jit(solution)/shard_map/ppermute | solution.py:47
  63.9 3.8 %collective-permute-start.10 = (f32[32,64]{1,0:T(8,128)S(1)}, f32[32,64]{1,0:T(8,128)S(1)}, u32[]{:S(2)}, u32[]{:S(2)}) collective-permute-start(f32[32,64]{1,0:T(8,128)S(1)} %constant_dynamic-slice_fusion.1), channel_id=1, source_target_pairs={{0,8},{4,12},{8,0},{12,4},{16,24},{20,28},{24,16},{28,20},{1,9},{5... | collective-permute-start | bytes 24584 | tf_op jit(solution)/shard_map/ppermute | solution.py:47
  67.8 3.7 %collective-permute-start.11 = (f32[16,64]{1,0:T(8,128)S(1)}, f32[16,64]{1,0:T(8,128)S(1)}, u32[]{:S(2)}, u32[]{:S(2)}) collective-permute-start(f32[16,64]{1,0:T(8,128)S(1)} %constant_dynamic-slice_fusion), channel_id=1, source_target_pairs={{0,4},{4,0},{8,12},{12,8},{16,20},{20,16},{24,28},{28,24},{1,5},{5... | collective-permute-start | bytes 12296 | tf_op jit(solution)/shard_map/ppermute | solution.py:47
  71.4 1.2 %collective-permute-start.12 = (f32[16,64]{1,0:T(8,128)S(1)}, f32[16,64]{1,0:T(8,128)S(1)}, u32[]{:S(2)}, u32[]{:S(2)}) collective-permute-start(f32[16,64]{1,0:T(8,128)S(1)} %dynamic-slice_add_fusion.2), channel_id=1, source_target_pairs={{0,1},{1,0},{2,3},{3,2},{4,5},{5,4},{6,7},{7,6},{8,9},{9,8},{10,11... | collective-permute-start | bytes 12296 | tf_op jit(solution)/shard_map/ppermute | solution.py:225
  72.6 3.7 %collective-permute-start.13 = (f32[16,64]{1,0:T(8,128)S(1)}, f32[16,64]{1,0:T(8,128)S(1)}, u32[]{:S(2)}, u32[]{:S(2)}) collective-permute-start(f32[16,64]{1,0:T(8,128)S(1)} %add.209), channel_id=1, source_target_pairs={{0,2},{1,3},{2,0},{3,1},{4,6},{5,7},{6,4},{7,5},{8,10},{9,11},{10,... | collective-permute-start | bytes 12296 | tf_op jit(solution)/shard_map/ppermute | solution.py:225
  (2 other events, 13.7 us)

commit v12 on v11

--- a/solution.py
+++ b/solution.py
@@ -163,10 +163,6 @@
         and is_power_of_two(n_tensor)
         and candidates.shape[0] % n_dp == 0
     )
-    if xor_ok:
-        gathered = all_gather_xor(unit_quarter, "dp", n_dp, levels_of(n_dp))
-    else:
-        gathered = lax.all_gather(unit_quarter, "dp", axis=0, tiled=True)
     all_texts = candidates.shape[0]
     shard_rows = index.shape[0]
     local_rows = candidates - row_base
@@ -202,25 +198,48 @@
         return picked
 
     wanted_all = jnp.clip(local_rows, 0, shard_rows - 1)
-    block_rows = math.gcd(all_texts, 128)
-    if block_rows == all_texts:
-        picked = pick((gathered, wanted_all))
-    else:
-        picked = lax.map(
-            pick,
-            (
-                gathered.reshape(all_texts // block_rows, block_rows, -1),
-                wanted_all.reshape(all_texts // block_rows, block_rows, -1),
-            ),
-        ).reshape(all_texts, -1)
-    partial_scores = jnp.where(held, picked, 0.0)
-    if not xor_ok:
+
+    def pick_all(units_rows, wanted, keep):
+        texts = units_rows.shape[0]
+        block_rows = math.gcd(texts, 128)
+        if block_rows == texts:
+            picked = pick((units_rows, wanted))
+        else:
+            picked = lax.map(
+                pick,
+                (
+                    units_rows.reshape(texts // block_rows, block_rows, -1),
+                    wanted.reshape(texts // block_rows, block_rows, -1),
+                ),
+            ).reshape(texts, -1)
+        return jnp.where(keep, picked, 0.0)
+
+    if not xor_ok or n_dp < 2:
+        gathered = lax.all_gather(unit_quarter, "dp", axis=0, tiled=True)
+        partial_scores = pick_all(gathered, wanted_all, held)
         slice_scores = lax.psum_scatter(
             partial_scores, ("dp", "tensor"), scatter_dimension=0, tiled=True
         )
         scores = lax.all_gather(slice_scores, "tensor", axis=0, tiled=True)
         return (states, scores)
-    text_scores, _ = reduce_scatter_xor(partial_scores, "dp", n_dp, levels_of(n_dp)[::-1])
+    levels = levels_of(n_dp)
+    last = levels[-1]
+    near = all_gather_xor(unit_quarter, "dp", n_dp, levels[:-1])
+    far = lax.ppermute(near, "dp", xor_pairs(n_dp, last))
+    top = (lax.axis_index("dp") // last) % 2
+    half = all_texts // 2
+    near_scores = pick_all(
+        near,
+        lax.dynamic_slice_in_dim(wanted_all, top * half, half, 0),
+        lax.dynamic_slice_in_dim(held, top * half, half, 0),
+    )
+    far_scores = pick_all(
+        far,
+        lax.dynamic_slice_in_dim(wanted_all, (1 - top) * half, half, 0),
+        lax.dynamic_slice_in_dim(held, (1 - top) * half, half, 0),
+    )
+    kept = near_scores + lax.ppermute(far_scores, "dp", xor_pairs(n_dp, last))
+    text_scores, _ = reduce_scatter_xor(kept, "dp", n_dp, levels[:-1][::-1])
     for k in levels_of(n_tensor):
         text_scores = text_scores + lax.ppermute(text_scores, "tensor", xor_pairs(n_tensor, k))
     return (states, text_scores)

time: 77.1 us -> 80.5 us (1.044)
  other arithmetic: 6.51 us -> 11.7 us
  waiting for transfers between devices: 33.3 us -> 29.7 us
  local copies, waits for them, and re-layouts: 1.22 us -> 2.89 us
    ppermute x0 -> x2, starting transfers between devices: none -> 5.83 us  [the longest x1 2.93 us: body(): kept = near_scores + lax.ppermute(far_scores, 'dp', xor_pairs(n_dp, last))]
    ppermute x3 -> x2, starting transfers between devices: 6.59 us -> 3.65 us  [reduce_scatter_xor(): got = lax.ppermute(theirs.astype(wire), axis, xor_pairs(n, k))]
    ppermute x3 -> x2, starting transfers between devices: 6.5 us -> 3.59 us  [all_gather_xor(): other = lax.ppermute(cur, axis, xor_pairs(n, k))]
    ppermute x3 -> x2, waiting for transfers between devices: 5.74 us -> 3.81 us  [reduce_scatter_xor(): got = lax.ppermute(theirs.astype(wire), axis, xor_pairs(n, k))]
    ppermute x3 -> x2, waiting for transfers between devices: 5.57 us -> 3.67 us  [all_gather_xor(): other = lax.ppermute(cur, axis, xor_pairs(n, k))]
    convert_element_type x2, other arithmetic: 0.41 us -> 2.13 us  [settle_by_chip(): layer_norm(total + bias + own_residual.astype(jnp.float32), gain, shift)]
    unnamed x27 -> x37, local copies, waits for them, and re-layouts: 0.39 us -> 2.06 us
    ppermute x0 -> x2, waiting for transfers between devices: none -> 1.31 us  [the longest x1 0.67 us: body(): far = lax.ppermute(near, 'dp', xor_pairs(n_dp, last))]
  transfers between devices with their start and end apart: 14 -> 14, of which waited for: 14 -> 14; matrix products, arithmetic and copies ran while one was open for 0% -> 5% of each run, Pallas kernels for 0% -> 0%
where the time goes in v12:
time: 80.5 us; the launch traced here: 80.2 us
  waiting for transfers between devices  29.7 us (37%)
  starting transfers between devices  20.3 us (25%)
  matrix products  14.6 us (18%)
  other arithmetic  11.7 us (15%)
  local copies, waits for them, and re-layouts  2.89 us (4%)
  between operations  1.09 us (1%)
    ppermute x2, waiting for transfers between devices, settle_by_chip(): across = lax.ppermute(chip_sum, 'tensor', xor_pairs(4, 2))  13.1 us
    dot_general x1, matrix products, body(): jnp.dot(activated, w_down, preferred_element_type=jnp.float32)  5.31 us
    ppermute x2, starting transfers between devices, settle_by_chip(): across = lax.ppermute(chip_sum, 'tensor', xor_pairs(4, 2))  4.72 us
    ppermute x2, waiting for transfers between devices, reduce_scatter_xor(): got = lax.ppermute(theirs.astype(wire), axis, xor_pairs(n, k))  3.81 us
    ppermute x2, waiting for transfers between devices, all_gather_xor(): other = lax.ppermute(cur, axis, xor_pairs(n, k))  3.67 us
    ppermute x2, starting transfers between devices, reduce_scatter_xor(): got = lax.ppermute(theirs.astype(wire), axis, xor_pairs(n, k))  3.65 us
    ppermute x2, starting transfers between devices, all_gather_xor(): other = lax.ppermute(cur, axis, xor_pairs(n, k))  3.59 us
    ppermute x2, waiting for transfers between devices, body(): lax.ppermute(text_scores, 'tensor', xor_pairs(n_tensor, k))  3.09 us
  transfers between devices with their start and end apart: 14, of which 14 were waited for; matrix products, arithmetic and copies ran while one was open for 5% of the time, Pallas kernels for 0%

profile of v12, /device:TPU:0, one launch (start us, length us, event | category | flops | bytes accessed | tf_op | source)
XLA Modules:
  0.0 80.2 jit_solution(14875137803778981720)
XLA Ops:
  0.7 2.3 %fusion.106 = (bf16[3,256,256]{1,2,0:T(8,128)(2,1)S(1)}, f32[3,256,256]{1,2,0:T(8,128)S(1)}) fusion(f32[3,256]{1,0:T(4,128)} %param.19, bf16[3,1024,256]{2,1,0:T(8,128)(2,1)} %param.18, bf16[256,1024]{1,0:T(8,128)(2,1)} %param.16), kind=kOutput, calls=%fused_computation.182 | convolution fusion | flops 403046400 | bytes 3279872 | tf_op jit(solution)/shard_map/td,jdf->jtf/dot_general | solution.py:125
  6.8 1.4 %convolution_convert_fusion = bf16[256,1024]{1,0:T(8,128)(2,1)S(1)} fusion(bf16[256,256]{0,1:T(8,128)(2,1)S(1)} %bitcast.53, bf16[256,1024]{1,0:T(8,128)(2,1)} %param.20), kind=kOutput, calls=%fused_computation.14 | convolution fusion | flops 134479872 | bytes 1179648 | tf_op jit(solution)/shard_map/dot_general | solution.py:140
  11.1 2.9 %collective-permute-start.1 = (bf16[128,1024]{1,0:T(8,128)(2,1)S(1)}, bf16[128,1024]{1,0:T(8,128)(2,1)S(1)}, u32[]{:S(2)}, u32[]{:S(2)}) collective-permute-start(bf16[128,1024]{1,0:T(8,128)(2,1)S(1)} %add_convert_fusion.3), channel_id=1, source_target_pairs={{0,2},{1,3},{2,0},{3,1},{4,6},{5,7},{6,4},{7,5},{8,10},{9,11},{10,... | collective-permute-start | bytes 786440 | tf_op jit(solution)/shard_map/ppermute | solution.py:91
  14.0 6.6 %collective-permute-done.1 = bf16[128,1024]{1,0:T(8,128)(2,1)S(1)} collective-permute-done((bf16[128,1024]{1,0:T(8,128)(2,1)S(1)}, bf16[128,1024]{1,0:T(8,128)(2,1)S(1)}, u32[]{:S(2)}, u32[]{:S(2)}) %collective-permute-start.1) | collective-permute-done | bytes 262176 | tf_op jit(solution)/shard_map/ppermute | solution.py:91
  21.4 1.5 %collective-permute-done.2 = bf16[128,1024]{1,0:T(8,128)(2,1)S(1)} collective-permute-done((bf16[128,1024]{1,0:T(8,128)(2,1)S(1)}, bf16[128,1024]{1,0:T(8,128)(2,1)S(1)}, u32[]{:S(2)}, u32[]{:S(2)}) %collective-permute-start.2) | collective-permute-done | bytes 262176 | tf_op jit(solution)/shard_map/ppermute | solution.py:97
  23.1 5.3 %convolution_convert_fusion.1 = bf16[256,1024]{1,0:T(8,128)(2,1)S(1)} fusion(bf16[1024,1024]{1,0:T(8,128)(2,1)S(1)} %copy-done, bf16[256,1024]{1,0:T(8,128)(2,1)S(1)} %maximum_select_fusion, bf16[1024,1024]{1,0:T(8,128)(2,1)} %param.24, f32[1024]{0:T(1024)S(1)} %copy-done.15), kind=kOutput, calls=%fused_computation.15 | convolution fusion | flops 1091305472 | bytes 5246976 | tf_op jit(solution)/shard_map/dot_general | solution.py:145
  28.7 1.4 %collective-permute-done.3 = bf16[128,1024]{1,0:T(8,128)(2,1)S(1)} collective-permute-done((bf16[128,1024]{1,0:T(8,128)(2,1)S(1)}, bf16[128,1024]{1,0:T(8,128)(2,1)S(1)}, u32[]{:S(2)}, u32[]{:S(2)}) %collective-permute-start.3) | collective-permute-done | bytes 262176 | tf_op jit(solution)/shard_map/ppermute | solution.py:89
  30.2 1.8 %collective-permute-start.4 = (bf16[128,1024]{1,0:T(8,128)(2,1)S(1)}, bf16[128,1024]{1,0:T(8,128)(2,1)S(1)}, u32[]{:S(2)}, u32[]{:S(2)}) collective-permute-start(bf16[128,1024]{1,0:T(8,128)(2,1)S(1)} %add_convert_fusion.1), channel_id=1, source_target_pairs={{0,2},{1,3},{2,0},{3,1},{4,6},{5,7},{6,4},{7,5},{8,10},{9,11},{10,... | collective-permute-start | bytes 786440 | tf_op jit(solution)/shard_map/ppermute | solution.py:91
  32.1 6.5 %collective-permute-done.4 = bf16[128,1024]{1,0:T(8,128)(2,1)S(1)} collective-permute-done((bf16[128,1024]{1,0:T(8,128)(2,1)S(1)}, bf16[128,1024]{1,0:T(8,128)(2,1)S(1)}, u32[]{:S(2)}, u32[]{:S(2)}) %collective-permute-start.4) | collective-permute-done | bytes 262176 | tf_op jit(solution)/shard_map/ppermute | solution.py:91
  39.3 1.4 %multiply_reduce_fusion = f32[128]{0:T(128)S(1)} fusion(f32[128]{0:T(128)S(1)} %broadcast_multiply_fusion, bf16[256,1024]{1,0:T(8,128)(2,1)} %copy-done.3, s32[]{:T(128)S(6)} %select_n.135, f32[1024]{0:T(1024)S(1)} %copy-done.7, bf16[128,1024]{1,0:T(8,128)(2,1)} %copy-done.4, bf16[128,1024]{1,0:T(8,128)(2,1)S(1)} %add_convert_fusion.1), kind=kLoop, calls=%fused_computation.55 | loop fusion | flops 1179520 | bytes 791556 | tf_op jit(solution)/shard_map/reduce_sum | solution.py:14
  40.7 1.9 %add_convert_fusion = bf16[128,1024]{1,0:T(8,128)(2,1)} fusion(f32[1024]{0:T(1024)S(1)} %copy-done.12, f32[1024]{0:T(1024)S(1)} %copy-done.13, f32[128]{0:T(128)S(1)} %add_rsqrt_fusion.1, f32[128]{0:T(128)S(1)} %broadcast_multiply_fusion, bf16[256,1024]{1,0:T(8,128)(2,1)} %copy-done.3, s32[]{:T(128)S(6)} %select_n.135, f32[1024]{0:T(1024)S(1)} %copy-done.7, ...), kind=kLoop, calls=%fused_computation.54 | loop fusion | flops 1441792 | bytes 1061892 | tf_op jit(solution)/shard_map/convert_element_type | solution.py:94
  47.4 1.8 %collective-permute-start.6 = (bf16[16,256]{1,0:T(8,128)(2,1)S(1)}, bf16[16,256]{1,0:T(8,128)(2,1)S(1)}, u32[]{:S(2)}, u32[]{:S(2)}) collective-permute-start(bf16[16,256]{1,0:T(8,128)(2,1)S(1)} %fusion.67), channel_id=1, source_target_pairs={{0,4},{4,0},{8,12},{12,8},{16,20},{20,16},{24,28},{28,24},{1,5},{5... | collective-permute-start | bytes 24584 | tf_op jit(solution)/shard_map/ppermute | solution.py:58
  49.3 1.8 %collective-permute-done.6 = bf16[16,256]{1,0:T(8,128)(2,1)S(1)} collective-permute-done((bf16[16,256]{1,0:T(8,128)(2,1)S(1)}, bf16[16,256]{1,0:T(8,128)(2,1)S(1)}, u32[]{:S(2)}, u32[]{:S(2)}) %collective-permute-start.6) | collective-permute-done | bytes 8224 | tf_op jit(solution)/shard_map/ppermute | solution.py:58
  51.1 1.8 %collective-permute-start.7 = (bf16[32,256]{1,0:T(8,128)(2,1)S(1)}, bf16[32,256]{1,0:T(8,128)(2,1)S(1)}, u32[]{:S(2)}, u32[]{:S(2)}) collective-permute-start(bf16[32,256]{1,0:T(8,128)(2,1)S(1)} %maximum_select_fusion.3), channel_id=1, source_target_pairs={{0,8},{4,12},{8,0},{12,4},{16,24},{20,28},{24,16},{28,20},{1,9},{5... | collective-permute-start | bytes 49160 | tf_op jit(solution)/shard_map/ppermute | solution.py:58
  53.0 1.8 %collective-permute-done.7 = bf16[32,256]{1,0:T(8,128)(2,1)S(1)} collective-permute-done((bf16[32,256]{1,0:T(8,128)(2,1)S(1)}, bf16[32,256]{1,0:T(8,128)(2,1)S(1)}, u32[]{:S(2)}, u32[]{:S(2)}) %collective-permute-start.7) | collective-permute-done | bytes 16416 | tf_op jit(solution)/shard_map/ppermute | solution.py:58
  54.8 2.9 %collective-permute-start.8 = (bf16[64,256]{1,0:T(8,128)(2,1)S(1)}, bf16[64,256]{1,0:T(8,128)(2,1)S(1)}, u32[]{:S(2)}, u32[]{:S(2)}) collective-permute-start(bf16[64,256]{1,0:T(8,128)(2,1)S(1)} %maximum_select_fusion.2), channel_id=1, source_target_pairs={{0,16},{4,20},{8,24},{12,28},{16,0},{20,4},{24,8},{28,12},{1,17},{... | collective-permute-start | bytes 98312 | tf_op jit(solution)/shard_map/ppermute | solution.py:228
  61.0 1.3 %fusion.2 = f32[64,64]{1,0:T(8,128)S(1)} fusion(f32[64,64,256]{2,1,0:T(8,128)S(1)} %fusion.22, s32[64,64]{1,0:T(8,128)S(1)} %get-tuple-element.14), kind=kLoop, calls=%fused_computation.3 | loop fusion | flops 2093056 | bytes 4227072 | tf_op jit(solution)/shard_map/reduce_sum | solution.py:193
  62.4 2.9 %collective-permute-start.9 = (f32[64,64]{1,0:T(8,128)S(1)}, f32[64,64]{1,0:T(8,128)S(1)}, u32[]{:S(2)}, u32[]{:S(2)}) collective-permute-start(f32[64,64]{1,0:T(8,128)S(1)} %dynamic-slice_select_fusion), channel_id=1, source_target_pairs={{0,16},{4,20},{8,24},{12,28},{16,0},{20,4},{24,8},{28,12},{1,17},{... | collective-permute-start | bytes 49160 | tf_op jit(solution)/shard_map/ppermute | solution.py:241
  67.3 1.9 %collective-permute-start.10 = (f32[32,64]{1,0:T(8,128)S(1)}, f32[32,64]{1,0:T(8,128)S(1)}, u32[]{:S(2)}, u32[]{:S(2)}) collective-permute-start(f32[32,64]{1,0:T(8,128)S(1)} %constant_dynamic-slice_fusion.1), channel_id=1, source_target_pairs={{0,8},{4,12},{8,0},{12,4},{16,24},{20,28},{24,16},{28,20},{1,9},{5... | collective-permute-start | bytes 24584 | tf_op jit(solution)/shard_map/ppermute | solution.py:47
  69.2 1.9 %collective-permute-done.10 = f32[32,64]{1,0:T(8,128)S(1)} collective-permute-done((f32[32,64]{1,0:T(8,128)S(1)}, f32[32,64]{1,0:T(8,128)S(1)}, u32[]{:S(2)}, u32[]{:S(2)}) %collective-permute-start.10) | collective-permute-done | bytes 8224 | tf_op jit(solution)/shard_map/ppermute | solution.py:47
  71.1 1.8 %collective-permute-start.11 = (f32[16,64]{1,0:T(8,128)S(1)}, f32[16,64]{1,0:T(8,128)S(1)}, u32[]{:S(2)}, u32[]{:S(2)}) collective-permute-start(f32[16,64]{1,0:T(8,128)S(1)} %constant_dynamic-slice_fusion), channel_id=1, source_target_pairs={{0,4},{4,0},{8,12},{12,8},{16,20},{20,16},{24,28},{28,24},{1,5},{5... | collective-permute-start | bytes 12296 | tf_op jit(solution)/shard_map/ppermute | solution.py:47
  72.9 1.9 %collective-permute-done.11 = f32[16,64]{1,0:T(8,128)S(1)} collective-permute-done((f32[16,64]{1,0:T(8,128)S(1)}, f32[16,64]{1,0:T(8,128)S(1)}, u32[]{:S(2)}, u32[]{:S(2)}) %collective-permute-start.11) | collective-permute-done | bytes 4128 | tf_op jit(solution)/shard_map/ppermute | solution.py:47
  75.9 1.7 %collective-permute-start.13 = (f32[16,64]{1,0:T(8,128)S(1)}, f32[16,64]{1,0:T(8,128)S(1)}, u32[]{:S(2)}, u32[]{:S(2)}) collective-permute-start(f32[16,64]{1,0:T(8,128)S(1)} %add.220), channel_id=1, source_target_pairs={{0,2},{1,3},{2,0},{3,1},{4,6},{5,7},{6,4},{7,5},{8,10},{9,11},{10,... | collective-permute-start | bytes 12296 | tf_op jit(solution)/shard_map/ppermute | solution.py:244
  77.7 1.9 %collective-permute-done.13 = f32[16,64]{1,0:T(8,128)S(1)} collective-permute-done((f32[16,64]{1,0:T(8,128)S(1)}, f32[16,64]{1,0:T(8,128)S(1)}, u32[]{:S(2)}, u32[]{:S(2)}) %collective-permute-start.13) | collective-permute-done | bytes 4128 | tf_op jit(solution)/shard_map/ppermute | solution.py:244
  (94 shorter events, 20.5 us)
Async XLA Ops:
  0.6 22.4 %copy-start = (bf16[1024,1024]{1,0:T(8,128)(2,1)S(1)}, bf16[1024,1024]{1,0:T(8,128)(2,1)}, u32[]{:S(2)}) copy-start(bf16[1024,1024]{1,0:T(8,128)(2,1)} %param.26) | copy-start | bytes 6291460
  6.8 13.9 %copy-start.2 = (bf16[256,1024]{1,0:T(8,128)(2,1)S(1)}, bf16[256,1024]{1,0:T(8,128)(2,1)}, u32[]{:S(2)}) copy-start(bf16[256,1024]{1,0:T(8,128)(2,1)} %param.16) | copy-start | bytes 1572868
  6.8 13.9 %copy-start.6 = (f32[1024]{0:T(1024)S(1)}, f32[1024]{0:T(1024)}, u32[]{:S(2)}) copy-start(f32[1024]{0:T(1024)} %param.21) | copy-start | bytes 12292
  6.8 14.3 %copy-start.10 = (f32[1024]{0:T(1024)S(1)}, f32[1024]{0:T(1024)}, u32[]{:S(2)}) copy-start(f32[1024]{0:T(1024)} %param.23) | copy-start | bytes 12292
  6.8 14.3 %copy-start.11 = (f32[1024]{0:T(1024)S(1)}, f32[1024]{0:T(1024)}, u32[]{:S(2)}) copy-start(f32[1024]{0:T(1024)} %param.22) | copy-start | bytes 12292
  8.3 1.8 %collective-permute-start = (bf16[128,1024]{1,0:T(8,128)(2,1)S(1)}, bf16[128,1024]{1,0:T(8,128)(2,1)}, u32[]{:S(2)}, u32[]{:S(2)}) collective-permute-start(bf16[128,1024]{1,0:T(8,128)(2,1)S(1)} %constant_dynamic-slice_fusion.3), channel_id=1, source_target_pairs={{0,1},{1,0},{2,3},{3,2},{4,5},{5,4},{6,7},{7,6},{8,9},{9,8},{10,11... | collective-permute-start | bytes 786440 | tf_op jit(solution)/shard_map/ppermute | solution.py:89
  8.8 14.3 %copy-start.15 = (f32[1024]{0:T(1024)S(1)}, f32[1024]{0:T(1024)}, u32[]{:S(2)}) copy-start(f32[1024]{0:T(1024)} %param.25) | copy-start | bytes 12292
  11.1 9.5 %collective-permute-start.1 = (bf16[128,1024]{1,0:T(8,128)(2,1)S(1)}, bf16[128,1024]{1,0:T(8,128)(2,1)S(1)}, u32[]{:S(2)}, u32[]{:S(2)}) collective-permute-start(bf16[128,1024]{1,0:T(8,128)(2,1)S(1)} %add_convert_fusion.3), channel_id=1, source_target_pairs={{0,2},{1,3},{2,0},{3,1},{4,6},{5,7},{6,4},{7,5},{8,10},{9,11},{10,... | collective-permute-start | bytes 786440 | tf_op jit(solution)/shard_map/ppermute | solution.py:91
  21.3 1.6 %collective-permute-start.2 = (bf16[128,1024]{1,0:T(8,128)(2,1)S(1)}, bf16[128,1024]{1,0:T(8,128)(2,1)S(1)}, u32[]{:S(2)}, u32[]{:S(2)}) collective-permute-start(bf16[128,1024]{1,0:T(8,128)(2,1)S(1)} %add_convert_fusion.2), channel_id=1, source_target_pairs={{0,1},{1,0},{2,3},{3,2},{4,5},{5,4},{6,7},{7,6},{8,9},{9,8},{10,11... | collective-permute-start | bytes 786440 | tf_op jit(solution)/shard_map/ppermute | solution.py:97
  23.1 15.5 %copy-start.3 = (bf16[256,1024]{1,0:T(8,128)(2,1)}, bf16[256,1024]{1,0:T(8,128)(2,1)S(1)}, u32[]{:S(2)}) copy-start(bf16[256,1024]{1,0:T(8,128)(2,1)S(1)} %maximum_select_fusion) | copy-start | bytes 1572868
  23.1 15.5 %copy-start.7 = (f32[1024]{0:T(1024)S(1)}, f32[1024]{0:T(1024)}, u32[]{:S(2)}) copy-start(f32[1024]{0:T(1024)} %param.27) | copy-start | bytes 12292
  28.4 12.2 %copy-start.12 = (f32[1024]{0:T(1024)S(1)}, f32[1024]{0:T(1024)}, u32[]{:S(2)}) copy-start(f32[1024]{0:T(1024)} %param.29) | copy-start | bytes 12292
  28.5 1.6 %collective-permute-start.3 = (bf16[128,1024]{1,0:T(8,128)(2,1)S(1)}, bf16[128,1024]{1,0:T(8,128)(2,1)S(1)}, u32[]{:S(2)}, u32[]{:S(2)}) collective-permute-start(bf16[128,1024]{1,0:T(8,128)(2,1)S(1)} %constant_dynamic-slice_fusion.2), channel_id=1, source_target_pairs={{0,1},{1,0},{2,3},{3,2},{4,5},{5,4},{6,7},{7,6},{8,9},{9,8},{10,11... | collective-permute-start | bytes 786440 | tf_op jit(solution)/shard_map/ppermute | solution.py:89
  30.2 8.4 %collective-permute-start.4 = (bf16[128,1024]{1,0:T(8,128)(2,1)S(1)}, bf16[128,1024]{1,0:T(8,128)(2,1)S(1)}, u32[]{:S(2)}, u32[]{:S(2)}) collective-permute-start(bf16[128,1024]{1,0:T(8,128)(2,1)S(1)} %add_convert_fusion.1), channel_id=1, source_target_pairs={{0,2},{1,3},{2,0},{3,1},{4,6},{5,7},{6,4},{7,5},{8,10},{9,11},{10,... | collective-permute-start | bytes 786440 | tf_op jit(solution)/shard_map/ppermute | solution.py:91
  39.3 18.4 %copy-start.1 = (bf16[2048,256]{1,0:T(8,128)(2,1)S(1)}, bf16[2048,256]{1,0:T(8,128)(2,1)}, u32[]{:S(2)}) copy-start(bf16[2048,256]{1,0:T(8,128)(2,1)} %param.30) | copy-start | bytes 3145732
  42.6 1.7 %collective-permute-start.5 = (bf16[128,1024]{1,0:T(8,128)(2,1)}, bf16[128,1024]{1,0:T(8,128)(2,1)S(1)}, u32[]{:S(2)}, u32[]{:S(2)}) collective-permute-start(bf16[128,1024]{1,0:T(8,128)(2,1)} %add_convert_fusion), channel_id=1, source_target_pairs={{0,1},{1,0},{2,3},{3,2},{4,5},{5,4},{6,7},{7,6},{8,9},{9,8},{10,11... | collective-permute-start | bytes 786440 | tf_op jit(solution)/shard_map/ppermute | solution.py:97
  47.4 3.7 %collective-permute-start.6 = (bf16[16,256]{1,0:T(8,128)(2,1)S(1)}, bf16[16,256]{1,0:T(8,128)(2,1)S(1)}, u32[]{:S(2)}, u32[]{:S(2)}) collective-permute-start(bf16[16,256]{1,0:T(8,128)(2,1)S(1)} %fusion.67), channel_id=1, source_target_pairs={{0,4},{4,0},{8,12},{12,8},{16,20},{20,16},{24,28},{28,24},{1,5},{5... | collective-permute-start | bytes 24584 | tf_op jit(solution)/shard_map/ppermute | solution.py:58
  51.1 3.7 %collective-permute-start.7 = (bf16[32,256]{1,0:T(8,128)(2,1)S(1)}, bf16[32,256]{1,0:T(8,128)(2,1)S(1)}, u32[]{:S(2)}, u32[]{:S(2)}) collective-permute-start(bf16[32,256]{1,0:T(8,128)(2,1)S(1)} %maximum_select_fusion.3), channel_id=1, source_target_pairs={{0,8},{4,12},{8,0},{12,4},{16,24},{20,28},{24,16},{28,20},{1,9},{5... | collective-permute-start | bytes 49160 | tf_op jit(solution)/shard_map/ppermute | solution.py:58
  54.8 4.9 %collective-permute-start.8 = (bf16[64,256]{1,0:T(8,128)(2,1)S(1)}, bf16[64,256]{1,0:T(8,128)(2,1)S(1)}, u32[]{:S(2)}, u32[]{:S(2)}) collective-permute-start(bf16[64,256]{1,0:T(8,128)(2,1)S(1)} %maximum_select_fusion.2), channel_id=1, source_target_pairs={{0,16},{4,20},{8,24},{12,28},{16,0},{20,4},{24,8},{28,12},{1,17},{... | collective-permute-start | bytes 98312 | tf_op jit(solution)/shard_map/ppermute | solution.py:228
  62.4 4.9 %collective-permute-start.9 = (f32[64,64]{1,0:T(8,128)S(1)}, f32[64,64]{1,0:T(8,128)S(1)}, u32[]{:S(2)}, u32[]{:S(2)}) collective-permute-start(f32[64,64]{1,0:T(8,128)S(1)} %dynamic-slice_select_fusion), channel_id=1, source_target_pairs={{0,16},{4,20},{8,24},{12,28},{16,0},{20,4},{24,8},{28,12},{1,17},{... | collective-permute-start | bytes 49160 | tf_op jit(solution)/shard_map/ppermute | solution.py:241
  67.3 3.8 %collective-permute-start.10 = (f32[32,64]{1,0:T(8,128)S(1)}, f32[32,64]{1,0:T(8,128)S(1)}, u32[]{:S(2)}, u32[]{:S(2)}) collective-permute-start(f32[32,64]{1,0:T(8,128)S(1)} %constant_dynamic-slice_fusion.1), channel_id=1, source_target_pairs={{0,8},{4,12},{8,0},{12,4},{16,24},{20,28},{24,16},{28,20},{1,9},{5... | collective-permute-start | bytes 24584 | tf_op jit(solution)/shard_map/ppermute | solution.py:47
  71.1 3.7 %collective-permute-start.11 = (f32[16,64]{1,0:T(8,128)S(1)}, f32[16,64]{1,0:T(8,128)S(1)}, u32[]{:S(2)}, u32[]{:S(2)}) collective-permute-start(f32[16,64]{1,0:T(8,128)S(1)} %constant_dynamic-slice_fusion), channel_id=1, source_target_pairs={{0,4},{4,0},{8,12},{12,8},{16,20},{20,16},{24,28},{28,24},{1,5},{5... | collective-permute-start | bytes 12296 | tf_op jit(solution)/shard_map/ppermute | solution.py:47
  74.8 1.2 %collective-permute-start.12 = (f32[16,64]{1,0:T(8,128)S(1)}, f32[16,64]{1,0:T(8,128)S(1)}, u32[]{:S(2)}, u32[]{:S(2)}) collective-permute-start(f32[16,64]{1,0:T(8,128)S(1)} %dynamic-slice_add_fusion.1), channel_id=1, source_target_pairs={{0,1},{1,0},{2,3},{3,2},{4,5},{5,4},{6,7},{7,6},{8,9},{9,8},{10,11... | collective-permute-start | bytes 12296 | tf_op jit(solution)/shard_map/ppermute | solution.py:244
  75.9 3.7 %collective-permute-start.13 = (f32[16,64]{1,0:T(8,128)S(1)}, f32[16,64]{1,0:T(8,128)S(1)}, u32[]{:S(2)}, u32[]{:S(2)}) collective-permute-start(f32[16,64]{1,0:T(8,128)S(1)} %add.220), channel_id=1, source_target_pairs={{0,2},{1,3},{2,0},{3,1},{4,6},{5,7},{6,4},{7,5},{8,10},{9,11},{10,... | collective-permute-start | bytes 12296 | tf_op jit(solution)/shard_map/ppermute | solution.py:244
  (6 other events, 26.2 us)

commit v13 on v11

--- a/solution.py
+++ b/solution.py
@@ -82,11 +82,17 @@
 def settle_by_chip(partial_value, residual, bias, gain, shift):
     index = lax.axis_index("tensor")
     low = index % 2
-    half = partial_value.shape[0] // 2
-    rounded = partial_value.astype(jnp.bfloat16)
-    mine = lax.dynamic_slice_in_dim(rounded, low * half, half, 0)
-    theirs = lax.dynamic_slice_in_dim(rounded, (1 - low) * half, half, 0)
-    got = lax.ppermute(theirs, "tensor", xor_pairs(4, 1))
+    if callable(partial_value):
+        half = residual.shape[0] // 2
+        theirs = partial_value((1 - low) * half, half).astype(jnp.bfloat16)
+        got = lax.ppermute(theirs, "tensor", xor_pairs(4, 1))
+        mine = partial_value(low * half, half).astype(jnp.bfloat16)
+    else:
+        half = partial_value.shape[0] // 2
+        rounded = partial_value.astype(jnp.bfloat16)
+        mine = lax.dynamic_slice_in_dim(rounded, low * half, half, 0)
+        theirs = lax.dynamic_slice_in_dim(rounded, (1 - low) * half, half, 0)
+        got = lax.ppermute(theirs, "tensor", xor_pairs(4, 1))
     chip_sum = (mine.astype(jnp.float32) + got.astype(jnp.float32)).astype(jnp.bfloat16)
     across = lax.ppermute(chip_sum, "tensor", xor_pairs(4, 2))
     total = chip_sum.astype(jnp.float32) + across.astype(jnp.float32)
@@ -137,8 +143,16 @@
     weights = (expo / jnp.sum(expo, axis=-1, keepdims=True)).astype(jnp.bfloat16)
     context = jnp.einsum("hts,shd->thd", weights, values, preferred_element_type=jnp.float32)
     context = context.astype(jnp.bfloat16).reshape(tokens_here, local_width)
-    partial_value = jnp.dot(context, w_output, preferred_element_type=jnp.float32)
-    attended = settle(partial_value, hidden, b_output, first_gain, first_shift, n_tensor)
+    if n_tensor == 4 and tokens_here % 2 == 0:
+
+        def projected_rows(start, count):
+            rows = lax.dynamic_slice_in_dim(context, start, count, 0)
+            return jnp.dot(rows, w_output, preferred_element_type=jnp.float32)
+
+        attended = settle_by_chip(projected_rows, hidden, b_output, first_gain, first_shift)
+    else:
+        partial_value = jnp.dot(context, w_output, preferred_element_type=jnp.float32)
+        attended = settle(partial_value, hidden, b_output, first_gain, first_shift, n_tensor)
     activated = jax.nn.gelu(
         jnp.dot(attended, w_up, preferred_element_type=jnp.float32) + b_up, approximate=False
     ).astype(jnp.bfloat16)

time: 77.1 us -> 77.2 us (level)
  matrix products: 14.3 us -> 16 us
  other arithmetic: 6.51 us -> 5.5 us
    convert_element_type x2 -> x1, other arithmetic: 1.08 us -> 0.07 us  [settle_by_chip(): (mine.astype(jnp.float32) + got.astype(jnp.float32)).astype(jnp.bfloat16)]
    dot_general x1, matrix products: 0.34 us -> 1.33 us  [body(): jnp.einsum('thd,shd->hts', queries, keys, preferred_element_type=jnp.floa...]
where the time goes in v13:
time: 77.2 us; the launch traced here: 76.9 us
  waiting for transfers between devices  33.3 us (43%)
  starting transfers between devices  20.4 us (26%)
  matrix products  16 us (21%)
  other arithmetic  5.5 us (7%)
  between operations  1.09 us (1%)
    ppermute x2, waiting for transfers between devices, settle_by_chip(): across = lax.ppermute(chip_sum, 'tensor', xor_pairs(4, 2))  13.2 us
    ppermute x3, starting transfers between devices, reduce_scatter_xor(): got = lax.ppermute(theirs.astype(wire), axis, xor_pairs(n, k))  6.58 us
    ppermute x3, starting transfers between devices, all_gather_xor(): other = lax.ppermute(cur, axis, xor_pairs(n, k))  6.51 us
    ppermute x3, waiting for transfers between devices, reduce_scatter_xor(): got = lax.ppermute(theirs.astype(wire), axis, xor_pairs(n, k))  5.75 us
    ppermute x3, waiting for transfers between devices, all_gather_xor(): other = lax.ppermute(cur, axis, xor_pairs(n, k))  5.55 us
    dot_general x1, matrix products, body(): jnp.dot(activated, w_down, preferred_element_type=jnp.float32)  5.11 us
    ppermute x2, starting transfers between devices, settle_by_chip(): across = lax.ppermute(chip_sum, 'tensor', xor_pairs(4, 2))  4.72 us
    ppermute x2, waiting for transfers between devices, body(): lax.ppermute(text_scores, 'tensor', xor_pairs(n_tensor, k))  3.09 us
  transfers between devices with their start and end apart: 14, of which 14 were waited for; matrix products, arithmetic and copies ran while one was open for 0% of the time, Pallas kernels for 0%

profile of v13, /device:TPU:0, one launch (start us, length us, event | category | flops | bytes accessed | tf_op | source)
XLA Modules:
  0.0 76.9 jit_solution(5639996235050032173)
XLA Ops:
  0.7 2.3 %fusion.110 = (bf16[3,256,256]{1,2,0:T(8,128)(2,1)S(1)}, f32[3,256,256]{1,2,0:T(8,128)S(1)}) fusion(f32[3,256]{1,0:T(4,128)} %param.19, bf16[3,1024,256]{2,1,0:T(8,128)(2,1)} %param.18, bf16[256,1024]{1,0:T(8,128)(2,1)} %param.16), kind=kOutput, calls=%fused_computation.173 | convolution fusion | flops 403046400 | bytes 3279872 | tf_op jit(solution)/shard_map/td,jdf->jtf/dot_general | solution.py:131
  5.4 2.0 %convolution_convert_fusion.3 = bf16[4,64,256]{2,1,0:T(8,128)(2,1)S(1)} fusion(bf16[256,4,64]{0,2,1:T(8,128)(2,1)S(1)} %bitcast.44, f32[4,256]{1,0:T(4,128)S(1)} %fusion.111, f32[4,256,256]{1,2,0:T(8,128)} %convolution_select_fusion), kind=kOutput, calls=%fused_computation.16 | convolution fusion | flops 34407680 | bytes 1314816 | tf_op jit(solution)/shard_map/hts,shd->thd/dot_general | solution.py:144
  10.7 2.9 %collective-permute-start.1 = (bf16[128,1024]{1,0:T(8,128)(2,1)S(1)}, bf16[128,1024]{1,0:T(8,128)(2,1)S(1)}, u32[]{:S(2)}, u32[]{:S(2)}) collective-permute-start(bf16[128,1024]{1,0:T(8,128)(2,1)S(1)} %add_convert_fusion.3), channel_id=1, source_target_pairs={{0,2},{1,3},{2,0},{3,1},{4,6},{5,7},{6,4},{7,5},{8,10},{9,11},{10,... | collective-permute-start | bytes 786440 | tf_op jit(solution)/shard_map/ppermute | solution.py:97
  13.7 6.6 %collective-permute-done.1 = bf16[128,1024]{1,0:T(8,128)(2,1)S(1)} collective-permute-done((bf16[128,1024]{1,0:T(8,128)(2,1)S(1)}, bf16[128,1024]{1,0:T(8,128)(2,1)S(1)}, u32[]{:S(2)}, u32[]{:S(2)}) %collective-permute-start.1) | collective-permute-done | bytes 262176 | tf_op jit(solution)/shard_map/ppermute | solution.py:97
  21.0 1.5 %collective-permute-done.2 = bf16[128,1024]{1,0:T(8,128)(2,1)S(1)} collective-permute-done((bf16[128,1024]{1,0:T(8,128)(2,1)S(1)}, bf16[128,1024]{1,0:T(8,128)(2,1)S(1)}, u32[]{:S(2)}, u32[]{:S(2)}) %collective-permute-start.2) | collective-permute-done | bytes 262176 | tf_op jit(solution)/shard_map/ppermute | solution.py:103
  22.7 5.1 %convolution_convert_fusion = bf16[256,1024]{1,0:T(8,128)(2,1)S(1)} fusion(bf16[1024,1024]{1,0:T(8,128)(2,1)S(1)} %copy-done, bf16[256,1024]{1,0:T(8,128)(2,1)S(1)} %maximum_select_fusion, bf16[1024,1024]{1,0:T(8,128)(2,1)} %param.24, f32[1024]{0:T(1024)S(1)} %copy-done.13), kind=kOutput, calls=%fused_computation.10 | convolution fusion | flops 1091305472 | bytes 5246976 | tf_op jit(solution)/shard_map/dot_general | solution.py:159
  29.6 1.8 %collective-permute-start.4 = (bf16[128,1024]{1,0:T(8,128)(2,1)S(1)}, bf16[128,1024]{1,0:T(8,128)(2,1)S(1)}, u32[]{:S(2)}, u32[]{:S(2)}) collective-permute-start(bf16[128,1024]{1,0:T(8,128)(2,1)S(1)} %add_convert_fusion.1), channel_id=1, source_target_pairs={{0,2},{1,3},{2,0},{3,1},{4,6},{5,7},{6,4},{7,5},{8,10},{9,11},{10,... | collective-permute-start | bytes 786440 | tf_op jit(solution)/shard_map/ppermute | solution.py:97
  31.4 6.6 %collective-permute-done.4 = bf16[128,1024]{1,0:T(8,128)(2,1)S(1)} collective-permute-done((bf16[128,1024]{1,0:T(8,128)(2,1)S(1)}, bf16[128,1024]{1,0:T(8,128)(2,1)S(1)}, u32[]{:S(2)}, u32[]{:S(2)}) %collective-permute-start.4) | collective-permute-done | bytes 262176 | tf_op jit(solution)/shard_map/ppermute | solution.py:97
  40.9 1.8 %collective-permute-start.6 = (bf16[16,256]{1,0:T(8,128)(2,1)S(1)}, bf16[16,256]{1,0:T(8,128)(2,1)S(1)}, u32[]{:S(2)}, u32[]{:S(2)}) collective-permute-start(bf16[16,256]{1,0:T(8,128)(2,1)S(1)} %fusion.69), channel_id=1, source_target_pairs={{0,4},{4,0},{8,12},{12,8},{16,20},{20,16},{24,28},{28,24},{1,5},{5... | collective-permute-start | bytes 24584 | tf_op jit(solution)/shard_map/ppermute | solution.py:58
  42.6 1.9 %collective-permute-done.6 = bf16[16,256]{1,0:T(8,128)(2,1)S(1)} collective-permute-done((bf16[16,256]{1,0:T(8,128)(2,1)S(1)}, bf16[16,256]{1,0:T(8,128)(2,1)S(1)}, u32[]{:S(2)}, u32[]{:S(2)}) %collective-permute-start.6) | collective-permute-done | bytes 8224 | tf_op jit(solution)/shard_map/ppermute | solution.py:58
  44.5 1.8 %collective-permute-start.7 = (bf16[32,256]{1,0:T(8,128)(2,1)S(1)}, bf16[32,256]{1,0:T(8,128)(2,1)S(1)}, u32[]{:S(2)}, u32[]{:S(2)}) collective-permute-start(bf16[32,256]{1,0:T(8,128)(2,1)S(1)} %maximum_select_fusion.5), channel_id=1, source_target_pairs={{0,8},{4,12},{8,0},{12,4},{16,24},{20,28},{24,16},{28,20},{1,9},{5... | collective-permute-start | bytes 49160 | tf_op jit(solution)/shard_map/ppermute | solution.py:58
  46.4 1.8 %collective-permute-done.7 = bf16[32,256]{1,0:T(8,128)(2,1)S(1)} collective-permute-done((bf16[32,256]{1,0:T(8,128)(2,1)S(1)}, bf16[32,256]{1,0:T(8,128)(2,1)S(1)}, u32[]{:S(2)}, u32[]{:S(2)}) %collective-permute-start.7) | collective-permute-done | bytes 16416 | tf_op jit(solution)/shard_map/ppermute | solution.py:58
  48.3 2.9 %collective-permute-start.8 = (bf16[64,256]{1,0:T(8,128)(2,1)S(1)}, bf16[64,256]{1,0:T(8,128)(2,1)S(1)}, u32[]{:S(2)}, u32[]{:S(2)}) collective-permute-start(bf16[64,256]{1,0:T(8,128)(2,1)S(1)} %maximum_select_fusion.4), channel_id=1, source_target_pairs={{0,16},{4,20},{8,24},{12,28},{16,0},{20,4},{24,8},{28,12},{1,17},{... | collective-permute-start | bytes 98312 | tf_op jit(solution)/shard_map/ppermute | solution.py:58
  51.3 1.9 %collective-permute-done.8 = bf16[64,256]{1,0:T(8,128)(2,1)S(1)} collective-permute-done((bf16[64,256]{1,0:T(8,128)(2,1)S(1)}, bf16[64,256]{1,0:T(8,128)(2,1)S(1)}, u32[]{:S(2)}, u32[]{:S(2)}) %collective-permute-start.8) | collective-permute-done | bytes 32800 | tf_op jit(solution)/shard_map/ppermute | solution.py:58
  53.1 1.7 %convert_bitcast_fusion = (bf16[16,8,16,128]{3,1,2,0:T(8,128)(2,1)S(1)}, bf16[16,8,16,128]{3,1,2,0:T(8,128)(2,1)S(1)}) fusion(bf16[2048,256]{1,0:T(8,128)(2,1)} %param.30, bf16[64,256]{1,0:T(8,128)(2,1)S(1)} %collective-permute-done.8, bf16[64,256]{1,0:T(8,128)(2,1)S(1)} %maximum_select_fusion.4, pred[]{:T(512)S(6)} %eq.90), kind=kOutput, calls=%fused_computation.89 | convolution fusion | flops 135561216 | bytes 2162689 | tf_op jit(solution)/shard_map/dot_general | solution.py:192
  56.4 2.7 %fusion.2 = f32[128,64]{1,0:T(8,128)S(1)} fusion(f32[128,64,256]{2,1,0:T(8,128)S(1)} %fusion.10, s32[128,64]{1,0:T(8,128)S(1)} %get-tuple-element.6), kind=kLoop, calls=%fused_computation.3 | loop fusion | flops 4186112 | bytes 8454144 | tf_op jit(solution)/shard_map/reduce_sum | solution.py:211
  59.1 2.9 %collective-permute-start.9 = (f32[64,64]{1,0:T(8,128)S(1)}, f32[64,64]{1,0:T(8,128)S(1)}, u32[]{:S(2)}, u32[]{:S(2)}) collective-permute-start(f32[64,64]{1,0:T(8,128)S(1)} %constant_dynamic-slice_fusion.2), channel_id=1, source_target_pairs={{0,16},{4,20},{8,24},{12,28},{16,0},{20,4},{24,8},{28,12},{1,17},{... | collective-permute-start | bytes 49160 | tf_op jit(solution)/shard_map/ppermute | solution.py:47
  62.1 1.9 %collective-permute-done.9 = f32[64,64]{1,0:T(8,128)S(1)} collective-permute-done((f32[64,64]{1,0:T(8,128)S(1)}, f32[64,64]{1,0:T(8,128)S(1)}, u32[]{:S(2)}, u32[]{:S(2)}) %collective-permute-start.9) | collective-permute-done | bytes 16416 | tf_op jit(solution)/shard_map/ppermute | solution.py:47
  64.0 1.9 %collective-permute-start.10 = (f32[32,64]{1,0:T(8,128)S(1)}, f32[32,64]{1,0:T(8,128)S(1)}, u32[]{:S(2)}, u32[]{:S(2)}) collective-permute-start(f32[32,64]{1,0:T(8,128)S(1)} %constant_dynamic-slice_fusion.1), channel_id=1, source_target_pairs={{0,8},{4,12},{8,0},{12,4},{16,24},{20,28},{24,16},{28,20},{1,9},{5... | collective-permute-start | bytes 24584 | tf_op jit(solution)/shard_map/ppermute | solution.py:47
  65.9 1.9 %collective-permute-done.10 = f32[32,64]{1,0:T(8,128)S(1)} collective-permute-done((f32[32,64]{1,0:T(8,128)S(1)}, f32[32,64]{1,0:T(8,128)S(1)}, u32[]{:S(2)}, u32[]{:S(2)}) %collective-permute-start.10) | collective-permute-done | bytes 8224 | tf_op jit(solution)/shard_map/ppermute | solution.py:47
  67.8 1.8 %collective-permute-start.11 = (f32[16,64]{1,0:T(8,128)S(1)}, f32[16,64]{1,0:T(8,128)S(1)}, u32[]{:S(2)}, u32[]{:S(2)}) collective-permute-start(f32[16,64]{1,0:T(8,128)S(1)} %constant_dynamic-slice_fusion), channel_id=1, source_target_pairs={{0,4},{4,0},{8,12},{12,8},{16,20},{20,16},{24,28},{28,24},{1,5},{5... | collective-permute-start | bytes 12296 | tf_op jit(solution)/shard_map/ppermute | solution.py:47
  69.6 1.9 %collective-permute-done.11 = f32[16,64]{1,0:T(8,128)S(1)} collective-permute-done((f32[16,64]{1,0:T(8,128)S(1)}, f32[16,64]{1,0:T(8,128)S(1)}, u32[]{:S(2)}, u32[]{:S(2)}) %collective-permute-start.11) | collective-permute-done | bytes 4128 | tf_op jit(solution)/shard_map/ppermute | solution.py:47
  72.7 1.7 %collective-permute-start.13 = (f32[16,64]{1,0:T(8,128)S(1)}, f32[16,64]{1,0:T(8,128)S(1)}, u32[]{:S(2)}, u32[]{:S(2)}) collective-permute-start(f32[16,64]{1,0:T(8,128)S(1)} %add.209), channel_id=1, source_target_pairs={{0,2},{1,3},{2,0},{3,1},{4,6},{5,7},{6,4},{7,5},{8,10},{9,11},{10,... | collective-permute-start | bytes 12296 | tf_op jit(solution)/shard_map/ppermute | solution.py:239
  74.4 1.9 %collective-permute-done.13 = f32[16,64]{1,0:T(8,128)S(1)} collective-permute-done((f32[16,64]{1,0:T(8,128)S(1)}, f32[16,64]{1,0:T(8,128)S(1)}, u32[]{:S(2)}, u32[]{:S(2)}) %collective-permute-start.13) | collective-permute-done | bytes 4128 | tf_op jit(solution)/shard_map/ppermute | solution.py:239
  (82 shorter events, 14.5 us)
Async XLA Ops:
  0.6 22.1 %copy-start = (bf16[1024,1024]{1,0:T(8,128)(2,1)S(1)}, bf16[1024,1024]{1,0:T(8,128)(2,1)}, u32[]{:S(2)}) copy-start(bf16[1024,1024]{1,0:T(8,128)(2,1)} %param.26) | copy-start | bytes 6291460
  5.4 14.9 %copy-start.4 = (f32[1024]{0:T(1024)S(1)}, f32[1024]{0:T(1024)}, u32[]{:S(2)}) copy-start(f32[1024]{0:T(1024)} %param.21) | copy-start | bytes 12292
  7.4 12.9 %copy-start.1 = (bf16[256,1024]{1,0:T(8,128)(2,1)S(1)}, bf16[256,1024]{1,0:T(8,128)(2,1)}, u32[]{:S(2)}) copy-start(bf16[256,1024]{1,0:T(8,128)(2,1)} %param.16) | copy-start | bytes 1572868
  7.4 13.3 %copy-start.7 = (f32[1024]{0:T(1024)S(1)}, f32[1024]{0:T(1024)}, u32[]{:S(2)}) copy-start(f32[1024]{0:T(1024)} %param.23) | copy-start | bytes 12292
  7.4 13.3 %copy-start.8 = (f32[1024]{0:T(1024)S(1)}, f32[1024]{0:T(1024)}, u32[]{:S(2)}) copy-start(f32[1024]{0:T(1024)} %param.22) | copy-start | bytes 12292
  7.7 1.8 %collective-permute-start = (bf16[128,1024]{1,0:T(8,128)(2,1)S(1)}, bf16[128,1024]{1,0:T(8,128)(2,1)}, u32[]{:S(2)}, u32[]{:S(2)}) collective-permute-start(bf16[128,1024]{1,0:T(8,128)(2,1)S(1)} %convolution_convert_fusion.1), channel_id=1, source_target_pairs={{0,1},{1,0},{2,3},{3,2},{4,5},{5,4},{6,7},{7,6},{8,9},{9,8},{10,11... | collective-permute-start | bytes 786440 | tf_op jit(solution)/shard_map/ppermute | solution.py:88
  10.7 12.0 %copy-start.13 = (f32[1024]{0:T(1024)S(1)}, f32[1024]{0:T(1024)}, u32[]{:S(2)}) copy-start(f32[1024]{0:T(1024)} %param.25) | copy-start | bytes 12292
  10.7 9.5 %collective-permute-start.1 = (bf16[128,1024]{1,0:T(8,128)(2,1)S(1)}, bf16[128,1024]{1,0:T(8,128)(2,1)S(1)}, u32[]{:S(2)}, u32[]{:S(2)}) collective-permute-start(bf16[128,1024]{1,0:T(8,128)(2,1)S(1)} %add_convert_fusion.3), channel_id=1, source_target_pairs={{0,2},{1,3},{2,0},{3,1},{4,6},{5,7},{6,4},{7,5},{8,10},{9,11},{10,... | collective-permute-start | bytes 786440 | tf_op jit(solution)/shard_map/ppermute | solution.py:97
  21.0 1.6 %collective-permute-start.2 = (bf16[128,1024]{1,0:T(8,128)(2,1)S(1)}, bf16[128,1024]{1,0:T(8,128)(2,1)S(1)}, u32[]{:S(2)}, u32[]{:S(2)}) collective-permute-start(bf16[128,1024]{1,0:T(8,128)(2,1)S(1)} %add_convert_fusion.2), channel_id=1, source_target_pairs={{0,1},{1,0},{2,3},{3,2},{4,5},{5,4},{6,7},{7,6},{8,9},{9,8},{10,11... | collective-permute-start | bytes 786440 | tf_op jit(solution)/shard_map/ppermute | solution.py:103
  22.7 15.3 %copy-start.5 = (f32[1024]{0:T(1024)S(1)}, f32[1024]{0:T(1024)}, u32[]{:S(2)}) copy-start(f32[1024]{0:T(1024)} %param.27) | copy-start | bytes 12292
  27.9 10.9 %copy-start.12 = (s32[1,16]{1,0:T(1,128)S(1)}, s32[1,16]{1,0:T(1,128)}, u32[]{:S(2)}) copy-start(s32[1,16]{1,0:T(1,128)} %param.17) | copy-start | bytes 196
  27.9 1.6 %collective-permute-start.3 = (bf16[128,1024]{1,0:T(8,128)(2,1)S(1)}, bf16[128,1024]{1,0:T(8,128)(2,1)S(1)}, u32[]{:S(2)}, u32[]{:S(2)}) collective-permute-start(bf16[128,1024]{1,0:T(8,128)(2,1)S(1)} %constant_dynamic-slice_fusion.3), channel_id=1, source_target_pairs={{0,1},{1,0},{2,3},{3,2},{4,5},{5,4},{6,7},{7,6},{8,9},{9,8},{10,11... | collective-permute-start | bytes 786440 | tf_op jit(solution)/shard_map/ppermute | solution.py:95
  29.6 16.7 %copy-start.6 = (s32[128,64]{0,1:T(8,128)S(1)}, s32[128,64]{0,1:T(8,128)}, u32[]{:S(2)}) copy-start(s32[128,64]{0,1:T(8,128)} %param.31) | copy-start | bytes 98308
  29.6 8.4 %collective-permute-start.4 = (bf16[128,1024]{1,0:T(8,128)(2,1)S(1)}, bf16[128,1024]{1,0:T(8,128)(2,1)S(1)}, u32[]{:S(2)}, u32[]{:S(2)}) collective-permute-start(bf16[128,1024]{1,0:T(8,128)(2,1)S(1)} %add_convert_fusion.1), channel_id=1, source_target_pairs={{0,2},{1,3},{2,0},{3,1},{4,6},{5,7},{6,4},{7,5},{8,10},{9,11},{10,... | collective-permute-start | bytes 786440 | tf_op jit(solution)/shard_map/ppermute | solution.py:97
  38.7 1.6 %collective-permute-start.5 = (bf16[128,1024]{1,0:T(8,128)(2,1)S(1)}, bf16[128,1024]{1,0:T(8,128)(2,1)S(1)}, u32[]{:S(2)}, u32[]{:S(2)}) collective-permute-start(bf16[128,1024]{1,0:T(8,128)(2,1)S(1)} %add_convert_fusion), channel_id=1, source_target_pairs={{0,1},{1,0},{2,3},{3,2},{4,5},{5,4},{6,7},{7,6},{8,9},{9,8},{10,11... | collective-permute-start | bytes 786440 | tf_op jit(solution)/shard_map/ppermute | solution.py:103
  40.5 14.5 %copy-start.3 = (bf16[256,1024]{1,0:T(8,128)(2,1)}, bf16[256,1024]{1,0:T(8,128)(2,1)S(1)}, u32[]{:S(2)}) copy-start(bf16[256,1024]{1,0:T(8,128)(2,1)S(1)} %maximum_select_fusion.1) | copy-start | bytes 1572868
  40.9 3.7 %collective-permute-start.6 = (bf16[16,256]{1,0:T(8,128)(2,1)S(1)}, bf16[16,256]{1,0:T(8,128)(2,1)S(1)}, u32[]{:S(2)}, u32[]{:S(2)}) collective-permute-start(bf16[16,256]{1,0:T(8,128)(2,1)S(1)} %fusion.69), channel_id=1, source_target_pairs={{0,4},{4,0},{8,12},{12,8},{16,20},{20,16},{24,28},{28,24},{1,5},{5... | collective-permute-start | bytes 24584 | tf_op jit(solution)/shard_map/ppermute | solution.py:58
  44.5 3.7 %collective-permute-start.7 = (bf16[32,256]{1,0:T(8,128)(2,1)S(1)}, bf16[32,256]{1,0:T(8,128)(2,1)S(1)}, u32[]{:S(2)}, u32[]{:S(2)}) collective-permute-start(bf16[32,256]{1,0:T(8,128)(2,1)S(1)} %maximum_select_fusion.5), channel_id=1, source_target_pairs={{0,8},{4,12},{8,0},{12,4},{16,24},{20,28},{24,16},{28,20},{1,9},{5... | collective-permute-start | bytes 49160 | tf_op jit(solution)/shard_map/ppermute | solution.py:58
  48.3 4.9 %collective-permute-start.8 = (bf16[64,256]{1,0:T(8,128)(2,1)S(1)}, bf16[64,256]{1,0:T(8,128)(2,1)S(1)}, u32[]{:S(2)}, u32[]{:S(2)}) collective-permute-start(bf16[64,256]{1,0:T(8,128)(2,1)S(1)} %maximum_select_fusion.4), channel_id=1, source_target_pairs={{0,16},{4,20},{8,24},{12,28},{16,0},{20,4},{24,8},{28,12},{1,17},{... | collective-permute-start | bytes 98312 | tf_op jit(solution)/shard_map/ppermute | solution.py:58
  59.1 4.9 %collective-permute-start.9 = (f32[64,64]{1,0:T(8,128)S(1)}, f32[64,64]{1,0:T(8,128)S(1)}, u32[]{:S(2)}, u32[]{:S(2)}) collective-permute-start(f32[64,64]{1,0:T(8,128)S(1)} %constant_dynamic-slice_fusion.2), channel_id=1, source_target_pairs={{0,16},{4,20},{8,24},{12,28},{16,0},{20,4},{24,8},{28,12},{1,17},{... | collective-permute-start | bytes 49160 | tf_op jit(solution)/shard_map/ppermute | solution.py:47
  64.0 3.8 %collective-permute-start.10 = (f32[32,64]{1,0:T(8,128)S(1)}, f32[32,64]{1,0:T(8,128)S(1)}, u32[]{:S(2)}, u32[]{:S(2)}) collective-permute-start(f32[32,64]{1,0:T(8,128)S(1)} %constant_dynamic-slice_fusion.1), channel_id=1, source_target_pairs={{0,8},{4,12},{8,0},{12,4},{16,24},{20,28},{24,16},{28,20},{1,9},{5... | collective-permute-start | bytes 24584 | tf_op jit(solution)/shard_map/ppermute | solution.py:47
  67.8 3.7 %collective-permute-start.11 = (f32[16,64]{1,0:T(8,128)S(1)}, f32[16,64]{1,0:T(8,128)S(1)}, u32[]{:S(2)}, u32[]{:S(2)}) collective-permute-start(f32[16,64]{1,0:T(8,128)S(1)} %constant_dynamic-slice_fusion), channel_id=1, source_target_pairs={{0,4},{4,0},{8,12},{12,8},{16,20},{20,16},{24,28},{28,24},{1,5},{5... | collective-permute-start | bytes 12296 | tf_op jit(solution)/shard_map/ppermute | solution.py:47
  71.5 1.2 %collective-permute-start.12 = (f32[16,64]{1,0:T(8,128)S(1)}, f32[16,64]{1,0:T(8,128)S(1)}, u32[]{:S(2)}, u32[]{:S(2)}) collective-permute-start(f32[16,64]{1,0:T(8,128)S(1)} %dynamic-slice_add_fusion.2), channel_id=1, source_target_pairs={{0,1},{1,0},{2,3},{3,2},{4,5},{5,4},{6,7},{7,6},{8,9},{9,8},{10,11... | collective-permute-start | bytes 12296 | tf_op jit(solution)/shard_map/ppermute | solution.py:239
  72.7 3.7 %collective-permute-start.13 = (f32[16,64]{1,0:T(8,128)S(1)}, f32[16,64]{1,0:T(8,128)S(1)}, u32[]{:S(2)}, u32[]{:S(2)}) collective-permute-start(f32[16,64]{1,0:T(8,128)S(1)} %add.209), channel_id=1, source_target_pairs={{0,2},{1,3},{2,0},{3,1},{4,6},{5,7},{6,4},{7,5},{8,10},{9,11},{10,... | collective-permute-start | bytes 12296 | tf_op jit(solution)/shard_map/ppermute | solution.py:239
  (4 other events, 25.7 us)

commit v14 on v11

--- a/solution.py
+++ b/solution.py
@@ -121,13 +121,17 @@
     tokens_here = hidden.shape[0]
     local_width = w_qkv.shape[2]
     local_heads = local_width // HEAD
+    scale = jnp.array([0.125, 1.0, 1.0], jnp.float32)[:, None, None]
     projected = (
-        jnp.einsum("td,jdf->jtf", hidden, w_qkv, preferred_element_type=jnp.float32)
-        + b_qkv[:, None, :]
-    )
-    queries = (projected[0] * 0.125).astype(jnp.bfloat16).reshape(tokens_here, local_heads, HEAD)
-    keys = projected[1].astype(jnp.bfloat16).reshape(tokens_here, local_heads, HEAD)
-    values = projected[2].astype(jnp.bfloat16).reshape(tokens_here, local_heads, HEAD)
+        (
+            jnp.einsum("td,jdf->jtf", hidden, w_qkv, preferred_element_type=jnp.float32)
+            + b_qkv[:, None, :]
+        )
+        * scale
+    ).astype(jnp.bfloat16)
+    queries = projected[0].reshape(tokens_here, local_heads, HEAD)
+    keys = projected[1].reshape(tokens_here, local_heads, HEAD)
+    values = projected[2].reshape(tokens_here, local_heads, HEAD)
     segment = segment_of(lengths[0], tokens_here)
     same = segment[:, None] == segment[None, :]
     logits = jnp.einsum("thd,shd->hts", queries, keys, preferred_element_type=jnp.float32)

time: 77.1 us -> 77.1 us (level)
  no operation moved by 1% of the time
where the time goes in v14:
time: 77.1 us; the launch traced here: 76.8 us
  waiting for transfers between devices  33.3 us (43%)
  starting transfers between devices  20.5 us (27%)
  matrix products  14.3 us (19%)
  other arithmetic  6.5 us (8%)
  local copies, waits for them, and re-layouts  1.23 us (2%)
  between operations  1.05 us (1%)
    ppermute x2, waiting for transfers between devices, settle_by_chip(): across = lax.ppermute(chip_sum, 'tensor', xor_pairs(4, 2))  13.2 us
    ppermute x3, starting transfers between devices, reduce_scatter_xor(): got = lax.ppermute(theirs.astype(wire), axis, xor_pairs(n, k))  6.61 us
    ppermute x3, starting transfers between devices, all_gather_xor(): other = lax.ppermute(cur, axis, xor_pairs(n, k))  6.53 us
    ppermute x3, waiting for transfers between devices, reduce_scatter_xor(): got = lax.ppermute(theirs.astype(wire), axis, xor_pairs(n, k))  5.72 us
    ppermute x3, waiting for transfers between devices, all_gather_xor(): other = lax.ppermute(cur, axis, xor_pairs(n, k))  5.54 us
    dot_general x1, matrix products, body(): jnp.dot(activated, w_down, preferred_element_type=jnp.float32)  5.11 us
    ppermute x2, starting transfers between devices, settle_by_chip(): across = lax.ppermute(chip_sum, 'tensor', xor_pairs(4, 2))  4.72 us
    ppermute x2, waiting for transfers between devices, body(): lax.ppermute(text_scores, 'tensor', xor_pairs(n_tensor, k))  3.08 us
  transfers between devices with their start and end apart: 14, of which 14 were waited for; matrix products, arithmetic and copies ran while one was open for 0% of the time, Pallas kernels for 0%

profile of v14, /device:TPU:0, one launch (start us, length us, event | category | flops | bytes accessed | tf_op | source)
XLA Modules:
  0.0 76.8 jit_solution(1225405064590020161)
XLA Ops:
  0.7 2.3 %fusion.7 = bf16[3,256,256]{1,2,0:T(8,128)(2,1)S(1)} fusion(bf16[3,1024,256]{2,1,0:T(8,128)(2,1)} %param.19, bf16[256,1024]{1,0:T(8,128)(2,1)} %param.17, f32[3]{0:T(128)} %constant.200.clone, f32[3,256]{1,0:T(4,128)} %param.20), kind=kOutput, calls=%fused_computation.15 | convolution fusion | flops 403243008 | bytes 2493452 | tf_op jit(solution)/shard_map/td,jdf->jtf/dot_general | solution.py:127
  10.6 2.9 %collective-permute-start.1 = (bf16[128,1024]{1,0:T(8,128)(2,1)S(1)}, bf16[128,1024]{1,0:T(8,128)(2,1)S(1)}, u32[]{:S(2)}, u32[]{:S(2)}) collective-permute-start(bf16[128,1024]{1,0:T(8,128)(2,1)S(1)} %add_convert_fusion.3), channel_id=1, source_target_pairs={{0,2},{1,3},{2,0},{3,1},{4,6},{5,7},{6,4},{7,5},{8,10},{9,11},{10,... | collective-permute-start | bytes 786440 | tf_op jit(solution)/shard_map/ppermute | solution.py:91
  13.6 6.6 %collective-permute-done.1 = bf16[128,1024]{1,0:T(8,128)(2,1)S(1)} collective-permute-done((bf16[128,1024]{1,0:T(8,128)(2,1)S(1)}, bf16[128,1024]{1,0:T(8,128)(2,1)S(1)}, u32[]{:S(2)}, u32[]{:S(2)}) %collective-permute-start.1) | collective-permute-done | bytes 262176 | tf_op jit(solution)/shard_map/ppermute | solution.py:91
  20.9 1.5 %collective-permute-done.2 = bf16[128,1024]{1,0:T(8,128)(2,1)S(1)} collective-permute-done((bf16[128,1024]{1,0:T(8,128)(2,1)S(1)}, bf16[128,1024]{1,0:T(8,128)(2,1)S(1)}, u32[]{:S(2)}, u32[]{:S(2)}) %collective-permute-start.2) | collective-permute-done | bytes 262176 | tf_op jit(solution)/shard_map/ppermute | solution.py:97
  22.6 5.1 %convolution_convert_fusion.1 = bf16[256,1024]{1,0:T(8,128)(2,1)S(1)} fusion(bf16[1024,1024]{1,0:T(8,128)(2,1)S(1)} %copy-done, bf16[256,1024]{1,0:T(8,128)(2,1)S(1)} %maximum_select_fusion, bf16[1024,1024]{1,0:T(8,128)(2,1)} %param.25, f32[1024]{0:T(1024)S(1)} %copy-done.11), kind=kOutput, calls=%fused_computation.11 | convolution fusion | flops 1091305472 | bytes 5246976 | tf_op jit(solution)/shard_map/dot_general | solution.py:149
  29.5 1.8 %collective-permute-start.4 = (bf16[128,1024]{1,0:T(8,128)(2,1)S(1)}, bf16[128,1024]{1,0:T(8,128)(2,1)S(1)}, u32[]{:S(2)}, u32[]{:S(2)}) collective-permute-start(bf16[128,1024]{1,0:T(8,128)(2,1)S(1)} %add_convert_fusion.1), channel_id=1, source_target_pairs={{0,2},{1,3},{2,0},{3,1},{4,6},{5,7},{6,4},{7,5},{8,10},{9,11},{10,... | collective-permute-start | bytes 786440 | tf_op jit(solution)/shard_map/ppermute | solution.py:91
  31.3 6.6 %collective-permute-done.4 = bf16[128,1024]{1,0:T(8,128)(2,1)S(1)} collective-permute-done((bf16[128,1024]{1,0:T(8,128)(2,1)S(1)}, bf16[128,1024]{1,0:T(8,128)(2,1)S(1)}, u32[]{:S(2)}, u32[]{:S(2)}) %collective-permute-start.4) | collective-permute-done | bytes 262176 | tf_op jit(solution)/shard_map/ppermute | solution.py:91
  38.7 1.5 %collective-permute-done.5 = bf16[128,1024]{1,0:T(8,128)(2,1)S(1)} collective-permute-done((bf16[128,1024]{1,0:T(8,128)(2,1)S(1)}, bf16[128,1024]{1,0:T(8,128)(2,1)S(1)}, u32[]{:S(2)}, u32[]{:S(2)}) %collective-permute-start.5) | collective-permute-done | bytes 262176 | tf_op jit(solution)/shard_map/ppermute | solution.py:97
  40.7 1.8 %collective-permute-start.6 = (bf16[16,256]{1,0:T(8,128)(2,1)S(1)}, bf16[16,256]{1,0:T(8,128)(2,1)S(1)}, u32[]{:S(2)}, u32[]{:S(2)}) collective-permute-start(bf16[16,256]{1,0:T(8,128)(2,1)S(1)} %fusion.65), channel_id=1, source_target_pairs={{0,4},{4,0},{8,12},{12,8},{16,20},{20,16},{24,28},{28,24},{1,5},{5... | collective-permute-start | bytes 24584 | tf_op jit(solution)/shard_map/ppermute | solution.py:58
  42.5 1.9 %collective-permute-done.6 = bf16[16,256]{1,0:T(8,128)(2,1)S(1)} collective-permute-done((bf16[16,256]{1,0:T(8,128)(2,1)S(1)}, bf16[16,256]{1,0:T(8,128)(2,1)S(1)}, u32[]{:S(2)}, u32[]{:S(2)}) %collective-permute-start.6) | collective-permute-done | bytes 8224 | tf_op jit(solution)/shard_map/ppermute | solution.py:58
  44.4 1.8 %collective-permute-start.7 = (bf16[32,256]{1,0:T(8,128)(2,1)S(1)}, bf16[32,256]{1,0:T(8,128)(2,1)S(1)}, u32[]{:S(2)}, u32[]{:S(2)}) collective-permute-start(bf16[32,256]{1,0:T(8,128)(2,1)S(1)} %maximum_select_fusion.5), channel_id=1, source_target_pairs={{0,8},{4,12},{8,0},{12,4},{16,24},{20,28},{24,16},{28,20},{1,9},{5... | collective-permute-start | bytes 49160 | tf_op jit(solution)/shard_map/ppermute | solution.py:58
  46.3 1.8 %collective-permute-done.7 = bf16[32,256]{1,0:T(8,128)(2,1)S(1)} collective-permute-done((bf16[32,256]{1,0:T(8,128)(2,1)S(1)}, bf16[32,256]{1,0:T(8,128)(2,1)S(1)}, u32[]{:S(2)}, u32[]{:S(2)}) %collective-permute-start.7) | collective-permute-done | bytes 16416 | tf_op jit(solution)/shard_map/ppermute | solution.py:58
  48.2 2.9 %collective-permute-start.8 = (bf16[64,256]{1,0:T(8,128)(2,1)S(1)}, bf16[64,256]{1,0:T(8,128)(2,1)S(1)}, u32[]{:S(2)}, u32[]{:S(2)}) collective-permute-start(bf16[64,256]{1,0:T(8,128)(2,1)S(1)} %maximum_select_fusion.4), channel_id=1, source_target_pairs={{0,16},{4,20},{8,24},{12,28},{16,0},{20,4},{24,8},{28,12},{1,17},{... | collective-permute-start | bytes 98312 | tf_op jit(solution)/shard_map/ppermute | solution.py:58
  51.2 1.9 %collective-permute-done.8 = bf16[64,256]{1,0:T(8,128)(2,1)S(1)} collective-permute-done((bf16[64,256]{1,0:T(8,128)(2,1)S(1)}, bf16[64,256]{1,0:T(8,128)(2,1)S(1)}, u32[]{:S(2)}, u32[]{:S(2)}) %collective-permute-start.8) | collective-permute-done | bytes 32800 | tf_op jit(solution)/shard_map/ppermute | solution.py:58
  53.0 1.7 %convert_bitcast_fusion = (bf16[16,8,16,128]{3,1,2,0:T(8,128)(2,1)S(1)}, bf16[16,8,16,128]{3,1,2,0:T(8,128)(2,1)S(1)}) fusion(bf16[2048,256]{1,0:T(8,128)(2,1)} %param.31, bf16[64,256]{1,0:T(8,128)(2,1)S(1)} %collective-permute-done.8, bf16[64,256]{1,0:T(8,128)(2,1)S(1)} %maximum_select_fusion.4, pred[]{:T(512)S(6)} %eq.90), kind=kOutput, calls=%fused_computation.87 | convolution fusion | flops 135561216 | bytes 2162689 | tf_op jit(solution)/shard_map/dot_general | solution.py:182
  56.3 2.7 %fusion.2 = f32[128,64]{1,0:T(8,128)S(1)} fusion(f32[128,64,256]{2,1,0:T(8,128)S(1)} %fusion.11, s32[128,64]{1,0:T(8,128)S(1)} %get-tuple-element.7), kind=kLoop, calls=%fused_computation.3 | loop fusion | flops 4186112 | bytes 8454144 | tf_op jit(solution)/shard_map/reduce_sum | solution.py:201
  59.0 2.9 %collective-permute-start.9 = (f32[64,64]{1,0:T(8,128)S(1)}, f32[64,64]{1,0:T(8,128)S(1)}, u32[]{:S(2)}, u32[]{:S(2)}) collective-permute-start(f32[64,64]{1,0:T(8,128)S(1)} %constant_dynamic-slice_fusion.2), channel_id=1, source_target_pairs={{0,16},{4,20},{8,24},{12,28},{16,0},{20,4},{24,8},{28,12},{1,17},{... | collective-permute-start | bytes 49160 | tf_op jit(solution)/shard_map/ppermute | solution.py:47
  62.0 1.9 %collective-permute-done.9 = f32[64,64]{1,0:T(8,128)S(1)} collective-permute-done((f32[64,64]{1,0:T(8,128)S(1)}, f32[64,64]{1,0:T(8,128)S(1)}, u32[]{:S(2)}, u32[]{:S(2)}) %collective-permute-start.9) | collective-permute-done | bytes 16416 | tf_op jit(solution)/shard_map/ppermute | solution.py:47
  63.9 1.9 %collective-permute-start.10 = (f32[32,64]{1,0:T(8,128)S(1)}, f32[32,64]{1,0:T(8,128)S(1)}, u32[]{:S(2)}, u32[]{:S(2)}) collective-permute-start(f32[32,64]{1,0:T(8,128)S(1)} %constant_dynamic-slice_fusion.1), channel_id=1, source_target_pairs={{0,8},{4,12},{8,0},{12,4},{16,24},{20,28},{24,16},{28,20},{1,9},{5... | collective-permute-start | bytes 24584 | tf_op jit(solution)/shard_map/ppermute | solution.py:47
  65.8 1.9 %collective-permute-done.10 = f32[32,64]{1,0:T(8,128)S(1)} collective-permute-done((f32[32,64]{1,0:T(8,128)S(1)}, f32[32,64]{1,0:T(8,128)S(1)}, u32[]{:S(2)}, u32[]{:S(2)}) %collective-permute-start.10) | collective-permute-done | bytes 8224 | tf_op jit(solution)/shard_map/ppermute | solution.py:47
  67.7 1.8 %collective-permute-start.11 = (f32[16,64]{1,0:T(8,128)S(1)}, f32[16,64]{1,0:T(8,128)S(1)}, u32[]{:S(2)}, u32[]{:S(2)}) collective-permute-start(f32[16,64]{1,0:T(8,128)S(1)} %constant_dynamic-slice_fusion), channel_id=1, source_target_pairs={{0,4},{4,0},{8,12},{12,8},{16,20},{20,16},{24,28},{28,24},{1,5},{5... | collective-permute-start | bytes 12296 | tf_op jit(solution)/shard_map/ppermute | solution.py:47
  69.5 1.9 %collective-permute-done.11 = f32[16,64]{1,0:T(8,128)S(1)} collective-permute-done((f32[16,64]{1,0:T(8,128)S(1)}, f32[16,64]{1,0:T(8,128)S(1)}, u32[]{:S(2)}, u32[]{:S(2)}) %collective-permute-start.11) | collective-permute-done | bytes 4128 | tf_op jit(solution)/shard_map/ppermute | solution.py:47
  72.6 1.7 %collective-permute-start.13 = (f32[16,64]{1,0:T(8,128)S(1)}, f32[16,64]{1,0:T(8,128)S(1)}, u32[]{:S(2)}, u32[]{:S(2)}) collective-permute-start(f32[16,64]{1,0:T(8,128)S(1)} %add.206), channel_id=1, source_target_pairs={{0,2},{1,3},{2,0},{3,1},{4,6},{5,7},{6,4},{7,5},{8,10},{9,11},{10,... | collective-permute-start | bytes 12296 | tf_op jit(solution)/shard_map/ppermute | solution.py:229
  74.3 1.9 %collective-permute-done.13 = f32[16,64]{1,0:T(8,128)S(1)} collective-permute-done((f32[16,64]{1,0:T(8,128)S(1)}, f32[16,64]{1,0:T(8,128)S(1)}, u32[]{:S(2)}, u32[]{:S(2)}) %collective-permute-start.13) | collective-permute-done | bytes 4128 | tf_op jit(solution)/shard_map/ppermute | solution.py:229
  (78 shorter events, 14.9 us)
Async XLA Ops:
  0.6 22.0 %copy-start = (bf16[1024,1024]{1,0:T(8,128)(2,1)S(1)}, bf16[1024,1024]{1,0:T(8,128)(2,1)}, u32[]{:S(2)}) copy-start(bf16[1024,1024]{1,0:T(8,128)(2,1)} %param.27) | copy-start | bytes 6291460
  6.3 13.9 %copy-start.2 = (bf16[256,1024]{1,0:T(8,128)(2,1)S(1)}, bf16[256,1024]{1,0:T(8,128)(2,1)}, u32[]{:S(2)}) copy-start(bf16[256,1024]{1,0:T(8,128)(2,1)} %param.17) | copy-start | bytes 1572868
  6.3 13.9 %copy-start.3 = (f32[1024]{0:T(1024)S(1)}, f32[1024]{0:T(1024)}, u32[]{:S(2)}) copy-start(f32[1024]{0:T(1024)} %param.22) | copy-start | bytes 12292
  6.3 14.3 %copy-start.6 = (f32[1024]{0:T(1024)S(1)}, f32[1024]{0:T(1024)}, u32[]{:S(2)}) copy-start(f32[1024]{0:T(1024)} %param.24) | copy-start | bytes 12292
  6.3 14.3 %copy-start.7 = (f32[1024]{0:T(1024)S(1)}, f32[1024]{0:T(1024)}, u32[]{:S(2)}) copy-start(f32[1024]{0:T(1024)} %param.23) | copy-start | bytes 12292
  7.8 1.8 %collective-permute-start = (bf16[128,1024]{1,0:T(8,128)(2,1)S(1)}, bf16[128,1024]{1,0:T(8,128)(2,1)}, u32[]{:S(2)}, u32[]{:S(2)}) collective-permute-start(bf16[128,1024]{1,0:T(8,128)(2,1)S(1)} %constant_dynamic-slice_fusion.4), channel_id=1, source_target_pairs={{0,1},{1,0},{2,3},{3,2},{4,5},{5,4},{6,7},{7,6},{8,9},{9,8},{10,11... | collective-permute-start | bytes 786440 | tf_op jit(solution)/shard_map/ppermute | solution.py:89
  8.3 14.3 %copy-start.11 = (f32[1024]{0:T(1024)S(1)}, f32[1024]{0:T(1024)}, u32[]{:S(2)}) copy-start(f32[1024]{0:T(1024)} %param.26) | copy-start | bytes 12292
  10.6 9.5 %collective-permute-start.1 = (bf16[128,1024]{1,0:T(8,128)(2,1)S(1)}, bf16[128,1024]{1,0:T(8,128)(2,1)S(1)}, u32[]{:S(2)}, u32[]{:S(2)}) collective-permute-start(bf16[128,1024]{1,0:T(8,128)(2,1)S(1)} %add_convert_fusion.3), channel_id=1, source_target_pairs={{0,2},{1,3},{2,0},{3,1},{4,6},{5,7},{6,4},{7,5},{8,10},{9,11},{10,... | collective-permute-start | bytes 786440 | tf_op jit(solution)/shard_map/ppermute | solution.py:91
  20.9 1.6 %collective-permute-start.2 = (bf16[128,1024]{1,0:T(8,128)(2,1)S(1)}, bf16[128,1024]{1,0:T(8,128)(2,1)S(1)}, u32[]{:S(2)}, u32[]{:S(2)}) collective-permute-start(bf16[128,1024]{1,0:T(8,128)(2,1)S(1)} %add_convert_fusion.2), channel_id=1, source_target_pairs={{0,1},{1,0},{2,3},{3,2},{4,5},{5,4},{6,7},{7,6},{8,9},{9,8},{10,11... | collective-permute-start | bytes 786440 | tf_op jit(solution)/shard_map/ppermute | solution.py:97
  22.6 15.3 %copy-start.4 = (f32[1024]{0:T(1024)S(1)}, f32[1024]{0:T(1024)}, u32[]{:S(2)}) copy-start(f32[1024]{0:T(1024)} %param.28) | copy-start | bytes 12292
  27.7 10.6 %copy-start.8 = (f32[1024]{0:T(1024)S(1)}, f32[1024]{0:T(1024)}, u32[]{:S(2)}) copy-start(f32[1024]{0:T(1024)} %param.30) | copy-start | bytes 12292
  27.8 1.6 %collective-permute-start.3 = (bf16[128,1024]{1,0:T(8,128)(2,1)S(1)}, bf16[128,1024]{1,0:T(8,128)(2,1)S(1)}, u32[]{:S(2)}, u32[]{:S(2)}) collective-permute-start(bf16[128,1024]{1,0:T(8,128)(2,1)S(1)} %constant_dynamic-slice_fusion.3), channel_id=1, source_target_pairs={{0,1},{1,0},{2,3},{3,2},{4,5},{5,4},{6,7},{7,6},{8,9},{9,8},{10,11... | collective-permute-start | bytes 786440 | tf_op jit(solution)/shard_map/ppermute | solution.py:89
  29.5 16.8 %copy-start.5 = (s32[128,64]{0,1:T(8,128)S(1)}, s32[128,64]{0,1:T(8,128)}, u32[]{:S(2)}) copy-start(s32[128,64]{0,1:T(8,128)} %param.32) | copy-start | bytes 98308
  29.5 8.4 %collective-permute-start.4 = (bf16[128,1024]{1,0:T(8,128)(2,1)S(1)}, bf16[128,1024]{1,0:T(8,128)(2,1)S(1)}, u32[]{:S(2)}, u32[]{:S(2)}) collective-permute-start(bf16[128,1024]{1,0:T(8,128)(2,1)S(1)} %add_convert_fusion.1), channel_id=1, source_target_pairs={{0,2},{1,3},{2,0},{3,1},{4,6},{5,7},{6,4},{7,5},{8,10},{9,11},{10,... | collective-permute-start | bytes 786440 | tf_op jit(solution)/shard_map/ppermute | solution.py:91
  38.6 1.6 %collective-permute-start.5 = (bf16[128,1024]{1,0:T(8,128)(2,1)S(1)}, bf16[128,1024]{1,0:T(8,128)(2,1)S(1)}, u32[]{:S(2)}, u32[]{:S(2)}) collective-permute-start(bf16[128,1024]{1,0:T(8,128)(2,1)S(1)} %add_convert_fusion), channel_id=1, source_target_pairs={{0,1},{1,0},{2,3},{3,2},{4,5},{5,4},{6,7},{7,6},{8,9},{9,8},{10,11... | collective-permute-start | bytes 786440 | tf_op jit(solution)/shard_map/ppermute | solution.py:97
  40.4 14.5 %copy-start.1 = (bf16[256,1024]{1,0:T(8,128)(2,1)}, bf16[256,1024]{1,0:T(8,128)(2,1)S(1)}, u32[]{:S(2)}) copy-start(bf16[256,1024]{1,0:T(8,128)(2,1)S(1)} %maximum_select_fusion.1) | copy-start | bytes 1572868
  40.7 3.7 %collective-permute-start.6 = (bf16[16,256]{1,0:T(8,128)(2,1)S(1)}, bf16[16,256]{1,0:T(8,128)(2,1)S(1)}, u32[]{:S(2)}, u32[]{:S(2)}) collective-permute-start(bf16[16,256]{1,0:T(8,128)(2,1)S(1)} %fusion.65), channel_id=1, source_target_pairs={{0,4},{4,0},{8,12},{12,8},{16,20},{20,16},{24,28},{28,24},{1,5},{5... | collective-permute-start | bytes 24584 | tf_op jit(solution)/shard_map/ppermute | solution.py:58
  44.4 3.7 %collective-permute-start.7 = (bf16[32,256]{1,0:T(8,128)(2,1)S(1)}, bf16[32,256]{1,0:T(8,128)(2,1)S(1)}, u32[]{:S(2)}, u32[]{:S(2)}) collective-permute-start(bf16[32,256]{1,0:T(8,128)(2,1)S(1)} %maximum_select_fusion.5), channel_id=1, source_target_pairs={{0,8},{4,12},{8,0},{12,4},{16,24},{20,28},{24,16},{28,20},{1,9},{5... | collective-permute-start | bytes 49160 | tf_op jit(solution)/shard_map/ppermute | solution.py:58
  48.2 4.9 %collective-permute-start.8 = (bf16[64,256]{1,0:T(8,128)(2,1)S(1)}, bf16[64,256]{1,0:T(8,128)(2,1)S(1)}, u32[]{:S(2)}, u32[]{:S(2)}) collective-permute-start(bf16[64,256]{1,0:T(8,128)(2,1)S(1)} %maximum_select_fusion.4), channel_id=1, source_target_pairs={{0,16},{4,20},{8,24},{12,28},{16,0},{20,4},{24,8},{28,12},{1,17},{... | collective-permute-start | bytes 98312 | tf_op jit(solution)/shard_map/ppermute | solution.py:58
  59.0 4.9 %collective-permute-start.9 = (f32[64,64]{1,0:T(8,128)S(1)}, f32[64,64]{1,0:T(8,128)S(1)}, u32[]{:S(2)}, u32[]{:S(2)}) collective-permute-start(f32[64,64]{1,0:T(8,128)S(1)} %constant_dynamic-slice_fusion.2), channel_id=1, source_target_pairs={{0,16},{4,20},{8,24},{12,28},{16,0},{20,4},{24,8},{28,12},{1,17},{... | collective-permute-start | bytes 49160 | tf_op jit(solution)/shard_map/ppermute | solution.py:47
  63.9 3.8 %collective-permute-start.10 = (f32[32,64]{1,0:T(8,128)S(1)}, f32[32,64]{1,0:T(8,128)S(1)}, u32[]{:S(2)}, u32[]{:S(2)}) collective-permute-start(f32[32,64]{1,0:T(8,128)S(1)} %constant_dynamic-slice_fusion.1), channel_id=1, source_target_pairs={{0,8},{4,12},{8,0},{12,4},{16,24},{20,28},{24,16},{28,20},{1,9},{5... | collective-permute-start | bytes 24584 | tf_op jit(solution)/shard_map/ppermute | solution.py:47
  67.7 3.7 %collective-permute-start.11 = (f32[16,64]{1,0:T(8,128)S(1)}, f32[16,64]{1,0:T(8,128)S(1)}, u32[]{:S(2)}, u32[]{:S(2)}) collective-permute-start(f32[16,64]{1,0:T(8,128)S(1)} %constant_dynamic-slice_fusion), channel_id=1, source_target_pairs={{0,4},{4,0},{8,12},{12,8},{16,20},{20,16},{24,28},{28,24},{1,5},{5... | collective-permute-start | bytes 12296 | tf_op jit(solution)/shard_map/ppermute | solution.py:47
  71.4 1.2 %collective-permute-start.12 = (f32[16,64]{1,0:T(8,128)S(1)}, f32[16,64]{1,0:T(8,128)S(1)}, u32[]{:S(2)}, u32[]{:S(2)}) collective-permute-start(f32[16,64]{1,0:T(8,128)S(1)} %dynamic-slice_add_fusion.2), channel_id=1, source_target_pairs={{0,1},{1,0},{2,3},{3,2},{4,5},{5,4},{6,7},{7,6},{8,9},{9,8},{10,11... | collective-permute-start | bytes 12296 | tf_op jit(solution)/shard_map/ppermute | solution.py:229
  72.6 3.7 %collective-permute-start.13 = (f32[16,64]{1,0:T(8,128)S(1)}, f32[16,64]{1,0:T(8,128)S(1)}, u32[]{:S(2)}, u32[]{:S(2)}) collective-permute-start(f32[16,64]{1,0:T(8,128)S(1)} %add.206), channel_id=1, source_target_pairs={{0,2},{1,3},{2,0},{3,1},{4,6},{5,7},{6,4},{7,5},{8,10},{9,11},{10,... | collective-permute-start | bytes 12296 | tf_op jit(solution)/shard_map/ppermute | solution.py:229
  (2 other events, 13.7 us)

commit v15 on v14

--- a/solution.py
+++ b/solution.py
@@ -121,25 +121,28 @@
     tokens_here = hidden.shape[0]
     local_width = w_qkv.shape[2]
     local_heads = local_width // HEAD
-    scale = jnp.array([0.125, 1.0, 1.0], jnp.float32)[:, None, None]
+    scale = jnp.array([0.125, 1.0, 1.0], jnp.float32)[:, None, None, None]
     projected = (
         (
-            jnp.einsum("td,jdf->jtf", hidden, w_qkv, preferred_element_type=jnp.float32)
-            + b_qkv[:, None, :]
+            jnp.einsum(
+                "td,jdhe->jhte",
+                hidden,
+                w_qkv.reshape(3, w_qkv.shape[1], local_heads, HEAD),
+                preferred_element_type=jnp.float32,
+            )
+            + b_qkv.reshape(3, local_heads, 1, HEAD)
         )
         * scale
     ).astype(jnp.bfloat16)
-    queries = projected[0].reshape(tokens_here, local_heads, HEAD)
-    keys = projected[1].reshape(tokens_here, local_heads, HEAD)
-    values = projected[2].reshape(tokens_here, local_heads, HEAD)
+    queries, keys, values = projected[0], projected[1], projected[2]
     segment = segment_of(lengths[0], tokens_here)
     same = segment[:, None] == segment[None, :]
-    logits = jnp.einsum("thd,shd->hts", queries, keys, preferred_element_type=jnp.float32)
+    logits = jnp.einsum("htd,hsd->hts", queries, keys, preferred_element_type=jnp.float32)
     logits = jnp.where(same[None], logits, -1e30)
     top = jnp.max(logits, axis=-1, keepdims=True)
     expo = jnp.exp(logits - top)
     weights = (expo / jnp.sum(expo, axis=-1, keepdims=True)).astype(jnp.bfloat16)
-    context = jnp.einsum("hts,shd->thd", weights, values, preferred_element_type=jnp.float32)
+    context = jnp.einsum("hts,hsd->thd", weights, values, preferred_element_type=jnp.float32)
     context = context.astype(jnp.bfloat16).reshape(tokens_here, local_width)
     partial_value = jnp.dot(context, w_output, preferred_element_type=jnp.float32)
     attended = settle(partial_value, hidden, b_output, first_gain, first_shift, n_tensor)

time: 77.1 us -> 80.6 us (1.045)
  local copies, waits for them, and re-layouts: 1.23 us -> 3.39 us
  matrix products: 14.3 us -> 15.6 us
    unnamed x27 -> x32, local copies, waits for them, and re-layouts: 0.39 us -> 3.15 us
    dot_general x3, matrix products: 3.98 us -> 5.28 us  [the longest x1 2.02 us: body(): jnp.einsum('td,jdhe->jhte', hidden, w_qkv.reshape(3, w_qkv.shape[1], loca...]
where the time goes in v15:
time: 80.6 us; the launch traced here: 80.3 us
  waiting for transfers between devices  33.4 us (41%)
  starting transfers between devices  20.4 us (25%)
  matrix products  15.6 us (19%)
  other arithmetic  6.5 us (8%)
  local copies, waits for them, and re-layouts  3.39 us (4%)
  between operations  1.07 us (1%)
    ppermute x2, waiting for transfers between devices, settle_by_chip(): across = lax.ppermute(chip_sum, 'tensor', xor_pairs(4, 2))  13.2 us
    ppermute x3, starting transfers between devices, reduce_scatter_xor(): got = lax.ppermute(theirs.astype(wire), axis, xor_pairs(n, k))  6.56 us
    ppermute x3, starting transfers between devices, all_gather_xor(): other = lax.ppermute(cur, axis, xor_pairs(n, k))  6.47 us
    ppermute x3, waiting for transfers between devices, reduce_scatter_xor(): got = lax.ppermute(theirs.astype(wire), axis, xor_pairs(n, k))  5.77 us
    ppermute x3, waiting for transfers between devices, all_gather_xor(): other = lax.ppermute(cur, axis, xor_pairs(n, k))  5.6 us
    dot_general x1, matrix products, body(): jnp.dot(activated, w_down, preferred_element_type=jnp.float32)  5.11 us
    ppermute x2, starting transfers between devices, settle_by_chip(): across = lax.ppermute(chip_sum, 'tensor', xor_pairs(4, 2))  4.73 us
    unnamed x32, local copies, waits for them, and re-layouts  3.15 us
  transfers between devices with their start and end apart: 14, of which 14 were waited for; matrix products, arithmetic and copies ran while one was open for 0% of the time, Pallas kernels for 0%

profile of v15, /device:TPU:0, one launch (start us, length us, event | category | flops | bytes accessed | tf_op | source)
XLA Modules:
  0.0 80.3 jit_solution(14700830113197085849)
XLA Ops:
  0.7 2.8 %copy.27 = bf16[3,1024,256]{1,2,0:T(8,128)(2,1)} copy(bf16[3,1024,256]{2,1,0:T(8,128)(2,1)} %param.19) | data formatting | bytes 3145728 | tf_op args[2]
  4.0 2.0 %fusion.7 = bf16[3,4,256,64]{2,3,1,0:T(8,128)(2,1)S(1)} fusion(bf16[3,1024,4,64]{1,3,2,0:T(8,128)(2,1)} %bitcast.48, bf16[256,1024]{1,0:T(8,128)(2,1)S(1)} %copy-done.2, f32[3]{0:T(128)S(1)} %copy-done.13, f32[3,4,64]{2,1,0:T(4,128)S(1)} %add.170), kind=kOutput, calls=%fused_computation.15 | convolution fusion | flops 403243008 | bytes 2493452 | tf_op jit(solution)/shard_map/td,jdhe->jhte/dot_general | solution.py:127
  7.9 1.9 %convolution_convert_fusion.2 = bf16[4,64,256]{2,1,0:T(8,128)(2,1)S(1)} fusion(f32[4,256]{1,0:T(4,128)S(1)} %fusion.103, bf16[3,4,256,64]{2,3,1,0:T(8,128)(2,1)S(1)} %fusion.7, f32[4,256,256]{1,2,0:T(8,128)} %convolution_select_fusion), kind=kOutput, calls=%fused_computation.16 | convolution fusion | flops 34407680 | bytes 2363392 | tf_op jit(solution)/shard_map/hts,hsd->thd/dot_general | solution.py:145
  14.1 2.9 %collective-permute-start.1 = (bf16[128,1024]{1,0:T(8,128)(2,1)S(1)}, bf16[128,1024]{1,0:T(8,128)(2,1)S(1)}, u32[]{:S(2)}, u32[]{:S(2)}) collective-permute-start(bf16[128,1024]{1,0:T(8,128)(2,1)S(1)} %add_convert_fusion.3), channel_id=1, source_target_pairs={{0,2},{1,3},{2,0},{3,1},{4,6},{5,7},{6,4},{7,5},{8,10},{9,11},{10,... | collective-permute-start | bytes 786440 | tf_op jit(solution)/shard_map/ppermute | solution.py:91
  17.0 6.6 %collective-permute-done.1 = bf16[128,1024]{1,0:T(8,128)(2,1)S(1)} collective-permute-done((bf16[128,1024]{1,0:T(8,128)(2,1)S(1)}, bf16[128,1024]{1,0:T(8,128)(2,1)S(1)}, u32[]{:S(2)}, u32[]{:S(2)}) %collective-permute-start.1) | collective-permute-done | bytes 262176 | tf_op jit(solution)/shard_map/ppermute | solution.py:91
  26.1 5.1 %convolution_convert_fusion.1 = bf16[256,1024]{1,0:T(8,128)(2,1)S(1)} fusion(bf16[1024,1024]{1,0:T(8,128)(2,1)S(1)} %copy-done, bf16[256,1024]{1,0:T(8,128)(2,1)S(1)} %maximum_select_fusion, bf16[1024,1024]{1,0:T(8,128)(2,1)} %param.25, f32[1024]{0:T(1024)S(1)} %copy-done.12), kind=kOutput, calls=%fused_computation.11 | convolution fusion | flops 1091305472 | bytes 5246976 | tf_op jit(solution)/shard_map/dot_general | solution.py:152
  33.0 1.8 %collective-permute-start.4 = (bf16[128,1024]{1,0:T(8,128)(2,1)S(1)}, bf16[128,1024]{1,0:T(8,128)(2,1)S(1)}, u32[]{:S(2)}, u32[]{:S(2)}) collective-permute-start(bf16[128,1024]{1,0:T(8,128)(2,1)S(1)} %add_convert_fusion.1), channel_id=1, source_target_pairs={{0,2},{1,3},{2,0},{3,1},{4,6},{5,7},{6,4},{7,5},{8,10},{9,11},{10,... | collective-permute-start | bytes 786440 | tf_op jit(solution)/shard_map/ppermute | solution.py:91
  34.8 6.6 %collective-permute-done.4 = bf16[128,1024]{1,0:T(8,128)(2,1)S(1)} collective-permute-done((bf16[128,1024]{1,0:T(8,128)(2,1)S(1)}, bf16[128,1024]{1,0:T(8,128)(2,1)S(1)}, u32[]{:S(2)}, u32[]{:S(2)}) %collective-permute-start.4) | collective-permute-done | bytes 262176 | tf_op jit(solution)/shard_map/ppermute | solution.py:91
  44.2 1.8 %collective-permute-start.6 = (bf16[16,256]{1,0:T(8,128)(2,1)S(1)}, bf16[16,256]{1,0:T(8,128)(2,1)S(1)}, u32[]{:S(2)}, u32[]{:S(2)}) collective-permute-start(bf16[16,256]{1,0:T(8,128)(2,1)S(1)} %fusion.65), channel_id=1, source_target_pairs={{0,4},{4,0},{8,12},{12,8},{16,20},{20,16},{24,28},{28,24},{1,5},{5... | collective-permute-start | bytes 24584 | tf_op jit(solution)/shard_map/ppermute | solution.py:58
  46.0 1.9 %collective-permute-done.6 = bf16[16,256]{1,0:T(8,128)(2,1)S(1)} collective-permute-done((bf16[16,256]{1,0:T(8,128)(2,1)S(1)}, bf16[16,256]{1,0:T(8,128)(2,1)S(1)}, u32[]{:S(2)}, u32[]{:S(2)}) %collective-permute-start.6) | collective-permute-done | bytes 8224 | tf_op jit(solution)/shard_map/ppermute | solution.py:58
  47.9 1.8 %collective-permute-start.7 = (bf16[32,256]{1,0:T(8,128)(2,1)S(1)}, bf16[32,256]{1,0:T(8,128)(2,1)S(1)}, u32[]{:S(2)}, u32[]{:S(2)}) collective-permute-start(bf16[32,256]{1,0:T(8,128)(2,1)S(1)} %maximum_select_fusion.5), channel_id=1, source_target_pairs={{0,8},{4,12},{8,0},{12,4},{16,24},{20,28},{24,16},{28,20},{1,9},{5... | collective-permute-start | bytes 49160 | tf_op jit(solution)/shard_map/ppermute | solution.py:58
  49.8 1.8 %collective-permute-done.7 = bf16[32,256]{1,0:T(8,128)(2,1)S(1)} collective-permute-done((bf16[32,256]{1,0:T(8,128)(2,1)S(1)}, bf16[32,256]{1,0:T(8,128)(2,1)S(1)}, u32[]{:S(2)}, u32[]{:S(2)}) %collective-permute-start.7) | collective-permute-done | bytes 16416 | tf_op jit(solution)/shard_map/ppermute | solution.py:58
  51.6 2.9 %collective-permute-start.8 = (bf16[64,256]{1,0:T(8,128)(2,1)S(1)}, bf16[64,256]{1,0:T(8,128)(2,1)S(1)}, u32[]{:S(2)}, u32[]{:S(2)}) collective-permute-start(bf16[64,256]{1,0:T(8,128)(2,1)S(1)} %maximum_select_fusion.4), channel_id=1, source_target_pairs={{0,16},{4,20},{8,24},{12,28},{16,0},{20,4},{24,8},{28,12},{1,17},{... | collective-permute-start | bytes 98312 | tf_op jit(solution)/shard_map/ppermute | solution.py:58
  54.6 1.9 %collective-permute-done.8 = bf16[64,256]{1,0:T(8,128)(2,1)S(1)} collective-permute-done((bf16[64,256]{1,0:T(8,128)(2,1)S(1)}, bf16[64,256]{1,0:T(8,128)(2,1)S(1)}, u32[]{:S(2)}, u32[]{:S(2)}) %collective-permute-start.8) | collective-permute-done | bytes 32800 | tf_op jit(solution)/shard_map/ppermute | solution.py:58
  56.5 1.7 %convert_bitcast_fusion = (bf16[16,8,16,128]{3,1,2,0:T(8,128)(2,1)S(1)}, bf16[16,8,16,128]{3,1,2,0:T(8,128)(2,1)S(1)}) fusion(bf16[2048,256]{1,0:T(8,128)(2,1)} %param.31, bf16[64,256]{1,0:T(8,128)(2,1)S(1)} %collective-permute-done.8, bf16[64,256]{1,0:T(8,128)(2,1)S(1)} %maximum_select_fusion.4, pred[]{:T(512)S(6)} %eq.90), kind=kOutput, calls=%fused_computation.87 | convolution fusion | flops 135561216 | bytes 2162689 | tf_op jit(solution)/shard_map/dot_general | solution.py:185
  59.8 2.7 %fusion.2 = f32[128,64]{1,0:T(8,128)S(1)} fusion(f32[128,64,256]{2,1,0:T(8,128)S(1)} %fusion.11, s32[128,64]{1,0:T(8,128)S(1)} %get-tuple-element.4), kind=kLoop, calls=%fused_computation.3 | loop fusion | flops 4186112 | bytes 8454144 | tf_op jit(solution)/shard_map/reduce_sum | solution.py:204
  62.5 2.9 %collective-permute-start.9 = (f32[64,64]{1,0:T(8,128)S(1)}, f32[64,64]{1,0:T(8,128)S(1)}, u32[]{:S(2)}, u32[]{:S(2)}) collective-permute-start(f32[64,64]{1,0:T(8,128)S(1)} %constant_dynamic-slice_fusion.2), channel_id=1, source_target_pairs={{0,16},{4,20},{8,24},{12,28},{16,0},{20,4},{24,8},{28,12},{1,17},{... | collective-permute-start | bytes 49160 | tf_op jit(solution)/shard_map/ppermute | solution.py:47
  65.4 2.0 %collective-permute-done.9 = f32[64,64]{1,0:T(8,128)S(1)} collective-permute-done((f32[64,64]{1,0:T(8,128)S(1)}, f32[64,64]{1,0:T(8,128)S(1)}, u32[]{:S(2)}, u32[]{:S(2)}) %collective-permute-start.9) | collective-permute-done | bytes 16416 | tf_op jit(solution)/shard_map/ppermute | solution.py:47
  67.4 1.9 %collective-permute-start.10 = (f32[32,64]{1,0:T(8,128)S(1)}, f32[32,64]{1,0:T(8,128)S(1)}, u32[]{:S(2)}, u32[]{:S(2)}) collective-permute-start(f32[32,64]{1,0:T(8,128)S(1)} %constant_dynamic-slice_fusion.1), channel_id=1, source_target_pairs={{0,8},{4,12},{8,0},{12,4},{16,24},{20,28},{24,16},{28,20},{1,9},{5... | collective-permute-start | bytes 24584 | tf_op jit(solution)/shard_map/ppermute | solution.py:47
  69.3 1.9 %collective-permute-done.10 = f32[32,64]{1,0:T(8,128)S(1)} collective-permute-done((f32[32,64]{1,0:T(8,128)S(1)}, f32[32,64]{1,0:T(8,128)S(1)}, u32[]{:S(2)}, u32[]{:S(2)}) %collective-permute-start.10) | collective-permute-done | bytes 8224 | tf_op jit(solution)/shard_map/ppermute | solution.py:47
  71.2 1.8 %collective-permute-start.11 = (f32[16,64]{1,0:T(8,128)S(1)}, f32[16,64]{1,0:T(8,128)S(1)}, u32[]{:S(2)}, u32[]{:S(2)}) collective-permute-start(f32[16,64]{1,0:T(8,128)S(1)} %constant_dynamic-slice_fusion), channel_id=1, source_target_pairs={{0,4},{4,0},{8,12},{12,8},{16,20},{20,16},{24,28},{28,24},{1,5},{5... | collective-permute-start | bytes 12296 | tf_op jit(solution)/shard_map/ppermute | solution.py:47
  73.0 1.9 %collective-permute-done.11 = f32[16,64]{1,0:T(8,128)S(1)} collective-permute-done((f32[16,64]{1,0:T(8,128)S(1)}, f32[16,64]{1,0:T(8,128)S(1)}, u32[]{:S(2)}, u32[]{:S(2)}) %collective-permute-start.11) | collective-permute-done | bytes 4128 | tf_op jit(solution)/shard_map/ppermute | solution.py:47
  76.0 1.7 %collective-permute-start.13 = (f32[16,64]{1,0:T(8,128)S(1)}, f32[16,64]{1,0:T(8,128)S(1)}, u32[]{:S(2)}, u32[]{:S(2)}) collective-permute-start(f32[16,64]{1,0:T(8,128)S(1)} %add.209), channel_id=1, source_target_pairs={{0,2},{1,3},{2,0},{3,1},{4,6},{5,7},{6,4},{7,5},{8,10},{9,11},{10,... | collective-permute-start | bytes 12296 | tf_op jit(solution)/shard_map/ppermute | solution.py:232
  77.8 1.9 %collective-permute-done.13 = f32[16,64]{1,0:T(8,128)S(1)} collective-permute-done((f32[16,64]{1,0:T(8,128)S(1)}, f32[16,64]{1,0:T(8,128)S(1)}, u32[]{:S(2)}, u32[]{:S(2)}) %collective-permute-start.13) | collective-permute-done | bytes 4128 | tf_op jit(solution)/shard_map/ppermute | solution.py:232
  (83 shorter events, 17.1 us)
Async XLA Ops:
  0.6 25.4 %copy-start = (bf16[1024,1024]{1,0:T(8,128)(2,1)S(1)}, bf16[1024,1024]{1,0:T(8,128)(2,1)}, u32[]{:S(2)}) copy-start(bf16[1024,1024]{1,0:T(8,128)(2,1)} %param.27) | copy-start | bytes 6291460
  9.8 13.8 %copy-start.3 = (f32[1024]{0:T(1024)S(1)}, f32[1024]{0:T(1024)}, u32[]{:S(2)}) copy-start(f32[1024]{0:T(1024)} %param.22) | copy-start | bytes 12292
  9.8 14.3 %copy-start.6 = (f32[1024]{0:T(1024)S(1)}, f32[1024]{0:T(1024)}, u32[]{:S(2)}) copy-start(f32[1024]{0:T(1024)} %param.24) | copy-start | bytes 12292
  9.8 14.3 %copy-start.7 = (f32[1024]{0:T(1024)S(1)}, f32[1024]{0:T(1024)}, u32[]{:S(2)}) copy-start(f32[1024]{0:T(1024)} %param.23) | copy-start | bytes 12292
  11.3 1.8 %collective-permute-start = (bf16[128,1024]{1,0:T(8,128)(2,1)S(1)}, bf16[128,1024]{1,0:T(8,128)(2,1)}, u32[]{:S(2)}, u32[]{:S(2)}) collective-permute-start(bf16[128,1024]{1,0:T(8,128)(2,1)S(1)} %constant_dynamic-slice_fusion.4), channel_id=1, source_target_pairs={{0,1},{1,0},{2,3},{3,2},{4,5},{5,4},{6,7},{7,6},{8,9},{9,8},{10,11... | collective-permute-start | bytes 786440 | tf_op jit(solution)/shard_map/ppermute | solution.py:89
  11.8 14.3 %copy-start.12 = (f32[1024]{0:T(1024)S(1)}, f32[1024]{0:T(1024)}, u32[]{:S(2)}) copy-start(f32[1024]{0:T(1024)} %param.26) | copy-start | bytes 12292
  14.1 9.5 %collective-permute-start.1 = (bf16[128,1024]{1,0:T(8,128)(2,1)S(1)}, bf16[128,1024]{1,0:T(8,128)(2,1)S(1)}, u32[]{:S(2)}, u32[]{:S(2)}) collective-permute-start(bf16[128,1024]{1,0:T(8,128)(2,1)S(1)} %add_convert_fusion.3), channel_id=1, source_target_pairs={{0,2},{1,3},{2,0},{3,1},{4,6},{5,7},{6,4},{7,5},{8,10},{9,11},{10,... | collective-permute-start | bytes 786440 | tf_op jit(solution)/shard_map/ppermute | solution.py:91
  24.3 1.6 %collective-permute-start.2 = (bf16[128,1024]{1,0:T(8,128)(2,1)S(1)}, bf16[128,1024]{1,0:T(8,128)(2,1)S(1)}, u32[]{:S(2)}, u32[]{:S(2)}) collective-permute-start(bf16[128,1024]{1,0:T(8,128)(2,1)S(1)} %add_convert_fusion.2), channel_id=1, source_target_pairs={{0,1},{1,0},{2,3},{3,2},{4,5},{5,4},{6,7},{7,6},{8,9},{9,8},{10,11... | collective-permute-start | bytes 786440 | tf_op jit(solution)/shard_map/ppermute | solution.py:97
  26.1 15.3 %copy-start.4 = (f32[1024]{0:T(1024)S(1)}, f32[1024]{0:T(1024)}, u32[]{:S(2)}) copy-start(f32[1024]{0:T(1024)} %param.28) | copy-start | bytes 12292
  31.2 10.6 %copy-start.8 = (f32[1024]{0:T(1024)S(1)}, f32[1024]{0:T(1024)}, u32[]{:S(2)}) copy-start(f32[1024]{0:T(1024)} %param.30) | copy-start | bytes 12292
  31.2 10.6 %copy-start.9 = (f32[1024]{0:T(1024)S(1)}, f32[1024]{0:T(1024)}, u32[]{:S(2)}) copy-start(f32[1024]{0:T(1024)} %param.29) | copy-start | bytes 12292
  31.3 1.6 %collective-permute-start.3 = (bf16[128,1024]{1,0:T(8,128)(2,1)S(1)}, bf16[128,1024]{1,0:T(8,128)(2,1)S(1)}, u32[]{:S(2)}, u32[]{:S(2)}) collective-permute-start(bf16[128,1024]{1,0:T(8,128)(2,1)S(1)} %constant_dynamic-slice_fusion.3), channel_id=1, source_target_pairs={{0,1},{1,0},{2,3},{3,2},{4,5},{5,4},{6,7},{7,6},{8,9},{9,8},{10,11... | collective-permute-start | bytes 786440 | tf_op jit(solution)/shard_map/ppermute | solution.py:89
  33.0 16.8 %copy-start.5 = (s32[128,64]{0,1:T(8,128)S(1)}, s32[128,64]{0,1:T(8,128)}, u32[]{:S(2)}) copy-start(s32[128,64]{0,1:T(8,128)} %param.32) | copy-start | bytes 98308
  33.0 8.4 %collective-permute-start.4 = (bf16[128,1024]{1,0:T(8,128)(2,1)S(1)}, bf16[128,1024]{1,0:T(8,128)(2,1)S(1)}, u32[]{:S(2)}, u32[]{:S(2)}) collective-permute-start(bf16[128,1024]{1,0:T(8,128)(2,1)S(1)} %add_convert_fusion.1), channel_id=1, source_target_pairs={{0,2},{1,3},{2,0},{3,1},{4,6},{5,7},{6,4},{7,5},{8,10},{9,11},{10,... | collective-permute-start | bytes 786440 | tf_op jit(solution)/shard_map/ppermute | solution.py:91
  42.1 1.6 %collective-permute-start.5 = (bf16[128,1024]{1,0:T(8,128)(2,1)S(1)}, bf16[128,1024]{1,0:T(8,128)(2,1)S(1)}, u32[]{:S(2)}, u32[]{:S(2)}) collective-permute-start(bf16[128,1024]{1,0:T(8,128)(2,1)S(1)} %add_convert_fusion), channel_id=1, source_target_pairs={{0,1},{1,0},{2,3},{3,2},{4,5},{5,4},{6,7},{7,6},{8,9},{9,8},{10,11... | collective-permute-start | bytes 786440 | tf_op jit(solution)/shard_map/ppermute | solution.py:97
  43.8 14.5 %copy-start.1 = (bf16[256,1024]{1,0:T(8,128)(2,1)}, bf16[256,1024]{1,0:T(8,128)(2,1)S(1)}, u32[]{:S(2)}) copy-start(bf16[256,1024]{1,0:T(8,128)(2,1)S(1)} %maximum_select_fusion.1) | copy-start | bytes 1572868
  44.2 3.7 %collective-permute-start.6 = (bf16[16,256]{1,0:T(8,128)(2,1)S(1)}, bf16[16,256]{1,0:T(8,128)(2,1)S(1)}, u32[]{:S(2)}, u32[]{:S(2)}) collective-permute-start(bf16[16,256]{1,0:T(8,128)(2,1)S(1)} %fusion.65), channel_id=1, source_target_pairs={{0,4},{4,0},{8,12},{12,8},{16,20},{20,16},{24,28},{28,24},{1,5},{5... | collective-permute-start | bytes 24584 | tf_op jit(solution)/shard_map/ppermute | solution.py:58
  47.9 3.7 %collective-permute-start.7 = (bf16[32,256]{1,0:T(8,128)(2,1)S(1)}, bf16[32,256]{1,0:T(8,128)(2,1)S(1)}, u32[]{:S(2)}, u32[]{:S(2)}) collective-permute-start(bf16[32,256]{1,0:T(8,128)(2,1)S(1)} %maximum_select_fusion.5), channel_id=1, source_target_pairs={{0,8},{4,12},{8,0},{12,4},{16,24},{20,28},{24,16},{28,20},{1,9},{5... | collective-permute-start | bytes 49160 | tf_op jit(solution)/shard_map/ppermute | solution.py:58
  51.6 4.9 %collective-permute-start.8 = (bf16[64,256]{1,0:T(8,128)(2,1)S(1)}, bf16[64,256]{1,0:T(8,128)(2,1)S(1)}, u32[]{:S(2)}, u32[]{:S(2)}) collective-permute-start(bf16[64,256]{1,0:T(8,128)(2,1)S(1)} %maximum_select_fusion.4), channel_id=1, source_target_pairs={{0,16},{4,20},{8,24},{12,28},{16,0},{20,4},{24,8},{28,12},{1,17},{... | collective-permute-start | bytes 98312 | tf_op jit(solution)/shard_map/ppermute | solution.py:58
  62.5 4.9 %collective-permute-start.9 = (f32[64,64]{1,0:T(8,128)S(1)}, f32[64,64]{1,0:T(8,128)S(1)}, u32[]{:S(2)}, u32[]{:S(2)}) collective-permute-start(f32[64,64]{1,0:T(8,128)S(1)} %constant_dynamic-slice_fusion.2), channel_id=1, source_target_pairs={{0,16},{4,20},{8,24},{12,28},{16,0},{20,4},{24,8},{28,12},{1,17},{... | collective-permute-start | bytes 49160 | tf_op jit(solution)/shard_map/ppermute | solution.py:47
  67.4 3.8 %collective-permute-start.10 = (f32[32,64]{1,0:T(8,128)S(1)}, f32[32,64]{1,0:T(8,128)S(1)}, u32[]{:S(2)}, u32[]{:S(2)}) collective-permute-start(f32[32,64]{1,0:T(8,128)S(1)} %constant_dynamic-slice_fusion.1), channel_id=1, source_target_pairs={{0,8},{4,12},{8,0},{12,4},{16,24},{20,28},{24,16},{28,20},{1,9},{5... | collective-permute-start | bytes 24584 | tf_op jit(solution)/shard_map/ppermute | solution.py:47
  71.2 3.7 %collective-permute-start.11 = (f32[16,64]{1,0:T(8,128)S(1)}, f32[16,64]{1,0:T(8,128)S(1)}, u32[]{:S(2)}, u32[]{:S(2)}) collective-permute-start(f32[16,64]{1,0:T(8,128)S(1)} %constant_dynamic-slice_fusion), channel_id=1, source_target_pairs={{0,4},{4,0},{8,12},{12,8},{16,20},{20,16},{24,28},{28,24},{1,5},{5... | collective-permute-start | bytes 12296 | tf_op jit(solution)/shard_map/ppermute | solution.py:47
  74.9 1.2 %collective-permute-start.12 = (f32[16,64]{1,0:T(8,128)S(1)}, f32[16,64]{1,0:T(8,128)S(1)}, u32[]{:S(2)}, u32[]{:S(2)}) collective-permute-start(f32[16,64]{1,0:T(8,128)S(1)} %dynamic-slice_add_fusion.2), channel_id=1, source_target_pairs={{0,1},{1,0},{2,3},{3,2},{4,5},{5,4},{6,7},{7,6},{8,9},{9,8},{10,11... | collective-permute-start | bytes 12296 | tf_op jit(solution)/shard_map/ppermute | solution.py:232
  76.0 3.7 %collective-permute-start.13 = (f32[16,64]{1,0:T(8,128)S(1)}, f32[16,64]{1,0:T(8,128)S(1)}, u32[]{:S(2)}, u32[]{:S(2)}) collective-permute-start(f32[16,64]{1,0:T(8,128)S(1)} %add.209), channel_id=1, source_target_pairs={{0,2},{1,3},{2,0},{3,1},{4,6},{5,7},{6,4},{7,5},{8,10},{9,11},{10,... | collective-permute-start | bytes 12296 | tf_op jit(solution)/shard_map/ppermute | solution.py:232
  (4 other events, 12.3 us)

commit v16 on v11

--- a/solution.py
+++ b/solution.py
@@ -164,12 +164,20 @@
         and candidates.shape[0] % n_dp == 0
     )
     if xor_ok:
-        gathered = all_gather_xor(unit_quarter, "dp", n_dp, levels_of(n_dp))
+        dp_levels = levels_of(n_dp)
+        gather_levels = dp_levels[-1:] + dp_levels[:-1]
+        layout = gather_levels[::-1]
+        gathered = all_gather_xor(unit_quarter, "dp", n_dp, gather_levels)
     else:
         gathered = lax.all_gather(unit_quarter, "dp", axis=0, tiled=True)
     all_texts = candidates.shape[0]
     shard_rows = index.shape[0]
     local_rows = candidates - row_base
+    if xor_ok and n_dp > 1:
+        bits = len(dp_levels)
+        grouped = local_rows.reshape([2] * bits + [-1, local_rows.shape[1]])
+        order = [bits - 1 - int(math.log2(k)) for k in layout]
+        local_rows = grouped.transpose(order + [bits, bits + 1]).reshape(local_rows.shape)
     held = (local_rows >= 0) & (local_rows < shard_rows)
 
     def pick(packed):
@@ -220,7 +228,7 @@
         )
         scores = lax.all_gather(slice_scores, "tensor", axis=0, tiled=True)
         return (states, scores)
-    text_scores, _ = reduce_scatter_xor(partial_scores, "dp", n_dp, levels_of(n_dp)[::-1])
+    text_scores, _ = reduce_scatter_xor(partial_scores, "dp", n_dp, layout)
     for k in levels_of(n_tensor):
         text_scores = text_scores + lax.ppermute(text_scores, "tensor", xor_pairs(n_tensor, k))
     return (states, text_scores)

time: 77.1 us -> 77.8 us (level)
  local copies, waits for them, and re-layouts: 1.22 us -> 2.03 us
    another operation x1, local copies, waits for them, and re-layouts: 0.08 us -> 0.88 us
where the time goes in v16:
time: 77.8 us; the launch traced here: 77.5 us
  waiting for transfers between devices  33.3 us (43%)
  starting transfers between devices  20.4 us (26%)
  matrix products  14.2 us (18%)
  other arithmetic  6.53 us (8%)
  local copies, waits for them, and re-layouts  2.03 us (3%)
  between operations  1.14 us (1%)
    ppermute x2, waiting for transfers between devices, settle_by_chip(): across = lax.ppermute(chip_sum, 'tensor', xor_pairs(4, 2))  13.2 us
    ppermute x3, starting transfers between devices, reduce_scatter_xor(): got = lax.ppermute(theirs.astype(wire), axis, xor_pairs(n, k))  6.56 us
    ppermute x3, starting transfers between devices, all_gather_xor(): other = lax.ppermute(cur, axis, xor_pairs(n, k))  6.49 us
    ppermute x3, waiting for transfers between devices, reduce_scatter_xor(): got = lax.ppermute(theirs.astype(wire), axis, xor_pairs(n, k))  5.78 us
    ppermute x3, waiting for transfers between devices, all_gather_xor(): other = lax.ppermute(cur, axis, xor_pairs(n, k))  5.57 us
    dot_general x1, matrix products, body(): jnp.dot(activated, w_down, preferred_element_type=jnp.float32)  5.12 us
    ppermute x2, starting transfers between devices, settle_by_chip(): across = lax.ppermute(chip_sum, 'tensor', xor_pairs(4, 2))  4.72 us
    ppermute x2, waiting for transfers between devices, body(): lax.ppermute(text_scores, 'tensor', xor_pairs(n_tensor, k))  3.09 us
  transfers between devices with their start and end apart: 14, of which 14 were waited for; matrix products, arithmetic and copies ran while one was open for 0% of the time, Pallas kernels for 0%

profile of v16, /device:TPU:0, one launch (start us, length us, event | category | flops | bytes accessed | tf_op | source)
XLA Modules:
  0.0 77.5 jit_solution(8541315902281210864)
XLA Ops:
  1.9 2.2 %fusion.104 = (bf16[3,256,256]{1,2,0:T(8,128)(2,1)S(1)}, f32[3,256,256]{1,2,0:T(8,128)S(1)}) fusion(f32[3,256]{1,0:T(4,128)} %param.19, bf16[3,1024,256]{2,1,0:T(8,128)(2,1)} %param.18, bf16[256,1024]{1,0:T(8,128)(2,1)} %param.16), kind=kOutput, calls=%fused_computation.170 | convolution fusion | flops 403046400 | bytes 3279872 | tf_op jit(solution)/shard_map/td,jdf->jtf/dot_general | solution.py:125
  7.0 1.4 %convolution_convert_fusion = bf16[256,1024]{1,0:T(8,128)(2,1)S(1)} fusion(bf16[256,256]{0,1:T(8,128)(2,1)S(1)} %bitcast.77, bf16[256,1024]{1,0:T(8,128)(2,1)} %param.20), kind=kOutput, calls=%fused_computation.10 | convolution fusion | flops 134479872 | bytes 1179648 | tf_op jit(solution)/shard_map/dot_general | solution.py:140
  11.3 2.9 %collective-permute-start.1 = (bf16[128,1024]{1,0:T(8,128)(2,1)S(1)}, bf16[128,1024]{1,0:T(8,128)(2,1)S(1)}, u32[]{:S(2)}, u32[]{:S(2)}) collective-permute-start(bf16[128,1024]{1,0:T(8,128)(2,1)S(1)} %add_convert_fusion.3), channel_id=1, source_target_pairs={{0,2},{1,3},{2,0},{3,1},{4,6},{5,7},{6,4},{7,5},{8,10},{9,11},{10,... | collective-permute-start | bytes 786440 | tf_op jit(solution)/shard_map/ppermute | solution.py:91
  14.2 6.6 %collective-permute-done.1 = bf16[128,1024]{1,0:T(8,128)(2,1)S(1)} collective-permute-done((bf16[128,1024]{1,0:T(8,128)(2,1)S(1)}, bf16[128,1024]{1,0:T(8,128)(2,1)S(1)}, u32[]{:S(2)}, u32[]{:S(2)}) %collective-permute-start.1) | collective-permute-done | bytes 262176 | tf_op jit(solution)/shard_map/ppermute | solution.py:91
  21.6 1.5 %collective-permute-done.2 = bf16[128,1024]{1,0:T(8,128)(2,1)S(1)} collective-permute-done((bf16[128,1024]{1,0:T(8,128)(2,1)S(1)}, bf16[128,1024]{1,0:T(8,128)(2,1)S(1)}, u32[]{:S(2)}, u32[]{:S(2)}) %collective-permute-start.2) | collective-permute-done | bytes 262176 | tf_op jit(solution)/shard_map/ppermute | solution.py:97
  23.3 5.1 %convolution_convert_fusion.1 = bf16[256,1024]{1,0:T(8,128)(2,1)S(1)} fusion(bf16[1024,1024]{1,0:T(8,128)(2,1)S(1)} %copy-done, bf16[256,1024]{1,0:T(8,128)(2,1)S(1)} %maximum_select_fusion, bf16[1024,1024]{1,0:T(8,128)(2,1)} %param.24, f32[1024]{0:T(1024)S(1)} %copy-done.11), kind=kOutput, calls=%fused_computation.11 | convolution fusion | flops 1091305472 | bytes 5246976 | tf_op jit(solution)/shard_map/dot_general | solution.py:145
  30.2 1.8 %collective-permute-start.4 = (bf16[128,1024]{1,0:T(8,128)(2,1)S(1)}, bf16[128,1024]{1,0:T(8,128)(2,1)S(1)}, u32[]{:S(2)}, u32[]{:S(2)}) collective-permute-start(bf16[128,1024]{1,0:T(8,128)(2,1)S(1)} %add_convert_fusion.1), channel_id=1, source_target_pairs={{0,2},{1,3},{2,0},{3,1},{4,6},{5,7},{6,4},{7,5},{8,10},{9,11},{10,... | collective-permute-start | bytes 786440 | tf_op jit(solution)/shard_map/ppermute | solution.py:91
  32.0 6.6 %collective-permute-done.4 = bf16[128,1024]{1,0:T(8,128)(2,1)S(1)} collective-permute-done((bf16[128,1024]{1,0:T(8,128)(2,1)S(1)}, bf16[128,1024]{1,0:T(8,128)(2,1)S(1)}, u32[]{:S(2)}, u32[]{:S(2)}) %collective-permute-start.4) | collective-permute-done | bytes 262176 | tf_op jit(solution)/shard_map/ppermute | solution.py:91
  41.4 2.8 %collective-permute-start.6 = (bf16[16,256]{1,0:T(8,128)(2,1)S(1)}, bf16[16,256]{1,0:T(8,128)(2,1)S(1)}, u32[]{:S(2)}, u32[]{:S(2)}) collective-permute-start(bf16[16,256]{1,0:T(8,128)(2,1)S(1)} %fusion.65), channel_id=1, source_target_pairs={{0,16},{4,20},{8,24},{12,28},{16,0},{20,4},{24,8},{28,12},{1,17},{... | collective-permute-start | bytes 24584 | tf_op jit(solution)/shard_map/ppermute | solution.py:58
  44.3 1.7 %collective-permute-done.6 = bf16[16,256]{1,0:T(8,128)(2,1)S(1)} collective-permute-done((bf16[16,256]{1,0:T(8,128)(2,1)S(1)}, bf16[16,256]{1,0:T(8,128)(2,1)S(1)}, u32[]{:S(2)}, u32[]{:S(2)}) %collective-permute-start.6) | collective-permute-done | bytes 8224 | tf_op jit(solution)/shard_map/ppermute | solution.py:58
  46.0 1.8 %collective-permute-start.7 = (bf16[32,256]{1,0:T(8,128)(2,1)S(1)}, bf16[32,256]{1,0:T(8,128)(2,1)S(1)}, u32[]{:S(2)}, u32[]{:S(2)}) collective-permute-start(bf16[32,256]{1,0:T(8,128)(2,1)S(1)} %maximum_select_fusion.5), channel_id=1, source_target_pairs={{0,4},{4,0},{8,12},{12,8},{16,20},{20,16},{24,28},{28,24},{1,5},{5... | collective-permute-start | bytes 49160 | tf_op jit(solution)/shard_map/ppermute | solution.py:58
  47.8 1.9 %collective-permute-done.7 = bf16[32,256]{1,0:T(8,128)(2,1)S(1)} collective-permute-done((bf16[32,256]{1,0:T(8,128)(2,1)S(1)}, bf16[32,256]{1,0:T(8,128)(2,1)S(1)}, u32[]{:S(2)}, u32[]{:S(2)}) %collective-permute-start.7) | collective-permute-done | bytes 16416 | tf_op jit(solution)/shard_map/ppermute | solution.py:58
  49.7 1.9 %collective-permute-start.8 = (bf16[64,256]{1,0:T(8,128)(2,1)S(1)}, bf16[64,256]{1,0:T(8,128)(2,1)S(1)}, u32[]{:S(2)}, u32[]{:S(2)}) collective-permute-start(bf16[64,256]{1,0:T(8,128)(2,1)S(1)} %maximum_select_fusion.4), channel_id=1, source_target_pairs={{0,8},{4,12},{8,0},{12,4},{16,24},{20,28},{24,16},{28,20},{1,9},{5... | collective-permute-start | bytes 98312 | tf_op jit(solution)/shard_map/ppermute | solution.py:58
  51.7 2.0 %collective-permute-done.8 = bf16[64,256]{1,0:T(8,128)(2,1)S(1)} collective-permute-done((bf16[64,256]{1,0:T(8,128)(2,1)S(1)}, bf16[64,256]{1,0:T(8,128)(2,1)S(1)}, u32[]{:S(2)}, u32[]{:S(2)}) %collective-permute-start.8) | collective-permute-done | bytes 32800 | tf_op jit(solution)/shard_map/ppermute | solution.py:58
  53.7 1.7 %convert_bitcast_fusion = (bf16[16,8,16,128]{3,1,2,0:T(8,128)(2,1)S(1)}, bf16[16,8,16,128]{3,1,2,0:T(8,128)(2,1)S(1)}) fusion(bf16[2048,256]{1,0:T(8,128)(2,1)} %param.30, bf16[64,256]{1,0:T(8,128)(2,1)S(1)} %collective-permute-done.8, bf16[64,256]{1,0:T(8,128)(2,1)S(1)} %maximum_select_fusion.4, pred[]{:T(512)S(6)} %eq.90), kind=kOutput, calls=%fused_computation.87 | convolution fusion | flops 135561216 | bytes 2162689 | tf_op jit(solution)/shard_map/dot_general | solution.py:186
  57.0 2.7 %fusion.2 = f32[128,64]{1,0:T(8,128)S(1)} fusion(f32[128,64,256]{2,1,0:T(8,128)S(1)} %fusion.9, s32[128,64]{1,0:T(8,128)S(1)} %get-tuple-element.6), kind=kLoop, calls=%fused_computation.3 | loop fusion | flops 4186112 | bytes 8454144 | tf_op jit(solution)/shard_map/reduce_sum | solution.py:205
  59.7 1.9 %collective-permute-start.9 = (f32[64,64]{1,0:T(8,128)S(1)}, f32[64,64]{1,0:T(8,128)S(1)}, u32[]{:S(2)}, u32[]{:S(2)}) collective-permute-start(f32[64,64]{1,0:T(8,128)S(1)} %constant_dynamic-slice_fusion.2), channel_id=1, source_target_pairs={{0,8},{4,12},{8,0},{12,4},{16,24},{20,28},{24,16},{28,20},{1,9},{5... | collective-permute-start | bytes 49160 | tf_op jit(solution)/shard_map/ppermute | solution.py:47
  61.6 2.1 %collective-permute-done.9 = f32[64,64]{1,0:T(8,128)S(1)} collective-permute-done((f32[64,64]{1,0:T(8,128)S(1)}, f32[64,64]{1,0:T(8,128)S(1)}, u32[]{:S(2)}, u32[]{:S(2)}) %collective-permute-start.9) | collective-permute-done | bytes 16416 | tf_op jit(solution)/shard_map/ppermute | solution.py:47
  63.7 1.8 %collective-permute-start.10 = (f32[32,64]{1,0:T(8,128)S(1)}, f32[32,64]{1,0:T(8,128)S(1)}, u32[]{:S(2)}, u32[]{:S(2)}) collective-permute-start(f32[32,64]{1,0:T(8,128)S(1)} %constant_dynamic-slice_fusion.1), channel_id=1, source_target_pairs={{0,4},{4,0},{8,12},{12,8},{16,20},{20,16},{24,28},{28,24},{1,5},{5... | collective-permute-start | bytes 24584 | tf_op jit(solution)/shard_map/ppermute | solution.py:47
  65.5 2.0 %collective-permute-done.10 = f32[32,64]{1,0:T(8,128)S(1)} collective-permute-done((f32[32,64]{1,0:T(8,128)S(1)}, f32[32,64]{1,0:T(8,128)S(1)}, u32[]{:S(2)}, u32[]{:S(2)}) %collective-permute-start.10) | collective-permute-done | bytes 8224 | tf_op jit(solution)/shard_map/ppermute | solution.py:47
  67.5 2.8 %collective-permute-start.11 = (f32[16,64]{1,0:T(8,128)S(1)}, f32[16,64]{1,0:T(8,128)S(1)}, u32[]{:S(2)}, u32[]{:S(2)}) collective-permute-start(f32[16,64]{1,0:T(8,128)S(1)} %constant_dynamic-slice_fusion), channel_id=1, source_target_pairs={{0,16},{4,20},{8,24},{12,28},{16,0},{20,4},{24,8},{28,12},{1,17},{... | collective-permute-start | bytes 12296 | tf_op jit(solution)/shard_map/ppermute | solution.py:47
  70.3 1.7 %collective-permute-done.11 = f32[16,64]{1,0:T(8,128)S(1)} collective-permute-done((f32[16,64]{1,0:T(8,128)S(1)}, f32[16,64]{1,0:T(8,128)S(1)}, u32[]{:S(2)}, u32[]{:S(2)}) %collective-permute-start.11) | collective-permute-done | bytes 4128 | tf_op jit(solution)/shard_map/ppermute | solution.py:47
  73.2 1.7 %collective-permute-start.13 = (f32[16,64]{1,0:T(8,128)S(1)}, f32[16,64]{1,0:T(8,128)S(1)}, u32[]{:S(2)}, u32[]{:S(2)}) collective-permute-start(f32[16,64]{1,0:T(8,128)S(1)} %add.217), channel_id=1, source_target_pairs={{0,2},{1,3},{2,0},{3,1},{4,6},{5,7},{6,4},{7,5},{8,10},{9,11},{10,... | collective-permute-start | bytes 12296 | tf_op jit(solution)/shard_map/ppermute | solution.py:233
  75.0 1.9 %collective-permute-done.13 = f32[16,64]{1,0:T(8,128)S(1)} collective-permute-done((f32[16,64]{1,0:T(8,128)S(1)}, f32[16,64]{1,0:T(8,128)S(1)}, u32[]{:S(2)}, u32[]{:S(2)}) %collective-permute-start.13) | collective-permute-done | bytes 4128 | tf_op jit(solution)/shard_map/ppermute | solution.py:233
  (83 shorter events, 15.8 us)
Async XLA Ops:
  0.6 22.6 %copy-start = (bf16[1024,1024]{1,0:T(8,128)(2,1)S(1)}, bf16[1024,1024]{1,0:T(8,128)(2,1)}, u32[]{:S(2)}) copy-start(bf16[1024,1024]{1,0:T(8,128)(2,1)} %param.26) | copy-start | bytes 6291460
  7.0 13.9 %copy-start.1 = (bf16[256,1024]{1,0:T(8,128)(2,1)S(1)}, bf16[256,1024]{1,0:T(8,128)(2,1)}, u32[]{:S(2)}) copy-start(bf16[256,1024]{1,0:T(8,128)(2,1)} %param.16) | copy-start | bytes 1572868
  7.0 13.9 %copy-start.3 = (f32[1024]{0:T(1024)S(1)}, f32[1024]{0:T(1024)}, u32[]{:S(2)}) copy-start(f32[1024]{0:T(1024)} %param.21) | copy-start | bytes 12292
  7.0 14.3 %copy-start.6 = (f32[1024]{0:T(1024)S(1)}, f32[1024]{0:T(1024)}, u32[]{:S(2)}) copy-start(f32[1024]{0:T(1024)} %param.23) | copy-start | bytes 12292
  7.0 14.3 %copy-start.7 = (f32[1024]{0:T(1024)S(1)}, f32[1024]{0:T(1024)}, u32[]{:S(2)}) copy-start(f32[1024]{0:T(1024)} %param.22) | copy-start | bytes 12292
  8.5 1.8 %collective-permute-start = (bf16[128,1024]{1,0:T(8,128)(2,1)S(1)}, bf16[128,1024]{1,0:T(8,128)(2,1)}, u32[]{:S(2)}, u32[]{:S(2)}) collective-permute-start(bf16[128,1024]{1,0:T(8,128)(2,1)S(1)} %constant_dynamic-slice_fusion.4), channel_id=1, source_target_pairs={{0,1},{1,0},{2,3},{3,2},{4,5},{5,4},{6,7},{7,6},{8,9},{9,8},{10,11... | collective-permute-start | bytes 786440 | tf_op jit(solution)/shard_map/ppermute | solution.py:89
  9.0 14.3 %copy-start.11 = (f32[1024]{0:T(1024)S(1)}, f32[1024]{0:T(1024)}, u32[]{:S(2)}) copy-start(f32[1024]{0:T(1024)} %param.25) | copy-start | bytes 12292
  11.3 9.5 %collective-permute-start.1 = (bf16[128,1024]{1,0:T(8,128)(2,1)S(1)}, bf16[128,1024]{1,0:T(8,128)(2,1)S(1)}, u32[]{:S(2)}, u32[]{:S(2)}) collective-permute-start(bf16[128,1024]{1,0:T(8,128)(2,1)S(1)} %add_convert_fusion.3), channel_id=1, source_target_pairs={{0,2},{1,3},{2,0},{3,1},{4,6},{5,7},{6,4},{7,5},{8,10},{9,11},{10,... | collective-permute-start | bytes 786440 | tf_op jit(solution)/shard_map/ppermute | solution.py:91
  21.5 1.6 %collective-permute-start.2 = (bf16[128,1024]{1,0:T(8,128)(2,1)S(1)}, bf16[128,1024]{1,0:T(8,128)(2,1)S(1)}, u32[]{:S(2)}, u32[]{:S(2)}) collective-permute-start(bf16[128,1024]{1,0:T(8,128)(2,1)S(1)} %add_convert_fusion.2), channel_id=1, source_target_pairs={{0,1},{1,0},{2,3},{3,2},{4,5},{5,4},{6,7},{7,6},{8,9},{9,8},{10,11... | collective-permute-start | bytes 786440 | tf_op jit(solution)/shard_map/ppermute | solution.py:97
  23.3 15.3 %copy-start.4 = (f32[1024]{0:T(1024)S(1)}, f32[1024]{0:T(1024)}, u32[]{:S(2)}) copy-start(f32[1024]{0:T(1024)} %param.27) | copy-start | bytes 12292
  28.5 10.9 %copy-start.5 = (s32[128,64]{0,1:T(8,128)S(1)}, s32[128,64]{0,1:T(8,128)}, u32[]{:S(2)}) copy-start(s32[128,64]{0,1:T(8,128)} %param.31) | copy-start | bytes 98308
  28.5 11.0 %copy-start.10 = (s32[1,16]{1,0:T(1,128)S(1)}, s32[1,16]{1,0:T(1,128)}, u32[]{:S(2)}) copy-start(s32[1,16]{1,0:T(1,128)} %param.17) | copy-start | bytes 196
  28.5 1.6 %collective-permute-start.3 = (bf16[128,1024]{1,0:T(8,128)(2,1)S(1)}, bf16[128,1024]{1,0:T(8,128)(2,1)S(1)}, u32[]{:S(2)}, u32[]{:S(2)}) collective-permute-start(bf16[128,1024]{1,0:T(8,128)(2,1)S(1)} %constant_dynamic-slice_fusion.3), channel_id=1, source_target_pairs={{0,1},{1,0},{2,3},{3,2},{4,5},{5,4},{6,7},{7,6},{8,9},{9,8},{10,11... | collective-permute-start | bytes 786440 | tf_op jit(solution)/shard_map/ppermute | solution.py:89
  30.2 8.4 %collective-permute-start.4 = (bf16[128,1024]{1,0:T(8,128)(2,1)S(1)}, bf16[128,1024]{1,0:T(8,128)(2,1)S(1)}, u32[]{:S(2)}, u32[]{:S(2)}) collective-permute-start(bf16[128,1024]{1,0:T(8,128)(2,1)S(1)} %add_convert_fusion.1), channel_id=1, source_target_pairs={{0,2},{1,3},{2,0},{3,1},{4,6},{5,7},{6,4},{7,5},{8,10},{9,11},{10,... | collective-permute-start | bytes 786440 | tf_op jit(solution)/shard_map/ppermute | solution.py:91
  39.3 1.6 %collective-permute-start.5 = (bf16[128,1024]{1,0:T(8,128)(2,1)S(1)}, bf16[128,1024]{1,0:T(8,128)(2,1)S(1)}, u32[]{:S(2)}, u32[]{:S(2)}) collective-permute-start(bf16[128,1024]{1,0:T(8,128)(2,1)S(1)} %add_convert_fusion), channel_id=1, source_target_pairs={{0,1},{1,0},{2,3},{3,2},{4,5},{5,4},{6,7},{7,6},{8,9},{9,8},{10,11... | collective-permute-start | bytes 786440 | tf_op jit(solution)/shard_map/ppermute | solution.py:97
  41.0 14.5 %copy-start.2 = (bf16[256,1024]{1,0:T(8,128)(2,1)}, bf16[256,1024]{1,0:T(8,128)(2,1)S(1)}, u32[]{:S(2)}) copy-start(bf16[256,1024]{1,0:T(8,128)(2,1)S(1)} %maximum_select_fusion.1) | copy-start | bytes 1572868
  41.4 4.6 %collective-permute-start.6 = (bf16[16,256]{1,0:T(8,128)(2,1)S(1)}, bf16[16,256]{1,0:T(8,128)(2,1)S(1)}, u32[]{:S(2)}, u32[]{:S(2)}) collective-permute-start(bf16[16,256]{1,0:T(8,128)(2,1)S(1)} %fusion.65), channel_id=1, source_target_pairs={{0,16},{4,20},{8,24},{12,28},{16,0},{20,4},{24,8},{28,12},{1,17},{... | collective-permute-start | bytes 24584 | tf_op jit(solution)/shard_map/ppermute | solution.py:58
  46.0 3.7 %collective-permute-start.7 = (bf16[32,256]{1,0:T(8,128)(2,1)S(1)}, bf16[32,256]{1,0:T(8,128)(2,1)S(1)}, u32[]{:S(2)}, u32[]{:S(2)}) collective-permute-start(bf16[32,256]{1,0:T(8,128)(2,1)S(1)} %maximum_select_fusion.5), channel_id=1, source_target_pairs={{0,4},{4,0},{8,12},{12,8},{16,20},{20,16},{24,28},{28,24},{1,5},{5... | collective-permute-start | bytes 49160 | tf_op jit(solution)/shard_map/ppermute | solution.py:58
  49.7 4.0 %collective-permute-start.8 = (bf16[64,256]{1,0:T(8,128)(2,1)S(1)}, bf16[64,256]{1,0:T(8,128)(2,1)S(1)}, u32[]{:S(2)}, u32[]{:S(2)}) collective-permute-start(bf16[64,256]{1,0:T(8,128)(2,1)S(1)} %maximum_select_fusion.4), channel_id=1, source_target_pairs={{0,8},{4,12},{8,0},{12,4},{16,24},{20,28},{24,16},{28,20},{1,9},{5... | collective-permute-start | bytes 98312 | tf_op jit(solution)/shard_map/ppermute | solution.py:58
  59.7 4.0 %collective-permute-start.9 = (f32[64,64]{1,0:T(8,128)S(1)}, f32[64,64]{1,0:T(8,128)S(1)}, u32[]{:S(2)}, u32[]{:S(2)}) collective-permute-start(f32[64,64]{1,0:T(8,128)S(1)} %constant_dynamic-slice_fusion.2), channel_id=1, source_target_pairs={{0,8},{4,12},{8,0},{12,4},{16,24},{20,28},{24,16},{28,20},{1,9},{5... | collective-permute-start | bytes 49160 | tf_op jit(solution)/shard_map/ppermute | solution.py:47
  63.7 3.8 %collective-permute-start.10 = (f32[32,64]{1,0:T(8,128)S(1)}, f32[32,64]{1,0:T(8,128)S(1)}, u32[]{:S(2)}, u32[]{:S(2)}) collective-permute-start(f32[32,64]{1,0:T(8,128)S(1)} %constant_dynamic-slice_fusion.1), channel_id=1, source_target_pairs={{0,4},{4,0},{8,12},{12,8},{16,20},{20,16},{24,28},{28,24},{1,5},{5... | collective-permute-start | bytes 24584 | tf_op jit(solution)/shard_map/ppermute | solution.py:47
  67.5 4.5 %collective-permute-start.11 = (f32[16,64]{1,0:T(8,128)S(1)}, f32[16,64]{1,0:T(8,128)S(1)}, u32[]{:S(2)}, u32[]{:S(2)}) collective-permute-start(f32[16,64]{1,0:T(8,128)S(1)} %constant_dynamic-slice_fusion), channel_id=1, source_target_pairs={{0,16},{4,20},{8,24},{12,28},{16,0},{20,4},{24,8},{28,12},{1,17},{... | collective-permute-start | bytes 12296 | tf_op jit(solution)/shard_map/ppermute | solution.py:47
  72.1 1.2 %collective-permute-start.12 = (f32[16,64]{1,0:T(8,128)S(1)}, f32[16,64]{1,0:T(8,128)S(1)}, u32[]{:S(2)}, u32[]{:S(2)}) collective-permute-start(f32[16,64]{1,0:T(8,128)S(1)} %dynamic-slice_add_fusion.2), channel_id=1, source_target_pairs={{0,1},{1,0},{2,3},{3,2},{4,5},{5,4},{6,7},{7,6},{8,9},{9,8},{10,11... | collective-permute-start | bytes 12296 | tf_op jit(solution)/shard_map/ppermute | solution.py:233
  73.2 3.7 %collective-permute-start.13 = (f32[16,64]{1,0:T(8,128)S(1)}, f32[16,64]{1,0:T(8,128)S(1)}, u32[]{:S(2)}, u32[]{:S(2)}) collective-permute-start(f32[16,64]{1,0:T(8,128)S(1)} %add.217), channel_id=1, source_target_pairs={{0,2},{1,3},{2,0},{3,1},{4,6},{5,7},{6,4},{7,5},{8,10},{9,11},{10,... | collective-permute-start | bytes 12296 | tf_op jit(solution)/shard_map/ppermute | solution.py:233
  (2 other events, 21.3 us)

commit v17 on v11

--- a/solution.py
+++ b/solution.py
@@ -181,20 +181,20 @@
         minor = 128
         if shard_rows % minor == 0:
             major = shard_rows // minor
-            major_hot = (
-                (wanted // minor)[:, :, None] == jnp.arange(major, dtype=jnp.int32)[None, None, :]
+            minor_hot = (
+                (wanted % minor)[:, :, None] == jnp.arange(minor, dtype=jnp.int32)[None, None, :]
             ).astype(jnp.bfloat16)
             high = tile.astype(jnp.bfloat16)
             low = (tile - high.astype(jnp.float32)).astype(jnp.bfloat16)
             parts = jnp.concatenate(
-                [high.reshape(texts, major, minor), low.reshape(texts, major, minor)], axis=2
+                [high.reshape(texts, major, minor), low.reshape(texts, major, minor)], axis=1
             )
             chosen_parts = jnp.einsum(
-                "tca,tab->tcb", major_hot, parts, preferred_element_type=jnp.float32
+                "tcb,tab->tca", minor_hot, parts, preferred_element_type=jnp.float32
             )
-            rows_of = chosen_parts[:, :, :minor] + chosen_parts[:, :, minor:]
-            minor_hot = (wanted % minor)[:, :, None] == jnp.arange(minor, dtype=jnp.int32)[None, None, :]
-            picked = jnp.sum(jnp.where(minor_hot, rows_of, 0.0), axis=2)
+            blocks_of = chosen_parts[:, :, :major] + chosen_parts[:, :, major:]
+            major_hot = (wanted // minor)[:, :, None] == jnp.arange(major, dtype=jnp.int32)[None, None, :]
+            picked = jnp.sum(jnp.where(major_hot, blocks_of, 0.0), axis=2)
         else:
             row_ids = jnp.arange(shard_rows, dtype=jnp.int32)
             chosen = wanted[:, :, None] == row_ids[None, None, :]

time: 77.1 us -> 76.2 us (0.988)
  other arithmetic: 6.51 us -> 4.27 us
  matrix products: 14.3 us -> 15.6 us
    reduce_sum x1, other arithmetic: 2.66 us -> 0.42 us  [pick(): picked = jnp.sum(jnp.where(major_hot, blocks_of, 0.0), axis=2)]
    dot_general x1, matrix products: 1.3 us -> 2.63 us  [pick(): jnp.einsum('tcb,tab->tca', minor_hot, parts, preferred_element_type=jnp.f...]
where the time goes in v17:
time: 76.2 us; the launch traced here: 75.9 us
  waiting for transfers between devices  33.3 us (44%)
  starting transfers between devices  20.4 us (27%)
  matrix products  15.6 us (20%)
  other arithmetic  4.27 us (6%)
  local copies, waits for them, and re-layouts  1.22 us (2%)
  between operations  1.06 us (1%)
    ppermute x2, waiting for transfers between devices, settle_by_chip(): across = lax.ppermute(chip_sum, 'tensor', xor_pairs(4, 2))  13.2 us
    ppermute x3, starting transfers between devices, reduce_scatter_xor(): got = lax.ppermute(theirs.astype(wire), axis, xor_pairs(n, k))  6.59 us
    ppermute x3, starting transfers between devices, all_gather_xor(): other = lax.ppermute(cur, axis, xor_pairs(n, k))  6.5 us
    ppermute x3, waiting for transfers between devices, reduce_scatter_xor(): got = lax.ppermute(theirs.astype(wire), axis, xor_pairs(n, k))  5.74 us
    ppermute x3, waiting for transfers between devices, all_gather_xor(): other = lax.ppermute(cur, axis, xor_pairs(n, k))  5.57 us
    dot_general x1, matrix products, body(): jnp.dot(activated, w_down, preferred_element_type=jnp.float32)  5.11 us
    ppermute x2, starting transfers between devices, settle_by_chip(): across = lax.ppermute(chip_sum, 'tensor', xor_pairs(4, 2))  4.74 us
    ppermute x2, waiting for transfers between devices, body(): lax.ppermute(text_scores, 'tensor', xor_pairs(n_tensor, k))  3.08 us
  transfers between devices with their start and end apart: 14, of which 14 were waited for; matrix products, arithmetic and copies ran while one was open for 0% of the time, Pallas kernels for 0%

profile of v17, /device:TPU:0, one launch (start us, length us, event | category | flops | bytes accessed | tf_op | source)
XLA Modules:
  0.0 75.9 jit_solution(4700352949303860888)
XLA Ops:
  0.7 2.3 %fusion.103 = (bf16[3,256,256]{1,2,0:T(8,128)(2,1)S(1)}, f32[3,256,256]{1,2,0:T(8,128)S(1)}) fusion(f32[3,256]{1,0:T(4,128)} %param.19, bf16[3,1024,256]{2,1,0:T(8,128)(2,1)} %param.18, bf16[256,1024]{1,0:T(8,128)(2,1)} %param.16), kind=kOutput, calls=%fused_computation.168 | convolution fusion | flops 403046400 | bytes 3279872 | tf_op jit(solution)/shard_map/td,jdf->jtf/dot_general | solution.py:125
  10.7 2.9 %collective-permute-start.1 = (bf16[128,1024]{1,0:T(8,128)(2,1)S(1)}, bf16[128,1024]{1,0:T(8,128)(2,1)S(1)}, u32[]{:S(2)}, u32[]{:S(2)}) collective-permute-start(bf16[128,1024]{1,0:T(8,128)(2,1)S(1)} %add_convert_fusion.3), channel_id=1, source_target_pairs={{0,2},{1,3},{2,0},{3,1},{4,6},{5,7},{6,4},{7,5},{8,10},{9,11},{10,... | collective-permute-start | bytes 786440 | tf_op jit(solution)/shard_map/ppermute | solution.py:91
  13.6 6.6 %collective-permute-done.1 = bf16[128,1024]{1,0:T(8,128)(2,1)S(1)} collective-permute-done((bf16[128,1024]{1,0:T(8,128)(2,1)S(1)}, bf16[128,1024]{1,0:T(8,128)(2,1)S(1)}, u32[]{:S(2)}, u32[]{:S(2)}) %collective-permute-start.1) | collective-permute-done | bytes 262176 | tf_op jit(solution)/shard_map/ppermute | solution.py:91
  21.0 1.5 %collective-permute-done.2 = bf16[128,1024]{1,0:T(8,128)(2,1)S(1)} collective-permute-done((bf16[128,1024]{1,0:T(8,128)(2,1)S(1)}, bf16[128,1024]{1,0:T(8,128)(2,1)S(1)}, u32[]{:S(2)}, u32[]{:S(2)}) %collective-permute-start.2) | collective-permute-done | bytes 262176 | tf_op jit(solution)/shard_map/ppermute | solution.py:97
  22.7 5.1 %convolution_convert_fusion.1 = bf16[256,1024]{1,0:T(8,128)(2,1)S(1)} fusion(bf16[1024,1024]{1,0:T(8,128)(2,1)S(1)} %copy-done, bf16[256,1024]{1,0:T(8,128)(2,1)S(1)} %maximum_select_fusion, bf16[1024,1024]{1,0:T(8,128)(2,1)} %param.24, f32[1024]{0:T(1024)S(1)} %copy-done.11), kind=kOutput, calls=%fused_computation.10 | convolution fusion | flops 1091305472 | bytes 5246976 | tf_op jit(solution)/shard_map/dot_general | solution.py:145
  29.5 1.8 %collective-permute-start.4 = (bf16[128,1024]{1,0:T(8,128)(2,1)S(1)}, bf16[128,1024]{1,0:T(8,128)(2,1)S(1)}, u32[]{:S(2)}, u32[]{:S(2)}) collective-permute-start(bf16[128,1024]{1,0:T(8,128)(2,1)S(1)} %add_convert_fusion.1), channel_id=1, source_target_pairs={{0,2},{1,3},{2,0},{3,1},{4,6},{5,7},{6,4},{7,5},{8,10},{9,11},{10,... | collective-permute-start | bytes 786440 | tf_op jit(solution)/shard_map/ppermute | solution.py:91
  31.3 6.6 %collective-permute-done.4 = bf16[128,1024]{1,0:T(8,128)(2,1)S(1)} collective-permute-done((bf16[128,1024]{1,0:T(8,128)(2,1)S(1)}, bf16[128,1024]{1,0:T(8,128)(2,1)S(1)}, u32[]{:S(2)}, u32[]{:S(2)}) %collective-permute-start.4) | collective-permute-done | bytes 262176 | tf_op jit(solution)/shard_map/ppermute | solution.py:91
  38.7 1.5 %collective-permute-done.5 = bf16[128,1024]{1,0:T(8,128)(2,1)S(1)} collective-permute-done((bf16[128,1024]{1,0:T(8,128)(2,1)S(1)}, bf16[128,1024]{1,0:T(8,128)(2,1)S(1)}, u32[]{:S(2)}, u32[]{:S(2)}) %collective-permute-start.5) | collective-permute-done | bytes 262176 | tf_op jit(solution)/shard_map/ppermute | solution.py:97
  40.8 1.8 %collective-permute-start.6 = (bf16[16,256]{1,0:T(8,128)(2,1)S(1)}, bf16[16,256]{1,0:T(8,128)(2,1)S(1)}, u32[]{:S(2)}, u32[]{:S(2)}) collective-permute-start(bf16[16,256]{1,0:T(8,128)(2,1)S(1)} %fusion.64), channel_id=1, source_target_pairs={{0,4},{4,0},{8,12},{12,8},{16,20},{20,16},{24,28},{28,24},{1,5},{5... | collective-permute-start | bytes 24584 | tf_op jit(solution)/shard_map/ppermute | solution.py:58
  42.6 1.9 %collective-permute-done.6 = bf16[16,256]{1,0:T(8,128)(2,1)S(1)} collective-permute-done((bf16[16,256]{1,0:T(8,128)(2,1)S(1)}, bf16[16,256]{1,0:T(8,128)(2,1)S(1)}, u32[]{:S(2)}, u32[]{:S(2)}) %collective-permute-start.6) | collective-permute-done | bytes 8224 | tf_op jit(solution)/shard_map/ppermute | solution.py:58
  44.4 1.8 %collective-permute-start.7 = (bf16[32,256]{1,0:T(8,128)(2,1)S(1)}, bf16[32,256]{1,0:T(8,128)(2,1)S(1)}, u32[]{:S(2)}, u32[]{:S(2)}) collective-permute-start(bf16[32,256]{1,0:T(8,128)(2,1)S(1)} %maximum_select_fusion.5), channel_id=1, source_target_pairs={{0,8},{4,12},{8,0},{12,4},{16,24},{20,28},{24,16},{28,20},{1,9},{5... | collective-permute-start | bytes 49160 | tf_op jit(solution)/shard_map/ppermute | solution.py:58
  46.4 1.8 %collective-permute-done.7 = bf16[32,256]{1,0:T(8,128)(2,1)S(1)} collective-permute-done((bf16[32,256]{1,0:T(8,128)(2,1)S(1)}, bf16[32,256]{1,0:T(8,128)(2,1)S(1)}, u32[]{:S(2)}, u32[]{:S(2)}) %collective-permute-start.7) | collective-permute-done | bytes 16416 | tf_op jit(solution)/shard_map/ppermute | solution.py:58
  48.2 2.9 %collective-permute-start.8 = (bf16[64,256]{1,0:T(8,128)(2,1)S(1)}, bf16[64,256]{1,0:T(8,128)(2,1)S(1)}, u32[]{:S(2)}, u32[]{:S(2)}) collective-permute-start(bf16[64,256]{1,0:T(8,128)(2,1)S(1)} %maximum_select_fusion.4), channel_id=1, source_target_pairs={{0,16},{4,20},{8,24},{12,28},{16,0},{20,4},{24,8},{28,12},{1,17},{... | collective-permute-start | bytes 98312 | tf_op jit(solution)/shard_map/ppermute | solution.py:58
  51.2 1.9 %collective-permute-done.8 = bf16[64,256]{1,0:T(8,128)(2,1)S(1)} collective-permute-done((bf16[64,256]{1,0:T(8,128)(2,1)S(1)}, bf16[64,256]{1,0:T(8,128)(2,1)S(1)}, u32[]{:S(2)}, u32[]{:S(2)}) %collective-permute-start.8) | collective-permute-done | bytes 32800 | tf_op jit(solution)/shard_map/ppermute | solution.py:58
  53.1 1.7 %convert_bitcast_fusion = (bf16[16,8,16,128]{3,1,2,0:T(8,128)(2,1)S(1)}, bf16[16,8,16,128]{3,1,2,0:T(8,128)(2,1)S(1)}) fusion(bf16[2048,256]{1,0:T(8,128)(2,1)} %param.30, bf16[64,256]{1,0:T(8,128)(2,1)S(1)} %collective-permute-done.8, bf16[64,256]{1,0:T(8,128)(2,1)S(1)} %maximum_select_fusion.4, pred[]{:T(512)S(6)} %eq.90), kind=kOutput, calls=%fused_computation.87 | convolution fusion | flops 135561216 | bytes 2162689 | tf_op jit(solution)/shard_map/dot_general | solution.py:178
  55.0 2.6 %fusion.1 = f32[128,64,32]{1,2,0:T(8,128)S(1)} fusion(s32[128,64]{1,0:T(8,128)S(1)} %get-tuple-element.7, bf16[128,16,128]{2,1,0:T(8,128)(2,1)S(1)} %bitcast.37, bf16[128,16,128]{2,1,0:T(8,128)(2,1)S(1)} %bitcast.36), kind=kOutput, calls=%fused_computation.2 | convolution fusion | flops 70254592 | bytes 2129920 | tf_op jit(solution)/shard_map/tcb,tab->tca/dot_general | solution.py:192
  58.1 2.9 %collective-permute-start.9 = (f32[64,64]{1,0:T(8,128)S(1)}, f32[64,64]{1,0:T(8,128)S(1)}, u32[]{:S(2)}, u32[]{:S(2)}) collective-permute-start(f32[64,64]{1,0:T(8,128)S(1)} %constant_dynamic-slice_fusion.2), channel_id=1, source_target_pairs={{0,16},{4,20},{8,24},{12,28},{16,0},{20,4},{24,8},{28,12},{1,17},{... | collective-permute-start | bytes 49160 | tf_op jit(solution)/shard_map/ppermute | solution.py:47
  61.1 1.9 %collective-permute-done.9 = f32[64,64]{1,0:T(8,128)S(1)} collective-permute-done((f32[64,64]{1,0:T(8,128)S(1)}, f32[64,64]{1,0:T(8,128)S(1)}, u32[]{:S(2)}, u32[]{:S(2)}) %collective-permute-start.9) | collective-permute-done | bytes 16416 | tf_op jit(solution)/shard_map/ppermute | solution.py:47
  63.0 1.9 %collective-permute-start.10 = (f32[32,64]{1,0:T(8,128)S(1)}, f32[32,64]{1,0:T(8,128)S(1)}, u32[]{:S(2)}, u32[]{:S(2)}) collective-permute-start(f32[32,64]{1,0:T(8,128)S(1)} %constant_dynamic-slice_fusion.1), channel_id=1, source_target_pairs={{0,8},{4,12},{8,0},{12,4},{16,24},{20,28},{24,16},{28,20},{1,9},{5... | collective-permute-start | bytes 24584 | tf_op jit(solution)/shard_map/ppermute | solution.py:47
  64.9 1.9 %collective-permute-done.10 = f32[32,64]{1,0:T(8,128)S(1)} collective-permute-done((f32[32,64]{1,0:T(8,128)S(1)}, f32[32,64]{1,0:T(8,128)S(1)}, u32[]{:S(2)}, u32[]{:S(2)}) %collective-permute-start.10) | collective-permute-done | bytes 8224 | tf_op jit(solution)/shard_map/ppermute | solution.py:47
  66.8 1.8 %collective-permute-start.11 = (f32[16,64]{1,0:T(8,128)S(1)}, f32[16,64]{1,0:T(8,128)S(1)}, u32[]{:S(2)}, u32[]{:S(2)}) collective-permute-start(f32[16,64]{1,0:T(8,128)S(1)} %constant_dynamic-slice_fusion), channel_id=1, source_target_pairs={{0,4},{4,0},{8,12},{12,8},{16,20},{20,16},{24,28},{28,24},{1,5},{5... | collective-permute-start | bytes 12296 | tf_op jit(solution)/shard_map/ppermute | solution.py:47
  68.6 1.9 %collective-permute-done.11 = f32[16,64]{1,0:T(8,128)S(1)} collective-permute-done((f32[16,64]{1,0:T(8,128)S(1)}, f32[16,64]{1,0:T(8,128)S(1)}, u32[]{:S(2)}, u32[]{:S(2)}) %collective-permute-start.11) | collective-permute-done | bytes 4128 | tf_op jit(solution)/shard_map/ppermute | solution.py:47
  71.7 1.7 %collective-permute-start.13 = (f32[16,64]{1,0:T(8,128)S(1)}, f32[16,64]{1,0:T(8,128)S(1)}, u32[]{:S(2)}, u32[]{:S(2)}) collective-permute-start(f32[16,64]{1,0:T(8,128)S(1)} %add.209), channel_id=1, source_target_pairs={{0,2},{1,3},{2,0},{3,1},{4,6},{5,7},{6,4},{7,5},{8,10},{9,11},{10,... | collective-permute-start | bytes 12296 | tf_op jit(solution)/shard_map/ppermute | solution.py:225
  73.4 1.9 %collective-permute-done.13 = f32[16,64]{1,0:T(8,128)S(1)} collective-permute-done((f32[16,64]{1,0:T(8,128)S(1)}, f32[16,64]{1,0:T(8,128)S(1)}, u32[]{:S(2)}, u32[]{:S(2)}) %collective-permute-start.13) | collective-permute-done | bytes 4128 | tf_op jit(solution)/shard_map/ppermute | solution.py:225
  (79 shorter events, 14.1 us)
Async XLA Ops:
  0.6 22.0 %copy-start = (bf16[1024,1024]{1,0:T(8,128)(2,1)S(1)}, bf16[1024,1024]{1,0:T(8,128)(2,1)}, u32[]{:S(2)}) copy-start(bf16[1024,1024]{1,0:T(8,128)(2,1)} %param.26) | copy-start | bytes 6291460
  6.3 13.9 %copy-start.1 = (bf16[256,1024]{1,0:T(8,128)(2,1)S(1)}, bf16[256,1024]{1,0:T(8,128)(2,1)}, u32[]{:S(2)}) copy-start(bf16[256,1024]{1,0:T(8,128)(2,1)} %param.16) | copy-start | bytes 1572868
  6.3 13.9 %copy-start.3 = (f32[1024]{0:T(1024)S(1)}, f32[1024]{0:T(1024)}, u32[]{:S(2)}) copy-start(f32[1024]{0:T(1024)} %param.21) | copy-start | bytes 12292
  6.3 14.3 %copy-start.6 = (f32[1024]{0:T(1024)S(1)}, f32[1024]{0:T(1024)}, u32[]{:S(2)}) copy-start(f32[1024]{0:T(1024)} %param.23) | copy-start | bytes 12292
  6.4 14.3 %copy-start.7 = (f32[1024]{0:T(1024)S(1)}, f32[1024]{0:T(1024)}, u32[]{:S(2)}) copy-start(f32[1024]{0:T(1024)} %param.22) | copy-start | bytes 12292
  7.8 1.8 %collective-permute-start = (bf16[128,1024]{1,0:T(8,128)(2,1)S(1)}, bf16[128,1024]{1,0:T(8,128)(2,1)}, u32[]{:S(2)}, u32[]{:S(2)}) collective-permute-start(bf16[128,1024]{1,0:T(8,128)(2,1)S(1)} %constant_dynamic-slice_fusion.4), channel_id=1, source_target_pairs={{0,1},{1,0},{2,3},{3,2},{4,5},{5,4},{6,7},{7,6},{8,9},{9,8},{10,11... | collective-permute-start | bytes 786440 | tf_op jit(solution)/shard_map/ppermute | solution.py:89
  8.3 14.3 %copy-start.11 = (f32[1024]{0:T(1024)S(1)}, f32[1024]{0:T(1024)}, u32[]{:S(2)}) copy-start(f32[1024]{0:T(1024)} %param.25) | copy-start | bytes 12292
  10.7 9.5 %collective-permute-start.1 = (bf16[128,1024]{1,0:T(8,128)(2,1)S(1)}, bf16[128,1024]{1,0:T(8,128)(2,1)S(1)}, u32[]{:S(2)}, u32[]{:S(2)}) collective-permute-start(bf16[128,1024]{1,0:T(8,128)(2,1)S(1)} %add_convert_fusion.3), channel_id=1, source_target_pairs={{0,2},{1,3},{2,0},{3,1},{4,6},{5,7},{6,4},{7,5},{8,10},{9,11},{10,... | collective-permute-start | bytes 786440 | tf_op jit(solution)/shard_map/ppermute | solution.py:91
  20.9 1.6 %collective-permute-start.2 = (bf16[128,1024]{1,0:T(8,128)(2,1)S(1)}, bf16[128,1024]{1,0:T(8,128)(2,1)S(1)}, u32[]{:S(2)}, u32[]{:S(2)}) collective-permute-start(bf16[128,1024]{1,0:T(8,128)(2,1)S(1)} %add_convert_fusion.2), channel_id=1, source_target_pairs={{0,1},{1,0},{2,3},{3,2},{4,5},{5,4},{6,7},{7,6},{8,9},{9,8},{10,11... | collective-permute-start | bytes 786440 | tf_op jit(solution)/shard_map/ppermute | solution.py:97
  22.6 15.3 %copy-start.4 = (f32[1024]{0:T(1024)S(1)}, f32[1024]{0:T(1024)}, u32[]{:S(2)}) copy-start(f32[1024]{0:T(1024)} %param.27) | copy-start | bytes 12292
  27.8 10.6 %copy-start.8 = (f32[1024]{0:T(1024)S(1)}, f32[1024]{0:T(1024)}, u32[]{:S(2)}) copy-start(f32[1024]{0:T(1024)} %param.29) | copy-start | bytes 12292
  27.8 1.6 %collective-permute-start.3 = (bf16[128,1024]{1,0:T(8,128)(2,1)S(1)}, bf16[128,1024]{1,0:T(8,128)(2,1)S(1)}, u32[]{:S(2)}, u32[]{:S(2)}) collective-permute-start(bf16[128,1024]{1,0:T(8,128)(2,1)S(1)} %constant_dynamic-slice_fusion.3), channel_id=1, source_target_pairs={{0,1},{1,0},{2,3},{3,2},{4,5},{5,4},{6,7},{7,6},{8,9},{9,8},{10,11... | collective-permute-start | bytes 786440 | tf_op jit(solution)/shard_map/ppermute | solution.py:89
  29.5 16.8 %copy-start.5 = (s32[128,64]{0,1:T(8,128)S(1)}, s32[128,64]{0,1:T(8,128)}, u32[]{:S(2)}) copy-start(s32[128,64]{0,1:T(8,128)} %param.31) | copy-start | bytes 98308
  29.5 8.4 %collective-permute-start.4 = (bf16[128,1024]{1,0:T(8,128)(2,1)S(1)}, bf16[128,1024]{1,0:T(8,128)(2,1)S(1)}, u32[]{:S(2)}, u32[]{:S(2)}) collective-permute-start(bf16[128,1024]{1,0:T(8,128)(2,1)S(1)} %add_convert_fusion.1), channel_id=1, source_target_pairs={{0,2},{1,3},{2,0},{3,1},{4,6},{5,7},{6,4},{7,5},{8,10},{9,11},{10,... | collective-permute-start | bytes 786440 | tf_op jit(solution)/shard_map/ppermute | solution.py:91
  38.6 1.6 %collective-permute-start.5 = (bf16[128,1024]{1,0:T(8,128)(2,1)S(1)}, bf16[128,1024]{1,0:T(8,128)(2,1)S(1)}, u32[]{:S(2)}, u32[]{:S(2)}) collective-permute-start(bf16[128,1024]{1,0:T(8,128)(2,1)S(1)} %add_convert_fusion), channel_id=1, source_target_pairs={{0,1},{1,0},{2,3},{3,2},{4,5},{5,4},{6,7},{7,6},{8,9},{9,8},{10,11... | collective-permute-start | bytes 786440 | tf_op jit(solution)/shard_map/ppermute | solution.py:97
  40.4 14.5 %copy-start.2 = (bf16[256,1024]{1,0:T(8,128)(2,1)}, bf16[256,1024]{1,0:T(8,128)(2,1)S(1)}, u32[]{:S(2)}) copy-start(bf16[256,1024]{1,0:T(8,128)(2,1)S(1)} %maximum_select_fusion.1) | copy-start | bytes 1572868
  40.8 3.7 %collective-permute-start.6 = (bf16[16,256]{1,0:T(8,128)(2,1)S(1)}, bf16[16,256]{1,0:T(8,128)(2,1)S(1)}, u32[]{:S(2)}, u32[]{:S(2)}) collective-permute-start(bf16[16,256]{1,0:T(8,128)(2,1)S(1)} %fusion.64), channel_id=1, source_target_pairs={{0,4},{4,0},{8,12},{12,8},{16,20},{20,16},{24,28},{28,24},{1,5},{5... | collective-permute-start | bytes 24584 | tf_op jit(solution)/shard_map/ppermute | solution.py:58
  44.4 3.7 %collective-permute-start.7 = (bf16[32,256]{1,0:T(8,128)(2,1)S(1)}, bf16[32,256]{1,0:T(8,128)(2,1)S(1)}, u32[]{:S(2)}, u32[]{:S(2)}) collective-permute-start(bf16[32,256]{1,0:T(8,128)(2,1)S(1)} %maximum_select_fusion.5), channel_id=1, source_target_pairs={{0,8},{4,12},{8,0},{12,4},{16,24},{20,28},{24,16},{28,20},{1,9},{5... | collective-permute-start | bytes 49160 | tf_op jit(solution)/shard_map/ppermute | solution.py:58
  48.2 4.9 %collective-permute-start.8 = (bf16[64,256]{1,0:T(8,128)(2,1)S(1)}, bf16[64,256]{1,0:T(8,128)(2,1)S(1)}, u32[]{:S(2)}, u32[]{:S(2)}) collective-permute-start(bf16[64,256]{1,0:T(8,128)(2,1)S(1)} %maximum_select_fusion.4), channel_id=1, source_target_pairs={{0,16},{4,20},{8,24},{12,28},{16,0},{20,4},{24,8},{28,12},{1,17},{... | collective-permute-start | bytes 98312 | tf_op jit(solution)/shard_map/ppermute | solution.py:58
  58.1 4.9 %collective-permute-start.9 = (f32[64,64]{1,0:T(8,128)S(1)}, f32[64,64]{1,0:T(8,128)S(1)}, u32[]{:S(2)}, u32[]{:S(2)}) collective-permute-start(f32[64,64]{1,0:T(8,128)S(1)} %constant_dynamic-slice_fusion.2), channel_id=1, source_target_pairs={{0,16},{4,20},{8,24},{12,28},{16,0},{20,4},{24,8},{28,12},{1,17},{... | collective-permute-start | bytes 49160 | tf_op jit(solution)/shard_map/ppermute | solution.py:47
  63.0 3.8 %collective-permute-start.10 = (f32[32,64]{1,0:T(8,128)S(1)}, f32[32,64]{1,0:T(8,128)S(1)}, u32[]{:S(2)}, u32[]{:S(2)}) collective-permute-start(f32[32,64]{1,0:T(8,128)S(1)} %constant_dynamic-slice_fusion.1), channel_id=1, source_target_pairs={{0,8},{4,12},{8,0},{12,4},{16,24},{20,28},{24,16},{28,20},{1,9},{5... | collective-permute-start | bytes 24584 | tf_op jit(solution)/shard_map/ppermute | solution.py:47
  66.8 3.7 %collective-permute-start.11 = (f32[16,64]{1,0:T(8,128)S(1)}, f32[16,64]{1,0:T(8,128)S(1)}, u32[]{:S(2)}, u32[]{:S(2)}) collective-permute-start(f32[16,64]{1,0:T(8,128)S(1)} %constant_dynamic-slice_fusion), channel_id=1, source_target_pairs={{0,4},{4,0},{8,12},{12,8},{16,20},{20,16},{24,28},{28,24},{1,5},{5... | collective-permute-start | bytes 12296 | tf_op jit(solution)/shard_map/ppermute | solution.py:47
  70.5 1.2 %collective-permute-start.12 = (f32[16,64]{1,0:T(8,128)S(1)}, f32[16,64]{1,0:T(8,128)S(1)}, u32[]{:S(2)}, u32[]{:S(2)}) collective-permute-start(f32[16,64]{1,0:T(8,128)S(1)} %dynamic-slice_add_fusion.2), channel_id=1, source_target_pairs={{0,1},{1,0},{2,3},{3,2},{4,5},{5,4},{6,7},{7,6},{8,9},{9,8},{10,11... | collective-permute-start | bytes 12296 | tf_op jit(solution)/shard_map/ppermute | solution.py:225
  71.7 3.7 %collective-permute-start.13 = (f32[16,64]{1,0:T(8,128)S(1)}, f32[16,64]{1,0:T(8,128)S(1)}, u32[]{:S(2)}, u32[]{:S(2)}) collective-permute-start(f32[16,64]{1,0:T(8,128)S(1)} %add.209), channel_id=1, source_target_pairs={{0,2},{1,3},{2,0},{3,1},{4,6},{5,7},{6,4},{7,5},{8,10},{9,11},{10,... | collective-permute-start | bytes 12296 | tf_op jit(solution)/shard_map/ppermute | solution.py:225
  (2 other events, 13.7 us)

commit v18 on v17

--- a/solution.py
+++ b/solution.py
@@ -178,7 +178,7 @@
         tile = lax.dot_general(
             units_block, index, (((1,), (1,)), ((), ())), preferred_element_type=jnp.float32
         )
-        minor = 128
+        minor = 256
         if shard_rows % minor == 0:
             major = shard_rows // minor
             minor_hot = (

time: 76.2 us -> 76.2 us (level)
  no operation moved by 1% of the time
where the time goes in v18:
time: 76.2 us; the launch traced here: 75.9 us
  waiting for transfers between devices  33.3 us (44%)
  starting transfers between devices  20.4 us (27%)
  matrix products  15.8 us (21%)
  other arithmetic  4.1 us (5%)
  local copies, waits for them, and re-layouts  1.22 us (2%)
  between operations  1.06 us (1%)
    ppermute x2, waiting for transfers between devices, settle_by_chip(): across = lax.ppermute(chip_sum, 'tensor', xor_pairs(4, 2))  13.2 us
    ppermute x3, starting transfers between devices, reduce_scatter_xor(): got = lax.ppermute(theirs.astype(wire), axis, xor_pairs(n, k))  6.59 us
    ppermute x3, starting transfers between devices, all_gather_xor(): other = lax.ppermute(cur, axis, xor_pairs(n, k))  6.5 us
    ppermute x3, waiting for transfers between devices, reduce_scatter_xor(): got = lax.ppermute(theirs.astype(wire), axis, xor_pairs(n, k))  5.74 us
    ppermute x3, waiting for transfers between devices, all_gather_xor(): other = lax.ppermute(cur, axis, xor_pairs(n, k))  5.57 us
    dot_general x1, matrix products, body(): jnp.dot(activated, w_down, preferred_element_type=jnp.float32)  5.11 us
    ppermute x2, starting transfers between devices, settle_by_chip(): across = lax.ppermute(chip_sum, 'tensor', xor_pairs(4, 2))  4.74 us
    ppermute x2, waiting for transfers between devices, body(): lax.ppermute(text_scores, 'tensor', xor_pairs(n_tensor, k))  3.08 us
  transfers between devices with their start and end apart: 14, of which 14 were waited for; matrix products, arithmetic and copies ran while one was open for 0% of the time, Pallas kernels for 0%

profile of v18, /device:TPU:0, one launch (start us, length us, event | category | flops | bytes accessed | tf_op | source)
XLA Modules:
  0.0 75.9 jit_solution(4947050341062473328)
XLA Ops:
  0.7 2.3 %fusion.102 = (bf16[3,256,256]{1,2,0:T(8,128)(2,1)S(1)}, f32[3,256,256]{1,2,0:T(8,128)S(1)}) fusion(f32[3,256]{1,0:T(4,128)} %param.19, bf16[3,1024,256]{2,1,0:T(8,128)(2,1)} %param.18, bf16[256,1024]{1,0:T(8,128)(2,1)} %param.16), kind=kOutput, calls=%fused_computation.166 | convolution fusion | flops 403046400 | bytes 3279872 | tf_op jit(solution)/shard_map/td,jdf->jtf/dot_general | solution.py:125
  10.7 2.9 %collective-permute-start.1 = (bf16[128,1024]{1,0:T(8,128)(2,1)S(1)}, bf16[128,1024]{1,0:T(8,128)(2,1)S(1)}, u32[]{:S(2)}, u32[]{:S(2)}) collective-permute-start(bf16[128,1024]{1,0:T(8,128)(2,1)S(1)} %add_convert_fusion.3), channel_id=1, source_target_pairs={{0,2},{1,3},{2,0},{3,1},{4,6},{5,7},{6,4},{7,5},{8,10},{9,11},{10,... | collective-permute-start | bytes 786440 | tf_op jit(solution)/shard_map/ppermute | solution.py:91
  13.6 6.6 %collective-permute-done.1 = bf16[128,1024]{1,0:T(8,128)(2,1)S(1)} collective-permute-done((bf16[128,1024]{1,0:T(8,128)(2,1)S(1)}, bf16[128,1024]{1,0:T(8,128)(2,1)S(1)}, u32[]{:S(2)}, u32[]{:S(2)}) %collective-permute-start.1) | collective-permute-done | bytes 262176 | tf_op jit(solution)/shard_map/ppermute | solution.py:91
  21.0 1.5 %collective-permute-done.2 = bf16[128,1024]{1,0:T(8,128)(2,1)S(1)} collective-permute-done((bf16[128,1024]{1,0:T(8,128)(2,1)S(1)}, bf16[128,1024]{1,0:T(8,128)(2,1)S(1)}, u32[]{:S(2)}, u32[]{:S(2)}) %collective-permute-start.2) | collective-permute-done | bytes 262176 | tf_op jit(solution)/shard_map/ppermute | solution.py:97
  22.7 5.1 %convolution_convert_fusion.1 = bf16[256,1024]{1,0:T(8,128)(2,1)S(1)} fusion(bf16[1024,1024]{1,0:T(8,128)(2,1)S(1)} %copy-done, bf16[256,1024]{1,0:T(8,128)(2,1)S(1)} %maximum_select_fusion, bf16[1024,1024]{1,0:T(8,128)(2,1)} %param.24, f32[1024]{0:T(1024)S(1)} %copy-done.11), kind=kOutput, calls=%fused_computation.10 | convolution fusion | flops 1091305472 | bytes 5246976 | tf_op jit(solution)/shard_map/dot_general | solution.py:145
  29.5 1.8 %collective-permute-start.4 = (bf16[128,1024]{1,0:T(8,128)(2,1)S(1)}, bf16[128,1024]{1,0:T(8,128)(2,1)S(1)}, u32[]{:S(2)}, u32[]{:S(2)}) collective-permute-start(bf16[128,1024]{1,0:T(8,128)(2,1)S(1)} %add_convert_fusion.1), channel_id=1, source_target_pairs={{0,2},{1,3},{2,0},{3,1},{4,6},{5,7},{6,4},{7,5},{8,10},{9,11},{10,... | collective-permute-start | bytes 786440 | tf_op jit(solution)/shard_map/ppermute | solution.py:91
  31.3 6.6 %collective-permute-done.4 = bf16[128,1024]{1,0:T(8,128)(2,1)S(1)} collective-permute-done((bf16[128,1024]{1,0:T(8,128)(2,1)S(1)}, bf16[128,1024]{1,0:T(8,128)(2,1)S(1)}, u32[]{:S(2)}, u32[]{:S(2)}) %collective-permute-start.4) | collective-permute-done | bytes 262176 | tf_op jit(solution)/shard_map/ppermute | solution.py:91
  38.7 1.5 %collective-permute-done.5 = bf16[128,1024]{1,0:T(8,128)(2,1)S(1)} collective-permute-done((bf16[128,1024]{1,0:T(8,128)(2,1)S(1)}, bf16[128,1024]{1,0:T(8,128)(2,1)S(1)}, u32[]{:S(2)}, u32[]{:S(2)}) %collective-permute-start.5) | collective-permute-done | bytes 262176 | tf_op jit(solution)/shard_map/ppermute | solution.py:97
  40.8 1.8 %collective-permute-start.6 = (bf16[16,256]{1,0:T(8,128)(2,1)S(1)}, bf16[16,256]{1,0:T(8,128)(2,1)S(1)}, u32[]{:S(2)}, u32[]{:S(2)}) collective-permute-start(bf16[16,256]{1,0:T(8,128)(2,1)S(1)} %fusion.63), channel_id=1, source_target_pairs={{0,4},{4,0},{8,12},{12,8},{16,20},{20,16},{24,28},{28,24},{1,5},{5... | collective-permute-start | bytes 24584 | tf_op jit(solution)/shard_map/ppermute | solution.py:58
  42.6 1.9 %collective-permute-done.6 = bf16[16,256]{1,0:T(8,128)(2,1)S(1)} collective-permute-done((bf16[16,256]{1,0:T(8,128)(2,1)S(1)}, bf16[16,256]{1,0:T(8,128)(2,1)S(1)}, u32[]{:S(2)}, u32[]{:S(2)}) %collective-permute-start.6) | collective-permute-done | bytes 8224 | tf_op jit(solution)/shard_map/ppermute | solution.py:58
  44.4 1.8 %collective-permute-start.7 = (bf16[32,256]{1,0:T(8,128)(2,1)S(1)}, bf16[32,256]{1,0:T(8,128)(2,1)S(1)}, u32[]{:S(2)}, u32[]{:S(2)}) collective-permute-start(bf16[32,256]{1,0:T(8,128)(2,1)S(1)} %maximum_select_fusion.5), channel_id=1, source_target_pairs={{0,8},{4,12},{8,0},{12,4},{16,24},{20,28},{24,16},{28,20},{1,9},{5... | collective-permute-start | bytes 49160 | tf_op jit(solution)/shard_map/ppermute | solution.py:58
  46.4 1.8 %collective-permute-done.7 = bf16[32,256]{1,0:T(8,128)(2,1)S(1)} collective-permute-done((bf16[32,256]{1,0:T(8,128)(2,1)S(1)}, bf16[32,256]{1,0:T(8,128)(2,1)S(1)}, u32[]{:S(2)}, u32[]{:S(2)}) %collective-permute-start.7) | collective-permute-done | bytes 16416 | tf_op jit(solution)/shard_map/ppermute | solution.py:58
  48.2 2.9 %collective-permute-start.8 = (bf16[64,256]{1,0:T(8,128)(2,1)S(1)}, bf16[64,256]{1,0:T(8,128)(2,1)S(1)}, u32[]{:S(2)}, u32[]{:S(2)}) collective-permute-start(bf16[64,256]{1,0:T(8,128)(2,1)S(1)} %maximum_select_fusion.4), channel_id=1, source_target_pairs={{0,16},{4,20},{8,24},{12,28},{16,0},{20,4},{24,8},{28,12},{1,17},{... | collective-permute-start | bytes 98312 | tf_op jit(solution)/shard_map/ppermute | solution.py:58
  51.2 1.9 %collective-permute-done.8 = bf16[64,256]{1,0:T(8,128)(2,1)S(1)} collective-permute-done((bf16[64,256]{1,0:T(8,128)(2,1)S(1)}, bf16[64,256]{1,0:T(8,128)(2,1)S(1)}, u32[]{:S(2)}, u32[]{:S(2)}) %collective-permute-start.8) | collective-permute-done | bytes 32800 | tf_op jit(solution)/shard_map/ppermute | solution.py:58
  53.1 1.7 %subtract_convert_fusion = (bf16[128,2048]{1,0:T(8,128)(2,1)S(1)}, bf16[128,2048]{1,0:T(8,128)(2,1)S(1)}) fusion(bf16[2048,256]{1,0:T(8,128)(2,1)} %param.30, bf16[64,256]{1,0:T(8,128)(2,1)S(1)} %collective-permute-done.8, bf16[64,256]{1,0:T(8,128)(2,1)S(1)} %maximum_select_fusion.4, pred[]{:T(512)S(6)} %eq.90), kind=kOutput, calls=%fused_computation.21 | convolution fusion | flops 135561216 | bytes 2162689 | tf_op jit(solution)/shard_map/dot_general | solution.py:178
  55.0 2.8 %fusion.1 = f32[128,64,16]{1,2,0:T(8,128)S(1)} fusion(s32[128,64]{1,0:T(8,128)S(1)} %get-tuple-element.7, bf16[128,8,256]{2,1,0:T(8,128)(2,1)S(1)} %bitcast.37, bf16[128,8,256]{2,1,0:T(8,128)(2,1)S(1)} %bitcast.36), kind=kOutput, calls=%fused_computation.2 | convolution fusion | flops 71303168 | bytes 1605632 | tf_op jit(solution)/shard_map/tcb,tab->tca/dot_general | solution.py:192
  58.1 2.9 %collective-permute-start.9 = (f32[64,64]{1,0:T(8,128)S(1)}, f32[64,64]{1,0:T(8,128)S(1)}, u32[]{:S(2)}, u32[]{:S(2)}) collective-permute-start(f32[64,64]{1,0:T(8,128)S(1)} %constant_dynamic-slice_fusion.2), channel_id=1, source_target_pairs={{0,16},{4,20},{8,24},{12,28},{16,0},{20,4},{24,8},{28,12},{1,17},{... | collective-permute-start | bytes 49160 | tf_op jit(solution)/shard_map/ppermute | solution.py:47
  61.0 1.9 %collective-permute-done.9 = f32[64,64]{1,0:T(8,128)S(1)} collective-permute-done((f32[64,64]{1,0:T(8,128)S(1)}, f32[64,64]{1,0:T(8,128)S(1)}, u32[]{:S(2)}, u32[]{:S(2)}) %collective-permute-start.9) | collective-permute-done | bytes 16416 | tf_op jit(solution)/shard_map/ppermute | solution.py:47
  63.0 1.9 %collective-permute-start.10 = (f32[32,64]{1,0:T(8,128)S(1)}, f32[32,64]{1,0:T(8,128)S(1)}, u32[]{:S(2)}, u32[]{:S(2)}) collective-permute-start(f32[32,64]{1,0:T(8,128)S(1)} %constant_dynamic-slice_fusion.1), channel_id=1, source_target_pairs={{0,8},{4,12},{8,0},{12,4},{16,24},{20,28},{24,16},{28,20},{1,9},{5... | collective-permute-start | bytes 24584 | tf_op jit(solution)/shard_map/ppermute | solution.py:47
  64.9 1.9 %collective-permute-done.10 = f32[32,64]{1,0:T(8,128)S(1)} collective-permute-done((f32[32,64]{1,0:T(8,128)S(1)}, f32[32,64]{1,0:T(8,128)S(1)}, u32[]{:S(2)}, u32[]{:S(2)}) %collective-permute-start.10) | collective-permute-done | bytes 8224 | tf_op jit(solution)/shard_map/ppermute | solution.py:47
  66.8 1.8 %collective-permute-start.11 = (f32[16,64]{1,0:T(8,128)S(1)}, f32[16,64]{1,0:T(8,128)S(1)}, u32[]{:S(2)}, u32[]{:S(2)}) collective-permute-start(f32[16,64]{1,0:T(8,128)S(1)} %constant_dynamic-slice_fusion), channel_id=1, source_target_pairs={{0,4},{4,0},{8,12},{12,8},{16,20},{20,16},{24,28},{28,24},{1,5},{5... | collective-permute-start | bytes 12296 | tf_op jit(solution)/shard_map/ppermute | solution.py:47
  68.6 1.9 %collective-permute-done.11 = f32[16,64]{1,0:T(8,128)S(1)} collective-permute-done((f32[16,64]{1,0:T(8,128)S(1)}, f32[16,64]{1,0:T(8,128)S(1)}, u32[]{:S(2)}, u32[]{:S(2)}) %collective-permute-start.11) | collective-permute-done | bytes 4128 | tf_op jit(solution)/shard_map/ppermute | solution.py:47
  71.6 1.7 %collective-permute-start.13 = (f32[16,64]{1,0:T(8,128)S(1)}, f32[16,64]{1,0:T(8,128)S(1)}, u32[]{:S(2)}, u32[]{:S(2)}) collective-permute-start(f32[16,64]{1,0:T(8,128)S(1)} %add.209), channel_id=1, source_target_pairs={{0,2},{1,3},{2,0},{3,1},{4,6},{5,7},{6,4},{7,5},{8,10},{9,11},{10,... | collective-permute-start | bytes 12296 | tf_op jit(solution)/shard_map/ppermute | solution.py:225
  73.4 1.9 %collective-permute-done.13 = f32[16,64]{1,0:T(8,128)S(1)} collective-permute-done((f32[16,64]{1,0:T(8,128)S(1)}, f32[16,64]{1,0:T(8,128)S(1)}, u32[]{:S(2)}, u32[]{:S(2)}) %collective-permute-start.13) | collective-permute-done | bytes 4128 | tf_op jit(solution)/shard_map/ppermute | solution.py:225
  (79 shorter events, 13.9 us)
Async XLA Ops:
  0.6 22.0 %copy-start = (bf16[1024,1024]{1,0:T(8,128)(2,1)S(1)}, bf16[1024,1024]{1,0:T(8,128)(2,1)}, u32[]{:S(2)}) copy-start(bf16[1024,1024]{1,0:T(8,128)(2,1)} %param.26) | copy-start | bytes 6291460
  6.3 13.9 %copy-start.1 = (bf16[256,1024]{1,0:T(8,128)(2,1)S(1)}, bf16[256,1024]{1,0:T(8,128)(2,1)}, u32[]{:S(2)}) copy-start(bf16[256,1024]{1,0:T(8,128)(2,1)} %param.16) | copy-start | bytes 1572868
  6.3 13.9 %copy-start.3 = (f32[1024]{0:T(1024)S(1)}, f32[1024]{0:T(1024)}, u32[]{:S(2)}) copy-start(f32[1024]{0:T(1024)} %param.21) | copy-start | bytes 12292
  6.3 14.3 %copy-start.6 = (f32[1024]{0:T(1024)S(1)}, f32[1024]{0:T(1024)}, u32[]{:S(2)}) copy-start(f32[1024]{0:T(1024)} %param.23) | copy-start | bytes 12292
  6.4 14.3 %copy-start.7 = (f32[1024]{0:T(1024)S(1)}, f32[1024]{0:T(1024)}, u32[]{:S(2)}) copy-start(f32[1024]{0:T(1024)} %param.22) | copy-start | bytes 12292
  7.8 1.8 %collective-permute-start = (bf16[128,1024]{1,0:T(8,128)(2,1)S(1)}, bf16[128,1024]{1,0:T(8,128)(2,1)}, u32[]{:S(2)}, u32[]{:S(2)}) collective-permute-start(bf16[128,1024]{1,0:T(8,128)(2,1)S(1)} %constant_dynamic-slice_fusion.4), channel_id=1, source_target_pairs={{0,1},{1,0},{2,3},{3,2},{4,5},{5,4},{6,7},{7,6},{8,9},{9,8},{10,11... | collective-permute-start | bytes 786440 | tf_op jit(solution)/shard_map/ppermute | solution.py:89
  8.3 14.3 %copy-start.11 = (f32[1024]{0:T(1024)S(1)}, f32[1024]{0:T(1024)}, u32[]{:S(2)}) copy-start(f32[1024]{0:T(1024)} %param.25) | copy-start | bytes 12292
  10.7 9.5 %collective-permute-start.1 = (bf16[128,1024]{1,0:T(8,128)(2,1)S(1)}, bf16[128,1024]{1,0:T(8,128)(2,1)S(1)}, u32[]{:S(2)}, u32[]{:S(2)}) collective-permute-start(bf16[128,1024]{1,0:T(8,128)(2,1)S(1)} %add_convert_fusion.3), channel_id=1, source_target_pairs={{0,2},{1,3},{2,0},{3,1},{4,6},{5,7},{6,4},{7,5},{8,10},{9,11},{10,... | collective-permute-start | bytes 786440 | tf_op jit(solution)/shard_map/ppermute | solution.py:91
  20.9 1.6 %collective-permute-start.2 = (bf16[128,1024]{1,0:T(8,128)(2,1)S(1)}, bf16[128,1024]{1,0:T(8,128)(2,1)S(1)}, u32[]{:S(2)}, u32[]{:S(2)}) collective-permute-start(bf16[128,1024]{1,0:T(8,128)(2,1)S(1)} %add_convert_fusion.2), channel_id=1, source_target_pairs={{0,1},{1,0},{2,3},{3,2},{4,5},{5,4},{6,7},{7,6},{8,9},{9,8},{10,11... | collective-permute-start | bytes 786440 | tf_op jit(solution)/shard_map/ppermute | solution.py:97
  22.6 15.3 %copy-start.4 = (f32[1024]{0:T(1024)S(1)}, f32[1024]{0:T(1024)}, u32[]{:S(2)}) copy-start(f32[1024]{0:T(1024)} %param.27) | copy-start | bytes 12292
  27.8 10.6 %copy-start.8 = (f32[1024]{0:T(1024)S(1)}, f32[1024]{0:T(1024)}, u32[]{:S(2)}) copy-start(f32[1024]{0:T(1024)} %param.29) | copy-start | bytes 12292
  27.8 1.6 %collective-permute-start.3 = (bf16[128,1024]{1,0:T(8,128)(2,1)S(1)}, bf16[128,1024]{1,0:T(8,128)(2,1)S(1)}, u32[]{:S(2)}, u32[]{:S(2)}) collective-permute-start(bf16[128,1024]{1,0:T(8,128)(2,1)S(1)} %constant_dynamic-slice_fusion.3), channel_id=1, source_target_pairs={{0,1},{1,0},{2,3},{3,2},{4,5},{5,4},{6,7},{7,6},{8,9},{9,8},{10,11... | collective-permute-start | bytes 786440 | tf_op jit(solution)/shard_map/ppermute | solution.py:89
  29.5 16.8 %copy-start.5 = (s32[128,64]{0,1:T(8,128)S(1)}, s32[128,64]{0,1:T(8,128)}, u32[]{:S(2)}) copy-start(s32[128,64]{0,1:T(8,128)} %param.31) | copy-start | bytes 98308
  29.5 8.4 %collective-permute-start.4 = (bf16[128,1024]{1,0:T(8,128)(2,1)S(1)}, bf16[128,1024]{1,0:T(8,128)(2,1)S(1)}, u32[]{:S(2)}, u32[]{:S(2)}) collective-permute-start(bf16[128,1024]{1,0:T(8,128)(2,1)S(1)} %add_convert_fusion.1), channel_id=1, source_target_pairs={{0,2},{1,3},{2,0},{3,1},{4,6},{5,7},{6,4},{7,5},{8,10},{9,11},{10,... | collective-permute-start | bytes 786440 | tf_op jit(solution)/shard_map/ppermute | solution.py:91
  38.6 1.6 %collective-permute-start.5 = (bf16[128,1024]{1,0:T(8,128)(2,1)S(1)}, bf16[128,1024]{1,0:T(8,128)(2,1)S(1)}, u32[]{:S(2)}, u32[]{:S(2)}) collective-permute-start(bf16[128,1024]{1,0:T(8,128)(2,1)S(1)} %add_convert_fusion), channel_id=1, source_target_pairs={{0,1},{1,0},{2,3},{3,2},{4,5},{5,4},{6,7},{7,6},{8,9},{9,8},{10,11... | collective-permute-start | bytes 786440 | tf_op jit(solution)/shard_map/ppermute | solution.py:97
  40.4 14.5 %copy-start.2 = (bf16[256,1024]{1,0:T(8,128)(2,1)}, bf16[256,1024]{1,0:T(8,128)(2,1)S(1)}, u32[]{:S(2)}) copy-start(bf16[256,1024]{1,0:T(8,128)(2,1)S(1)} %maximum_select_fusion.1) | copy-start | bytes 1572868
  40.8 3.7 %collective-permute-start.6 = (bf16[16,256]{1,0:T(8,128)(2,1)S(1)}, bf16[16,256]{1,0:T(8,128)(2,1)S(1)}, u32[]{:S(2)}, u32[]{:S(2)}) collective-permute-start(bf16[16,256]{1,0:T(8,128)(2,1)S(1)} %fusion.63), channel_id=1, source_target_pairs={{0,4},{4,0},{8,12},{12,8},{16,20},{20,16},{24,28},{28,24},{1,5},{5... | collective-permute-start | bytes 24584 | tf_op jit(solution)/shard_map/ppermute | solution.py:58
  44.4 3.7 %collective-permute-start.7 = (bf16[32,256]{1,0:T(8,128)(2,1)S(1)}, bf16[32,256]{1,0:T(8,128)(2,1)S(1)}, u32[]{:S(2)}, u32[]{:S(2)}) collective-permute-start(bf16[32,256]{1,0:T(8,128)(2,1)S(1)} %maximum_select_fusion.5), channel_id=1, source_target_pairs={{0,8},{4,12},{8,0},{12,4},{16,24},{20,28},{24,16},{28,20},{1,9},{5... | collective-permute-start | bytes 49160 | tf_op jit(solution)/shard_map/ppermute | solution.py:58
  48.2 4.9 %collective-permute-start.8 = (bf16[64,256]{1,0:T(8,128)(2,1)S(1)}, bf16[64,256]{1,0:T(8,128)(2,1)S(1)}, u32[]{:S(2)}, u32[]{:S(2)}) collective-permute-start(bf16[64,256]{1,0:T(8,128)(2,1)S(1)} %maximum_select_fusion.4), channel_id=1, source_target_pairs={{0,16},{4,20},{8,24},{12,28},{16,0},{20,4},{24,8},{28,12},{1,17},{... | collective-permute-start | bytes 98312 | tf_op jit(solution)/shard_map/ppermute | solution.py:58
  58.1 4.9 %collective-permute-start.9 = (f32[64,64]{1,0:T(8,128)S(1)}, f32[64,64]{1,0:T(8,128)S(1)}, u32[]{:S(2)}, u32[]{:S(2)}) collective-permute-start(f32[64,64]{1,0:T(8,128)S(1)} %constant_dynamic-slice_fusion.2), channel_id=1, source_target_pairs={{0,16},{4,20},{8,24},{12,28},{16,0},{20,4},{24,8},{28,12},{1,17},{... | collective-permute-start | bytes 49160 | tf_op jit(solution)/shard_map/ppermute | solution.py:47
  63.0 3.8 %collective-permute-start.10 = (f32[32,64]{1,0:T(8,128)S(1)}, f32[32,64]{1,0:T(8,128)S(1)}, u32[]{:S(2)}, u32[]{:S(2)}) collective-permute-start(f32[32,64]{1,0:T(8,128)S(1)} %constant_dynamic-slice_fusion.1), channel_id=1, source_target_pairs={{0,8},{4,12},{8,0},{12,4},{16,24},{20,28},{24,16},{28,20},{1,9},{5... | collective-permute-start | bytes 24584 | tf_op jit(solution)/shard_map/ppermute | solution.py:47
  66.8 3.7 %collective-permute-start.11 = (f32[16,64]{1,0:T(8,128)S(1)}, f32[16,64]{1,0:T(8,128)S(1)}, u32[]{:S(2)}, u32[]{:S(2)}) collective-permute-start(f32[16,64]{1,0:T(8,128)S(1)} %constant_dynamic-slice_fusion), channel_id=1, source_target_pairs={{0,4},{4,0},{8,12},{12,8},{16,20},{20,16},{24,28},{28,24},{1,5},{5... | collective-permute-start | bytes 12296 | tf_op jit(solution)/shard_map/ppermute | solution.py:47
  70.5 1.2 %collective-permute-start.12 = (f32[16,64]{1,0:T(8,128)S(1)}, f32[16,64]{1,0:T(8,128)S(1)}, u32[]{:S(2)}, u32[]{:S(2)}) collective-permute-start(f32[16,64]{1,0:T(8,128)S(1)} %dynamic-slice_add_fusion.2), channel_id=1, source_target_pairs={{0,1},{1,0},{2,3},{3,2},{4,5},{5,4},{6,7},{7,6},{8,9},{9,8},{10,11... | collective-permute-start | bytes 12296 | tf_op jit(solution)/shard_map/ppermute | solution.py:225
  71.6 3.7 %collective-permute-start.13 = (f32[16,64]{1,0:T(8,128)S(1)}, f32[16,64]{1,0:T(8,128)S(1)}, u32[]{:S(2)}, u32[]{:S(2)}) collective-permute-start(f32[16,64]{1,0:T(8,128)S(1)} %add.209), channel_id=1, source_target_pairs={{0,2},{1,3},{2,0},{3,1},{4,6},{5,7},{6,4},{7,5},{8,10},{9,11},{10,... | collective-permute-start | bytes 12296 | tf_op jit(solution)/shard_map/ppermute | solution.py:225
  (2 other events, 13.7 us)
